TPU v7x, 128 devices: a whole 4x4x4 slice. The times are simulated.
128 devices in a mesh: gx: 4 (over x), gy: 32 (over z, y, core).
Axes of the slice: x: 4, y: 4, z: 4, core: 2. Of those that a mesh axis runs over, the one named last changes fastest.
Arguments:
- src_points: bfloat16 [128, 1024, 128], P('gx'), may hold values from -0.47729708 to 0.47729708
- tgt_points: bfloat16 [128, 1024, 128], P(('gx', 'gy')), may hold values from -0.47729708 to 0.47729708
- src_log_mass: float32 [128, 1024], P('gx'), may hold values from -1 to 1
- tgt_log_mass: float32 [128, 1024], P(('gx', 'gy')), may hold values from -1 to 1
- near_pairs: int32 [768, 2], P(('gx', 'gy')), may hold values from 0 to 127, as said below
- target_slot: int32 [128], replicated, may hold values from 0 to 127, as said below
Outputs:
- f_pot: float32 [128, 1024], P('gx')
- g_pot: float32 [128, 1024], P(('gx', 'gy'))
- grad: float32 [128, 1024, 128], P(('gx', 'gy'))
Inputs may be any that keep to these rules, and one draw needn't show every extreme that they name: `near_pairs`: row p belongs to the block p // 6 = a 32 + b. Its source cluster s satisfies s // 32 = a and (s % 32) // 1 lies in b - 2 to b + 2; the slot of its target cluster, target_slot of it, is held by a device of gy index b and gx index a - 1, a or a + 1 (slot = gx index 32 + gy index). No pair stands twice. Every source cluster and every target cluster is in some pair. `target_slot`: A permutation; each target cluster's slot has the same value of // 32 as the cluster's number.
All inputs are finite; a program needn't handle non-finite values.
Results may differ from a plain program's by a relative error of at most 0.00099.
Values may be sent and summed in bfloat16 or wider, within the bound.
No kernel may reach another device: no remote copies, remote signals or barrier semaphores. Data moves between devices by JAX's collectives and lax.ppermute only.
A program may use at most 64 MiB of HBM per device.

v0:
```python
import jax
import jax.numpy as jnp
from jax import lax
from jax.sharding import PartitionSpec as P

ITERS = 3


EPSILON = 0.03
EMPTY_LOG = -1e30


def padded(block, sides, width):
    for axis, dim in sides:
        count = lax.axis_size(axis)
        forward = [(i, i + 1) for i in range(count - 1)]
        backward = [(target, source) for source, target in forward]
        low = lax.ppermute(
            lax.slice_in_dim(block, block.shape[dim] - width, None, axis=dim), axis, forward
        )
        high = lax.ppermute(lax.slice_in_dim(block, 0, width, axis=dim), axis, backward)
        block = jnp.concatenate([low, block, high], axis=dim)
    return block


def passed_along(block, axis, distance):
    devices = range(lax.axis_size(axis))
    route = [(i - distance, i) for i in devices if i - distance in devices]
    return lax.ppermute(block, axis, route)


def log_add(first, second):
    peak_val = jnp.maximum(first, second)
    return peak_val + jnp.log(jnp.exp(first - peak_val) + jnp.exp(second - peak_val))


def pick(table, position):
    return lax.dynamic_index_in_dim(table, position, 0, keepdims=False)


def cost_tile(src_rows, tgt_rows, src_sq, tgt_sq):
    inner = lax.dot_general(
        src_rows, tgt_rows, (((1,), (1,)), ((), ())), preferred_element_type=jnp.float32
    )
    return 0.5 * (src_sq[:, None] + tgt_sq[None, :]) - inner


def squares(points):
    return jnp.sum(jnp.square(points.astype(jnp.float32)), axis=-1)


def fetch_points(tgt_points):
    window_pts = padded(tgt_points, (("gx", 0),), tgt_points.shape[0])
    return (window_pts, squares(window_pts))


def fetch_potential(g_local):
    return padded(g_local, (("gx", 0),), g_local.shape[0])


def body(src_points, tgt_points, src_log_mass, tgt_log_mass, near_pairs, target_slot):
    owned = tgt_points.shape[0]
    group_size = src_points.shape[0]
    cluster_pts = src_points.shape[1]
    coords = src_points.shape[2]
    gx_count = lax.axis_size("gx")
    gy_count = lax.axis_size("gy")
    gx_index = lax.axis_index("gx")
    gy_index = lax.axis_index("gy")
    source_local = near_pairs[:, 0] - gx_index * group_size
    matches = (
        near_pairs[:, 1][:, None] == jnp.arange(target_slot.shape[0], dtype=jnp.int32)[None, :]
    )
    slot_ids = jnp.sum(jnp.where(matches, target_slot[None, :], 0), axis=1)
    window_ids = (slot_ids // owned // gy_count - gx_index + 1) * owned + slot_ids % owned
    pair_order = jnp.arange(near_pairs.shape[0], dtype=jnp.int32)
    src_sq = squares(src_points)
    g_local = jnp.zeros((owned, cluster_pts), jnp.float32)
    g_window = jnp.zeros((3 * owned, cluster_pts), jnp.float32)
    f_pot = jnp.zeros((group_size, cluster_pts), jnp.float32)
    for sweep_index in range(ITERS):
        window_pts, window_sq = fetch_points(tgt_points)
        if sweep_index > 0:
            g_window = fetch_potential(g_local)

        def row_update(running, pair_index):
            source = source_local[pair_index]
            target = window_ids[pair_index]
            costs = cost_tile(
                pick(src_points, source),
                pick(window_pts, target),
                pick(src_sq, source),
                pick(window_sq, target),
            )
            scores = (pick(g_window, target)[None, :] - costs) / EPSILON
            peak_val = jnp.max(scores, axis=1)
            partial_value = peak_val + jnp.log(jnp.sum(jnp.exp(scores - peak_val[:, None]), axis=1))
            current = pick(running, source)
            return (
                lax.dynamic_update_index_in_dim(
                    running, log_add(current, partial_value), source, 0
                ),
                None,
            )

        rows_part = lax.scan(
            row_update, jnp.full((group_size, cluster_pts), EMPTY_LOG, jnp.float32), pair_order
        )[0]
        row_peak = lax.pmax(rows_part, "gy")
        row_sums = lax.psum(jnp.exp(rows_part - row_peak), "gy")
        rows_total = row_peak + jnp.log(row_sums)
        f_pot = EPSILON * src_log_mass - EPSILON * rows_total

        def column_update(running, pair_index):
            source = source_local[pair_index]
            target = window_ids[pair_index]
            costs = cost_tile(
                pick(src_points, source),
                pick(window_pts, target),
                pick(src_sq, source),
                pick(window_sq, target),
            )
            scores = (pick(f_pot, source)[:, None] - costs) / EPSILON
            peak_val = jnp.max(scores, axis=0)
            partial_value = peak_val + jnp.log(jnp.sum(jnp.exp(scores - peak_val[None, :]), axis=0))
            current = pick(running, target)
            return (
                lax.dynamic_update_index_in_dim(
                    running, log_add(current, partial_value), target, 0
                ),
                None,
            )

        cols_part = lax.scan(
            column_update, jnp.full((3 * owned, cluster_pts), EMPTY_LOG, jnp.float32), pair_order
        )[0]
        from_left = passed_along(cols_part[2 * owned :], "gx", 1)
        from_right = passed_along(cols_part[:owned], "gx", -1)
        from_left = jnp.where(gx_index > 0, from_left, EMPTY_LOG)
        from_right = jnp.where(gx_index < gx_count - 1, from_right, EMPTY_LOG)
        cols_total = log_add(log_add(cols_part[owned : 2 * owned], from_left), from_right)
        g_local = EPSILON * tgt_log_mass - EPSILON * cols_total
    window_pts, window_sq = fetch_points(tgt_points)
    g_window = fetch_potential(g_local)
    span_rows = 5 * owned
    span_ids = source_local - (gy_index - 2) * owned

    def grad_update(totals, pair_index):
        source = source_local[pair_index]
        row = span_ids[pair_index]
        target = window_ids[pair_index]
        tgt_rows = pick(window_pts, target)
        costs = cost_tile(
            pick(src_points, source), tgt_rows, pick(src_sq, source), pick(window_sq, target)
        )
        weights = jnp.exp(
            (pick(f_pot, source)[:, None] + pick(g_window, target)[None, :] - costs) / EPSILON
        )
        mass_sum, moved = totals
        mass_sum = lax.dynamic_update_index_in_dim(
            mass_sum, pick(mass_sum, row) + jnp.sum(weights, axis=1), row, 0
        )
        product = jnp.dot(
            weights.astype(jnp.bfloat16), tgt_rows, preferred_element_type=jnp.float32
        )
        moved = lax.dynamic_update_index_in_dim(moved, pick(moved, row) + product, row, 0)
        return ((mass_sum, moved), None)

    start_vals = (
        jnp.zeros((span_rows, cluster_pts), jnp.float32),
        jnp.zeros((span_rows, cluster_pts, coords), jnp.float32),
    )
    mass_sum, moved = lax.scan(grad_update, start_vals, pair_order)[0]
    padding = jnp.zeros((2 * owned, cluster_pts, coords), src_points.dtype)
    padded_src = jnp.concatenate([padding, src_points, padding], axis=0)
    window_src = lax.dynamic_slice_in_dim(padded_src, gy_index * owned, span_rows, 0)
    span_parts = mass_sum[:, :, None] * window_src.astype(jnp.float32) - moved
    grad = span_parts[2 * owned : 3 * owned]
    for distance in (1, 2):
        upper = passed_along(
            span_parts[(2 - distance) * owned : (3 - distance) * owned], "gy", -distance
        )
        lower = passed_along(
            span_parts[(2 + distance) * owned : (3 + distance) * owned], "gy", distance
        )
        grad = grad + upper + lower
    return (f_pot, g_local, grad)


def solution(mesh):
    in_specs = (
        P("gx", None, None),
        P(("gx", "gy"), None, None),
        P("gx", None),
        P(("gx", "gy"), None),
        P(("gx", "gy"), None),
        P(),
    )
    out_specs = (P("gx", None), P(("gx", "gy"), None), P(("gx", "gy"), None, None))
    return jax.shard_map(body, mesh=mesh, in_specs=in_specs, out_specs=out_specs, check_vma=False)
```

profile of v0, /device:TPU:1, one launch (start us, length us, event | category | flops | bytes accessed | tf_op | source)
XLA Modules:
  0.0 1277.8 jit_solution(10727719089545220448)
XLA Ops:
  7.2 4.0 collective-permute-start
  13.2 7.8 multiply_reduce_fusion
  22.5 66.5 %while.72 = (s32[]{:T(128)}, f32[32,1024]{1,0:T(8,128)S(1)}, s32[6]{0:T(128)S(1)}, s32[6]{0:T(128)S(1)}, f32[32,1024]{1,0:T(8,128)S(1)}, /*index=5*/s32[6]{0:T(1...) while((s32[]{:T(128)}, f32[32,1024]{1,0:T(8,128)S(1)}, ...), condition=%wide.region_6.7_spmd, body=%wide.region_3.6_spmd.sunk | while | flops 282071040 | bytes 8991023 | solution.py:106
  89.7 105.4 %all-reduce.7.cloned.1.call-done = f32[32,1024]{1,0:T(8,128)} async-done(((f32[32,1024]{1,0:T(8,128)}), f32[32,1024]{1,0:T(8,128)}) %all-reduce.7.cloned.1.call-update) | async-done | bytes 131088 | tf_op jit(solution)/shard_map/pmax | solution.py:109
  196.8 102.8 %all-reduce.9.cloned.1.call-done = f32[32,1024]{1,0:T(8,128)} async-done(((f32[32,1024]{1,0:T(8,128)}), f32[32,1024]{1,0:T(8,128)}) %all-reduce.9.cloned.1.call-update) | async-done | bytes 131088 | tf_op jit(solution)/shard_map/psum | solution.py:110
  300.7 68.5 %while.73 = (s32[]{:T(128)}, f32[3,1024]{1,0:T(4,128)S(1)}, s32[6]{0:T(128)S(1)}, s32[6]{0:T(128)S(1)}, s32[6]{0:T(128)S(1)}, /*index=5*/f32[32,1024]{1,0:T(8,12...) while((s32[]{:T(128)}, f32[3,1024]{1,0:T(4,128)S(1)}, ...), condition=%wide.region_12.13_spmd, body=%wide.region_9.12_spmd.sunk | while | flops 282071040 | bytes 9007419 | solution.py:134
  370.5 4.0 collective-permute-start.2
  376.6 4.4 collective-permute-start.4
  381.6 68.8 %while.74 = (s32[]{:T(128)}, f32[32,1024]{1,0:T(8,128)S(1)}, s32[6]{0:T(128)S(1)}, s32[6]{0:T(128)S(1)}, s32[6]{0:T(128)S(1)}, /*index=5*/f32[3,1024]{1,0:T(4,12...) while((s32[]{:T(128)}, f32[32,1024]{1,0:T(8,128)S(1)}, ...), condition=%wide.region_16.17_spmd, body=%wide.region_13.16_spmd.sunk | while | flops 282071040 | bytes 9007419 | solution.py:106
  451.1 104.1 %all-reduce.11.cloned.1.call-done = f32[32,1024]{1,0:T(8,128)} async-done(((f32[32,1024]{1,0:T(8,128)}), f32[32,1024]{1,0:T(8,128)}) %all-reduce.11.cloned.1.call-update) | async-done | bytes 131088 | tf_op jit(solution)/shard_map/pmax | solution.py:109
  556.9 102.7 %all-reduce.13.cloned.1.call-done = f32[32,1024]{1,0:T(8,128)} async-done(((f32[32,1024]{1,0:T(8,128)}), f32[32,1024]{1,0:T(8,128)}) %all-reduce.13.cloned.1.call-update) | async-done | bytes 131088 | tf_op jit(solution)/shard_map/psum | solution.py:110
  660.6 68.6 %while.75 = (s32[]{:T(128)}, f32[3,1024]{1,0:T(4,128)S(1)}, s32[6]{0:T(128)S(1)}, s32[6]{0:T(128)S(1)}, s32[6]{0:T(128)S(1)}, /*index=5*/f32[32,1024]{1,0:T(8,12...) while((s32[]{:T(128)}, f32[3,1024]{1,0:T(4,128)S(1)}, ...), condition=%wide.region_22.23_spmd, body=%wide.region_19.22_spmd.sunk | while | flops 282071040 | bytes 9007419 | solution.py:134
  730.5 4.0 collective-permute-start.6
  736.6 4.2 collective-permute-start.8
  741.6 68.8 %while.76 = (s32[]{:T(128)}, f32[32,1024]{1,0:T(8,128)S(1)}, s32[6]{0:T(128)S(1)}, s32[6]{0:T(128)S(1)}, s32[6]{0:T(128)S(1)}, /*index=5*/f32[3,1024]{1,0:T(4,12...) while((s32[]{:T(128)}, f32[32,1024]{1,0:T(8,128)S(1)}, ...), condition=%wide.region_26.27_spmd, body=%wide.region_23.26_spmd.sunk | while | flops 282071040 | bytes 9007419 | solution.py:106
  811.1 104.1 %all-reduce.15.cloned.1.call-done = f32[32,1024]{1,0:T(8,128)} async-done(((f32[32,1024]{1,0:T(8,128)}), f32[32,1024]{1,0:T(8,128)}) %all-reduce.15.cloned.1.call-update) | async-done | bytes 131088 | tf_op jit(solution)/shard_map/pmax | solution.py:109
  916.9 102.7 %all-reduce.17.cloned.1.call-done = f32[32,1024]{1,0:T(8,128)} async-done(((f32[32,1024]{1,0:T(8,128)}), f32[32,1024]{1,0:T(8,128)}) %all-reduce.17.cloned.1.call-update) | async-done | bytes 131088 | tf_op jit(solution)/shard_map/psum | solution.py:110
  1020.6 68.5 %while.77 = (s32[]{:T(128)}, f32[3,1024]{1,0:T(4,128)S(1)}, s32[6]{0:T(128)S(1)}, s32[6]{0:T(128)S(1)}, s32[6]{0:T(128)S(1)}, /*index=5*/f32[32,1024]{1,0:T(8,12...) while((s32[]{:T(128)}, f32[3,1024]{1,0:T(4,128)S(1)}, ...), condition=%wide.region_32.33_spmd, body=%wide.region_29.32_spmd.sunk | while | flops 282071040 | bytes 9007419 | solution.py:134
  1090.5 4.0 collective-permute-start.10
  1096.6 4.5 collective-permute-start.12
  1103.5 140.3 %while.78 = (s32[]{:T(128)}, f32[5,1024]{1,0:T(8,128)}, f32[5,1024,128]{2,1,0:T(8,128)S(1)}, s32[6]{0:T(128)}, s32[6]{0:T(128)}, /*index=5*/s32[6]{0:T(128)}, f3...) while((s32[]{:T(128)}, f32[5,1024]{1,0:T(8,128)}, ...), condition=%wide.region_35.36_spmd, body=%wide.region_33.35_spmd.sunk | while | flops 551682048 | bytes 11428485 | solution.py:173
  1113.3 4.4 fusion.105
  1136.7 4.4 fusion.105
  1146.5 3.8 fusion.106
  1160.1 4.4 fusion.105
  1183.5 4.4 fusion.105
  1206.9 4.4 fusion.105
  1230.3 4.4 fusion.105
  1240.1 3.8 fusion.106
  1250.1 7.1 collective-permute-start.15
  1261.2 4.9 collective-permute-done.15
  1266.1 3.8 collective-permute-done.14
  (576 shorter events, 299.1 us)
Async XLA Ops:
  7.2 187.9 %all-reduce.7.cloned.1.call-start = ((), (), s32[]{:S(2)}) async-start(), calls=%async_computation | async-start | bytes 262144 | tf_op jit(solution)/shard_map/pmax | solution.py:109
  7.2 14.6 %collective-permute-start = (bf16[1,1024,128]{2,1,0:T(8,128)(2,1)}, bf16[1,1024,128]{2,1,0:T(8,128)(2,1)S(1)}, u32[]{:S(2)}, u32[]{:S(2)}) collective-permute-start(bf16[1,1024,128]{2,1,0:T(8,128)(2,1)} %param.21), channel_id=1, source_target_pairs={{0,32},{32,64},{64,96},{1,33},{33,65},{65,97},{2,34},{34,66},{66,9... | collective-permute-start | bytes 786440 | tf_op jit(solution)/shard_map/ppermute | solution.py:18
  11.2 10.7 collective-permute-start.1
  13.2 7.8 copy-start.14
  13.2 8.4 copy-start.15
  13.2 8.7 copy-start.4
  22.5 277.2 %copy-start.3 = (f32[32,1024]{1,0:T(8,128)S(1)}, f32[32,1024]{1,0:T(8,128)}, u32[]{:S(2)}) copy-start(f32[32,1024]{1,0:T(8,128)} %param.22) | copy-start | bytes 393220
  89.7 209.9 %all-reduce.9.cloned.1.call-start = ((), (), s32[]{:S(2)}) async-start(), calls=%async_computation.1 | async-start | bytes 262144 | tf_op jit(solution)/shard_map/psum | solution.py:110
  196.8 358.4 %all-reduce.11.cloned.1.call-start = ((), (), s32[]{:S(2)}) async-start(), calls=%async_computation.2 | async-start | bytes 262144 | tf_op jit(solution)/shard_map/pmax | solution.py:109
  300.7 74.5 %copy-start.10 = (f32[1,1024]{1,0:T(1,128)S(1)}, f32[1,1024]{1,0:T(1,128)}, u32[]{:S(2)}) copy-start(f32[1,1024]{1,0:T(1,128)} %param.23) | copy-start | bytes 12292
  369.2 5.3 collective-permute-start.3
  370.5 4.7 collective-permute-start.2
  375.3 5.7 collective-permute-start.5
  376.6 5.0 collective-permute-start.4
  451.0 208.6 %all-reduce.13.cloned.1.call-start = ((), (), s32[]{:S(2)}) async-start(), calls=%async_computation.3 | async-start | bytes 262144 | tf_op jit(solution)/shard_map/psum | solution.py:110
  556.9 358.3 %all-reduce.15.cloned.1.call-start = ((), (), s32[]{:S(2)}) async-start(), calls=%async_computation.4 | async-start | bytes 262144 | tf_op jit(solution)/shard_map/pmax | solution.py:109
  729.2 5.3 collective-permute-start.7
  730.5 4.7 collective-permute-start.6
  735.3 5.5 collective-permute-start.9
  736.6 5.0 collective-permute-start.8
  811.1 208.5 %all-reduce.17.cloned.1.call-start = ((), (), s32[]{:S(2)}) async-start(), calls=%async_computation.5 | async-start | bytes 262144 | tf_op jit(solution)/shard_map/psum | solution.py:110
  1089.1 13.6 %copy-start.5 = (f32[32,1024]{1,0:T(8,128)}, f32[32,1024]{1,0:T(8,128)S(1)}, u32[]{:S(2)}) copy-start(f32[32,1024]{1,0:T(8,128)S(1)} %get-tuple-element.1453) | copy-start | bytes 393220
  1089.1 13.6 %copy-start.13 = (s32[6]{0:T(128)}, s32[6]{0:T(128)S(1)}, u32[]{:S(2)}) copy-start(s32[6]{0:T(128)S(1)} %get-tuple-element.1487) | copy-start | bytes 76
  1089.1 13.6 %copy-start.16 = (s32[6]{0:T(128)}, s32[6]{0:T(128)S(1)}, u32[]{:S(2)}) copy-start(s32[6]{0:T(128)S(1)} %get-tuple-element.1493) | copy-start | bytes 76
  1089.2 5.3 collective-permute-start.11
  1090.5 4.7 collective-permute-start.10
  1095.3 5.8 collective-permute-start.13
  1096.6 5.0 collective-permute-start.12
  1246.1 13.1 %collective-permute-start.17 = (f32[1,1024,128]{2,1,0:T(8,128)S(1)}, f32[1,1024,128]{2,1,0:T(8,128)S(1)}, u32[]{:S(2)}, u32[]{:S(2)}) collective-permute-start(f32[1,1024,128]{2,1,0:T(8,128)S(1)} %get-tuple-element.563), channel_id=1, source_target_pairs={{0,2},{1,3},{2,4},{3,5},{4,6},{5,7},{6,8},{7,9},{8,10},{9,11},{10,... | collective-permute-start | bytes 1572872 | tf_op jit(solution)/shard_map/ppermute | solution.py:29
  1248.8 12.4 collective-permute-start.16
  1250.1 16.0 %collective-permute-start.15 = (f32[1,1024,128]{2,1,0:T(8,128)S(1)}, f32[1,1024,128]{2,1,0:T(8,128)S(1)}, u32[]{:S(2)}, u32[]{:S(2)}) collective-permute-start(f32[1,1024,128]{2,1,0:T(8,128)S(1)} %get-tuple-element.565), channel_id=1, source_target_pairs={{0,1},{1,2},{2,3},{3,4},{4,5},{5,6},{6,7},{7,8},{8,9},{9,10},{10,1... | collective-permute-start | bytes 1572872 | tf_op jit(solution)/shard_map/ppermute | solution.py:29
  1257.2 12.7 collective-permute-start.14
  (34 other events, 131.4 us)
Sparse Core Ops, SparseCore 0:
  89.8 105.2 all-reduce.6
  198.9 100.6 all-reduce.8
  451.1 104.0 all-reduce.10
  558.9 100.7 all-reduce.12
  811.2 103.9 all-reduce.14
  918.9 100.7 all-reduce.16
where the time goes:
time: 1290 us; the launch traced here: 1280 us
  waiting for transfers between devices  637 us (49%)
  loops' own time  255 us (20%)
  matrix products  120 us (9%)
  local copies, waits for them, and re-layouts  112 us (9%)
  other arithmetic  87.4 us (7%)
  starting transfers between devices  51.4 us (4%)
  between operations  14.7 us (1%)
    pmax x3, waiting for transfers between devices, body(): row_peak = lax.pmax(rows_part, 'gy')  314 us
    psum x3, waiting for transfers between devices, body(): row_sums = lax.psum(jnp.exp(rows_part - row_peak), 'gy')  308 us
    another operation x3, loops' own time, body(): lax.scan(column_update, jnp.full((3 * owned, cluster_pts), EMPTY_LOG, jnp...  106 us
    another operation x3, loops' own time, body(): lax.scan(row_update, jnp.full((group_size, cluster_pts), EMPTY_LOG, jnp.f...  106 us
    dot_general x42, matrix products, cost_tile(): lax.dot_general(src_rows, tgt_rows, (((1,), (1,)), ((), ())), preferred_e...  97.7 us
    another operation x1, loops' own time, body(): mass_sum, moved = lax.scan(grad_update, start_vals, pair_order)[0]  43 us
    reduce_sum x18, other arithmetic, column_update(): jnp.sum(jnp.exp(scores - peak_val[None, :]), axis=0)  29.4 us
    ppermute x10, starting transfers between devices, passed_along(): return lax.ppermute(block, axis, route)  28.9 us
  transfers between devices with their start and end apart: 24, of which 15 were waited for; matrix products, arithmetic and copies ran while one was open for 1% of the time, Pallas kernels for 0%

commit v1 on v0

--- a/solution.py
+++ b/solution.py
@@ -77,7 +77,7 @@
     src_sq = squares(src_points)
     g_local = jnp.zeros((owned, cluster_pts), jnp.float32)
     g_window = jnp.zeros((3 * owned, cluster_pts), jnp.float32)
-    f_pot = jnp.zeros((group_size, cluster_pts), jnp.float32)
+    span_ids = source_local - (gy_index - 2) * owned
     for sweep_index in range(ITERS):
         window_pts, window_sq = fetch_points(tgt_points)
         if sweep_index > 0:
@@ -106,10 +106,16 @@
         rows_part = lax.scan(
             row_update, jnp.full((group_size, cluster_pts), EMPTY_LOG, jnp.float32), pair_order
         )[0]
-        row_peak = lax.pmax(rows_part, "gy")
-        row_sums = lax.psum(jnp.exp(rows_part - row_peak), "gy")
-        rows_total = row_peak + jnp.log(row_sums)
-        f_pot = EPSILON * src_log_mass - EPSILON * rows_total
+        own_total = pick(rows_part, gy_index)
+        for distance in (1, 2, -1, -2):
+            sent = pick(rows_part, jnp.clip(gy_index + distance, 0, gy_count - 1))
+            got = passed_along(sent, "gy", distance)
+            has_sender = (gy_index - distance >= 0) & (gy_index - distance < gy_count)
+            own_total = log_add(own_total, jnp.where(has_sender, got, EMPTY_LOG))
+        f_own = EPSILON * pick(src_log_mass, gy_index) - EPSILON * own_total
+        f_span = [passed_along(f_own, "gy", -d) for d in (-2, -1)]
+        f_span = f_span + [f_own] + [passed_along(f_own, "gy", -d) for d in (1, 2)]
+        f_span = jnp.stack(f_span)
 
         def column_update(running, pair_index):
             source = source_local[pair_index]
@@ -120,7 +126,7 @@
                 pick(src_sq, source),
                 pick(window_sq, target),
             )
-            scores = (pick(f_pot, source)[:, None] - costs) / EPSILON
+            scores = (pick(f_span, span_ids[pair_index])[:, None] - costs) / EPSILON
             peak_val = jnp.max(scores, axis=0)
             partial_value = peak_val + jnp.log(jnp.sum(jnp.exp(scores - peak_val[None, :]), axis=0))
             current = pick(running, target)
@@ -143,7 +149,7 @@
     window_pts, window_sq = fetch_points(tgt_points)
     g_window = fetch_potential(g_local)
     span_rows = 5 * owned
-    span_ids = source_local - (gy_index - 2) * owned
+    f_pot = lax.all_gather(f_own[None], "gy", axis=0, tiled=True)
 
     def grad_update(totals, pair_index):
         source = source_local[pair_index]
@@ -154,7 +160,7 @@
             pick(src_points, source), tgt_rows, pick(src_sq, source), pick(window_sq, target)
         )
         weights = jnp.exp(
-            (pick(f_pot, source)[:, None] + pick(g_window, target)[None, :] - costs) / EPSILON
+            (pick(f_span, row)[:, None] + pick(g_window, target)[None, :] - costs) / EPSILON
         )
         mass_sum, moved = totals
         mass_sum = lax.dynamic_update_index_in_dim(

time: 1290 us -> 801 us (0.62)
  waiting for transfers between devices: 637 us -> 38.2 us
  starting transfers between devices: 51.4 us -> 119 us
  blocking collectives: 0 us -> 37.2 us
  loops' own time: 255 us -> 291 us
  matrix products: 120 us -> 94.6 us
  local copies, waits for them, and re-layouts: 112 us -> 130 us
  between operations: 14.7 us -> 1.58 us
    pmax x3 -> x0, waiting for transfers between devices: 314 us -> none  [body(): row_peak = lax.pmax(rows_part, 'gy')]
    psum x3 -> x0, waiting for transfers between devices: 308 us -> none  [body(): row_sums = lax.psum(jnp.exp(rows_part - row_peak), 'gy')]
    ppermute x10 -> x34, starting transfers between devices: 28.9 us -> 102 us  [passed_along(): return lax.ppermute(block, axis, route)]
    all_gather x0 -> x1, blocking collectives: none -> 37.2 us  [body(): f_pot = lax.all_gather(f_own[None], 'gy', axis=0, tiled=True)]
    another operation x3, loops' own time: 106 us -> 141 us  [body(): lax.scan(column_update, jnp.full((3 * owned, cluster_pts), EMPTY_LOG, jnp...]
    ppermute x10 -> x34, waiting for transfers between devices: 13 us -> 29.5 us  [passed_along(): return lax.ppermute(block, axis, route)]
    dot_general x6, matrix products: 22.7 us -> 9.63 us  [grad_update(): jnp.dot(weights.astype(jnp.bfloat16), tgt_rows, preferred_element_type=jn...]
  transfers between devices with their start and end apart: 24 -> 42, of which waited for: 15 -> 17; matrix products, arithmetic and copies ran while one was open for 1% -> 1% of each run, Pallas kernels for 0% -> 0%
where the time goes in v1:
time: 801 us; the launch traced here: 792 us
  loops' own time  291 us (36%)
  local copies, waits for them, and re-layouts  130 us (16%)
  starting transfers between devices  119 us (15%)
  matrix products  94.6 us (12%)
  other arithmetic  80.8 us (10%)
  waiting for transfers between devices  38.2 us (5%)
  blocking collectives  37.2 us (5%)
    another operation x3, loops' own time, body(): lax.scan(column_update, jnp.full((3 * owned, cluster_pts), EMPTY_LOG, jnp...  141 us
    another operation x3, loops' own time, body(): lax.scan(row_update, jnp.full((group_size, cluster_pts), EMPTY_LOG, jnp.f...  106 us
    ppermute x34, starting transfers between devices, passed_along(): return lax.ppermute(block, axis, route)  102 us
    dot_general x42, matrix products, cost_tile(): lax.dot_general(src_rows, tgt_rows, (((1,), (1,)), ((), ())), preferred_e...  85 us
    another operation x1, loops' own time, body(): mass_sum, moved = lax.scan(grad_update, start_vals, pair_order)[0]  43.9 us
    all_gather x1, blocking collectives, body(): f_pot = lax.all_gather(f_own[None], 'gy', axis=0, tiled=True)  37.2 us
    reduce_sum x18, other arithmetic, column_update(): jnp.sum(jnp.exp(scores - peak_val[None, :]), axis=0)  29.5 us
    ppermute x34, waiting for transfers between devices, passed_along(): return lax.ppermute(block, axis, route)  29.5 us
  transfers between devices with their start and end apart: 42, of which 17 were waited for; matrix products, arithmetic and copies ran while one was open for 1% of the time, Pallas kernels for 0%

profile of v1, /device:TPU:1, one launch (start us, length us, event | category | flops | bytes accessed | tf_op | source)
XLA Modules:
  0.0 792.3 jit_solution(5391893023546699672)
XLA Ops:
  0.6 4.0 collective-permute-start
  6.6 7.8 multiply_reduce_fusion
  15.3 66.5 %while.72 = (s32[]{:T(128)}, f32[32,1024]{1,0:T(8,128)S(1)}, s32[6]{0:T(128)S(1)}, s32[6]{0:T(128)S(1)}, f32[32,1024]{1,0:T(8,128)S(1)}, /*index=5*/s32[6]{0:T(1...) while((s32[]{:T(128)}, f32[32,1024]{1,0:T(8,128)S(1)}, ...), condition=%wide.region_6.7_spmd, body=%wide.region_3.6_spmd.sunk | while | flops 282071040 | bytes 8991015 | solution.py:106
  81.9 4.1 collective-permute-start.2
  86.0 3.2 collective-permute-start.3
  98.4 5.1 collective-permute-start.7
  108.5 3.3 collective-permute-done.9
  111.8 83.7 %while.73 = (s32[]{:T(128)}, f32[3,1024]{1,0:T(4,128)S(1)}, s32[6]{0:T(128)S(1)}, s32[6]{0:T(128)S(1)}, s32[6]{0:T(128)S(1)}, /*index=5*/f32[5,1024]{1,0:T(8,128...) while((s32[]{:T(128)}, f32[3,1024]{1,0:T(4,128)S(1)}, ...), condition=%wide.region_10.11_spmd, body=%wide.region_7.10_spmd.sunk | while | flops 282071040 | bytes 9007473 | solution.py:140
  195.5 4.2 collective-permute-start.10
  201.1 3.0 collective-permute-done.11
  204.2 3.5 collective-permute-start.12
  212.1 68.7 %while.74 = (s32[]{:T(128)}, f32[32,1024]{1,0:T(8,128)S(1)}, s32[6]{0:T(128)S(1)}, s32[6]{0:T(128)S(1)}, s32[6]{0:T(128)S(1)}, /*index=5*/f32[3,1024]{1,0:T(4,12...) while((s32[]{:T(128)}, f32[32,1024]{1,0:T(8,128)S(1)}, ...), condition=%wide.region_14.15_spmd, body=%wide.region_11.14_spmd.sunk | while | flops 282071040 | bytes 9007411 | solution.py:106
  280.8 7.1 collective-permute-start.14
  287.9 3.6 collective-permute-start.15
  296.4 3.3 collective-permute-done.17
  299.8 3.4 collective-permute-start.18
  303.2 5.1 collective-permute-start.19
  315.5 83.6 %while.75 = (s32[]{:T(128)}, f32[3,1024]{1,0:T(4,128)S(1)}, s32[6]{0:T(128)S(1)}, s32[6]{0:T(128)S(1)}, s32[6]{0:T(128)S(1)}, /*index=5*/f32[5,1024]{1,0:T(8,128...) while((s32[]{:T(128)}, f32[3,1024]{1,0:T(4,128)S(1)}, ...), condition=%wide.region_18.19_spmd, body=%wide.region_15.18_spmd.sunk | while | flops 282071040 | bytes 9007473 | solution.py:140
  403.3 3.0 collective-permute-done.23
  409.6 3.0 collective-permute-done.25
  412.7 68.7 %while.76 = (s32[]{:T(128)}, f32[32,1024]{1,0:T(8,128)S(1)}, s32[6]{0:T(128)S(1)}, s32[6]{0:T(128)S(1)}, s32[6]{0:T(128)S(1)}, /*index=5*/f32[3,1024]{1,0:T(4,12...) while((s32[]{:T(128)}, f32[32,1024]{1,0:T(8,128)S(1)}, ...), condition=%wide.region_22.23_spmd, body=%wide.region_19.22_spmd.sunk | while | flops 282071040 | bytes 9007411 | solution.py:106
  481.5 6.9 collective-permute-start.26
  488.4 3.7 collective-permute-start.27
  502.9 4.4 collective-permute-start.30
  507.3 3.8 collective-permute-start.31
  511.9 83.6 %while.77 = (s32[]{:T(128)}, f32[3,1024]{1,0:T(4,128)S(1)}, s32[6]{0:T(128)S(1)}, s32[6]{0:T(128)S(1)}, s32[6]{0:T(128)S(1)}, /*index=5*/f32[5,1024]{1,0:T(8,128...) while((s32[]{:T(128)}, f32[3,1024]{1,0:T(4,128)S(1)}, ...), condition=%wide.region_26.27_spmd, body=%wide.region_23.26_spmd.sunk | while | flops 282071040 | bytes 9007473 | solution.py:140
  598.6 3.0 collective-permute-done.35
  609.9 121.9 %while.78 = (s32[]{:T(128)}, f32[5,1024]{1,0:T(8,128)}, f32[5,1024,128]{2,1,0:T(8,128)S(1)}, s32[6]{0:T(128)}, s32[6]{0:T(128)}, /*index=5*/f32[5,1024]{1,0:T(8,...) while((s32[]{:T(128)}, f32[5,1024]{1,0:T(8,128)}, ...), condition=%wide.region_29.30_spmd, body=%wide.region_27.29_spmd.sunk | while | flops 551682048 | bytes 11395529 | solution.py:179
  736.4 3.1 collective-permute-start.38
  739.5 5.6 collective-permute-start.39
  746.4 6.0 collective-permute-start.41
  752.4 37.2 %all-gather = f32[32768]{0:T(1024)S(1)} all-gather(f32[1024]{0:T(1024)S(1)} %copy-done.6), channel_id=2, replica_groups=mesh['gx'=4,'gy'=32] {'gy'}, dimensions={0}, use_global_device_ids=true | all-gather | bytes 135168 | tf_op jit(solution)/shard_map/all_gather | solution.py:152
  (594 shorter events, 359.1 us)
Async XLA Ops:
  0.6 14.0 %collective-permute-start = (bf16[1,1024,128]{2,1,0:T(8,128)(2,1)}, bf16[1,1024,128]{2,1,0:T(8,128)(2,1)S(1)}, u32[]{:S(2)}, u32[]{:S(2)}) collective-permute-start(bf16[1,1024,128]{2,1,0:T(8,128)(2,1)} %param.21), channel_id=1, source_target_pairs={{0,32},{32,64},{64,96},{1,33},{33,65},{65,97},{2,34},{34,66},{66,9... | collective-permute-start | bytes 786440 | tf_op jit(solution)/shard_map/ppermute | solution.py:18
  4.6 10.2 %collective-permute-start.1 = (bf16[1,1024,128]{2,1,0:T(8,128)(2,1)}, bf16[1,1024,128]{2,1,0:T(8,128)(2,1)S(1)}, u32[]{:S(2)}, u32[]{:S(2)}) collective-permute-start(bf16[1,1024,128]{2,1,0:T(8,128)(2,1)} %param.21), channel_id=1, source_target_pairs={{32,0},{64,32},{96,64},{33,1},{65,33},{97,65},{34,2},{66,34},{98,6... | collective-permute-start | bytes 786440 | tf_op jit(solution)/shard_map/ppermute | solution.py:21
  81.9 11.3 %collective-permute-start.2 = (f32[1024]{0:T(1024)S(1)}, f32[1024]{0:T(1024)S(1)}, u32[]{:S(2)}, u32[]{:S(2)}) collective-permute-start(f32[1024]{0:T(1024)S(1)} %bitcast.368), channel_id=1, source_target_pairs={{0,1},{1,2},{2,3},{3,4},{4,5},{5,6},{6,7},{7,8},{8,9},{9,10},{10,1... | collective-permute-start | bytes 12296 | tf_op jit(solution)/shard_map/ppermute | solution.py:29
  86.0 7.2 collective-permute-start.3
  89.2 4.9 collective-permute-start.4
  91.1 4.4 collective-permute-start.5
  95.5 11.2 %collective-permute-start.6 = (f32[1024]{0:T(1024)S(1)}, f32[1024]{0:T(1024)S(1)}, u32[]{:S(2)}, u32[]{:S(2)}) collective-permute-start(f32[1024]{0:T(1024)S(1)} %multiply_subtract_fusion.6), channel_id=1, source_target_pairs={{0,2},{1,3},{2,4},{3,5},{4,6},{5,7},{6,8},{7,9},{8,10},{9,11},{10,... | collective-permute-start | bytes 12296 | tf_op jit(solution)/shard_map/ppermute | solution.py:29
  98.4 8.3 %collective-permute-start.7 = (f32[1024]{0:T(1024)S(1)}, f32[1024]{0:T(1024)S(1)}, u32[]{:S(2)}, u32[]{:S(2)}) collective-permute-start(f32[1024]{0:T(1024)S(1)} %multiply_subtract_fusion.6), channel_id=1, source_target_pairs={{0,1},{1,2},{2,3},{3,4},{4,5},{5,6},{6,7},{7,8},{8,9},{9,10},{10,1... | collective-permute-start | bytes 12296 | tf_op jit(solution)/shard_map/ppermute | solution.py:29
  103.5 4.9 collective-permute-start.8
  105.5 6.3 collective-permute-start.9
  195.5 5.5 collective-permute-start.10
  204.2 5.0 collective-permute-start.12
  280.8 13.9 %collective-permute-start.14 = (f32[1024]{0:T(1024)S(1)}, f32[1024]{0:T(1024)S(1)}, u32[]{:S(2)}, u32[]{:S(2)}) collective-permute-start(f32[1024]{0:T(1024)S(1)} %bitcast.382), channel_id=1, source_target_pairs={{0,1},{1,2},{2,3},{3,4},{4,5},{5,6},{6,7},{7,8},{8,9},{9,10},{10,1... | collective-permute-start | bytes 12296 | tf_op jit(solution)/shard_map/ppermute | solution.py:29
  287.9 6.9 collective-permute-start.15
  291.5 4.9 collective-permute-start.16
  293.4 6.3 collective-permute-start.17
  299.8 11.7 %collective-permute-start.18 = (f32[1024]{0:T(1024)S(1)}, f32[1024]{0:T(1024)S(1)}, u32[]{:S(2)}, u32[]{:S(2)}) collective-permute-start(f32[1024]{0:T(1024)S(1)} %multiply_subtract_fusion.4), channel_id=1, source_target_pairs={{0,2},{1,3},{2,4},{3,5},{4,6},{5,7},{6,8},{7,9},{8,10},{9,11},{10,... | collective-permute-start | bytes 12296 | tf_op jit(solution)/shard_map/ppermute | solution.py:29
  303.2 8.3 %collective-permute-start.19 = (f32[1024]{0:T(1024)S(1)}, f32[1024]{0:T(1024)S(1)}, u32[]{:S(2)}, u32[]{:S(2)}) collective-permute-start(f32[1024]{0:T(1024)S(1)} %multiply_subtract_fusion.4), channel_id=1, source_target_pairs={{0,1},{1,2},{2,3},{3,4},{4,5},{5,6},{6,7},{7,8},{8,9},{9,10},{10,1... | collective-permute-start | bytes 12296 | tf_op jit(solution)/shard_map/ppermute | solution.py:29
  308.3 4.9 collective-permute-start.20
  310.2 5.2 collective-permute-start.21
  481.5 13.8 %collective-permute-start.26 = (f32[1024]{0:T(1024)S(1)}, f32[1024]{0:T(1024)S(1)}, u32[]{:S(2)}, u32[]{:S(2)}) collective-permute-start(f32[1024]{0:T(1024)S(1)} %bitcast.376), channel_id=1, source_target_pairs={{0,1},{1,2},{2,3},{3,4},{4,5},{5,6},{6,7},{7,8},{8,9},{9,10},{10,1... | collective-permute-start | bytes 12296 | tf_op jit(solution)/shard_map/ppermute | solution.py:29
  488.4 6.9 collective-permute-start.27
  492.0 4.9 collective-permute-start.28
  494.0 4.8 collective-permute-start.29
  498.8 12.3 %collective-permute-start.32 = (f32[1024]{0:T(1024)S(1)}, f32[1024]{0:T(1024)S(1)}, u32[]{:S(2)}, u32[]{:S(2)}) collective-permute-start(f32[1024]{0:T(1024)S(1)} %multiply_subtract_fusion.2), channel_id=1, source_target_pairs={{1,0},{2,1},{3,2},{4,3},{5,4},{6,5},{7,6},{8,7},{9,8},{10,9},{11,1... | collective-permute-start | bytes 12296 | tf_op jit(solution)/shard_map/ppermute | solution.py:29
  501.6 9.6 %collective-permute-start.33 = (f32[1024]{0:T(1024)S(1)}, f32[1024]{0:T(1024)S(1)}, u32[]{:S(2)}, u32[]{:S(2)}) collective-permute-start(f32[1024]{0:T(1024)S(1)} %multiply_subtract_fusion.2), channel_id=1, source_target_pairs={{2,0},{3,1},{4,2},{5,3},{6,4},{7,5},{8,6},{9,7},{10,8},{11,9},{12,... | collective-permute-start | bytes 12296 | tf_op jit(solution)/shard_map/ppermute | solution.py:29
  502.9 8.3 %collective-permute-start.30 = (f32[1024]{0:T(1024)S(1)}, f32[1024]{0:T(1024)S(1)}, u32[]{:S(2)}, u32[]{:S(2)}) collective-permute-start(f32[1024]{0:T(1024)S(1)} %multiply_subtract_fusion.2), channel_id=1, source_target_pairs={{0,2},{1,3},{2,4},{3,5},{4,6},{5,7},{6,8},{7,9},{8,10},{9,11},{10,... | collective-permute-start | bytes 12296 | tf_op jit(solution)/shard_map/ppermute | solution.py:29
  507.3 4.6 collective-permute-start.31
  736.4 53.9 %collective-permute-start.38 = (f32[1,1024,128]{2,1,0:T(8,128)}, f32[1,1024,128]{2,1,0:T(8,128)S(1)}, u32[]{:S(2)}, u32[]{:S(2)}) collective-permute-start(f32[1,1024,128]{2,1,0:T(8,128)} %get-tuple-element.583), channel_id=1, source_target_pairs={{1,0},{2,1},{3,2},{4,3},{5,4},{6,5},{7,6},{8,7},{9,8},{10,9},{11,1... | collective-permute-start | bytes 1572872 | tf_op jit(solution)/shard_map/ppermute | solution.py:29
  739.5 50.8 %collective-permute-start.39 = (f32[1,1024,128]{2,1,0:T(8,128)}, f32[1,1024,128]{2,1,0:T(8,128)S(1)}, u32[]{:S(2)}, u32[]{:S(2)}) collective-permute-start(f32[1,1024,128]{2,1,0:T(8,128)} %get-tuple-element.586), channel_id=1, source_target_pairs={{0,1},{1,2},{2,3},{3,4},{4,5},{5,6},{6,7},{7,8},{8,9},{9,10},{10,1... | collective-permute-start | bytes 1572872 | tf_op jit(solution)/shard_map/ppermute | solution.py:29
  745.1 45.2 %collective-permute-start.40 = (f32[1,1024,128]{2,1,0:T(8,128)S(1)}, f32[1,1024,128]{2,1,0:T(8,128)S(1)}, u32[]{:S(2)}, u32[]{:S(2)}) collective-permute-start(f32[1,1024,128]{2,1,0:T(8,128)S(1)} %get-tuple-element.585), channel_id=1, source_target_pairs={{2,0},{3,1},{4,2},{5,3},{6,4},{7,5},{8,6},{9,7},{10,8},{11,9},{12,... | collective-permute-start | bytes 1572872 | tf_op jit(solution)/shard_map/ppermute | solution.py:29
  746.4 43.9 %collective-permute-start.41 = (f32[1,1024,128]{2,1,0:T(8,128)S(1)}, f32[1,1024,128]{2,1,0:T(8,128)S(1)}, u32[]{:S(2)}, u32[]{:S(2)}) collective-permute-start(f32[1,1024,128]{2,1,0:T(8,128)S(1)} %get-tuple-element.584), channel_id=1, source_target_pairs={{0,2},{1,3},{2,4},{3,5},{4,6},{5,7},{6,8},{7,9},{8,10},{9,11},{10,... | collective-permute-start | bytes 1572872 | tf_op jit(solution)/shard_map/ppermute | solution.py:29
  (34 other events, 276.1 us)

commit v2 on v1

v2 whole, which is shorter than its diff:
```python
import jax
import jax.numpy as jnp
from jax import lax
from jax.sharding import PartitionSpec as P
from jax.experimental import pallas as pl
from jax.experimental.pallas import tpu as pltpu

ITERS = 3


EMPTY_LOG = -1e30


def padded(block, sides, width):
    for axis, dim in sides:
        count = lax.axis_size(axis)
        forward = [(i, i + 1) for i in range(count - 1)]
        backward = [(target, source) for source, target in forward]
        low = lax.ppermute(
            lax.slice_in_dim(block, block.shape[dim] - width, None, axis=dim), axis, forward
        )
        high = lax.ppermute(lax.slice_in_dim(block, 0, width, axis=dim), axis, backward)
        block = jnp.concatenate([low, block, high], axis=dim)
    return block


def passed_along(block, axis, distance):
    devices = range(lax.axis_size(axis))
    route = [(i - distance, i) for i in devices if i - distance in devices]
    return lax.ppermute(block, axis, route)


def log_add(first, second):
    peak_val = jnp.maximum(first, second)
    return peak_val + jnp.log(jnp.exp(first - peak_val) + jnp.exp(second - peak_val))


def pick(table, position):
    return lax.dynamic_index_in_dim(table, position, 0, keepdims=False)


def cost_tile(src_rows, tgt_rows, src_sq, tgt_sq):
    inner = lax.dot_general(
        src_rows, tgt_rows, (((1,), (1,)), ((), ())), preferred_element_type=jnp.float32
    )
    return 0.5 * (src_sq[:, None] + tgt_sq[None, :]) - inner


def squares(points):
    return jnp.sum(jnp.square(points.astype(jnp.float32)), axis=-1)


def fetch_points(tgt_points):
    window_pts = padded(tgt_points, (("gx", 0),), tgt_points.shape[0])
    return (window_pts, squares(window_pts))


def fetch_potential(g_local):
    return padded(g_local, (("gx", 0),), g_local.shape[0])


EPSILON = 0.03
INV_EPS = 1.0 / EPSILON
CHUNK = 256


def _lse_kernel(a_ids, b_ids, a_ref, b_ref, v_ref, o_ref):
    tile = lax.dot_general(
        b_ref[0], a_ref[0], (((1,), (1,)), ((), ())), preferred_element_type=jnp.float32
    )
    scores = tile * INV_EPS + v_ref[0]
    peak = jnp.max(scores, axis=0, keepdims=True)
    total = jnp.sum(jnp.exp(scores - peak), axis=0, keepdims=True)
    o_ref[0] = peak + jnp.log(total)


def pair_lse(a_ids, b_ids, a_pts, b_pts, v_col, interpret=False):
    pairs = a_ids.shape[0]
    rows = a_pts.shape[1]
    coords = a_pts.shape[2]
    cols = b_pts.shape[1]
    spec = pltpu.PrefetchScalarGridSpec(
        num_scalar_prefetch=2,
        grid=(pairs, rows // CHUNK),
        in_specs=[
            pl.BlockSpec((1, CHUNK, coords), lambda p, c, ai, bi: (ai[p], c, 0)),
            pl.BlockSpec((1, cols, coords), lambda p, c, ai, bi: (bi[p], 0, 0)),
            pl.BlockSpec((1, cols, 1), lambda p, c, ai, bi: (p, 0, 0)),
        ],
        out_specs=pl.BlockSpec((1, 1, CHUNK), lambda p, c, ai, bi: (p, 0, c)),
    )
    return pl.pallas_call(
        _lse_kernel,
        grid_spec=spec,
        out_shape=jax.ShapeDtypeStruct((pairs, 1, rows), jnp.float32),
        interpret=interpret,
    )(a_ids, b_ids, a_pts, b_pts, v_col)


def _grad_kernel(a_ids, b_ids, a_ref, b_ref, v_ref, w_ref, o_ref):
    src = a_ref[0]
    tgt = b_ref[0]
    tile = lax.dot_general(src, tgt, (((1,), (1,)), ((), ())), preferred_element_type=jnp.float32)
    weights = jnp.exp(tile * INV_EPS + v_ref[0] + w_ref[0])
    mass = jnp.sum(weights, axis=1, keepdims=True)
    moved = jnp.dot(weights.astype(jnp.bfloat16), tgt, preferred_element_type=jnp.float32)
    o_ref[0] = mass * src.astype(jnp.float32) - moved


def pair_grad(a_ids, b_ids, a_pts, b_pts, v_row, w_col, interpret=False):
    pairs = a_ids.shape[0]
    rows = a_pts.shape[1]
    coords = a_pts.shape[2]
    cols = b_pts.shape[1]
    spec = pltpu.PrefetchScalarGridSpec(
        num_scalar_prefetch=2,
        grid=(pairs, rows // CHUNK),
        in_specs=[
            pl.BlockSpec((1, CHUNK, coords), lambda p, c, ai, bi: (ai[p], c, 0)),
            pl.BlockSpec((1, cols, coords), lambda p, c, ai, bi: (bi[p], 0, 0)),
            pl.BlockSpec((1, 1, cols), lambda p, c, ai, bi: (p, 0, 0)),
            pl.BlockSpec((1, CHUNK, 1), lambda p, c, ai, bi: (p, c, 0)),
        ],
        out_specs=pl.BlockSpec((1, CHUNK, coords), lambda p, c, ai, bi: (p, c, 0)),
    )
    return pl.pallas_call(
        _grad_kernel,
        grid_spec=spec,
        out_shape=jax.ShapeDtypeStruct((pairs, rows, coords), jnp.float32),
        interpret=interpret,
    )(a_ids, b_ids, a_pts, b_pts, v_row, w_col)


def grouped_lse(mask, values):
    masked = jnp.where(mask[:, :, None], values[None], EMPTY_LOG)
    peak_val = jnp.max(masked, axis=1)
    return peak_val + jnp.log(jnp.sum(jnp.exp(masked - peak_val[:, None]), axis=1))


def body(src_points, tgt_points, src_log_mass, tgt_log_mass, near_pairs, target_slot):
    owned = tgt_points.shape[0]
    group_size = src_points.shape[0]
    gx_count = lax.axis_size("gx")
    gy_count = lax.axis_size("gy")
    gx_index = lax.axis_index("gx")
    gy_index = lax.axis_index("gy")
    source_local = jnp.clip(near_pairs[:, 0] - gx_index * group_size, 0, group_size - 1)
    matches = (
        near_pairs[:, 1][:, None] == jnp.arange(target_slot.shape[0], dtype=jnp.int32)[None, :]
    )
    slot_ids = jnp.sum(jnp.where(matches, target_slot[None, :], 0), axis=1)
    window_ids = (slot_ids // owned // gy_count - gx_index + 1) * owned + slot_ids % owned
    window_ids = jnp.clip(window_ids, 0, 3 * owned - 1)
    span_ids = jnp.clip(source_local - (gy_index - 2) * owned, 0, 5 * owned - 1)
    span_mask = span_ids[None, :] == jnp.arange(5 * owned, dtype=jnp.int32)[:, None]
    window_mask = window_ids[None, :] == jnp.arange(3 * owned, dtype=jnp.int32)[:, None]
    src_sq = squares(src_points)
    pair_src_sq = src_sq[source_local]
    window_pts, window_sq = fetch_points(tgt_points)
    pair_tgt_sq = window_sq[window_ids]
    g_local = None
    g_window = jnp.zeros((3 * owned, src_points.shape[1]), jnp.float32)
    for sweep_index in range(ITERS):
        if sweep_index > 0:
            g_window = fetch_potential(g_local)
        v_row = (g_window[window_ids] - 0.5 * pair_tgt_sq) / EPSILON
        part = pair_lse(source_local, window_ids, src_points, window_pts, v_row[:, :, None])
        part = part[:, 0] - 0.5 * pair_src_sq / EPSILON
        rows_span = grouped_lse(span_mask, part)
        own_total = rows_span[2]
        for distance in (1, 2, -1, -2):
            got = passed_along(rows_span[2 + distance], "gy", distance)
            has_sender = (gy_index - distance >= 0) & (gy_index - distance < gy_count)
            own_total = log_add(own_total, jnp.where(has_sender, got, EMPTY_LOG))
        f_own = EPSILON * pick(src_log_mass, gy_index) - EPSILON * own_total
        f_span = [passed_along(f_own, "gy", -d) for d in (-2, -1)]
        f_span = f_span + [f_own] + [passed_along(f_own, "gy", -d) for d in (1, 2)]
        f_span = jnp.stack(f_span)
        v_col = (f_span[span_ids] - 0.5 * pair_src_sq) / EPSILON
        part = pair_lse(window_ids, source_local, window_pts, src_points, v_col[:, :, None])
        part = part[:, 0] - 0.5 * pair_tgt_sq / EPSILON
        cols_part = grouped_lse(window_mask, part)
        from_left = passed_along(cols_part[2 * owned :], "gx", 1)
        from_right = passed_along(cols_part[:owned], "gx", -1)
        from_left = jnp.where(gx_index > 0, from_left, EMPTY_LOG)
        from_right = jnp.where(gx_index < gx_count - 1, from_right, EMPTY_LOG)
        cols_total = log_add(log_add(cols_part[owned : 2 * owned], from_left), from_right)
        g_local = EPSILON * tgt_log_mass - EPSILON * cols_total
    f_pot = lax.all_gather(f_own[None], "gy", axis=0, tiled=True)
    g_window = fetch_potential(g_local)
    v_row = (g_window[window_ids] - 0.5 * pair_tgt_sq) / EPSILON
    w_col = (f_span[span_ids] - 0.5 * pair_src_sq) / EPSILON
    contrib = pair_grad(
        source_local, window_ids, src_points, window_pts, v_row[:, None, :], w_col[:, :, None]
    )
    span_parts = jnp.sum(jnp.where(span_mask[:, :, None, None], contrib[None], 0.0), axis=1)
    grad = span_parts[2 * owned : 3 * owned]
    for distance in (1, 2):
        upper = passed_along(
            span_parts[(2 - distance) * owned : (3 - distance) * owned], "gy", -distance
        )
        lower = passed_along(
            span_parts[(2 + distance) * owned : (3 + distance) * owned], "gy", distance
        )
        grad = grad + upper + lower
    return (f_pot, g_local, grad)


def solution(mesh):
    in_specs = (
        P("gx", None, None),
        P(("gx", "gy"), None, None),
        P("gx", None),
        P(("gx", "gy"), None),
        P(("gx", "gy"), None),
        P(),
    )
    out_specs = (P("gx", None), P(("gx", "gy"), None), P(("gx", "gy"), None, None))
    return jax.shard_map(body, mesh=mesh, in_specs=in_specs, out_specs=out_specs, check_vma=False)
```

time: 801 us -> 390 us (0.49)
  loops' own time: 291 us -> 0 us
  Pallas kernels: 0 us -> 144 us
  local copies, waits for them, and re-layouts: 130 us -> 21.2 us
  matrix products: 94.6 us -> 0 us
  other arithmetic: 80.8 us -> 23.3 us
    another operation x7 -> x0, loops' own time: 291 us -> none  [the longest x3 141 us: body(): lax.scan(column_update, jnp.full((3 * owned, cluster_pts), EMPTY_LOG, jnp...]
    pallas_call x0 -> x7, Pallas kernels: none -> 144 us  [the longest x6 123 us: pair_lse(): pl.pallas_call(_lse_kernel, grid_spec=spec, out_shape=jax.ShapeDtypeStruc...]
    dynamic_slice x237 -> x0, local copies, waits for them, and re-layouts: 113 us -> none  [the longest x42 28.3 us: body(): lax.scan(row_update, jnp.full((group_size, cluster_pts), EMPTY_LOG, jnp.f...]
    dot_general x48 -> x0, matrix products: 94.6 us -> none  [the longest x42 85 us: cost_tile(): lax.dot_general(src_rows, tgt_rows, (((1,), (1,)), ((), ())), preferred_e...]
    reduce_sum x36 -> x7, other arithmetic: 57 us -> 4.54 us  [the longest x1 3.75 us: body(): jnp.sum(jnp.where(span_mask[:, :, None, None], contrib[None], 0.0), axis=1)]
    div x0 -> x7, local copies, waits for them, and re-layouts: none -> 13.8 us  [the longest x4 7.19 us: body(): v_row = (g_window[window_ids] - 0.5 * pair_tgt_sq) / EPSILON]
    dynamic_update_slice x42 -> x0, local copies, waits for them, and re-layouts: 11.6 us -> none  [the longest x6 8.34 us: grad_update(): lax.dynamic_update_index_in_dim(mass_sum, pick(mass_sum, row) + jnp.sum(w...]
    add x79 -> x6, other arithmetic: 9.7 us -> 0.09 us  [grouped_lse(): peak_val + jnp.log(jnp.sum(jnp.exp(masked - peak_val[:, None]), axis=1))]
  transfers between devices with their start and end apart: 42 -> 42, of which waited for: 17 -> 18; matrix products, arithmetic and copies ran while one was open for 1% -> 3% of each run, Pallas kernels for 0% -> 0%
where the time goes in v2:
time: 390 us; the launch traced here: 385 us
  Pallas kernels  144 us (37%)
  starting transfers between devices  117 us (30%)
  waiting for transfers between devices  43.2 us (11%)
  blocking collectives  34.1 us (9%)
  other arithmetic  23.3 us (6%)
  local copies, waits for them, and re-layouts  21.2 us (5%)
    pallas_call x6, Pallas kernels, pair_lse(): pl.pallas_call(_lse_kernel, grid_spec=spec, out_shape=jax.ShapeDtypeStruc...  123 us
    ppermute x34, starting transfers between devices, passed_along(): return lax.ppermute(block, axis, route)  101 us
    ppermute x34, waiting for transfers between devices, passed_along(): return lax.ppermute(block, axis, route)  34.3 us
    all_gather x1, blocking collectives, body(): f_pot = lax.all_gather(f_own[None], 'gy', axis=0, tiled=True)  34.1 us
    pallas_call x1, Pallas kernels, pair_grad(): pl.pallas_call(_grad_kernel, grid_spec=spec, out_shape=jax.ShapeDtypeStru...  20.7 us
    ppermute x4, starting transfers between devices, padded(): lax.ppermute(lax.slice_in_dim(block, block.shape[dim] - width, None, axis...  10.4 us
    ppermute x4, waiting for transfers between devices, padded(): lax.ppermute(lax.slice_in_dim(block, 0, width, axis=dim), axis, backward)  8.95 us
    reduce_sum x2, other arithmetic, squares(): return jnp.sum(jnp.square(points.astype(jnp.float32)), axis=-1)  8.3 us
  transfers between devices with their start and end apart: 42, of which 18 were waited for; matrix products, arithmetic and copies ran while one was open for 3% of the time, Pallas kernels for 0%

profile of v2, /device:TPU:1, one launch (start us, length us, event | category | flops | bytes accessed | tf_op | source)
XLA Modules:
  0.0 384.5 jit_solution(17349614600295753419)
XLA Ops:
  0.6 4.0 %collective-permute-start = (bf16[1,1024,128]{2,1,0:T(8,128)(2,1)}, bf16[1,1024,128]{2,1,0:T(8,128)(2,1)S(1)}, u32[]{:S(2)}, u32[]{:S(2)}) collective-permute-start(bf16[1,1024,128]{2,1,0:T(8,128)(2,1)} %param.7), channel_id=1, source_target_pairs={{0,32},{32,64},{64,96},{1,33},{33,65},{65,97},{2,34},{34,66},{66,9... | collective-permute-start | bytes 786440 | tf_op jit(solution)/shard_map/ppermute | solution.py:19
  7.6 7.8 %multiply_reduce_fusion = f32[32,1024]{1,0:T(8,128)S(1)} fusion(bf16[32,1024,128]{2,1,0:T(8,128)(2,1)} %a_ref.7), kind=kLoop, calls=%fused_computation.9 | loop fusion | flops 12550144 | bytes 8519680 | tf_op jit(solution)/shard_map/reduce_sum | solution.py:50
  20.0 20.5 %shard_map.85 = f32[6,1,1024]{2,1,0:T(1,128)} custom-call(s32[6]{0:T(128)} %bitcast.79, s32[6]{0:T(128)} %copy-done.4, bf16[32,1024,128]{2,1,0:T(8,128)(2,1)} %a_ref.7, bf16[3,1024,128]{2,1,0:T(8,128)(2,1)} %copy-done, f32[6,1024,1]{2,1,0:T(8,128)} %copy.29.v_ref), custom_call_target="tpu_custom_call" | custom-call | tf_op jit(solution)/shard_map/pallas_call | solution.py:92
  41.6 4.0 %collective-permute-start.2 = (f32[1024]{0:T(1024)S(1)}, f32[1024]{0:T(1024)S(1)}, u32[]{:S(2)}, u32[]{:S(2)}) collective-permute-start(f32[1024]{0:T(1024)S(1)} %bitcast.94), channel_id=1, source_target_pairs={{0,1},{1,2},{2,3},{3,4},{4,5},{5,6},{6,7},{7,8},{8,9},{9,10},{10,1... | collective-permute-start | bytes 12296 | tf_op jit(solution)/shard_map/ppermute | solution.py:30
  45.6 3.3 collective-permute-start.3
  58.2 5.1 %collective-permute-start.7 = (f32[1024]{0:T(1024)S(1)}, f32[1024]{0:T(1024)S(1)}, u32[]{:S(2)}, u32[]{:S(2)}) collective-permute-start(f32[1024]{0:T(1024)S(1)} %multiply_subtract_fusion.5), channel_id=1, source_target_pairs={{0,1},{1,2},{2,3},{3,4},{4,5},{5,6},{6,7},{7,8},{8,9},{9,10},{10,1... | collective-permute-start | bytes 12296 | tf_op jit(solution)/shard_map/ppermute | solution.py:30
  68.2 3.4 collective-permute-done.9
  74.4 20.7 %shard_map.86 = f32[6,1,1024]{2,1,0:T(1,128)} custom-call(s32[6]{0:T(128)} %copy-done.4, s32[6]{0:T(128)} %bitcast.80, bf16[3,1024,128]{2,1,0:T(8,128)(2,1)} %copy-done, bf16[32,1024,128]{2,1,0:T(8,128)(2,1)} %a_ref.7, f32[6,1024,1]{2,1,0:T(8,128)} %copy.30.v_ref), custom_call_target="tpu_custom_call" | custom-call | tf_op jit(solution)/shard_map/pallas_call | solution.py:92
  96.1 4.3 %collective-permute-start.10 = (f32[1,1024]{1,0:T(1,128)S(1)}, f32[1,1024]{1,0:T(1,128)S(1)}, u32[]{:S(2)}, u32[]{:S(2)}) collective-permute-start(f32[1,1024]{1,0:T(1,128)S(1)} %get-tuple-element.28), channel_id=1, source_target_pairs={{0,32},{32,64},{64,96},{1,33},{33,65},{65,97},{2,34},{34,66},{66,9... | collective-permute-start | bytes 12296 | tf_op jit(solution)/shard_map/ppermute | solution.py:30
  101.7 3.3 collective-permute-done.11
  115.1 20.5 %shard_map.87 = f32[6,1,1024]{2,1,0:T(1,128)} custom-call(s32[6]{0:T(128)} %bitcast.81, s32[6]{0:T(128)} %copy-done.4, bf16[32,1024,128]{2,1,0:T(8,128)(2,1)} %a_ref.7, bf16[3,1024,128]{2,1,0:T(8,128)(2,1)} %copy-done, f32[6,1024,1]{2,1,0:T(8,128)} %copy.31.v_ref), custom_call_target="tpu_custom_call" | custom-call | tf_op jit(solution)/shard_map/pallas_call | solution.py:92
  136.7 7.4 %collective-permute-start.14 = (f32[1024]{0:T(1024)S(1)}, f32[1024]{0:T(1024)S(1)}, u32[]{:S(2)}, u32[]{:S(2)}) collective-permute-start(f32[1024]{0:T(1024)S(1)} %bitcast.101), channel_id=1, source_target_pairs={{0,1},{1,2},{2,3},{3,4},{4,5},{5,6},{6,7},{7,8},{8,9},{9,10},{10,1... | collective-permute-start | bytes 12296 | tf_op jit(solution)/shard_map/ppermute | solution.py:30
  144.1 3.6 collective-permute-start.15
  152.6 3.2 collective-permute-done.17
  155.9 3.4 collective-permute-start.18
  159.3 5.1 %collective-permute-start.19 = (f32[1024]{0:T(1024)S(1)}, f32[1024]{0:T(1024)S(1)}, u32[]{:S(2)}, u32[]{:S(2)}) collective-permute-start(f32[1024]{0:T(1024)S(1)} %multiply_subtract_fusion.3), channel_id=1, source_target_pairs={{0,1},{1,2},{2,3},{3,4},{4,5},{5,6},{6,7},{7,8},{8,9},{9,10},{10,1... | collective-permute-start | bytes 12296 | tf_op jit(solution)/shard_map/ppermute | solution.py:30
  174.4 20.6 %shard_map.88 = f32[6,1,1024]{2,1,0:T(1,128)} custom-call(s32[6]{0:T(128)} %copy-done.4, s32[6]{0:T(128)} %bitcast.82, bf16[3,1024,128]{2,1,0:T(8,128)(2,1)} %copy-done, bf16[32,1024,128]{2,1,0:T(8,128)(2,1)} %a_ref.7, f32[6,1024,1]{2,1,0:T(8,128)} %copy.32.v_ref), custom_call_target="tpu_custom_call" | custom-call | tf_op jit(solution)/shard_map/pallas_call | solution.py:92
  200.2 3.0 collective-permute-done.23
  212.3 20.5 %shard_map.89 = f32[6,1,1024]{2,1,0:T(1,128)} custom-call(s32[6]{0:T(128)} %bitcast.83, s32[6]{0:T(128)} %copy-done.4, bf16[32,1024,128]{2,1,0:T(8,128)(2,1)} %a_ref.7, bf16[3,1024,128]{2,1,0:T(8,128)(2,1)} %copy-done, f32[6,1024,1]{2,1,0:T(8,128)} %copy.33.v_ref), custom_call_target="tpu_custom_call" | custom-call | tf_op jit(solution)/shard_map/pallas_call | solution.py:92
  233.9 6.8 %collective-permute-start.26 = (f32[1024]{0:T(1024)S(1)}, f32[1024]{0:T(1024)S(1)}, u32[]{:S(2)}, u32[]{:S(2)}) collective-permute-start(f32[1024]{0:T(1024)S(1)} %bitcast.102), channel_id=1, source_target_pairs={{0,1},{1,2},{2,3},{3,4},{4,5},{5,6},{6,7},{7,8},{8,9},{9,10},{10,1... | collective-permute-start | bytes 12296 | tf_op jit(solution)/shard_map/ppermute | solution.py:30
  240.7 3.8 %collective-permute-start.27 = (f32[1024]{0:T(1024)S(1)}, f32[1024]{0:T(1024)S(1)}, u32[]{:S(2)}, u32[]{:S(2)}) collective-permute-start(f32[1024]{0:T(1024)S(1)} %bitcast.100), channel_id=1, source_target_pairs={{0,2},{1,3},{2,4},{3,5},{4,6},{5,7},{6,8},{7,9},{8,10},{9,11},{10,... | collective-permute-start | bytes 12296 | tf_op jit(solution)/shard_map/ppermute | solution.py:30
  251.3 3.4 collective-permute-start.30
  254.7 5.1 %collective-permute-start.31 = (f32[1024]{0:T(1024)S(1)}, f32[1024]{0:T(1024)S(1)}, u32[]{:S(2)}, u32[]{:S(2)}) collective-permute-start(f32[1024]{0:T(1024)S(1)} %multiply_subtract_fusion.1), channel_id=1, source_target_pairs={{0,1},{1,2},{2,3},{3,4},{4,5},{5,6},{6,7},{7,8},{8,9},{9,10},{10,1... | collective-permute-start | bytes 12296 | tf_op jit(solution)/shard_map/ppermute | solution.py:30
  264.7 3.4 collective-permute-done.33
  270.9 20.6 %shard_map.90 = f32[6,1,1024]{2,1,0:T(1,128)} custom-call(s32[6]{0:T(128)} %copy-done.4, s32[6]{0:T(128)} %bitcast.84, bf16[3,1024,128]{2,1,0:T(8,128)(2,1)} %copy-done, bf16[32,1024,128]{2,1,0:T(8,128)(2,1)} %a_ref.7, f32[6,1024,1]{2,1,0:T(8,128)} %copy.34.v_ref.w_ref), custom_call_target="tpu_custom_call" | custom-call | tf_op jit(solution)/shard_map/pallas_call | solution.py:92
  295.5 3.3 collective-permute-done.35
  306.1 20.7 %shard_map.91 = f32[6,1024,128]{2,1,0:T(8,128)} custom-call(s32[6]{0:T(128)} %bitcast.85, s32[6]{0:T(128)} %copy-done.4, bf16[32,1024,128]{2,1,0:T(8,128)(2,1)} %a_ref.7, bf16[3,1024,128]{2,1,0:T(8,128)(2,1)} %copy-done, f32[6,1,1024]{2,1,0:T(1,128)} %div.94.v_ref, f32[6,1024,1]{2,1,0:T(8,128)} %copy.34.v_ref.w_ref), custom_call_target="tpu_custom_call" | custom-call | tf_op jit(solution)/shard_map/pallas_call | solution.py:126
  326.8 3.8 select_reduce_fusion
  332.0 3.6 collective-permute-start.38
  335.6 5.4 %collective-permute-start.39 = (f32[1,1024,128]{2,1,0:T(8,128)}, f32[1,1024,128]{2,1,0:T(8,128)}, u32[]{:S(2)}, u32[]{:S(2)}) collective-permute-start(f32[1,1024,128]{2,1,0:T(8,128)} %get-tuple-element.8), channel_id=1, source_target_pairs={{0,1},{1,2},{2,3},{3,4},{4,5},{5,6},{6,7},{7,8},{8,9},{9,10},{10,1... | collective-permute-start | bytes 1572872 | tf_op jit(solution)/shard_map/ppermute | solution.py:30
  342.3 5.2 %collective-permute-start.41 = (f32[1,1024,128]{2,1,0:T(8,128)}, f32[1,1024,128]{2,1,0:T(8,128)}, u32[]{:S(2)}, u32[]{:S(2)}) collective-permute-start(f32[1,1024,128]{2,1,0:T(8,128)} %get-tuple-element.6), channel_id=1, source_target_pairs={{0,2},{1,3},{2,4},{3,5},{4,6},{5,7},{6,8},{7,9},{8,10},{9,11},{10,... | collective-permute-start | bytes 1572872 | tf_op jit(solution)/shard_map/ppermute | solution.py:30
  347.5 34.1 %all-gather = f32[32768]{0:T(1024)S(1)} all-gather(f32[1024]{0:T(1024)S(1)} %multiply_subtract_fusion.1), channel_id=2, replica_groups=mesh['gx'=4,'gy'=32] {'gy'}, dimensions={0}, use_global_device_ids=true | all-gather | bytes 135168 | tf_op jit(solution)/shard_map/all_gather | solution.py:189
  (158 shorter events, 100.1 us)
Async XLA Ops:
  0.6 16.0 %collective-permute-start = (bf16[1,1024,128]{2,1,0:T(8,128)(2,1)}, bf16[1,1024,128]{2,1,0:T(8,128)(2,1)S(1)}, u32[]{:S(2)}, u32[]{:S(2)}) collective-permute-start(bf16[1,1024,128]{2,1,0:T(8,128)(2,1)} %param.7), channel_id=1, source_target_pairs={{0,32},{32,64},{64,96},{1,33},{33,65},{65,97},{2,34},{34,66},{66,9... | collective-permute-start | bytes 786440 | tf_op jit(solution)/shard_map/ppermute | solution.py:19
  4.6 12.1 %collective-permute-start.1 = (bf16[1,1024,128]{2,1,0:T(8,128)(2,1)}, bf16[1,1024,128]{2,1,0:T(8,128)(2,1)S(1)}, u32[]{:S(2)}, u32[]{:S(2)}) collective-permute-start(bf16[1,1024,128]{2,1,0:T(8,128)(2,1)} %param.7), channel_id=1, source_target_pairs={{32,0},{64,32},{96,64},{33,1},{65,33},{97,65},{34,2},{66,34},{98,6... | collective-permute-start | bytes 786440 | tf_op jit(solution)/shard_map/ppermute | solution.py:22
  41.6 11.3 %collective-permute-start.2 = (f32[1024]{0:T(1024)S(1)}, f32[1024]{0:T(1024)S(1)}, u32[]{:S(2)}, u32[]{:S(2)}) collective-permute-start(f32[1024]{0:T(1024)S(1)} %bitcast.94), channel_id=1, source_target_pairs={{0,1},{1,2},{2,3},{3,4},{4,5},{5,6},{6,7},{7,8},{8,9},{9,10},{10,1... | collective-permute-start | bytes 12296 | tf_op jit(solution)/shard_map/ppermute | solution.py:30
  45.6 7.3 %collective-permute-start.3 = (f32[1024]{0:T(1024)S(1)}, f32[1024]{0:T(1024)S(1)}, u32[]{:S(2)}, u32[]{:S(2)}) collective-permute-start(f32[1024]{0:T(1024)S(1)} %bitcast.93), channel_id=1, source_target_pairs={{0,2},{1,3},{2,4},{3,5},{4,6},{5,7},{6,8},{7,9},{8,10},{9,11},{10,... | collective-permute-start | bytes 12296 | tf_op jit(solution)/shard_map/ppermute | solution.py:30
  49.0 4.9 %collective-permute-start.4 = (f32[1024]{0:T(1024)S(1)}, f32[1024]{0:T(1024)S(1)}, u32[]{:S(2)}, u32[]{:S(2)}) collective-permute-start(f32[1024]{0:T(1024)S(1)} %bitcast.92), channel_id=1, source_target_pairs={{1,0},{2,1},{3,2},{4,3},{5,4},{6,5},{7,6},{8,7},{9,8},{10,9},{11,1... | collective-permute-start | bytes 12296 | tf_op jit(solution)/shard_map/ppermute | solution.py:30
  55.3 11.2 %collective-permute-start.6 = (f32[1024]{0:T(1024)S(1)}, f32[1024]{0:T(1024)S(1)}, u32[]{:S(2)}, u32[]{:S(2)}) collective-permute-start(f32[1024]{0:T(1024)S(1)} %multiply_subtract_fusion.5), channel_id=1, source_target_pairs={{0,2},{1,3},{2,4},{3,5},{4,6},{5,7},{6,8},{7,9},{8,10},{9,11},{10,... | collective-permute-start | bytes 12296 | tf_op jit(solution)/shard_map/ppermute | solution.py:30
  58.2 8.3 %collective-permute-start.7 = (f32[1024]{0:T(1024)S(1)}, f32[1024]{0:T(1024)S(1)}, u32[]{:S(2)}, u32[]{:S(2)}) collective-permute-start(f32[1024]{0:T(1024)S(1)} %multiply_subtract_fusion.5), channel_id=1, source_target_pairs={{0,1},{1,2},{2,3},{3,4},{4,5},{5,6},{6,7},{7,8},{8,9},{9,10},{10,1... | collective-permute-start | bytes 12296 | tf_op jit(solution)/shard_map/ppermute | solution.py:30
  63.3 4.9 %collective-permute-start.8 = (f32[1024]{0:T(1024)S(1)}, f32[1024]{0:T(1024)S(1)}, u32[]{:S(2)}, u32[]{:S(2)}) collective-permute-start(f32[1024]{0:T(1024)S(1)} %multiply_subtract_fusion.5), channel_id=1, source_target_pairs={{1,0},{2,1},{3,2},{4,3},{5,4},{6,5},{7,6},{8,7},{9,8},{10,9},{11,1... | collective-permute-start | bytes 12296 | tf_op jit(solution)/shard_map/ppermute | solution.py:30
  65.2 6.4 %collective-permute-start.9 = (f32[1024]{0:T(1024)S(1)}, f32[1024]{0:T(1024)S(1)}, u32[]{:S(2)}, u32[]{:S(2)}) collective-permute-start(f32[1024]{0:T(1024)S(1)} %multiply_subtract_fusion.5), channel_id=1, source_target_pairs={{2,0},{3,1},{4,2},{5,3},{6,4},{7,5},{8,6},{9,7},{10,8},{11,9},{12,... | collective-permute-start | bytes 12296 | tf_op jit(solution)/shard_map/ppermute | solution.py:30
  96.1 5.6 %collective-permute-start.10 = (f32[1,1024]{1,0:T(1,128)S(1)}, f32[1,1024]{1,0:T(1,128)S(1)}, u32[]{:S(2)}, u32[]{:S(2)}) collective-permute-start(f32[1,1024]{1,0:T(1,128)S(1)} %get-tuple-element.28), channel_id=1, source_target_pairs={{0,32},{32,64},{64,96},{1,33},{33,65},{65,97},{2,34},{34,66},{66,9... | collective-permute-start | bytes 12296 | tf_op jit(solution)/shard_map/ppermute | solution.py:30
  100.4 4.6 %collective-permute-start.11 = (f32[1,1024]{1,0:T(1,128)S(1)}, f32[1,1024]{1,0:T(1,128)S(1)}, u32[]{:S(2)}, u32[]{:S(2)}) collective-permute-start(f32[1,1024]{1,0:T(1,128)S(1)} %get-tuple-element.29), channel_id=1, source_target_pairs={{32,0},{64,32},{96,64},{33,1},{65,33},{97,65},{34,2},{66,34},{98,6... | collective-permute-start | bytes 12296 | tf_op jit(solution)/shard_map/ppermute | solution.py:30
  136.7 14.3 %collective-permute-start.14 = (f32[1024]{0:T(1024)S(1)}, f32[1024]{0:T(1024)S(1)}, u32[]{:S(2)}, u32[]{:S(2)}) collective-permute-start(f32[1024]{0:T(1024)S(1)} %bitcast.101), channel_id=1, source_target_pairs={{0,1},{1,2},{2,3},{3,4},{4,5},{5,6},{6,7},{7,8},{8,9},{9,10},{10,1... | collective-permute-start | bytes 12296 | tf_op jit(solution)/shard_map/ppermute | solution.py:30
  144.1 6.9 %collective-permute-start.15 = (f32[1024]{0:T(1024)S(1)}, f32[1024]{0:T(1024)S(1)}, u32[]{:S(2)}, u32[]{:S(2)}) collective-permute-start(f32[1024]{0:T(1024)S(1)} %bitcast.99), channel_id=1, source_target_pairs={{0,2},{1,3},{2,4},{3,5},{4,6},{5,7},{6,8},{7,9},{8,10},{9,11},{10,... | collective-permute-start | bytes 12296 | tf_op jit(solution)/shard_map/ppermute | solution.py:30
  147.7 4.9 %collective-permute-start.16 = (f32[1024]{0:T(1024)S(1)}, f32[1024]{0:T(1024)S(1)}, u32[]{:S(2)}, u32[]{:S(2)}) collective-permute-start(f32[1024]{0:T(1024)S(1)} %bitcast.97), channel_id=1, source_target_pairs={{1,0},{2,1},{3,2},{4,3},{5,4},{6,5},{7,6},{8,7},{9,8},{10,9},{11,1... | collective-permute-start | bytes 12296 | tf_op jit(solution)/shard_map/ppermute | solution.py:30
  149.6 6.2 %collective-permute-start.17 = (f32[1024]{0:T(1024)S(1)}, f32[1024]{0:T(1024)S(1)}, u32[]{:S(2)}, u32[]{:S(2)}) collective-permute-start(f32[1024]{0:T(1024)S(1)} %bitcast.95), channel_id=1, source_target_pairs={{2,0},{3,1},{4,2},{5,3},{6,4},{7,5},{8,6},{9,7},{10,8},{11,9},{12,... | collective-permute-start | bytes 12296 | tf_op jit(solution)/shard_map/ppermute | solution.py:30
  155.9 11.7 %collective-permute-start.18 = (f32[1024]{0:T(1024)S(1)}, f32[1024]{0:T(1024)S(1)}, u32[]{:S(2)}, u32[]{:S(2)}) collective-permute-start(f32[1024]{0:T(1024)S(1)} %multiply_subtract_fusion.3), channel_id=1, source_target_pairs={{0,2},{1,3},{2,4},{3,5},{4,6},{5,7},{6,8},{7,9},{8,10},{9,11},{10,... | collective-permute-start | bytes 12296 | tf_op jit(solution)/shard_map/ppermute | solution.py:30
  159.3 8.3 %collective-permute-start.19 = (f32[1024]{0:T(1024)S(1)}, f32[1024]{0:T(1024)S(1)}, u32[]{:S(2)}, u32[]{:S(2)}) collective-permute-start(f32[1024]{0:T(1024)S(1)} %multiply_subtract_fusion.3), channel_id=1, source_target_pairs={{0,1},{1,2},{2,3},{3,4},{4,5},{5,6},{6,7},{7,8},{8,9},{9,10},{10,1... | collective-permute-start | bytes 12296 | tf_op jit(solution)/shard_map/ppermute | solution.py:30
  164.4 4.9 %collective-permute-start.20 = (f32[1024]{0:T(1024)S(1)}, f32[1024]{0:T(1024)S(1)}, u32[]{:S(2)}, u32[]{:S(2)}) collective-permute-start(f32[1024]{0:T(1024)S(1)} %multiply_subtract_fusion.3), channel_id=1, source_target_pairs={{1,0},{2,1},{3,2},{4,3},{5,4},{6,5},{7,6},{8,7},{9,8},{10,9},{11,1... | collective-permute-start | bytes 12296 | tf_op jit(solution)/shard_map/ppermute | solution.py:30
  166.3 5.2 %collective-permute-start.21 = (f32[1024]{0:T(1024)S(1)}, f32[1024]{0:T(1024)S(1)}, u32[]{:S(2)}, u32[]{:S(2)}) collective-permute-start(f32[1024]{0:T(1024)S(1)} %multiply_subtract_fusion.3), channel_id=1, source_target_pairs={{2,0},{3,1},{4,2},{5,3},{6,4},{7,5},{8,6},{9,7},{10,8},{11,9},{12,... | collective-permute-start | bytes 12296 | tf_op jit(solution)/shard_map/ppermute | solution.py:30
  233.9 13.9 %collective-permute-start.26 = (f32[1024]{0:T(1024)S(1)}, f32[1024]{0:T(1024)S(1)}, u32[]{:S(2)}, u32[]{:S(2)}) collective-permute-start(f32[1024]{0:T(1024)S(1)} %bitcast.102), channel_id=1, source_target_pairs={{0,1},{1,2},{2,3},{3,4},{4,5},{5,6},{6,7},{7,8},{8,9},{9,10},{10,1... | collective-permute-start | bytes 12296 | tf_op jit(solution)/shard_map/ppermute | solution.py:30
  240.7 7.1 %collective-permute-start.27 = (f32[1024]{0:T(1024)S(1)}, f32[1024]{0:T(1024)S(1)}, u32[]{:S(2)}, u32[]{:S(2)}) collective-permute-start(f32[1024]{0:T(1024)S(1)} %bitcast.100), channel_id=1, source_target_pairs={{0,2},{1,3},{2,4},{3,5},{4,6},{5,7},{6,8},{7,9},{8,10},{9,11},{10,... | collective-permute-start | bytes 12296 | tf_op jit(solution)/shard_map/ppermute | solution.py:30
  244.6 4.9 %collective-permute-start.28 = (f32[1024]{0:T(1024)S(1)}, f32[1024]{0:T(1024)S(1)}, u32[]{:S(2)}, u32[]{:S(2)}) collective-permute-start(f32[1024]{0:T(1024)S(1)} %bitcast.98), channel_id=1, source_target_pairs={{1,0},{2,1},{3,2},{4,3},{5,4},{6,5},{7,6},{8,7},{9,8},{10,9},{11,1... | collective-permute-start | bytes 12296 | tf_op jit(solution)/shard_map/ppermute | solution.py:30
  246.5 4.7 %collective-permute-start.29 = (f32[1024]{0:T(1024)S(1)}, f32[1024]{0:T(1024)S(1)}, u32[]{:S(2)}, u32[]{:S(2)}) collective-permute-start(f32[1024]{0:T(1024)S(1)} %bitcast.96), channel_id=1, source_target_pairs={{2,0},{3,1},{4,2},{5,3},{6,4},{7,5},{8,6},{9,7},{10,8},{11,9},{12,... | collective-permute-start | bytes 12296 | tf_op jit(solution)/shard_map/ppermute | solution.py:30
  251.3 11.7 %collective-permute-start.30 = (f32[1024]{0:T(1024)S(1)}, f32[1024]{0:T(1024)S(1)}, u32[]{:S(2)}, u32[]{:S(2)}) collective-permute-start(f32[1024]{0:T(1024)S(1)} %multiply_subtract_fusion.1), channel_id=1, source_target_pairs={{0,2},{1,3},{2,4},{3,5},{4,6},{5,7},{6,8},{7,9},{8,10},{9,11},{10,... | collective-permute-start | bytes 12296 | tf_op jit(solution)/shard_map/ppermute | solution.py:30
  254.7 8.3 %collective-permute-start.31 = (f32[1024]{0:T(1024)S(1)}, f32[1024]{0:T(1024)S(1)}, u32[]{:S(2)}, u32[]{:S(2)}) collective-permute-start(f32[1024]{0:T(1024)S(1)} %multiply_subtract_fusion.1), channel_id=1, source_target_pairs={{0,1},{1,2},{2,3},{3,4},{4,5},{5,6},{6,7},{7,8},{8,9},{9,10},{10,1... | collective-permute-start | bytes 12296 | tf_op jit(solution)/shard_map/ppermute | solution.py:30
  259.8 4.9 %collective-permute-start.32 = (f32[1024]{0:T(1024)S(1)}, f32[1024]{0:T(1024)S(1)}, u32[]{:S(2)}, u32[]{:S(2)}) collective-permute-start(f32[1024]{0:T(1024)S(1)} %multiply_subtract_fusion.1), channel_id=1, source_target_pairs={{1,0},{2,1},{3,2},{4,3},{5,4},{6,5},{7,6},{8,7},{9,8},{10,9},{11,1... | collective-permute-start | bytes 12296 | tf_op jit(solution)/shard_map/ppermute | solution.py:30
  261.7 6.4 %collective-permute-start.33 = (f32[1024]{0:T(1024)S(1)}, f32[1024]{0:T(1024)S(1)}, u32[]{:S(2)}, u32[]{:S(2)}) collective-permute-start(f32[1024]{0:T(1024)S(1)} %multiply_subtract_fusion.1), channel_id=1, source_target_pairs={{2,0},{3,1},{4,2},{5,3},{6,4},{7,5},{8,6},{9,7},{10,8},{11,9},{12,... | collective-permute-start | bytes 12296 | tf_op jit(solution)/shard_map/ppermute | solution.py:30
  294.2 4.6 %collective-permute-start.35 = (f32[1,1024]{1,0:T(1,128)S(1)}, f32[1,1024]{1,0:T(1,128)S(1)}, u32[]{:S(2)}, u32[]{:S(2)}) collective-permute-start(f32[1,1024]{1,0:T(1,128)S(1)} %get-tuple-element.25), channel_id=1, source_target_pairs={{32,0},{64,32},{96,64},{33,1},{65,33},{97,65},{34,2},{66,34},{98,6... | collective-permute-start | bytes 12296 | tf_op jit(solution)/shard_map/ppermute | solution.py:30
  332.0 50.3 %collective-permute-start.38 = (f32[1,1024,128]{2,1,0:T(8,128)}, f32[1,1024,128]{2,1,0:T(8,128)S(1)}, u32[]{:S(2)}, u32[]{:S(2)}) collective-permute-start(f32[1,1024,128]{2,1,0:T(8,128)} %get-tuple-element.5), channel_id=1, source_target_pairs={{1,0},{2,1},{3,2},{4,3},{5,4},{6,5},{7,6},{8,7},{9,8},{10,9},{11,1... | collective-permute-start | bytes 1572872 | tf_op jit(solution)/shard_map/ppermute | solution.py:30
  335.6 46.6 %collective-permute-start.39 = (f32[1,1024,128]{2,1,0:T(8,128)}, f32[1,1024,128]{2,1,0:T(8,128)}, u32[]{:S(2)}, u32[]{:S(2)}) collective-permute-start(f32[1,1024,128]{2,1,0:T(8,128)} %get-tuple-element.8), channel_id=1, source_target_pairs={{0,1},{1,2},{2,3},{3,4},{4,5},{5,6},{6,7},{7,8},{8,9},{9,10},{10,1... | collective-permute-start | bytes 1572872 | tf_op jit(solution)/shard_map/ppermute | solution.py:30
  341.0 41.2 %collective-permute-start.40 = (f32[1,1024,128]{2,1,0:T(8,128)}, f32[1,1024,128]{2,1,0:T(8,128)}, u32[]{:S(2)}, u32[]{:S(2)}) collective-permute-start(f32[1,1024,128]{2,1,0:T(8,128)} %get-tuple-element.7), channel_id=1, source_target_pairs={{2,0},{3,1},{4,2},{5,3},{6,4},{7,5},{8,6},{9,7},{10,8},{11,9},{12,... | collective-permute-start | bytes 1572872 | tf_op jit(solution)/shard_map/ppermute | solution.py:30
  342.3 39.9 %collective-permute-start.41 = (f32[1,1024,128]{2,1,0:T(8,128)}, f32[1,1024,128]{2,1,0:T(8,128)}, u32[]{:S(2)}, u32[]{:S(2)}) collective-permute-start(f32[1,1024,128]{2,1,0:T(8,128)} %get-tuple-element.6), channel_id=1, source_target_pairs={{0,2},{1,3},{2,4},{3,5},{4,6},{5,7},{6,8},{7,9},{8,10},{9,11},{10,... | collective-permute-start | bytes 1572872 | tf_op jit(solution)/shard_map/ppermute | solution.py:30
  (16 other events, 127.1 us)

commit v3 on v2

--- a/solution.py
+++ b/solution.py
@@ -61,7 +61,7 @@
 
 EPSILON = 0.03
 INV_EPS = 1.0 / EPSILON
-CHUNK = 256
+CHUNK = 512
 
 
 def _lse_kernel(a_ids, b_ids, a_ref, b_ref, v_ref, o_ref):
@@ -137,6 +137,41 @@
     return peak_val + jnp.log(jnp.sum(jnp.exp(masked - peak_val[:, None]), axis=1))
 
 
+def spread(block, axis, reach, has_sender):
+    width = block.shape[0]
+    index = lax.axis_index(axis)
+    count = lax.axis_size(axis)
+    parts = [block]
+    pad = jnp.full((reach,) + block.shape[1:], EMPTY_LOG, block.dtype)
+    for distance in range(-reach, reach + 1):
+        if distance == 0:
+            continue
+        got = passed_along(block, axis, distance)
+        valid = (index - distance >= 0) & (index - distance < count)
+        got = jnp.where(valid, got, EMPTY_LOG)
+        got = jnp.concatenate([pad, got, pad], axis=0)
+        parts.append(lax.slice_in_dim(got, reach + distance, reach + distance + width, axis=0))
+    parts = jnp.stack(parts)
+    peak_val = jnp.max(parts, axis=0)
+    return peak_val + jnp.log(jnp.sum(jnp.exp(parts - peak_val[None]), axis=0))
+
+
+def gather_rows(row, axis):
+    index = lax.axis_index(axis)
+    count = lax.axis_size(axis)
+    block = row
+    step = 1
+    while step < count:
+        route = [(i, i ^ step) for i in range(count)]
+        other = lax.ppermute(block, axis, route)
+        upper = (index // step) % 2 == 1
+        block = jnp.where(
+            upper, jnp.concatenate([other, block], axis=0), jnp.concatenate([block, other], axis=0)
+        )
+        step *= 2
+    return block
+
+
 def body(src_points, tgt_points, src_log_mass, tgt_log_mass, near_pairs, target_slot):
     owned = tgt_points.shape[0]
     group_size = src_points.shape[0]
@@ -154,40 +189,28 @@
     span_ids = jnp.clip(source_local - (gy_index - 2) * owned, 0, 5 * owned - 1)
     span_mask = span_ids[None, :] == jnp.arange(5 * owned, dtype=jnp.int32)[:, None]
     window_mask = window_ids[None, :] == jnp.arange(3 * owned, dtype=jnp.int32)[:, None]
-    src_sq = squares(src_points)
-    pair_src_sq = src_sq[source_local]
+    pair_src_sq = squares(src_points[source_local])
     window_pts, window_sq = fetch_points(tgt_points)
     pair_tgt_sq = window_sq[window_ids]
-    g_local = None
+    window_mass = fetch_potential(tgt_log_mass)
+    mass_pad = jnp.zeros((2 * owned,) + src_log_mass.shape[1:], src_log_mass.dtype)
+    span_mass = lax.dynamic_slice_in_dim(
+        jnp.concatenate([mass_pad, src_log_mass, mass_pad], axis=0), gy_index * owned, 5 * owned, 0
+    )
     g_window = jnp.zeros((3 * owned, src_points.shape[1]), jnp.float32)
     for sweep_index in range(ITERS):
-        if sweep_index > 0:
-            g_window = fetch_potential(g_local)
         v_row = (g_window[window_ids] - 0.5 * pair_tgt_sq) / EPSILON
         part = pair_lse(source_local, window_ids, src_points, window_pts, v_row[:, :, None])
         part = part[:, 0] - 0.5 * pair_src_sq / EPSILON
-        rows_span = grouped_lse(span_mask, part)
-        own_total = rows_span[2]
-        for distance in (1, 2, -1, -2):
-            got = passed_along(rows_span[2 + distance], "gy", distance)
-            has_sender = (gy_index - distance >= 0) & (gy_index - distance < gy_count)
-            own_total = log_add(own_total, jnp.where(has_sender, got, EMPTY_LOG))
-        f_own = EPSILON * pick(src_log_mass, gy_index) - EPSILON * own_total
-        f_span = [passed_along(f_own, "gy", -d) for d in (-2, -1)]
-        f_span = f_span + [f_own] + [passed_along(f_own, "gy", -d) for d in (1, 2)]
-        f_span = jnp.stack(f_span)
+        rows_total = spread(grouped_lse(span_mask, part), "gy", 4 * owned, None)
+        f_span = EPSILON * span_mass - EPSILON * rows_total
         v_col = (f_span[span_ids] - 0.5 * pair_src_sq) / EPSILON
         part = pair_lse(window_ids, source_local, window_pts, src_points, v_col[:, :, None])
         part = part[:, 0] - 0.5 * pair_tgt_sq / EPSILON
-        cols_part = grouped_lse(window_mask, part)
-        from_left = passed_along(cols_part[2 * owned :], "gx", 1)
-        from_right = passed_along(cols_part[:owned], "gx", -1)
-        from_left = jnp.where(gx_index > 0, from_left, EMPTY_LOG)
-        from_right = jnp.where(gx_index < gx_count - 1, from_right, EMPTY_LOG)
-        cols_total = log_add(log_add(cols_part[owned : 2 * owned], from_left), from_right)
-        g_local = EPSILON * tgt_log_mass - EPSILON * cols_total
-    f_pot = lax.all_gather(f_own[None], "gy", axis=0, tiled=True)
-    g_window = fetch_potential(g_local)
+        cols_total = spread(grouped_lse(window_mask, part), "gx", 2 * owned, None)
+        g_window = EPSILON * window_mass - EPSILON * cols_total
+    f_pot = gather_rows(f_span[2 * owned : 3 * owned], "gy")
+    g_local = g_window[owned : 2 * owned]
     v_row = (g_window[window_ids] - 0.5 * pair_tgt_sq) / EPSILON
     w_col = (f_span[span_ids] - 0.5 * pair_src_sq) / EPSILON
     contrib = pair_grad(

time: 390 us -> 329 us (0.84)
  starting transfers between devices: 117 us -> 162 us
  Pallas kernels: 144 us -> 101 us
  blocking collectives: 34.1 us -> 0 us
  waiting for transfers between devices: 43.2 us -> 17.2 us
  other arithmetic: 23.3 us -> 17.5 us
  local copies, waits for them, and re-layouts: 21.2 us -> 25.2 us
    pallas_call x6, Pallas kernels: 123 us -> 86.7 us  [pair_lse(): pl.pallas_call(_lse_kernel, grid_spec=spec, out_shape=jax.ShapeDtypeStruc...]
    ppermute x34 -> x40, starting transfers between devices: 101 us -> 137 us  [passed_along(): return lax.ppermute(block, axis, route)]
    all_gather x1 -> x0, blocking collectives: 34.1 us -> none  [body(): f_pot = lax.all_gather(f_own[None], 'gy', axis=0, tiled=True)]
    ppermute x34 -> x40, waiting for transfers between devices: 34.3 us -> 3.92 us  [passed_along(): return lax.ppermute(block, axis, route)]
    ppermute x0 -> x5, starting transfers between devices: none -> 14 us  [gather_rows(): other = lax.ppermute(block, axis, route)]
    ppermute x0 -> x5, waiting for transfers between devices: none -> 13.3 us  [gather_rows(): other = lax.ppermute(block, axis, route)]
    ppermute x4 -> x2, waiting for transfers between devices: 8.95 us -> 0.01 us  [padded(): lax.ppermute(lax.slice_in_dim(block, 0, width, axis=dim), axis, backward)]
    reduce_sum x2, other arithmetic: 8.3 us -> 1.37 us  [squares(): return jnp.sum(jnp.square(points.astype(jnp.float32)), axis=-1)]
  transfers between devices with their start and end apart: 42 -> 49, of which waited for: 18 -> 8; matrix products, arithmetic and copies ran while one was open for 3% -> 5% of each run, Pallas kernels for 0% -> 4%
where the time goes in v3:
time: 329 us; the launch traced here: 325 us
  starting transfers between devices  162 us (49%)
  Pallas kernels  101 us (31%)
  local copies, waits for them, and re-layouts  25.2 us (8%)
  other arithmetic  17.5 us (5%)
  waiting for transfers between devices  17.2 us (5%)
    ppermute x40, starting transfers between devices, passed_along(): return lax.ppermute(block, axis, route)  137 us
    pallas_call x6, Pallas kernels, pair_lse(): pl.pallas_call(_lse_kernel, grid_spec=spec, out_shape=jax.ShapeDtypeStruc...  86.7 us
    pallas_call x1, Pallas kernels, pair_grad(): pl.pallas_call(_grad_kernel, grid_spec=spec, out_shape=jax.ShapeDtypeStru...  14.2 us
    ppermute x5, starting transfers between devices, gather_rows(): other = lax.ppermute(block, axis, route)  14 us
    ppermute x5, waiting for transfers between devices, gather_rows(): other = lax.ppermute(block, axis, route)  13.3 us
    ppermute x2, starting transfers between devices, padded(): lax.ppermute(lax.slice_in_dim(block, block.shape[dim] - width, None, axis...  7.79 us
    div x4, local copies, waits for them, and re-layouts, body(): v_row = (g_window[window_ids] - 0.5 * pair_tgt_sq) / EPSILON  7.26 us
    div x3, local copies, waits for them, and re-layouts, body(): v_col = (f_span[span_ids] - 0.5 * pair_src_sq) / EPSILON  6.63 us
  transfers between devices with their start and end apart: 49, of which 8 were waited for; matrix products, arithmetic and copies ran while one was open for 5% of the time, Pallas kernels for 4%

profile of v3, /device:TPU:1, one launch (start us, length us, event | category | flops | bytes accessed | tf_op | source)
XLA Modules:
  0.0 324.8 jit_solution(119505636200284927)
XLA Ops:
  0.6 4.1 %collective-permute-start = (bf16[1,1024,128]{2,1,0:T(8,128)(2,1)}, bf16[1,1024,128]{2,1,0:T(8,128)(2,1)S(1)}, u32[]{:S(2)}, u32[]{:S(2)}) collective-permute-start(bf16[1,1024,128]{2,1,0:T(8,128)(2,1)} %param.7), channel_id=1, source_target_pairs={{0,32},{32,64},{64,96},{1,33},{33,65},{65,97},{2,34},{34,66},{66,9... | collective-permute-start | bytes 786440 | tf_op jit(solution)/shard_map/ppermute | solution.py:19
  8.2 4.2 %gather_fusion.2 = bf16[6,1024,128]{2,1,0:T(8,128)(2,1)S(1)} fusion(bf16[32,1024,128]{2,1,0:T(8,128)(2,1)} %a_ref.7, s32[1024]{0:T(1024)S(1)} %get-tuple-element.25), kind=kCustom, calls=%fused_computation.2 | custom fusion | bytes 3145752 | tf_op jit(solution)/shard_map/gather | solution.py:192
  17.4 14.5 %shard_map.85 = f32[6,1,1024]{2,1,0:T(1,128)} custom-call(s32[6]{0:T(128)} %bitcast.128, s32[6]{0:T(128)} %get-tuple-element.22.b_ids.a_ids, bf16[32,1024,128]{2,1,0:T(8,128)(2,1)} %a_ref.7, bf16[3,1024,128]{2,1,0:T(8,128)(2,1)} %copy-done, f32[6,1024,1]{2,1,0:T(8,128)} %copy.22.v_ref), custom_call_target="tpu_custom_call" | custom-call | tf_op jit(solution)/shard_map/pallas_call | solution.py:92
  40.3 4.2 %collective-permute-start.8 = (f32[5,1024]{1,0:T(8,128)S(1)}, f32[5,1024]{1,0:T(8,128)S(1)}, u32[]{:S(2)}, u32[]{:S(2)}) collective-permute-start(f32[5,1024]{1,0:T(8,128)S(1)} %get-tuple-element.16), channel_id=1, source_target_pairs={{0,1},{1,2},{2,3},{3,4},{4,5},{5,6},{6,7},{7,8},{8,9},{9,10},{10,1... | collective-permute-start | bytes 61448 | tf_op jit(solution)/shard_map/ppermute | solution.py:30
  44.5 4.3 %collective-permute-start.9 = (f32[5,1024]{1,0:T(8,128)S(1)}, f32[5,1024]{1,0:T(8,128)S(1)}, u32[]{:S(2)}, u32[]{:S(2)}) collective-permute-start(f32[5,1024]{1,0:T(8,128)S(1)} %get-tuple-element.16), channel_id=1, source_target_pairs={{0,2},{1,3},{2,4},{3,5},{4,6},{5,7},{6,8},{7,9},{8,10},{9,11},{10,... | collective-permute-start | bytes 61448 | tf_op jit(solution)/shard_map/ppermute | solution.py:30
  48.9 5.0 %collective-permute-start.10 = (f32[5,1024]{1,0:T(8,128)S(1)}, f32[5,1024]{1,0:T(8,128)S(1)}, u32[]{:S(2)}, u32[]{:S(2)}) collective-permute-start(f32[5,1024]{1,0:T(8,128)S(1)} %get-tuple-element.16), channel_id=1, source_target_pairs={{0,3},{1,4},{2,5},{3,6},{4,7},{5,8},{6,9},{7,10},{8,11},{9,12},{10... | collective-permute-start | bytes 61448 | tf_op jit(solution)/shard_map/ppermute | solution.py:30
  53.9 5.9 %collective-permute-start.11 = (f32[5,1024]{1,0:T(8,128)S(1)}, f32[5,1024]{1,0:T(8,128)S(1)}, u32[]{:S(2)}, u32[]{:S(2)}) collective-permute-start(f32[5,1024]{1,0:T(8,128)S(1)} %get-tuple-element.16), channel_id=1, source_target_pairs={{0,4},{1,5},{2,6},{3,7},{4,8},{5,9},{6,10},{7,11},{8,12},{9,13},{1... | collective-permute-start | bytes 61448 | tf_op jit(solution)/shard_map/ppermute | solution.py:30
  63.9 14.6 %shard_map.86 = f32[6,1,1024]{2,1,0:T(1,128)} custom-call(s32[6]{0:T(128)} %get-tuple-element.22.b_ids.a_ids, s32[6]{0:T(128)} %bitcast.129, bf16[3,1024,128]{2,1,0:T(8,128)(2,1)} %copy-done, bf16[32,1024,128]{2,1,0:T(8,128)(2,1)} %a_ref.7, f32[6,1024,1]{2,1,0:T(8,128)} %copy.23.v_ref), custom_call_target="tpu_custom_call" | custom-call | tf_op jit(solution)/shard_map/pallas_call | solution.py:92
  87.1 4.6 %collective-permute-start.14 = (f32[3,1024]{1,0:T(4,128)S(1)}, f32[3,1024]{1,0:T(4,128)S(1)}, u32[]{:S(2)}, u32[]{:S(2)}) collective-permute-start(f32[3,1024]{1,0:T(4,128)S(1)} %get-tuple-element.12), channel_id=1, source_target_pairs={{0,32},{32,64},{64,96},{1,33},{33,65},{65,97},{2,34},{34,66},{66,9... | collective-permute-start | bytes 36872 | tf_op jit(solution)/shard_map/ppermute | solution.py:30
  91.8 6.1 %collective-permute-start.15 = (f32[3,1024]{1,0:T(4,128)S(1)}, f32[3,1024]{1,0:T(4,128)S(1)}, u32[]{:S(2)}, u32[]{:S(2)}) collective-permute-start(f32[3,1024]{1,0:T(4,128)S(1)} %get-tuple-element.12), channel_id=1, source_target_pairs={{0,64},{32,96},{1,65},{33,97},{2,66},{34,98},{3,67},{35,99},{4,68}... | collective-permute-start | bytes 36872 | tf_op jit(solution)/shard_map/ppermute | solution.py:30
  101.7 14.3 %shard_map.87 = f32[6,1,1024]{2,1,0:T(1,128)} custom-call(s32[6]{0:T(128)} %bitcast.130, s32[6]{0:T(128)} %get-tuple-element.22.b_ids.a_ids, bf16[32,1024,128]{2,1,0:T(8,128)(2,1)} %a_ref.7, bf16[3,1024,128]{2,1,0:T(8,128)(2,1)} %copy-done, f32[6,1024,1]{2,1,0:T(8,128)} %copy.24.v_ref), custom_call_target="tpu_custom_call" | custom-call | tf_op jit(solution)/shard_map/pallas_call | solution.py:92
  121.0 5.6 %collective-permute-start.19 = (f32[5,1024]{1,0:T(8,128)S(1)}, f32[5,1024]{1,0:T(8,128)S(1)}, u32[]{:S(2)}, u32[]{:S(2)}) collective-permute-start(f32[5,1024]{1,0:T(8,128)S(1)} %get-tuple-element.10), channel_id=1, source_target_pairs={{1,0},{2,1},{3,2},{4,3},{5,4},{6,5},{7,6},{8,7},{9,8},{10,9},{11,1... | collective-permute-start | bytes 61448 | tf_op jit(solution)/shard_map/ppermute | solution.py:30
  126.5 4.2 %collective-permute-start.20 = (f32[5,1024]{1,0:T(8,128)S(1)}, f32[5,1024]{1,0:T(8,128)S(1)}, u32[]{:S(2)}, u32[]{:S(2)}) collective-permute-start(f32[5,1024]{1,0:T(8,128)S(1)} %get-tuple-element.10), channel_id=1, source_target_pairs={{0,1},{1,2},{2,3},{3,4},{4,5},{5,6},{6,7},{7,8},{8,9},{9,10},{10,1... | collective-permute-start | bytes 61448 | tf_op jit(solution)/shard_map/ppermute | solution.py:30
  130.7 4.6 %collective-permute-start.21 = (f32[5,1024]{1,0:T(8,128)S(1)}, f32[5,1024]{1,0:T(8,128)S(1)}, u32[]{:S(2)}, u32[]{:S(2)}) collective-permute-start(f32[5,1024]{1,0:T(8,128)S(1)} %get-tuple-element.10), channel_id=1, source_target_pairs={{0,2},{1,3},{2,4},{3,5},{4,6},{5,7},{6,8},{7,9},{8,10},{9,11},{10,... | collective-permute-start | bytes 61448 | tf_op jit(solution)/shard_map/ppermute | solution.py:30
  135.4 4.7 %collective-permute-start.22 = (f32[5,1024]{1,0:T(8,128)S(1)}, f32[5,1024]{1,0:T(8,128)S(1)}, u32[]{:S(2)}, u32[]{:S(2)}) collective-permute-start(f32[5,1024]{1,0:T(8,128)S(1)} %get-tuple-element.10), channel_id=1, source_target_pairs={{0,3},{1,4},{2,5},{3,6},{4,7},{5,8},{6,9},{7,10},{8,11},{9,12},{10... | collective-permute-start | bytes 61448 | tf_op jit(solution)/shard_map/ppermute | solution.py:30
  140.2 6.0 %collective-permute-start.23 = (f32[5,1024]{1,0:T(8,128)S(1)}, f32[5,1024]{1,0:T(8,128)S(1)}, u32[]{:S(2)}, u32[]{:S(2)}) collective-permute-start(f32[5,1024]{1,0:T(8,128)S(1)} %get-tuple-element.10), channel_id=1, source_target_pairs={{0,4},{1,5},{2,6},{3,7},{4,8},{5,9},{6,10},{7,11},{8,12},{9,13},{1... | collective-permute-start | bytes 61448 | tf_op jit(solution)/shard_map/ppermute | solution.py:30
  150.2 14.5 %shard_map.88 = f32[6,1,1024]{2,1,0:T(1,128)} custom-call(s32[6]{0:T(128)} %get-tuple-element.22.b_ids.a_ids, s32[6]{0:T(128)} %bitcast.131, bf16[3,1024,128]{2,1,0:T(8,128)(2,1)} %copy-done, bf16[32,1024,128]{2,1,0:T(8,128)(2,1)} %a_ref.7, f32[6,1024,1]{2,1,0:T(8,128)} %copy.25.v_ref), custom_call_target="tpu_custom_call" | custom-call | tf_op jit(solution)/shard_map/pallas_call | solution.py:92
  168.3 4.0 %collective-permute-start.26 = (f32[3,1024]{1,0:T(4,128)S(1)}, f32[3,1024]{1,0:T(4,128)S(1)}, u32[]{:S(2)}, u32[]{:S(2)}) collective-permute-start(f32[3,1024]{1,0:T(4,128)S(1)} %get-tuple-element.8), channel_id=1, source_target_pairs={{0,32},{32,64},{64,96},{1,33},{33,65},{65,97},{2,34},{34,66},{66,9... | collective-permute-start | bytes 36872 | tf_op jit(solution)/shard_map/ppermute | solution.py:30
  172.3 5.5 %collective-permute-start.27 = (f32[3,1024]{1,0:T(4,128)S(1)}, f32[3,1024]{1,0:T(4,128)S(1)}, u32[]{:S(2)}, u32[]{:S(2)}) collective-permute-start(f32[3,1024]{1,0:T(4,128)S(1)} %get-tuple-element.8), channel_id=1, source_target_pairs={{0,64},{32,96},{1,65},{33,97},{2,66},{34,98},{3,67},{35,99},{4,68}... | collective-permute-start | bytes 36872 | tf_op jit(solution)/shard_map/ppermute | solution.py:30
  181.6 14.3 %shard_map.89 = f32[6,1,1024]{2,1,0:T(1,128)} custom-call(s32[6]{0:T(128)} %bitcast.132, s32[6]{0:T(128)} %get-tuple-element.22.b_ids.a_ids, bf16[32,1024,128]{2,1,0:T(8,128)(2,1)} %a_ref.7, bf16[3,1024,128]{2,1,0:T(8,128)(2,1)} %copy-done, f32[6,1024,1]{2,1,0:T(8,128)} %copy.26.v_ref), custom_call_target="tpu_custom_call" | custom-call | tf_op jit(solution)/shard_map/pallas_call | solution.py:92
  201.1 4.9 %collective-permute-start.31 = (f32[5,1024]{1,0:T(8,128)S(1)}, f32[5,1024]{1,0:T(8,128)S(1)}, u32[]{:S(2)}, u32[]{:S(2)}) collective-permute-start(f32[5,1024]{1,0:T(8,128)S(1)} %get-tuple-element.6), channel_id=1, source_target_pairs={{1,0},{2,1},{3,2},{4,3},{5,4},{6,5},{7,6},{8,7},{9,8},{10,9},{11,1... | collective-permute-start | bytes 61448 | tf_op jit(solution)/shard_map/ppermute | solution.py:30
  206.1 4.2 %collective-permute-start.32 = (f32[5,1024]{1,0:T(8,128)S(1)}, f32[5,1024]{1,0:T(8,128)S(1)}, u32[]{:S(2)}, u32[]{:S(2)}) collective-permute-start(f32[5,1024]{1,0:T(8,128)S(1)} %get-tuple-element.6), channel_id=1, source_target_pairs={{0,1},{1,2},{2,3},{3,4},{4,5},{5,6},{6,7},{7,8},{8,9},{9,10},{10,1... | collective-permute-start | bytes 61448 | tf_op jit(solution)/shard_map/ppermute | solution.py:30
  210.2 4.6 %collective-permute-start.33 = (f32[5,1024]{1,0:T(8,128)S(1)}, f32[5,1024]{1,0:T(8,128)S(1)}, u32[]{:S(2)}, u32[]{:S(2)}) collective-permute-start(f32[5,1024]{1,0:T(8,128)S(1)} %get-tuple-element.6), channel_id=1, source_target_pairs={{0,2},{1,3},{2,4},{3,5},{4,6},{5,7},{6,8},{7,9},{8,10},{9,11},{10,... | collective-permute-start | bytes 61448 | tf_op jit(solution)/shard_map/ppermute | solution.py:30
  214.9 5.3 %collective-permute-start.34 = (f32[5,1024]{1,0:T(8,128)S(1)}, f32[5,1024]{1,0:T(8,128)S(1)}, u32[]{:S(2)}, u32[]{:S(2)}) collective-permute-start(f32[5,1024]{1,0:T(8,128)S(1)} %get-tuple-element.6), channel_id=1, source_target_pairs={{0,3},{1,4},{2,5},{3,6},{4,7},{5,8},{6,9},{7,10},{8,11},{9,12},{10... | collective-permute-start | bytes 61448 | tf_op jit(solution)/shard_map/ppermute | solution.py:30
  220.3 5.9 %collective-permute-start.35 = (f32[5,1024]{1,0:T(8,128)S(1)}, f32[5,1024]{1,0:T(8,128)S(1)}, u32[]{:S(2)}, u32[]{:S(2)}) collective-permute-start(f32[5,1024]{1,0:T(8,128)S(1)} %get-tuple-element.6), channel_id=1, source_target_pairs={{0,4},{1,5},{2,6},{3,7},{4,8},{5,9},{6,10},{7,11},{8,12},{9,13},{1... | collective-permute-start | bytes 61448 | tf_op jit(solution)/shard_map/ppermute | solution.py:30
  230.3 14.5 %shard_map.90 = f32[6,1,1024]{2,1,0:T(1,128)} custom-call(s32[6]{0:T(128)} %get-tuple-element.22.b_ids.a_ids, s32[6]{0:T(128)} %bitcast.133, bf16[3,1024,128]{2,1,0:T(8,128)(2,1)} %copy-done, bf16[32,1024,128]{2,1,0:T(8,128)(2,1)} %a_ref.7, f32[6,1024,1]{2,1,0:T(8,128)} %copy.27.v_ref.w_ref), custom_call_target="tpu_custom_call" | custom-call | tf_op jit(solution)/shard_map/pallas_call | solution.py:92
  250.1 4.0 %collective-permute-start.43 = (f32[3,1024]{1,0:T(4,128)S(1)}, f32[3,1024]{1,0:T(4,128)S(1)}, u32[]{:S(2)}, u32[]{:S(2)}) collective-permute-start(f32[3,1024]{1,0:T(4,128)S(1)} %get-tuple-element.4), channel_id=1, source_target_pairs={{0,32},{32,64},{64,96},{1,33},{33,65},{65,97},{2,34},{34,66},{66,9... | collective-permute-start | bytes 36872 | tf_op jit(solution)/shard_map/ppermute | solution.py:30
  254.1 5.5 %collective-permute-start.44 = (f32[3,1024]{1,0:T(4,128)S(1)}, f32[3,1024]{1,0:T(4,128)S(1)}, u32[]{:S(2)}, u32[]{:S(2)}) collective-permute-start(f32[3,1024]{1,0:T(4,128)S(1)} %get-tuple-element.4), channel_id=1, source_target_pairs={{0,64},{32,96},{1,65},{33,97},{2,66},{34,98},{3,67},{35,99},{4,68}... | collective-permute-start | bytes 36872 | tf_op jit(solution)/shard_map/ppermute | solution.py:30
  262.0 14.2 %shard_map.91 = f32[6,1024,128]{2,1,0:T(8,128)} custom-call(s32[6]{0:T(128)} %bitcast.134, s32[6]{0:T(128)} %get-tuple-element.22.b_ids.a_ids, bf16[32,1024,128]{2,1,0:T(8,128)(2,1)} %a_ref.7, bf16[3,1024,128]{2,1,0:T(8,128)(2,1)} %copy-done, f32[6,1,1024]{2,1,0:T(1,128)} %div.136.v_ref, f32[6,1024,1]{2,1,0:T(8,128)} %copy.27.v_ref.w_ref), custom_call_target="tpu_custom_call" | custom-call | tf_op jit(solution)/shard_map/pallas_call | solution.py:126
  288.8 7.7 %collective-permute-start.48 = (f32[1,1024,128]{2,1,0:T(8,128)}, f32[1,1024,128]{2,1,0:T(8,128)}, u32[]{:S(2)}, u32[]{:S(2)}) collective-permute-start(f32[1,1024,128]{2,1,0:T(8,128)} %get-tuple-element.18), channel_id=1, source_target_pairs={{0,2},{1,3},{2,4},{3,5},{4,6},{5,7},{6,8},{7,9},{8,10},{9,11},{10,... | collective-permute-start | bytes 1572872 | tf_op jit(solution)/shard_map/ppermute | solution.py:30
  296.6 4.5 %collective-permute-start.38 = (f32[4,1024]{1,0:T(4,128)S(1)}, f32[4,1024]{1,0:T(4,128)S(1)}, u32[]{:S(2)}, u32[]{:S(2)}) collective-permute-start(f32[4,1024]{1,0:T(4,128)S(1)} %maximum_select_fusion.3), channel_id=1, source_target_pairs={{0,4},{1,5},{2,6},{3,7},{4,0},{5,1},{6,2},{7,3},{8,12},{9,13},{10,... | collective-permute-start | bytes 49160 | tf_op jit(solution)/shard_map/ppermute | solution.py:166
  301.1 10.6 %collective-permute-done.38 = f32[4,1024]{1,0:T(4,128)S(1)} collective-permute-done((f32[4,1024]{1,0:T(4,128)S(1)}, f32[4,1024]{1,0:T(4,128)S(1)}, u32[]{:S(2)}, u32[]{:S(2)}) %collective-permute-start.38) | collective-permute-done | bytes 16416 | tf_op jit(solution)/shard_map/ppermute | solution.py:166
  (248 shorter events, 91.2 us)
Async XLA Ops:
  0.6 13.3 %collective-permute-start = (bf16[1,1024,128]{2,1,0:T(8,128)(2,1)}, bf16[1,1024,128]{2,1,0:T(8,128)(2,1)S(1)}, u32[]{:S(2)}, u32[]{:S(2)}) collective-permute-start(bf16[1,1024,128]{2,1,0:T(8,128)(2,1)} %param.7), channel_id=1, source_target_pairs={{0,32},{32,64},{64,96},{1,33},{33,65},{65,97},{2,34},{34,66},{66,9... | collective-permute-start | bytes 786440 | tf_op jit(solution)/shard_map/ppermute | solution.py:19
  34.3 14.6 %collective-permute-start.5 = (f32[5,1024]{1,0:T(8,128)S(1)}, f32[5,1024]{1,0:T(8,128)S(1)}, u32[]{:S(2)}, u32[]{:S(2)}) collective-permute-start(f32[5,1024]{1,0:T(8,128)S(1)} %get-tuple-element.16), channel_id=1, source_target_pairs={{3,0},{4,1},{5,2},{6,3},{7,4},{8,5},{9,6},{10,7},{11,8},{12,9},{13... | collective-permute-start | bytes 61448 | tf_op jit(solution)/shard_map/ppermute | solution.py:30
  35.6 18.3 %collective-permute-start.6 = (f32[5,1024]{1,0:T(8,128)S(1)}, f32[5,1024]{1,0:T(8,128)S(1)}, u32[]{:S(2)}, u32[]{:S(2)}) collective-permute-start(f32[5,1024]{1,0:T(8,128)S(1)} %get-tuple-element.16), channel_id=1, source_target_pairs={{2,0},{3,1},{4,2},{5,3},{6,4},{7,5},{8,6},{9,7},{10,8},{11,9},{12,... | collective-permute-start | bytes 61448 | tf_op jit(solution)/shard_map/ppermute | solution.py:30
  36.9 23.0 %collective-permute-start.7 = (f32[5,1024]{1,0:T(8,128)S(1)}, f32[5,1024]{1,0:T(8,128)S(1)}, u32[]{:S(2)}, u32[]{:S(2)}) collective-permute-start(f32[5,1024]{1,0:T(8,128)S(1)} %get-tuple-element.16), channel_id=1, source_target_pairs={{1,0},{2,1},{3,2},{4,3},{5,4},{6,5},{7,6},{8,7},{9,8},{10,9},{11,1... | collective-permute-start | bytes 61448 | tf_op jit(solution)/shard_map/ppermute | solution.py:30
  40.3 19.6 %collective-permute-start.8 = (f32[5,1024]{1,0:T(8,128)S(1)}, f32[5,1024]{1,0:T(8,128)S(1)}, u32[]{:S(2)}, u32[]{:S(2)}) collective-permute-start(f32[5,1024]{1,0:T(8,128)S(1)} %get-tuple-element.16), channel_id=1, source_target_pairs={{0,1},{1,2},{2,3},{3,4},{4,5},{5,6},{6,7},{7,8},{8,9},{9,10},{10,1... | collective-permute-start | bytes 61448 | tf_op jit(solution)/shard_map/ppermute | solution.py:30
  44.5 15.5 %collective-permute-start.9 = (f32[5,1024]{1,0:T(8,128)S(1)}, f32[5,1024]{1,0:T(8,128)S(1)}, u32[]{:S(2)}, u32[]{:S(2)}) collective-permute-start(f32[5,1024]{1,0:T(8,128)S(1)} %get-tuple-element.16), channel_id=1, source_target_pairs={{0,2},{1,3},{2,4},{3,5},{4,6},{5,7},{6,8},{7,9},{8,10},{9,11},{10,... | collective-permute-start | bytes 61448 | tf_op jit(solution)/shard_map/ppermute | solution.py:30
  79.5 12.3 %collective-permute-start.12 = (f32[3,1024]{1,0:T(4,128)S(1)}, f32[3,1024]{1,0:T(4,128)S(1)}, u32[]{:S(2)}, u32[]{:S(2)}) collective-permute-start(f32[3,1024]{1,0:T(4,128)S(1)} %get-tuple-element.12), channel_id=1, source_target_pairs={{64,0},{96,32},{65,1},{97,33},{66,2},{98,34},{67,3},{99,35},{68,4}... | collective-permute-start | bytes 36872 | tf_op jit(solution)/shard_map/ppermute | solution.py:30
  80.8 18.0 %collective-permute-start.2 = (f32[1,1024]{1,0:T(1,128)S(1)}, f32[1,1024]{1,0:T(1,128)S(1)}, u32[]{:S(2)}, u32[]{:S(2)}) collective-permute-start(f32[1,1024]{1,0:T(1,128)S(1)} %copy-done.4), channel_id=1, source_target_pairs={{0,32},{32,64},{64,96},{1,33},{33,65},{65,97},{2,34},{34,66},{66,9... | collective-permute-start | bytes 12296 | tf_op jit(solution)/shard_map/ppermute | solution.py:19
  84.5 14.3 %collective-permute-start.3 = (f32[1,1024]{1,0:T(1,128)S(1)}, f32[1,1024]{1,0:T(1,128)S(1)}, u32[]{:S(2)}, u32[]{:S(2)}) collective-permute-start(f32[1,1024]{1,0:T(1,128)S(1)} %copy-done.4), channel_id=1, source_target_pairs={{32,0},{64,32},{96,64},{33,1},{65,33},{97,65},{34,2},{66,34},{98,6... | collective-permute-start | bytes 12296 | tf_op jit(solution)/shard_map/ppermute | solution.py:22
  85.8 12.1 %collective-permute-start.13 = (f32[3,1024]{1,0:T(4,128)S(1)}, f32[3,1024]{1,0:T(4,128)S(1)}, u32[]{:S(2)}, u32[]{:S(2)}) collective-permute-start(f32[3,1024]{1,0:T(4,128)S(1)} %get-tuple-element.12), channel_id=1, source_target_pairs={{32,0},{64,32},{96,64},{33,1},{65,33},{97,65},{34,2},{66,34},{98,6... | collective-permute-start | bytes 36872 | tf_op jit(solution)/shard_map/ppermute | solution.py:30
  117.1 13.7 %collective-permute-start.16 = (f32[5,1024]{1,0:T(8,128)S(1)}, f32[5,1024]{1,0:T(8,128)S(1)}, u32[]{:S(2)}, u32[]{:S(2)}) collective-permute-start(f32[5,1024]{1,0:T(8,128)S(1)} %get-tuple-element.10), channel_id=1, source_target_pairs={{4,0},{5,1},{6,2},{7,3},{8,4},{9,5},{10,6},{11,7},{12,8},{13,9},{1... | collective-permute-start | bytes 61448 | tf_op jit(solution)/shard_map/ppermute | solution.py:30
  118.4 17.0 %collective-permute-start.17 = (f32[5,1024]{1,0:T(8,128)S(1)}, f32[5,1024]{1,0:T(8,128)S(1)}, u32[]{:S(2)}, u32[]{:S(2)}) collective-permute-start(f32[5,1024]{1,0:T(8,128)S(1)} %get-tuple-element.10), channel_id=1, source_target_pairs={{3,0},{4,1},{5,2},{6,3},{7,4},{8,5},{9,6},{10,7},{11,8},{12,9},{13... | collective-permute-start | bytes 61448 | tf_op jit(solution)/shard_map/ppermute | solution.py:30
  119.7 20.5 %collective-permute-start.18 = (f32[5,1024]{1,0:T(8,128)S(1)}, f32[5,1024]{1,0:T(8,128)S(1)}, u32[]{:S(2)}, u32[]{:S(2)}) collective-permute-start(f32[5,1024]{1,0:T(8,128)S(1)} %get-tuple-element.10), channel_id=1, source_target_pairs={{2,0},{3,1},{4,2},{5,3},{6,4},{7,5},{8,6},{9,7},{10,8},{11,9},{12,... | collective-permute-start | bytes 61448 | tf_op jit(solution)/shard_map/ppermute | solution.py:30
  121.0 25.3 %collective-permute-start.19 = (f32[5,1024]{1,0:T(8,128)S(1)}, f32[5,1024]{1,0:T(8,128)S(1)}, u32[]{:S(2)}, u32[]{:S(2)}) collective-permute-start(f32[5,1024]{1,0:T(8,128)S(1)} %get-tuple-element.10), channel_id=1, source_target_pairs={{1,0},{2,1},{3,2},{4,3},{5,4},{6,5},{7,6},{8,7},{9,8},{10,9},{11,1... | collective-permute-start | bytes 61448 | tf_op jit(solution)/shard_map/ppermute | solution.py:30
  126.5 19.8 %collective-permute-start.20 = (f32[5,1024]{1,0:T(8,128)S(1)}, f32[5,1024]{1,0:T(8,128)S(1)}, u32[]{:S(2)}, u32[]{:S(2)}) collective-permute-start(f32[5,1024]{1,0:T(8,128)S(1)} %get-tuple-element.10), channel_id=1, source_target_pairs={{0,1},{1,2},{2,3},{3,4},{4,5},{5,6},{6,7},{7,8},{8,9},{9,10},{10,1... | collective-permute-start | bytes 61448 | tf_op jit(solution)/shard_map/ppermute | solution.py:30
  130.7 15.7 %collective-permute-start.21 = (f32[5,1024]{1,0:T(8,128)S(1)}, f32[5,1024]{1,0:T(8,128)S(1)}, u32[]{:S(2)}, u32[]{:S(2)}) collective-permute-start(f32[5,1024]{1,0:T(8,128)S(1)} %get-tuple-element.10), channel_id=1, source_target_pairs={{0,2},{1,3},{2,4},{3,5},{4,6},{5,7},{6,8},{7,9},{8,10},{9,11},{10,... | collective-permute-start | bytes 61448 | tf_op jit(solution)/shard_map/ppermute | solution.py:30
  165.7 12.1 %collective-permute-start.24 = (f32[3,1024]{1,0:T(4,128)S(1)}, f32[3,1024]{1,0:T(4,128)S(1)}, u32[]{:S(2)}, u32[]{:S(2)}) collective-permute-start(f32[3,1024]{1,0:T(4,128)S(1)} %get-tuple-element.8), channel_id=1, source_target_pairs={{64,0},{96,32},{65,1},{97,33},{66,2},{98,34},{67,3},{99,35},{68,4}... | collective-permute-start | bytes 36872 | tf_op jit(solution)/shard_map/ppermute | solution.py:30
  197.0 13.2 %collective-permute-start.28 = (f32[5,1024]{1,0:T(8,128)S(1)}, f32[5,1024]{1,0:T(8,128)S(1)}, u32[]{:S(2)}, u32[]{:S(2)}) collective-permute-start(f32[5,1024]{1,0:T(8,128)S(1)} %get-tuple-element.6), channel_id=1, source_target_pairs={{4,0},{5,1},{6,2},{7,3},{8,4},{9,5},{10,6},{11,7},{12,8},{13,9},{1... | collective-permute-start | bytes 61448 | tf_op jit(solution)/shard_map/ppermute | solution.py:30
  198.4 16.6 %collective-permute-start.29 = (f32[5,1024]{1,0:T(8,128)S(1)}, f32[5,1024]{1,0:T(8,128)S(1)}, u32[]{:S(2)}, u32[]{:S(2)}) collective-permute-start(f32[5,1024]{1,0:T(8,128)S(1)} %get-tuple-element.6), channel_id=1, source_target_pairs={{3,0},{4,1},{5,2},{6,3},{7,4},{8,5},{9,6},{10,7},{11,8},{12,9},{13... | collective-permute-start | bytes 61448 | tf_op jit(solution)/shard_map/ppermute | solution.py:30
  199.8 20.5 %collective-permute-start.30 = (f32[5,1024]{1,0:T(8,128)S(1)}, f32[5,1024]{1,0:T(8,128)S(1)}, u32[]{:S(2)}, u32[]{:S(2)}) collective-permute-start(f32[5,1024]{1,0:T(8,128)S(1)} %get-tuple-element.6), channel_id=1, source_target_pairs={{2,0},{3,1},{4,2},{5,3},{6,4},{7,5},{8,6},{9,7},{10,8},{11,9},{12,... | collective-permute-start | bytes 61448 | tf_op jit(solution)/shard_map/ppermute | solution.py:30
  201.1 25.1 %collective-permute-start.31 = (f32[5,1024]{1,0:T(8,128)S(1)}, f32[5,1024]{1,0:T(8,128)S(1)}, u32[]{:S(2)}, u32[]{:S(2)}) collective-permute-start(f32[5,1024]{1,0:T(8,128)S(1)} %get-tuple-element.6), channel_id=1, source_target_pairs={{1,0},{2,1},{3,2},{4,3},{5,4},{6,5},{7,6},{8,7},{9,8},{10,9},{11,1... | collective-permute-start | bytes 61448 | tf_op jit(solution)/shard_map/ppermute | solution.py:30
  206.1 20.3 %collective-permute-start.32 = (f32[5,1024]{1,0:T(8,128)S(1)}, f32[5,1024]{1,0:T(8,128)S(1)}, u32[]{:S(2)}, u32[]{:S(2)}) collective-permute-start(f32[5,1024]{1,0:T(8,128)S(1)} %get-tuple-element.6), channel_id=1, source_target_pairs={{0,1},{1,2},{2,3},{3,4},{4,5},{5,6},{6,7},{7,8},{8,9},{9,10},{10,1... | collective-permute-start | bytes 61448 | tf_op jit(solution)/shard_map/ppermute | solution.py:30
  210.2 16.1 %collective-permute-start.33 = (f32[5,1024]{1,0:T(8,128)S(1)}, f32[5,1024]{1,0:T(8,128)S(1)}, u32[]{:S(2)}, u32[]{:S(2)}) collective-permute-start(f32[5,1024]{1,0:T(8,128)S(1)} %get-tuple-element.6), channel_id=1, source_target_pairs={{0,2},{1,3},{2,4},{3,5},{4,6},{5,7},{6,8},{7,9},{8,10},{9,11},{10,... | collective-permute-start | bytes 61448 | tf_op jit(solution)/shard_map/ppermute | solution.py:30
  245.7 13.9 %collective-permute-start.36 = (f32[1,1024]{1,0:T(1,128)S(1)}, f32[1,1024]{1,0:T(1,128)S(1)}, u32[]{:S(2)}, u32[]{:S(2)}) collective-permute-start(f32[1,1024]{1,0:T(1,128)S(1)} %slice.198), channel_id=1, source_target_pairs={{0,1},{1,0},{2,3},{3,2},{4,5},{5,4},{6,7},{7,6},{8,9},{9,8},{10,11... | collective-permute-start | bytes 12296 | tf_op jit(solution)/shard_map/ppermute | solution.py:166
  247.5 13.1 %collective-permute-start.41 = (f32[3,1024]{1,0:T(4,128)S(1)}, f32[3,1024]{1,0:T(4,128)S(1)}, u32[]{:S(2)}, u32[]{:S(2)}) collective-permute-start(f32[3,1024]{1,0:T(4,128)S(1)} %get-tuple-element.4), channel_id=1, source_target_pairs={{64,0},{96,32},{65,1},{97,33},{66,2},{98,34},{67,3},{99,35},{68,4}... | collective-permute-start | bytes 36872 | tf_op jit(solution)/shard_map/ppermute | solution.py:30
  248.8 11.8 %collective-permute-start.42 = (f32[3,1024]{1,0:T(4,128)S(1)}, f32[3,1024]{1,0:T(4,128)S(1)}, u32[]{:S(2)}, u32[]{:S(2)}) collective-permute-start(f32[3,1024]{1,0:T(4,128)S(1)} %get-tuple-element.4), channel_id=1, source_target_pairs={{32,0},{64,32},{96,64},{33,1},{65,33},{97,65},{34,2},{66,34},{98,6... | collective-permute-start | bytes 36872 | tf_op jit(solution)/shard_map/ppermute | solution.py:30
  259.6 36.9 %collective-permute-start.37 = (f32[2,1024]{1,0:T(2,128)S(1)}, f32[2,1024]{1,0:T(2,128)S(1)}, u32[]{:S(2)}, u32[]{:S(2)}) collective-permute-start(f32[2,1024]{1,0:T(2,128)S(1)} %maximum_select_fusion.4), channel_id=1, source_target_pairs={{0,2},{1,3},{2,0},{3,1},{4,6},{5,7},{6,4},{7,5},{8,10},{9,11},{10,... | collective-permute-start | bytes 24584 | tf_op jit(solution)/shard_map/ppermute | solution.py:166
  281.4 41.1 %collective-permute-start.45 = (f32[1,1024,128]{2,1,0:T(8,128)}, f32[1,1024,128]{2,1,0:T(8,128)S(1)}, u32[]{:S(2)}, u32[]{:S(2)}) collective-permute-start(f32[1,1024,128]{2,1,0:T(8,128)} %get-tuple-element.17), channel_id=1, source_target_pairs={{1,0},{2,1},{3,2},{4,3},{5,4},{6,5},{7,6},{8,7},{9,8},{10,9},{11,1... | collective-permute-start | bytes 1572872 | tf_op jit(solution)/shard_map/ppermute | solution.py:30
  284.8 37.8 %collective-permute-start.46 = (f32[1,1024,128]{2,1,0:T(8,128)}, f32[1,1024,128]{2,1,0:T(8,128)}, u32[]{:S(2)}, u32[]{:S(2)}) collective-permute-start(f32[1,1024,128]{2,1,0:T(8,128)} %get-tuple-element.20), channel_id=1, source_target_pairs={{0,1},{1,2},{2,3},{3,4},{4,5},{5,6},{6,7},{7,8},{8,9},{9,10},{10,1... | collective-permute-start | bytes 1572872 | tf_op jit(solution)/shard_map/ppermute | solution.py:30
  287.5 35.0 %collective-permute-start.47 = (f32[1,1024,128]{2,1,0:T(8,128)}, f32[1,1024,128]{2,1,0:T(8,128)}, u32[]{:S(2)}, u32[]{:S(2)}) collective-permute-start(f32[1,1024,128]{2,1,0:T(8,128)} %get-tuple-element.19), channel_id=1, source_target_pairs={{2,0},{3,1},{4,2},{5,3},{6,4},{7,5},{8,6},{9,7},{10,8},{11,9},{12,... | collective-permute-start | bytes 1572872 | tf_op jit(solution)/shard_map/ppermute | solution.py:30
  288.8 33.7 %collective-permute-start.48 = (f32[1,1024,128]{2,1,0:T(8,128)}, f32[1,1024,128]{2,1,0:T(8,128)}, u32[]{:S(2)}, u32[]{:S(2)}) collective-permute-start(f32[1,1024,128]{2,1,0:T(8,128)} %get-tuple-element.18), channel_id=1, source_target_pairs={{0,2},{1,3},{2,4},{3,5},{4,6},{5,7},{6,8},{7,9},{8,10},{9,11},{10,... | collective-permute-start | bytes 1572872 | tf_op jit(solution)/shard_map/ppermute | solution.py:30
  296.6 15.1 %collective-permute-start.38 = (f32[4,1024]{1,0:T(4,128)S(1)}, f32[4,1024]{1,0:T(4,128)S(1)}, u32[]{:S(2)}, u32[]{:S(2)}) collective-permute-start(f32[4,1024]{1,0:T(4,128)S(1)} %maximum_select_fusion.3), channel_id=1, source_target_pairs={{0,4},{1,5},{2,6},{3,7},{4,0},{5,1},{6,2},{7,3},{8,12},{9,13},{10,... | collective-permute-start | bytes 49160 | tf_op jit(solution)/shard_map/ppermute | solution.py:166
  (23 other events, 248.7 us)

commit v4 on v3

--- a/solution.py
+++ b/solution.py
@@ -61,20 +61,20 @@
 
 EPSILON = 0.03
 INV_EPS = 1.0 / EPSILON
-CHUNK = 512
+CHUNK = 1024
 
 
 def _lse_kernel(a_ids, b_ids, a_ref, b_ref, v_ref, o_ref):
     tile = lax.dot_general(
         b_ref[0], a_ref[0], (((1,), (1,)), ((), ())), preferred_element_type=jnp.float32
     )
-    scores = tile * INV_EPS + v_ref[0]
+    scores = tile * INV_EPS + jnp.transpose(v_ref[0])[:, :1]
     peak = jnp.max(scores, axis=0, keepdims=True)
     total = jnp.sum(jnp.exp(scores - peak), axis=0, keepdims=True)
     o_ref[0] = peak + jnp.log(total)
 
 
-def pair_lse(a_ids, b_ids, a_pts, b_pts, v_col, interpret=False):
+def pair_lse(a_ids, b_ids, a_pts, b_pts, v_rows, interpret=False):
     pairs = a_ids.shape[0]
     rows = a_pts.shape[1]
     coords = a_pts.shape[2]
@@ -85,7 +85,7 @@
         in_specs=[
             pl.BlockSpec((1, CHUNK, coords), lambda p, c, ai, bi: (ai[p], c, 0)),
             pl.BlockSpec((1, cols, coords), lambda p, c, ai, bi: (bi[p], 0, 0)),
-            pl.BlockSpec((1, cols, 1), lambda p, c, ai, bi: (p, 0, 0)),
+            pl.BlockSpec((1, 8, cols), lambda p, c, ai, bi: (p, 0, 0)),
         ],
         out_specs=pl.BlockSpec((1, 1, CHUNK), lambda p, c, ai, bi: (p, 0, c)),
     )
@@ -94,7 +94,7 @@
         grid_spec=spec,
         out_shape=jax.ShapeDtypeStruct((pairs, 1, rows), jnp.float32),
         interpret=interpret,
-    )(a_ids, b_ids, a_pts, b_pts, v_col)
+    )(a_ids, b_ids, a_pts, b_pts, v_rows)
 
 
 def _grad_kernel(a_ids, b_ids, a_ref, b_ref, v_ref, w_ref, o_ref):
@@ -156,6 +156,52 @@
     return peak_val + jnp.log(jnp.sum(jnp.exp(parts - peak_val[None]), axis=0))
 
 
+def shifted(block, shift, width):
+    reach = abs(shift) + width
+    pad = jnp.full((reach,) + block.shape[1:], EMPTY_LOG, block.dtype)
+    padded_block = jnp.concatenate([pad, block, pad], axis=0)
+    return lax.slice_in_dim(padded_block, reach + shift, reach + shift + width, axis=0)
+
+
+def received(block, axis, distance):
+    index = lax.axis_index(axis)
+    count = lax.axis_size(axis)
+    got = passed_along(block, axis, distance)
+    valid = (index - distance >= 0) & (index - distance < count)
+    return jnp.where(valid, got, EMPTY_LOG)
+
+
+def lse_stack(parts):
+    parts = jnp.stack(parts)
+    peak_val = jnp.max(parts, axis=0)
+    return peak_val + jnp.log(jnp.sum(jnp.exp(parts - peak_val[None]), axis=0))
+
+
+def spread_rows(block, axis, owned):
+    index = lax.axis_index(axis)
+    count = lax.axis_size(axis)
+    edge = lax.ppermute(block, axis, [(0, 2), (count - 1, count - 3)])
+    edge = jnp.where(
+        index == 2, shifted(edge, 2 * owned, 5 * owned), shifted(edge, -2 * owned, 5 * owned)
+    )
+    edge = jnp.where((index == 2) | (index == count - 3), edge, EMPTY_LOG)
+    first = lse_stack(
+        [
+            shifted(block, -owned, 7 * owned),
+            shifted(received(block, axis, 1), 0, 7 * owned),
+            shifted(received(block, axis, -1), -2 * owned, 7 * owned),
+        ]
+    )
+    return lse_stack(
+        [
+            shifted(first, owned, 5 * owned),
+            shifted(received(first, axis, 3), 4 * owned, 5 * owned),
+            shifted(received(first, axis, -3), -2 * owned, 5 * owned),
+            edge,
+        ]
+    )
+
+
 def gather_rows(row, axis):
     index = lax.axis_index(axis)
     count = lax.axis_size(axis)
@@ -200,12 +246,12 @@
     g_window = jnp.zeros((3 * owned, src_points.shape[1]), jnp.float32)
     for sweep_index in range(ITERS):
         v_row = (g_window[window_ids] - 0.5 * pair_tgt_sq) / EPSILON
-        part = pair_lse(source_local, window_ids, src_points, window_pts, v_row[:, :, None])
+        part = pair_lse(source_local, window_ids, src_points, window_pts, jnp.broadcast_to(v_row[:, None, :], (v_row.shape[0], 8, v_row.shape[1])))
         part = part[:, 0] - 0.5 * pair_src_sq / EPSILON
-        rows_total = spread(grouped_lse(span_mask, part), "gy", 4 * owned, None)
+        rows_total = spread_rows(grouped_lse(span_mask, part), "gy", owned)
         f_span = EPSILON * span_mass - EPSILON * rows_total
         v_col = (f_span[span_ids] - 0.5 * pair_src_sq) / EPSILON
-        part = pair_lse(window_ids, source_local, window_pts, src_points, v_col[:, :, None])
+        part = pair_lse(window_ids, source_local, window_pts, src_points, jnp.broadcast_to(v_col[:, None, :], (v_col.shape[0], 8, v_col.shape[1])))
         part = part[:, 0] - 0.5 * pair_tgt_sq / EPSILON
         cols_total = spread(grouped_lse(window_mask, part), "gx", 2 * owned, None)
         g_window = EPSILON * window_mass - EPSILON * cols_total

time: 329 us -> 277 us (0.84)
  starting transfers between devices: 162 us -> 125 us
  Pallas kernels: 101 us -> 84.8 us
  waiting for transfers between devices: 17.2 us -> 27.4 us
  local copies, waits for them, and re-layouts: 25.2 us -> 18 us
    ppermute x40 -> x28, starting transfers between devices: 137 us -> 99.5 us  [passed_along(): return lax.ppermute(block, axis, route)]
    pallas_call x6, Pallas kernels: 86.7 us -> 73.7 us  [pair_lse(): pl.pallas_call(_lse_kernel, grid_spec=spec, out_shape=jax.ShapeDtypeStruc...]
    ppermute x40 -> x28, waiting for transfers between devices: 3.92 us -> 14.1 us  [passed_along(): return lax.ppermute(block, axis, route)]
    div x4 -> x1, local copies, waits for them, and re-layouts: 7.26 us -> 0.63 us  [body(): v_row = (g_window[window_ids] - 0.5 * pair_tgt_sq) / EPSILON]
    div x3 -> x1, local copies, waits for them, and re-layouts: 6.63 us -> 2.21 us  [body(): v_col = (f_span[span_ids] - 0.5 * pair_src_sq) / EPSILON]
    broadcast_in_dim x0 -> x6, local copies, waits for them, and re-layouts: none -> 4.14 us  [the longest x3 2.07 us: body(): jnp.broadcast_to(v_row[:, None, :], (v_row.shape[0], 8, v_row.shape[1]))]
  transfers between devices with their start and end apart: 49 -> 40, of which waited for: 8 -> 11; matrix products, arithmetic and copies ran while one was open for 5% -> 7% of each run, Pallas kernels for 4% -> 4%
where the time goes in v4:
time: 277 us; the launch traced here: 275 us
  starting transfers between devices  125 us (45%)
  Pallas kernels  84.8 us (31%)
  waiting for transfers between devices  27.4 us (10%)
  local copies, waits for them, and re-layouts  18 us (6%)
  other arithmetic  17.5 us (6%)
    ppermute x28, starting transfers between devices, passed_along(): return lax.ppermute(block, axis, route)  99.5 us
    pallas_call x6, Pallas kernels, pair_lse(): pl.pallas_call(_lse_kernel, grid_spec=spec, out_shape=jax.ShapeDtypeStruc...  73.7 us
    ppermute x28, waiting for transfers between devices, passed_along(): return lax.ppermute(block, axis, route)  14.1 us
    ppermute x5, waiting for transfers between devices, gather_rows(): other = lax.ppermute(block, axis, route)  13.3 us
    ppermute x5, starting transfers between devices, gather_rows(): other = lax.ppermute(block, axis, route)  13.2 us
    pallas_call x1, Pallas kernels, pair_grad(): pl.pallas_call(_grad_kernel, grid_spec=spec, out_shape=jax.ShapeDtypeStru...  11.1 us
    ppermute x2, starting transfers between devices, padded(): lax.ppermute(lax.slice_in_dim(block, block.shape[dim] - width, None, axis...  7.82 us
  transfers between devices with their start and end apart: 40, of which 11 were waited for; matrix products, arithmetic and copies ran while one was open for 7% of the time, Pallas kernels for 4%

profile of v4, /device:TPU:1, one launch (start us, length us, event | category | flops | bytes accessed | tf_op | source)
XLA Modules:
  0.0 274.7 jit_solution(3721915854085289750)
XLA Ops:
  0.6 4.1 %collective-permute-start = (bf16[1,1024,128]{2,1,0:T(8,128)(2,1)}, bf16[1,1024,128]{2,1,0:T(8,128)(2,1)S(1)}, u32[]{:S(2)}, u32[]{:S(2)}) collective-permute-start(bf16[1,1024,128]{2,1,0:T(8,128)(2,1)} %param.7), channel_id=1, source_target_pairs={{0,32},{32,64},{64,96},{1,33},{33,65},{65,97},{2,34},{34,66},{66,9... | collective-permute-start | bytes 786440 | tf_op jit(solution)/shard_map/ppermute | solution.py:19
  8.2 4.2 %gather_fusion.2 = bf16[6,1024,128]{2,1,0:T(8,128)(2,1)S(1)} fusion(bf16[32,1024,128]{2,1,0:T(8,128)(2,1)} %a_ref.7, s32[1024]{0:T(1024)S(1)} %get-tuple-element.46), kind=kCustom, calls=%fused_computation.2 | custom fusion | bytes 3145752 | tf_op jit(solution)/shard_map/gather | solution.py:238
  15.9 12.4 %shard_map.85 = f32[6,1,1024]{2,1,0:T(1,128)} custom-call(s32[6]{0:T(128)} %bitcast.106, s32[6]{0:T(128)} %get-tuple-element.43.b_ids.a_ids, bf16[32,1024,128]{2,1,0:T(8,128)(2,1)} %a_ref.7, bf16[3,1024,128]{2,1,0:T(8,128)(2,1)} %copy-done, f32[6,8,1024]{2,1,0:T(8,128)} %broadcast_in_dim.237.v_ref), custom_call_target="tpu_custom_call" | custom-call | tf_op jit(solution)/shard_map/pallas_call | solution.py:92
  29.3 4.6 %collective-permute-start.4 = (f32[5,1024]{1,0:T(8,128)S(1)}, f32[5,1024]{1,0:T(8,128)S(1)}, u32[]{:S(2)}, u32[]{:S(2)}) collective-permute-start(f32[5,1024]{1,0:T(8,128)S(1)} %log_add_fusion.5), channel_id=1, source_target_pairs={{0,1},{1,2},{2,3},{3,4},{4,5},{5,6},{6,7},{7,8},{8,9},{9,10},{10,1... | collective-permute-start | bytes 61448 | tf_op jit(solution)/shard_map/ppermute | solution.py:30
  35.9 3.3 %collective-permute-done.5 = f32[5,1024]{1,0:T(8,128)S(1)} collective-permute-done((f32[5,1024]{1,0:T(8,128)S(1)}, f32[5,1024]{1,0:T(8,128)S(1)}, u32[]{:S(2)}, u32[]{:S(2)}) %collective-permute-start.5) | collective-permute-done | bytes 20512 | tf_op jit(solution)/shard_map/ppermute | solution.py:30
  41.3 5.8 %collective-permute-start.6 = (f32[7,1024]{1,0:T(8,128)S(1)}, f32[7,1024]{1,0:T(8,128)S(1)}, u32[]{:S(2)}, u32[]{:S(2)}) collective-permute-start(f32[7,1024]{1,0:T(8,128)S(1)} %log_add_fusion.4), channel_id=1, source_target_pairs={{0,3},{1,4},{2,5},{3,6},{4,7},{5,8},{6,9},{7,10},{8,11},{9,12},{10... | collective-permute-start | bytes 86024 | tf_op jit(solution)/shard_map/ppermute | solution.py:30
  49.5 12.4 %shard_map.86 = f32[6,1,1024]{2,1,0:T(1,128)} custom-call(s32[6]{0:T(128)} %get-tuple-element.43.b_ids.a_ids, s32[6]{0:T(128)} %bitcast.107, bf16[3,1024,128]{2,1,0:T(8,128)(2,1)} %copy-done, bf16[32,1024,128]{2,1,0:T(8,128)(2,1)} %a_ref.7, f32[6,8,1024]{2,1,0:T(8,128)} %broadcast_in_dim.241.v_ref), custom_call_target="tpu_custom_call" | custom-call | tf_op jit(solution)/shard_map/pallas_call | solution.py:92
  64.2 3.7 %collective-permute-start.2 = (f32[1,1024]{1,0:T(1,128)S(1)}, f32[1,1024]{1,0:T(1,128)S(1)}, u32[]{:S(2)}, u32[]{:S(2)}) collective-permute-start(f32[1,1024]{1,0:T(1,128)S(1)} %copy-done.4), channel_id=1, source_target_pairs={{0,32},{32,64},{64,96},{1,33},{33,65},{65,97},{2,34},{34,66},{66,9... | collective-permute-start | bytes 12296 | tf_op jit(solution)/shard_map/ppermute | solution.py:19
  70.5 4.6 %collective-permute-start.11 = (f32[3,1024]{1,0:T(4,128)S(1)}, f32[3,1024]{1,0:T(4,128)S(1)}, u32[]{:S(2)}, u32[]{:S(2)}) collective-permute-start(f32[3,1024]{1,0:T(4,128)S(1)} %get-tuple-element.8), channel_id=1, source_target_pairs={{0,32},{32,64},{64,96},{1,33},{33,65},{65,97},{2,34},{34,66},{66,9... | collective-permute-start | bytes 36872 | tf_op jit(solution)/shard_map/ppermute | solution.py:30
  75.2 6.1 %collective-permute-start.12 = (f32[3,1024]{1,0:T(4,128)S(1)}, f32[3,1024]{1,0:T(4,128)S(1)}, u32[]{:S(2)}, u32[]{:S(2)}) collective-permute-start(f32[3,1024]{1,0:T(4,128)S(1)} %get-tuple-element.8), channel_id=1, source_target_pairs={{0,64},{32,96},{1,65},{33,97},{2,66},{34,98},{3,67},{35,99},{4,68}... | collective-permute-start | bytes 36872 | tf_op jit(solution)/shard_map/ppermute | solution.py:30
  83.6 12.2 %shard_map.87 = f32[6,1,1024]{2,1,0:T(1,128)} custom-call(s32[6]{0:T(128)} %bitcast.108, s32[6]{0:T(128)} %get-tuple-element.43.b_ids.a_ids, bf16[32,1024,128]{2,1,0:T(8,128)(2,1)} %a_ref.7, bf16[3,1024,128]{2,1,0:T(8,128)(2,1)} %copy-done, f32[6,8,1024]{2,1,0:T(8,128)} %broadcast_in_dim.245.v_ref), custom_call_target="tpu_custom_call" | custom-call | tf_op jit(solution)/shard_map/pallas_call | solution.py:92
  96.8 3.8 %collective-permute-start.13 = (f32[5,1024]{1,0:T(8,128)S(1)}, f32[5,1024]{1,0:T(8,128)S(1)}, u32[]{:S(2)}, u32[]{:S(2)}) collective-permute-start(f32[5,1024]{1,0:T(8,128)S(1)} %log_add_fusion.3), channel_id=1, source_target_pairs={{0,1},{1,2},{2,3},{3,4},{4,5},{5,6},{6,7},{7,8},{8,9},{9,10},{10,1... | collective-permute-start | bytes 61448 | tf_op jit(solution)/shard_map/ppermute | solution.py:30
  102.6 3.3 %collective-permute-done.14 = f32[5,1024]{1,0:T(8,128)S(1)} collective-permute-done((f32[5,1024]{1,0:T(8,128)S(1)}, f32[5,1024]{1,0:T(8,128)S(1)}, u32[]{:S(2)}, u32[]{:S(2)}) %collective-permute-start.14) | collective-permute-done | bytes 20512 | tf_op jit(solution)/shard_map/ppermute | solution.py:30
  108.0 6.4 %collective-permute-start.15 = (f32[7,1024]{1,0:T(8,128)S(1)}, f32[7,1024]{1,0:T(8,128)S(1)}, u32[]{:S(2)}, u32[]{:S(2)}) collective-permute-start(f32[7,1024]{1,0:T(8,128)S(1)} %log_add_fusion.2), channel_id=1, source_target_pairs={{0,3},{1,4},{2,5},{3,6},{4,7},{5,8},{6,9},{7,10},{8,11},{9,12},{10... | collective-permute-start | bytes 86024 | tf_op jit(solution)/shard_map/ppermute | solution.py:30
  116.8 12.2 %shard_map.88 = f32[6,1,1024]{2,1,0:T(1,128)} custom-call(s32[6]{0:T(128)} %get-tuple-element.43.b_ids.a_ids, s32[6]{0:T(128)} %bitcast.109, bf16[3,1024,128]{2,1,0:T(8,128)(2,1)} %copy-done, bf16[32,1024,128]{2,1,0:T(8,128)(2,1)} %a_ref.7, f32[6,8,1024]{2,1,0:T(8,128)} %broadcast_in_dim.247.v_ref), custom_call_target="tpu_custom_call" | custom-call | tf_op jit(solution)/shard_map/pallas_call | solution.py:92
  132.7 4.0 %collective-permute-start.20 = (f32[3,1024]{1,0:T(4,128)S(1)}, f32[3,1024]{1,0:T(4,128)S(1)}, u32[]{:S(2)}, u32[]{:S(2)}) collective-permute-start(f32[3,1024]{1,0:T(4,128)S(1)} %get-tuple-element.6), channel_id=1, source_target_pairs={{0,32},{32,64},{64,96},{1,33},{33,65},{65,97},{2,34},{34,66},{66,9... | collective-permute-start | bytes 36872 | tf_op jit(solution)/shard_map/ppermute | solution.py:30
  136.7 5.7 %collective-permute-start.21 = (f32[3,1024]{1,0:T(4,128)S(1)}, f32[3,1024]{1,0:T(4,128)S(1)}, u32[]{:S(2)}, u32[]{:S(2)}) collective-permute-start(f32[3,1024]{1,0:T(4,128)S(1)} %get-tuple-element.6), channel_id=1, source_target_pairs={{0,64},{32,96},{1,65},{33,97},{2,66},{34,98},{3,67},{35,99},{4,68}... | collective-permute-start | bytes 36872 | tf_op jit(solution)/shard_map/ppermute | solution.py:30
  144.4 12.2 %shard_map.89 = f32[6,1,1024]{2,1,0:T(1,128)} custom-call(s32[6]{0:T(128)} %bitcast.110, s32[6]{0:T(128)} %get-tuple-element.43.b_ids.a_ids, bf16[32,1024,128]{2,1,0:T(8,128)(2,1)} %a_ref.7, bf16[3,1024,128]{2,1,0:T(8,128)(2,1)} %copy-done, f32[6,8,1024]{2,1,0:T(8,128)} %broadcast_in_dim.249.v_ref), custom_call_target="tpu_custom_call" | custom-call | tf_op jit(solution)/shard_map/pallas_call | solution.py:92
  157.7 6.0 %collective-permute-start.22 = (f32[5,1024]{1,0:T(8,128)S(1)}, f32[5,1024]{1,0:T(8,128)S(1)}, u32[]{:S(2)}, u32[]{:S(2)}) collective-permute-start(f32[5,1024]{1,0:T(8,128)S(1)} %log_add_fusion.1), channel_id=1, source_target_pairs={{0,1},{1,2},{2,3},{3,4},{4,5},{5,6},{6,7},{7,8},{8,9},{9,10},{10,1... | collective-permute-start | bytes 61448 | tf_op jit(solution)/shard_map/ppermute | solution.py:30
  165.7 3.3 %collective-permute-done.23 = f32[5,1024]{1,0:T(8,128)S(1)} collective-permute-done((f32[5,1024]{1,0:T(8,128)S(1)}, f32[5,1024]{1,0:T(8,128)S(1)}, u32[]{:S(2)}, u32[]{:S(2)}) %collective-permute-start.23) | collective-permute-done | bytes 20512 | tf_op jit(solution)/shard_map/ppermute | solution.py:30
  171.1 8.6 %collective-permute-start.24 = (f32[7,1024]{1,0:T(8,128)S(1)}, f32[7,1024]{1,0:T(8,128)S(1)}, u32[]{:S(2)}, u32[]{:S(2)}) collective-permute-start(f32[7,1024]{1,0:T(8,128)S(1)} %log_add_fusion), channel_id=1, source_target_pairs={{0,3},{1,4},{2,5},{3,6},{4,7},{5,8},{6,9},{7,10},{8,11},{9,12},{10... | collective-permute-start | bytes 86024 | tf_op jit(solution)/shard_map/ppermute | solution.py:30
  182.1 12.2 %shard_map.90 = f32[6,1,1024]{2,1,0:T(1,128)} custom-call(s32[6]{0:T(128)} %get-tuple-element.43.b_ids.a_ids, s32[6]{0:T(128)} %bitcast.111, bf16[3,1024,128]{2,1,0:T(8,128)(2,1)} %copy-done, bf16[32,1024,128]{2,1,0:T(8,128)(2,1)} %a_ref.7, f32[6,8,1024]{2,1,0:T(8,128)} %broadcast_in_dim.251.v_ref), custom_call_target="tpu_custom_call" | custom-call | tf_op jit(solution)/shard_map/pallas_call | solution.py:92
  198.6 4.0 %collective-permute-start.34 = (f32[3,1024]{1,0:T(4,128)S(1)}, f32[3,1024]{1,0:T(4,128)S(1)}, u32[]{:S(2)}, u32[]{:S(2)}) collective-permute-start(f32[3,1024]{1,0:T(4,128)S(1)} %get-tuple-element.4), channel_id=1, source_target_pairs={{0,32},{32,64},{64,96},{1,33},{33,65},{65,97},{2,34},{34,66},{66,9... | collective-permute-start | bytes 36872 | tf_op jit(solution)/shard_map/ppermute | solution.py:30
  202.6 5.5 %collective-permute-start.35 = (f32[3,1024]{1,0:T(4,128)S(1)}, f32[3,1024]{1,0:T(4,128)S(1)}, u32[]{:S(2)}, u32[]{:S(2)}) collective-permute-start(f32[3,1024]{1,0:T(4,128)S(1)} %get-tuple-element.4), channel_id=1, source_target_pairs={{0,64},{32,96},{1,65},{33,97},{2,66},{34,98},{3,67},{35,99},{4,68}... | collective-permute-start | bytes 36872 | tf_op jit(solution)/shard_map/ppermute | solution.py:30
  210.4 2.4 collective-permute-start.28
  214.2 11.1 %shard_map.91 = f32[6,1024,128]{2,1,0:T(8,128)} custom-call(s32[6]{0:T(128)} %bitcast.112, s32[6]{0:T(128)} %get-tuple-element.43.b_ids.a_ids, bf16[32,1024,128]{2,1,0:T(8,128)(2,1)} %a_ref.7, bf16[3,1024,128]{2,1,0:T(8,128)(2,1)} %copy-done, f32[6,1,1024]{2,1,0:T(1,128)} %div.120.v_ref, f32[6,1024,1]{2,1,0:T(8,128)} %copy.11.w_ref), custom_call_target="tpu_custom_call" | custom-call | tf_op jit(solution)/shard_map/pallas_call | solution.py:126
  225.4 3.8 %select_reduce_fusion = f32[5,1024,128]{2,1,0:T(8,128)S(1)} fusion(f32[6,1024,128]{2,1,0:T(8,128)} %shard_map.91, pred[5,6]{1,0:T(8,128)(4,1)S(1)} %iota_compare_fusion.1), kind=kLoop, calls=%fused_computation.9 | loop fusion | flops 7208960 | bytes 5767198 | tf_op jit(solution)/shard_map/reduce_sum | solution.py:265
  230.5 3.8 %collective-permute-start.36 = (f32[1,1024,128]{2,1,0:T(8,128)}, f32[1,1024,128]{2,1,0:T(8,128)S(1)}, u32[]{:S(2)}, u32[]{:S(2)}) collective-permute-start(f32[1,1024,128]{2,1,0:T(8,128)} %get-tuple-element.11), channel_id=1, source_target_pairs={{1,0},{2,1},{3,2},{4,3},{5,4},{6,5},{7,6},{8,7},{9,8},{10,9},{11,1... | collective-permute-start | bytes 1572872 | tf_op jit(solution)/shard_map/ppermute | solution.py:30
  237.5 10.1 %collective-permute-start.39 = (f32[1,1024,128]{2,1,0:T(8,128)}, f32[1,1024,128]{2,1,0:T(8,128)}, u32[]{:S(2)}, u32[]{:S(2)}) collective-permute-start(f32[1,1024,128]{2,1,0:T(8,128)} %get-tuple-element.12), channel_id=1, source_target_pairs={{0,2},{1,3},{2,4},{3,5},{4,6},{5,7},{6,8},{7,9},{8,10},{9,11},{10,... | collective-permute-start | bytes 1572872 | tf_op jit(solution)/shard_map/ppermute | solution.py:30
  247.7 4.2 %collective-permute-start.29 = (f32[4,1024]{1,0:T(4,128)S(1)}, f32[4,1024]{1,0:T(4,128)S(1)}, u32[]{:S(2)}, u32[]{:S(2)}) collective-permute-start(f32[4,1024]{1,0:T(4,128)S(1)} %maximum_select_fusion.3), channel_id=1, source_target_pairs={{0,4},{1,5},{2,6},{3,7},{4,0},{5,1},{6,2},{7,3},{8,12},{9,13},{10,... | collective-permute-start | bytes 49160 | tf_op jit(solution)/shard_map/ppermute | solution.py:212
  251.9 10.9 %collective-permute-done.29 = f32[4,1024]{1,0:T(4,128)S(1)} collective-permute-done((f32[4,1024]{1,0:T(4,128)S(1)}, f32[4,1024]{1,0:T(4,128)S(1)}, u32[]{:S(2)}, u32[]{:S(2)}) %collective-permute-start.29) | collective-permute-done | bytes 16416 | tf_op jit(solution)/shard_map/ppermute | solution.py:212
  266.2 3.8 %collective-permute-start.31 = (f32[16,1024]{1,0:T(8,128)S(1)}, f32[16,1024]{1,0:T(8,128)S(1)}, u32[]{:S(2)}, u32[]{:S(2)}) collective-permute-start(f32[16,1024]{1,0:T(8,128)S(1)} %maximum_select_fusion.1), channel_id=1, source_target_pairs={{0,16},{1,17},{2,18},{3,19},{4,20},{5,21},{6,22},{7,23},{8,24},{9,... | collective-permute-start | bytes 196616 | tf_op jit(solution)/shard_map/ppermute | solution.py:212
  (205 shorter events, 62.1 us)
Async XLA Ops:
  0.6 13.3 %collective-permute-start = (bf16[1,1024,128]{2,1,0:T(8,128)(2,1)}, bf16[1,1024,128]{2,1,0:T(8,128)(2,1)S(1)}, u32[]{:S(2)}, u32[]{:S(2)}) collective-permute-start(bf16[1,1024,128]{2,1,0:T(8,128)(2,1)} %param.7), channel_id=1, source_target_pairs={{0,32},{32,64},{64,96},{1,33},{33,65},{65,97},{2,34},{34,66},{66,9... | collective-permute-start | bytes 786440 | tf_op jit(solution)/shard_map/ppermute | solution.py:19
  4.7 9.3 %collective-permute-start.1 = (bf16[1,1024,128]{2,1,0:T(8,128)(2,1)}, bf16[1,1024,128]{2,1,0:T(8,128)(2,1)S(1)}, u32[]{:S(2)}, u32[]{:S(2)}) collective-permute-start(bf16[1,1024,128]{2,1,0:T(8,128)(2,1)} %param.7), channel_id=1, source_target_pairs={{32,0},{64,32},{96,64},{33,1},{65,33},{97,65},{34,2},{66,34},{98,6... | collective-permute-start | bytes 786440 | tf_op jit(solution)/shard_map/ppermute | solution.py:22
  39.2 7.8 %collective-permute-start.7 = (f32[7,1024]{1,0:T(8,128)S(1)}, f32[7,1024]{1,0:T(8,128)S(1)}, u32[]{:S(2)}, u32[]{:S(2)}) collective-permute-start(f32[7,1024]{1,0:T(8,128)S(1)} %log_add_fusion.4), channel_id=1, source_target_pairs={{3,0},{4,1},{5,2},{6,3},{7,4},{8,5},{9,6},{10,7},{11,8},{12,9},{13... | collective-permute-start | bytes 86024 | tf_op jit(solution)/shard_map/ppermute | solution.py:30
  40.6 7.5 %collective-permute-start.8 = (f32[5,1024]{1,0:T(8,128)S(1)}, f32[5,1024]{1,0:T(8,128)S(1)}, u32[]{:S(2)}, u32[]{:S(2)}) collective-permute-start(f32[5,1024]{1,0:T(8,128)S(1)} %log_add_fusion.5), channel_id=1, source_target_pairs={{0,2},{31,29},{32,34},{63,61},{64,66},{95,93},{96,98},{127,125}} | collective-permute-start | bytes 61448 | tf_op jit(solution)/shard_map/ppermute | solution.py:183
  41.3 6.8 %collective-permute-start.6 = (f32[7,1024]{1,0:T(8,128)S(1)}, f32[7,1024]{1,0:T(8,128)S(1)}, u32[]{:S(2)}, u32[]{:S(2)}) collective-permute-start(f32[7,1024]{1,0:T(8,128)S(1)} %log_add_fusion.4), channel_id=1, source_target_pairs={{0,3},{1,4},{2,5},{3,6},{4,7},{5,8},{6,9},{7,10},{8,11},{9,12},{10... | collective-permute-start | bytes 86024 | tf_op jit(solution)/shard_map/ppermute | solution.py:30
  62.9 12.3 %collective-permute-start.9 = (f32[3,1024]{1,0:T(4,128)S(1)}, f32[3,1024]{1,0:T(4,128)S(1)}, u32[]{:S(2)}, u32[]{:S(2)}) collective-permute-start(f32[3,1024]{1,0:T(4,128)S(1)} %get-tuple-element.8), channel_id=1, source_target_pairs={{64,0},{96,32},{65,1},{97,33},{66,2},{98,34},{67,3},{99,35},{68,4}... | collective-permute-start | bytes 36872 | tf_op jit(solution)/shard_map/ppermute | solution.py:30
  64.2 18.1 %collective-permute-start.2 = (f32[1,1024]{1,0:T(1,128)S(1)}, f32[1,1024]{1,0:T(1,128)S(1)}, u32[]{:S(2)}, u32[]{:S(2)}) collective-permute-start(f32[1,1024]{1,0:T(1,128)S(1)} %copy-done.4), channel_id=1, source_target_pairs={{0,32},{32,64},{64,96},{1,33},{33,65},{65,97},{2,34},{34,66},{66,9... | collective-permute-start | bytes 12296 | tf_op jit(solution)/shard_map/ppermute | solution.py:19
  67.9 14.3 %collective-permute-start.3 = (f32[1,1024]{1,0:T(1,128)S(1)}, f32[1,1024]{1,0:T(1,128)S(1)}, u32[]{:S(2)}, u32[]{:S(2)}) collective-permute-start(f32[1,1024]{1,0:T(1,128)S(1)} %copy-done.4), channel_id=1, source_target_pairs={{32,0},{64,32},{96,64},{33,1},{65,33},{97,65},{34,2},{66,34},{98,6... | collective-permute-start | bytes 12296 | tf_op jit(solution)/shard_map/ppermute | solution.py:22
  69.2 12.1 %collective-permute-start.10 = (f32[3,1024]{1,0:T(4,128)S(1)}, f32[3,1024]{1,0:T(4,128)S(1)}, u32[]{:S(2)}, u32[]{:S(2)}) collective-permute-start(f32[3,1024]{1,0:T(4,128)S(1)} %get-tuple-element.8), channel_id=1, source_target_pairs={{32,0},{64,32},{96,64},{33,1},{65,33},{97,65},{34,2},{66,34},{98,6... | collective-permute-start | bytes 36872 | tf_op jit(solution)/shard_map/ppermute | solution.py:30
  70.5 10.8 %collective-permute-start.11 = (f32[3,1024]{1,0:T(4,128)S(1)}, f32[3,1024]{1,0:T(4,128)S(1)}, u32[]{:S(2)}, u32[]{:S(2)}) collective-permute-start(f32[3,1024]{1,0:T(4,128)S(1)} %get-tuple-element.8), channel_id=1, source_target_pairs={{0,32},{32,64},{64,96},{1,33},{33,65},{65,97},{2,34},{34,66},{66,9... | collective-permute-start | bytes 36872 | tf_op jit(solution)/shard_map/ppermute | solution.py:30
  75.2 7.0 %collective-permute-start.12 = (f32[3,1024]{1,0:T(4,128)S(1)}, f32[3,1024]{1,0:T(4,128)S(1)}, u32[]{:S(2)}, u32[]{:S(2)}) collective-permute-start(f32[3,1024]{1,0:T(4,128)S(1)} %get-tuple-element.8), channel_id=1, source_target_pairs={{0,64},{32,96},{1,65},{33,97},{2,66},{34,98},{3,67},{35,99},{4,68}... | collective-permute-start | bytes 36872 | tf_op jit(solution)/shard_map/ppermute | solution.py:30
  106.0 8.4 %collective-permute-start.16 = (f32[7,1024]{1,0:T(8,128)S(1)}, f32[7,1024]{1,0:T(8,128)S(1)}, u32[]{:S(2)}, u32[]{:S(2)}) collective-permute-start(f32[7,1024]{1,0:T(8,128)S(1)} %log_add_fusion.2), channel_id=1, source_target_pairs={{3,0},{4,1},{5,2},{6,3},{7,4},{8,5},{9,6},{10,7},{11,8},{12,9},{13... | collective-permute-start | bytes 86024 | tf_op jit(solution)/shard_map/ppermute | solution.py:30
  107.3 8.1 %collective-permute-start.17 = (f32[5,1024]{1,0:T(8,128)S(1)}, f32[5,1024]{1,0:T(8,128)S(1)}, u32[]{:S(2)}, u32[]{:S(2)}) collective-permute-start(f32[5,1024]{1,0:T(8,128)S(1)} %log_add_fusion.3), channel_id=1, source_target_pairs={{0,2},{31,29},{32,34},{63,61},{64,66},{95,93},{96,98},{127,125}} | collective-permute-start | bytes 61448 | tf_op jit(solution)/shard_map/ppermute | solution.py:183
  108.0 7.5 %collective-permute-start.15 = (f32[7,1024]{1,0:T(8,128)S(1)}, f32[7,1024]{1,0:T(8,128)S(1)}, u32[]{:S(2)}, u32[]{:S(2)}) collective-permute-start(f32[7,1024]{1,0:T(8,128)S(1)} %log_add_fusion.2), channel_id=1, source_target_pairs={{0,3},{1,4},{2,5},{3,6},{4,7},{5,8},{6,9},{7,10},{8,11},{9,12},{10... | collective-permute-start | bytes 86024 | tf_op jit(solution)/shard_map/ppermute | solution.py:30
  130.1 12.3 %collective-permute-start.18 = (f32[3,1024]{1,0:T(4,128)S(1)}, f32[3,1024]{1,0:T(4,128)S(1)}, u32[]{:S(2)}, u32[]{:S(2)}) collective-permute-start(f32[3,1024]{1,0:T(4,128)S(1)} %get-tuple-element.6), channel_id=1, source_target_pairs={{64,0},{96,32},{65,1},{97,33},{66,2},{98,34},{67,3},{99,35},{68,4}... | collective-permute-start | bytes 36872 | tf_op jit(solution)/shard_map/ppermute | solution.py:30
  131.4 11.0 %collective-permute-start.19 = (f32[3,1024]{1,0:T(4,128)S(1)}, f32[3,1024]{1,0:T(4,128)S(1)}, u32[]{:S(2)}, u32[]{:S(2)}) collective-permute-start(f32[3,1024]{1,0:T(4,128)S(1)} %get-tuple-element.6), channel_id=1, source_target_pairs={{32,0},{64,32},{96,64},{33,1},{65,33},{97,65},{34,2},{66,34},{98,6... | collective-permute-start | bytes 36872 | tf_op jit(solution)/shard_map/ppermute | solution.py:30
  132.7 9.8 %collective-permute-start.20 = (f32[3,1024]{1,0:T(4,128)S(1)}, f32[3,1024]{1,0:T(4,128)S(1)}, u32[]{:S(2)}, u32[]{:S(2)}) collective-permute-start(f32[3,1024]{1,0:T(4,128)S(1)} %get-tuple-element.6), channel_id=1, source_target_pairs={{0,32},{32,64},{64,96},{1,33},{33,65},{65,97},{2,34},{34,66},{66,9... | collective-permute-start | bytes 36872 | tf_op jit(solution)/shard_map/ppermute | solution.py:30
  157.7 8.0 %collective-permute-start.22 = (f32[5,1024]{1,0:T(8,128)S(1)}, f32[5,1024]{1,0:T(8,128)S(1)}, u32[]{:S(2)}, u32[]{:S(2)}) collective-permute-start(f32[5,1024]{1,0:T(8,128)S(1)} %log_add_fusion.1), channel_id=1, source_target_pairs={{0,1},{1,2},{2,3},{3,4},{4,5},{5,6},{6,7},{7,8},{8,9},{9,10},{10,1... | collective-permute-start | bytes 61448 | tf_op jit(solution)/shard_map/ppermute | solution.py:30
  169.1 10.6 %collective-permute-start.25 = (f32[7,1024]{1,0:T(8,128)S(1)}, f32[7,1024]{1,0:T(8,128)S(1)}, u32[]{:S(2)}, u32[]{:S(2)}) collective-permute-start(f32[7,1024]{1,0:T(8,128)S(1)} %log_add_fusion), channel_id=1, source_target_pairs={{3,0},{4,1},{5,2},{6,3},{7,4},{8,5},{9,6},{10,7},{11,8},{12,9},{13... | collective-permute-start | bytes 86024 | tf_op jit(solution)/shard_map/ppermute | solution.py:30
  170.4 10.2 %collective-permute-start.26 = (f32[5,1024]{1,0:T(8,128)S(1)}, f32[5,1024]{1,0:T(8,128)S(1)}, u32[]{:S(2)}, u32[]{:S(2)}) collective-permute-start(f32[5,1024]{1,0:T(8,128)S(1)} %log_add_fusion.1), channel_id=1, source_target_pairs={{0,2},{31,29},{32,34},{63,61},{64,66},{95,93},{96,98},{127,125}} | collective-permute-start | bytes 61448 | tf_op jit(solution)/shard_map/ppermute | solution.py:183
  171.1 9.6 %collective-permute-start.24 = (f32[7,1024]{1,0:T(8,128)S(1)}, f32[7,1024]{1,0:T(8,128)S(1)}, u32[]{:S(2)}, u32[]{:S(2)}) collective-permute-start(f32[7,1024]{1,0:T(8,128)S(1)} %log_add_fusion), channel_id=1, source_target_pairs={{0,3},{1,4},{2,5},{3,6},{4,7},{5,8},{6,9},{7,10},{8,11},{9,12},{10... | collective-permute-start | bytes 86024 | tf_op jit(solution)/shard_map/ppermute | solution.py:30
  195.3 15.0 %collective-permute-start.27 = (f32[1,1024]{1,0:T(1,128)S(1)}, f32[1,1024]{1,0:T(1,128)S(1)}, u32[]{:S(2)}, u32[]{:S(2)}) collective-permute-start(f32[1,1024]{1,0:T(1,128)S(1)} %slice.201), channel_id=1, source_target_pairs={{0,1},{1,0},{2,3},{3,2},{4,5},{5,4},{6,7},{7,6},{8,9},{9,8},{10,11... | collective-permute-start | bytes 12296 | tf_op jit(solution)/shard_map/ppermute | solution.py:212
  196.0 16.7 %collective-permute-start.32 = (f32[3,1024]{1,0:T(4,128)S(1)}, f32[3,1024]{1,0:T(4,128)S(1)}, u32[]{:S(2)}, u32[]{:S(2)}) collective-permute-start(f32[3,1024]{1,0:T(4,128)S(1)} %get-tuple-element.4), channel_id=1, source_target_pairs={{64,0},{96,32},{65,1},{97,33},{66,2},{98,34},{67,3},{99,35},{68,4}... | collective-permute-start | bytes 36872 | tf_op jit(solution)/shard_map/ppermute | solution.py:30
  197.3 15.4 %collective-permute-start.33 = (f32[3,1024]{1,0:T(4,128)S(1)}, f32[3,1024]{1,0:T(4,128)S(1)}, u32[]{:S(2)}, u32[]{:S(2)}) collective-permute-start(f32[3,1024]{1,0:T(4,128)S(1)} %get-tuple-element.4), channel_id=1, source_target_pairs={{32,0},{64,32},{96,64},{33,1},{65,33},{97,65},{34,2},{66,34},{98,6... | collective-permute-start | bytes 36872 | tf_op jit(solution)/shard_map/ppermute | solution.py:30
  198.6 14.2 %collective-permute-start.34 = (f32[3,1024]{1,0:T(4,128)S(1)}, f32[3,1024]{1,0:T(4,128)S(1)}, u32[]{:S(2)}, u32[]{:S(2)}) collective-permute-start(f32[3,1024]{1,0:T(4,128)S(1)} %get-tuple-element.4), channel_id=1, source_target_pairs={{0,32},{32,64},{64,96},{1,33},{33,65},{65,97},{2,34},{34,66},{66,9... | collective-permute-start | bytes 36872 | tf_op jit(solution)/shard_map/ppermute | solution.py:30
  202.6 10.2 %collective-permute-start.35 = (f32[3,1024]{1,0:T(4,128)S(1)}, f32[3,1024]{1,0:T(4,128)S(1)}, u32[]{:S(2)}, u32[]{:S(2)}) collective-permute-start(f32[3,1024]{1,0:T(4,128)S(1)} %get-tuple-element.4), channel_id=1, source_target_pairs={{0,64},{32,96},{1,65},{33,97},{2,66},{34,98},{3,67},{35,99},{4,68}... | collective-permute-start | bytes 36872 | tf_op jit(solution)/shard_map/ppermute | solution.py:30
  210.4 37.3 %collective-permute-start.28 = (f32[2,1024]{1,0:T(2,128)S(1)}, f32[2,1024]{1,0:T(2,128)S(1)}, u32[]{:S(2)}, u32[]{:S(2)}) collective-permute-start(f32[2,1024]{1,0:T(2,128)S(1)} %maximum_select_fusion.4), channel_id=1, source_target_pairs={{0,2},{1,3},{2,0},{3,1},{4,6},{5,7},{6,4},{7,5},{8,10},{9,11},{10,... | collective-permute-start | bytes 24584 | tf_op jit(solution)/shard_map/ppermute | solution.py:212
  230.5 41.9 %collective-permute-start.36 = (f32[1,1024,128]{2,1,0:T(8,128)}, f32[1,1024,128]{2,1,0:T(8,128)S(1)}, u32[]{:S(2)}, u32[]{:S(2)}) collective-permute-start(f32[1,1024,128]{2,1,0:T(8,128)} %get-tuple-element.11), channel_id=1, source_target_pairs={{1,0},{2,1},{3,2},{4,3},{5,4},{6,5},{7,6},{8,7},{9,8},{10,9},{11,1... | collective-permute-start | bytes 1572872 | tf_op jit(solution)/shard_map/ppermute | solution.py:30
  234.3 38.1 %collective-permute-start.37 = (f32[1,1024,128]{2,1,0:T(8,128)}, f32[1,1024,128]{2,1,0:T(8,128)}, u32[]{:S(2)}, u32[]{:S(2)}) collective-permute-start(f32[1,1024,128]{2,1,0:T(8,128)} %get-tuple-element.14), channel_id=1, source_target_pairs={{0,1},{1,2},{2,3},{3,4},{4,5},{5,6},{6,7},{7,8},{8,9},{9,10},{10,1... | collective-permute-start | bytes 1572872 | tf_op jit(solution)/shard_map/ppermute | solution.py:30
  236.2 36.2 %collective-permute-start.38 = (f32[1,1024,128]{2,1,0:T(8,128)}, f32[1,1024,128]{2,1,0:T(8,128)}, u32[]{:S(2)}, u32[]{:S(2)}) collective-permute-start(f32[1,1024,128]{2,1,0:T(8,128)} %get-tuple-element.13), channel_id=1, source_target_pairs={{2,0},{3,1},{4,2},{5,3},{6,4},{7,5},{8,6},{9,7},{10,8},{11,9},{12,... | collective-permute-start | bytes 1572872 | tf_op jit(solution)/shard_map/ppermute | solution.py:30
  237.5 34.9 %collective-permute-start.39 = (f32[1,1024,128]{2,1,0:T(8,128)}, f32[1,1024,128]{2,1,0:T(8,128)}, u32[]{:S(2)}, u32[]{:S(2)}) collective-permute-start(f32[1,1024,128]{2,1,0:T(8,128)} %get-tuple-element.12), channel_id=1, source_target_pairs={{0,2},{1,3},{2,4},{3,5},{4,6},{5,7},{6,8},{7,9},{8,10},{9,11},{10,... | collective-permute-start | bytes 1572872 | tf_op jit(solution)/shard_map/ppermute | solution.py:30
  247.7 15.1 %collective-permute-start.29 = (f32[4,1024]{1,0:T(4,128)S(1)}, f32[4,1024]{1,0:T(4,128)S(1)}, u32[]{:S(2)}, u32[]{:S(2)}) collective-permute-start(f32[4,1024]{1,0:T(4,128)S(1)} %maximum_select_fusion.3), channel_id=1, source_target_pairs={{0,4},{1,5},{2,6},{3,7},{4,0},{5,1},{6,2},{7,3},{8,12},{9,13},{10,... | collective-permute-start | bytes 49160 | tf_op jit(solution)/shard_map/ppermute | solution.py:212
  (14 other events, 137.2 us)

commit v5 on v4

--- a/solution.py
+++ b/solution.py
@@ -30,22 +30,6 @@
     return lax.ppermute(block, axis, route)
 
 
-def log_add(first, second):
-    peak_val = jnp.maximum(first, second)
-    return peak_val + jnp.log(jnp.exp(first - peak_val) + jnp.exp(second - peak_val))
-
-
-def pick(table, position):
-    return lax.dynamic_index_in_dim(table, position, 0, keepdims=False)
-
-
-def cost_tile(src_rows, tgt_rows, src_sq, tgt_sq):
-    inner = lax.dot_general(
-        src_rows, tgt_rows, (((1,), (1,)), ((), ())), preferred_element_type=jnp.float32
-    )
-    return 0.5 * (src_sq[:, None] + tgt_sq[None, :]) - inner
-
-
 def squares(points):
     return jnp.sum(jnp.square(points.astype(jnp.float32)), axis=-1)
 
@@ -62,6 +46,7 @@
 EPSILON = 0.03
 INV_EPS = 1.0 / EPSILON
 CHUNK = 1024
+KERNEL_PARAMS = pltpu.CompilerParams()
 
 
 def _lse_kernel(a_ids, b_ids, a_ref, b_ref, v_ref, o_ref):
@@ -94,6 +79,7 @@
         grid_spec=spec,
         out_shape=jax.ShapeDtypeStruct((pairs, 1, rows), jnp.float32),
         interpret=interpret,
+        compiler_params=KERNEL_PARAMS,
     )(a_ids, b_ids, a_pts, b_pts, v_rows)
 
 
@@ -128,6 +114,7 @@
         grid_spec=spec,
         out_shape=jax.ShapeDtypeStruct((pairs, rows, coords), jnp.float32),
         interpret=interpret,
+        compiler_params=KERNEL_PARAMS,
     )(a_ids, b_ids, a_pts, b_pts, v_row, w_col)
 
 
@@ -137,7 +124,7 @@
     return peak_val + jnp.log(jnp.sum(jnp.exp(masked - peak_val[:, None]), axis=1))
 
 
-def spread(block, axis, reach, has_sender):
+def spread(block, axis, reach):
     width = block.shape[0]
     index = lax.axis_index(axis)
     count = lax.axis_size(axis)
@@ -221,7 +208,6 @@
 def body(src_points, tgt_points, src_log_mass, tgt_log_mass, near_pairs, target_slot):
     owned = tgt_points.shape[0]
     group_size = src_points.shape[0]
-    gx_count = lax.axis_size("gx")
     gy_count = lax.axis_size("gy")
     gx_index = lax.axis_index("gx")
     gy_index = lax.axis_index("gy")
@@ -244,16 +230,19 @@
         jnp.concatenate([mass_pad, src_log_mass, mass_pad], axis=0), gy_index * owned, 5 * owned, 0
     )
     g_window = jnp.zeros((3 * owned, src_points.shape[1]), jnp.float32)
-    for sweep_index in range(ITERS):
+    for _ in range(ITERS):
         v_row = (g_window[window_ids] - 0.5 * pair_tgt_sq) / EPSILON
         part = pair_lse(source_local, window_ids, src_points, window_pts, jnp.broadcast_to(v_row[:, None, :], (v_row.shape[0], 8, v_row.shape[1])))
         part = part[:, 0] - 0.5 * pair_src_sq / EPSILON
         rows_total = spread_rows(grouped_lse(span_mask, part), "gy", owned)
         f_span = EPSILON * span_mass - EPSILON * rows_total
         v_col = (f_span[span_ids] - 0.5 * pair_src_sq) / EPSILON
-        part = pair_lse(window_ids, source_local, window_pts, src_points, jnp.broadcast_to(v_col[:, None, :], (v_col.shape[0], 8, v_col.shape[1])))
+        part = pair_lse(
+            window_ids, source_local, window_pts, src_points,
+            jnp.broadcast_to(v_col[:, None, :], (v_col.shape[0], 8, v_col.shape[1])),
+        )
         part = part[:, 0] - 0.5 * pair_tgt_sq / EPSILON
-        cols_total = spread(grouped_lse(window_mask, part), "gx", 2 * owned, None)
+        cols_total = spread(grouped_lse(window_mask, part), "gx", 2 * owned)
         g_window = EPSILON * window_mass - EPSILON * cols_total
     f_pot = gather_rows(f_span[2 * owned : 3 * owned], "gy")
     g_local = g_window[owned : 2 * owned]
@@ -285,4 +274,5 @@
         P(),
     )
     out_specs = (P("gx", None), P(("gx", "gy"), None), P(("gx", "gy"), None, None))
+
     return jax.shard_map(body, mesh=mesh, in_specs=in_specs, out_specs=out_specs, check_vma=False)

time: 277 us -> 277 us (level)
  no operation moved by 1% of the time
where the time goes in v5:
time: 277 us; the launch traced here: 275 us
  starting transfers between devices  125 us (45%)
  Pallas kernels  84.8 us (31%)
  waiting for transfers between devices  27.4 us (10%)
  local copies, waits for them, and re-layouts  18 us (6%)
  other arithmetic  17.5 us (6%)
    ppermute x28, starting transfers between devices, passed_along(): return lax.ppermute(block, axis, route)  99.5 us
    pallas_call x6, Pallas kernels, pair_lse(): pl.pallas_call(_lse_kernel, grid_spec=spec, out_shape=jax.ShapeDtypeStruc...  73.7 us
    ppermute x28, waiting for transfers between devices, passed_along(): return lax.ppermute(block, axis, route)  14.1 us
    ppermute x5, waiting for transfers between devices, gather_rows(): other = lax.ppermute(block, axis, route)  13.3 us
    ppermute x5, starting transfers between devices, gather_rows(): other = lax.ppermute(block, axis, route)  13.2 us
    pallas_call x1, Pallas kernels, pair_grad(): pl.pallas_call(_grad_kernel, grid_spec=spec, out_shape=jax.ShapeDtypeStru...  11.1 us
    ppermute x2, starting transfers between devices, padded(): lax.ppermute(lax.slice_in_dim(block, block.shape[dim] - width, None, axis...  7.82 us
  transfers between devices with their start and end apart: 40, of which 11 were waited for; matrix products, arithmetic and copies ran while one was open for 7% of the time, Pallas kernels for 4%

profile of v5, /device:TPU:1, one launch (start us, length us, event | category | flops | bytes accessed | tf_op | source)
XLA Modules:
  0.0 274.7 jit_solution(3721915854085289750)
XLA Ops:
  0.6 4.1 %collective-permute-start = (bf16[1,1024,128]{2,1,0:T(8,128)(2,1)}, bf16[1,1024,128]{2,1,0:T(8,128)(2,1)S(1)}, u32[]{:S(2)}, u32[]{:S(2)}) collective-permute-start(bf16[1,1024,128]{2,1,0:T(8,128)(2,1)} %param.7), channel_id=1, source_target_pairs={{0,32},{32,64},{64,96},{1,33},{33,65},{65,97},{2,34},{34,66},{66,9... | collective-permute-start | bytes 786440 | tf_op jit(solution)/shard_map/ppermute | solution.py:19
  8.2 4.2 %gather_fusion.2 = bf16[6,1024,128]{2,1,0:T(8,128)(2,1)S(1)} fusion(bf16[32,1024,128]{2,1,0:T(8,128)(2,1)} %a_ref.7, s32[1024]{0:T(1024)S(1)} %get-tuple-element.46), kind=kCustom, calls=%fused_computation.2 | custom fusion | bytes 3145752 | tf_op jit(solution)/shard_map/gather | solution.py:224
  15.9 12.4 %shard_map.85 = f32[6,1,1024]{2,1,0:T(1,128)} custom-call(s32[6]{0:T(128)} %bitcast.106, s32[6]{0:T(128)} %get-tuple-element.43.b_ids.a_ids, bf16[32,1024,128]{2,1,0:T(8,128)(2,1)} %a_ref.7, bf16[3,1024,128]{2,1,0:T(8,128)(2,1)} %copy-done, f32[6,8,1024]{2,1,0:T(8,128)} %broadcast_in_dim.237.v_ref), custom_call_target="tpu_custom_call" | custom-call | tf_op jit(solution)/shard_map/pallas_call | solution.py:77
  29.3 4.6 %collective-permute-start.4 = (f32[5,1024]{1,0:T(8,128)S(1)}, f32[5,1024]{1,0:T(8,128)S(1)}, u32[]{:S(2)}, u32[]{:S(2)}) collective-permute-start(f32[5,1024]{1,0:T(8,128)S(1)} %log_add_fusion.5), channel_id=1, source_target_pairs={{0,1},{1,2},{2,3},{3,4},{4,5},{5,6},{6,7},{7,8},{8,9},{9,10},{10,1... | collective-permute-start | bytes 61448 | tf_op jit(solution)/shard_map/ppermute | solution.py:30
  35.9 3.3 %collective-permute-done.5 = f32[5,1024]{1,0:T(8,128)S(1)} collective-permute-done((f32[5,1024]{1,0:T(8,128)S(1)}, f32[5,1024]{1,0:T(8,128)S(1)}, u32[]{:S(2)}, u32[]{:S(2)}) %collective-permute-start.5) | collective-permute-done | bytes 20512 | tf_op jit(solution)/shard_map/ppermute | solution.py:30
  41.3 5.8 %collective-permute-start.6 = (f32[7,1024]{1,0:T(8,128)S(1)}, f32[7,1024]{1,0:T(8,128)S(1)}, u32[]{:S(2)}, u32[]{:S(2)}) collective-permute-start(f32[7,1024]{1,0:T(8,128)S(1)} %log_add_fusion.4), channel_id=1, source_target_pairs={{0,3},{1,4},{2,5},{3,6},{4,7},{5,8},{6,9},{7,10},{8,11},{9,12},{10... | collective-permute-start | bytes 86024 | tf_op jit(solution)/shard_map/ppermute | solution.py:30
  49.5 12.4 %shard_map.86 = f32[6,1,1024]{2,1,0:T(1,128)} custom-call(s32[6]{0:T(128)} %get-tuple-element.43.b_ids.a_ids, s32[6]{0:T(128)} %bitcast.107, bf16[3,1024,128]{2,1,0:T(8,128)(2,1)} %copy-done, bf16[32,1024,128]{2,1,0:T(8,128)(2,1)} %a_ref.7, f32[6,8,1024]{2,1,0:T(8,128)} %broadcast_in_dim.241.v_ref), custom_call_target="tpu_custom_call" | custom-call | tf_op jit(solution)/shard_map/pallas_call | solution.py:77
  64.2 3.7 %collective-permute-start.2 = (f32[1,1024]{1,0:T(1,128)S(1)}, f32[1,1024]{1,0:T(1,128)S(1)}, u32[]{:S(2)}, u32[]{:S(2)}) collective-permute-start(f32[1,1024]{1,0:T(1,128)S(1)} %copy-done.4), channel_id=1, source_target_pairs={{0,32},{32,64},{64,96},{1,33},{33,65},{65,97},{2,34},{34,66},{66,9... | collective-permute-start | bytes 12296 | tf_op jit(solution)/shard_map/ppermute | solution.py:19
  70.5 4.6 %collective-permute-start.11 = (f32[3,1024]{1,0:T(4,128)S(1)}, f32[3,1024]{1,0:T(4,128)S(1)}, u32[]{:S(2)}, u32[]{:S(2)}) collective-permute-start(f32[3,1024]{1,0:T(4,128)S(1)} %get-tuple-element.8), channel_id=1, source_target_pairs={{0,32},{32,64},{64,96},{1,33},{33,65},{65,97},{2,34},{34,66},{66,9... | collective-permute-start | bytes 36872 | tf_op jit(solution)/shard_map/ppermute | solution.py:30
  75.2 6.1 %collective-permute-start.12 = (f32[3,1024]{1,0:T(4,128)S(1)}, f32[3,1024]{1,0:T(4,128)S(1)}, u32[]{:S(2)}, u32[]{:S(2)}) collective-permute-start(f32[3,1024]{1,0:T(4,128)S(1)} %get-tuple-element.8), channel_id=1, source_target_pairs={{0,64},{32,96},{1,65},{33,97},{2,66},{34,98},{3,67},{35,99},{4,68}... | collective-permute-start | bytes 36872 | tf_op jit(solution)/shard_map/ppermute | solution.py:30
  83.6 12.2 %shard_map.87 = f32[6,1,1024]{2,1,0:T(1,128)} custom-call(s32[6]{0:T(128)} %bitcast.108, s32[6]{0:T(128)} %get-tuple-element.43.b_ids.a_ids, bf16[32,1024,128]{2,1,0:T(8,128)(2,1)} %a_ref.7, bf16[3,1024,128]{2,1,0:T(8,128)(2,1)} %copy-done, f32[6,8,1024]{2,1,0:T(8,128)} %broadcast_in_dim.245.v_ref), custom_call_target="tpu_custom_call" | custom-call | tf_op jit(solution)/shard_map/pallas_call | solution.py:77
  96.8 3.8 %collective-permute-start.13 = (f32[5,1024]{1,0:T(8,128)S(1)}, f32[5,1024]{1,0:T(8,128)S(1)}, u32[]{:S(2)}, u32[]{:S(2)}) collective-permute-start(f32[5,1024]{1,0:T(8,128)S(1)} %log_add_fusion.3), channel_id=1, source_target_pairs={{0,1},{1,2},{2,3},{3,4},{4,5},{5,6},{6,7},{7,8},{8,9},{9,10},{10,1... | collective-permute-start | bytes 61448 | tf_op jit(solution)/shard_map/ppermute | solution.py:30
  102.6 3.3 %collective-permute-done.14 = f32[5,1024]{1,0:T(8,128)S(1)} collective-permute-done((f32[5,1024]{1,0:T(8,128)S(1)}, f32[5,1024]{1,0:T(8,128)S(1)}, u32[]{:S(2)}, u32[]{:S(2)}) %collective-permute-start.14) | collective-permute-done | bytes 20512 | tf_op jit(solution)/shard_map/ppermute | solution.py:30
  108.0 6.4 %collective-permute-start.15 = (f32[7,1024]{1,0:T(8,128)S(1)}, f32[7,1024]{1,0:T(8,128)S(1)}, u32[]{:S(2)}, u32[]{:S(2)}) collective-permute-start(f32[7,1024]{1,0:T(8,128)S(1)} %log_add_fusion.2), channel_id=1, source_target_pairs={{0,3},{1,4},{2,5},{3,6},{4,7},{5,8},{6,9},{7,10},{8,11},{9,12},{10... | collective-permute-start | bytes 86024 | tf_op jit(solution)/shard_map/ppermute | solution.py:30
  116.8 12.2 %shard_map.88 = f32[6,1,1024]{2,1,0:T(1,128)} custom-call(s32[6]{0:T(128)} %get-tuple-element.43.b_ids.a_ids, s32[6]{0:T(128)} %bitcast.109, bf16[3,1024,128]{2,1,0:T(8,128)(2,1)} %copy-done, bf16[32,1024,128]{2,1,0:T(8,128)(2,1)} %a_ref.7, f32[6,8,1024]{2,1,0:T(8,128)} %broadcast_in_dim.247.v_ref), custom_call_target="tpu_custom_call" | custom-call | tf_op jit(solution)/shard_map/pallas_call | solution.py:77
  132.7 4.0 %collective-permute-start.20 = (f32[3,1024]{1,0:T(4,128)S(1)}, f32[3,1024]{1,0:T(4,128)S(1)}, u32[]{:S(2)}, u32[]{:S(2)}) collective-permute-start(f32[3,1024]{1,0:T(4,128)S(1)} %get-tuple-element.6), channel_id=1, source_target_pairs={{0,32},{32,64},{64,96},{1,33},{33,65},{65,97},{2,34},{34,66},{66,9... | collective-permute-start | bytes 36872 | tf_op jit(solution)/shard_map/ppermute | solution.py:30
  136.7 5.7 %collective-permute-start.21 = (f32[3,1024]{1,0:T(4,128)S(1)}, f32[3,1024]{1,0:T(4,128)S(1)}, u32[]{:S(2)}, u32[]{:S(2)}) collective-permute-start(f32[3,1024]{1,0:T(4,128)S(1)} %get-tuple-element.6), channel_id=1, source_target_pairs={{0,64},{32,96},{1,65},{33,97},{2,66},{34,98},{3,67},{35,99},{4,68}... | collective-permute-start | bytes 36872 | tf_op jit(solution)/shard_map/ppermute | solution.py:30
  144.4 12.2 %shard_map.89 = f32[6,1,1024]{2,1,0:T(1,128)} custom-call(s32[6]{0:T(128)} %bitcast.110, s32[6]{0:T(128)} %get-tuple-element.43.b_ids.a_ids, bf16[32,1024,128]{2,1,0:T(8,128)(2,1)} %a_ref.7, bf16[3,1024,128]{2,1,0:T(8,128)(2,1)} %copy-done, f32[6,8,1024]{2,1,0:T(8,128)} %broadcast_in_dim.249.v_ref), custom_call_target="tpu_custom_call" | custom-call | tf_op jit(solution)/shard_map/pallas_call | solution.py:77
  157.7 6.0 %collective-permute-start.22 = (f32[5,1024]{1,0:T(8,128)S(1)}, f32[5,1024]{1,0:T(8,128)S(1)}, u32[]{:S(2)}, u32[]{:S(2)}) collective-permute-start(f32[5,1024]{1,0:T(8,128)S(1)} %log_add_fusion.1), channel_id=1, source_target_pairs={{0,1},{1,2},{2,3},{3,4},{4,5},{5,6},{6,7},{7,8},{8,9},{9,10},{10,1... | collective-permute-start | bytes 61448 | tf_op jit(solution)/shard_map/ppermute | solution.py:30
  165.7 3.3 %collective-permute-done.23 = f32[5,1024]{1,0:T(8,128)S(1)} collective-permute-done((f32[5,1024]{1,0:T(8,128)S(1)}, f32[5,1024]{1,0:T(8,128)S(1)}, u32[]{:S(2)}, u32[]{:S(2)}) %collective-permute-start.23) | collective-permute-done | bytes 20512 | tf_op jit(solution)/shard_map/ppermute | solution.py:30
  171.1 8.6 %collective-permute-start.24 = (f32[7,1024]{1,0:T(8,128)S(1)}, f32[7,1024]{1,0:T(8,128)S(1)}, u32[]{:S(2)}, u32[]{:S(2)}) collective-permute-start(f32[7,1024]{1,0:T(8,128)S(1)} %log_add_fusion), channel_id=1, source_target_pairs={{0,3},{1,4},{2,5},{3,6},{4,7},{5,8},{6,9},{7,10},{8,11},{9,12},{10... | collective-permute-start | bytes 86024 | tf_op jit(solution)/shard_map/ppermute | solution.py:30
  182.1 12.2 %shard_map.90 = f32[6,1,1024]{2,1,0:T(1,128)} custom-call(s32[6]{0:T(128)} %get-tuple-element.43.b_ids.a_ids, s32[6]{0:T(128)} %bitcast.111, bf16[3,1024,128]{2,1,0:T(8,128)(2,1)} %copy-done, bf16[32,1024,128]{2,1,0:T(8,128)(2,1)} %a_ref.7, f32[6,8,1024]{2,1,0:T(8,128)} %broadcast_in_dim.251.v_ref), custom_call_target="tpu_custom_call" | custom-call | tf_op jit(solution)/shard_map/pallas_call | solution.py:77
  198.6 4.0 %collective-permute-start.34 = (f32[3,1024]{1,0:T(4,128)S(1)}, f32[3,1024]{1,0:T(4,128)S(1)}, u32[]{:S(2)}, u32[]{:S(2)}) collective-permute-start(f32[3,1024]{1,0:T(4,128)S(1)} %get-tuple-element.4), channel_id=1, source_target_pairs={{0,32},{32,64},{64,96},{1,33},{33,65},{65,97},{2,34},{34,66},{66,9... | collective-permute-start | bytes 36872 | tf_op jit(solution)/shard_map/ppermute | solution.py:30
  202.6 5.5 %collective-permute-start.35 = (f32[3,1024]{1,0:T(4,128)S(1)}, f32[3,1024]{1,0:T(4,128)S(1)}, u32[]{:S(2)}, u32[]{:S(2)}) collective-permute-start(f32[3,1024]{1,0:T(4,128)S(1)} %get-tuple-element.4), channel_id=1, source_target_pairs={{0,64},{32,96},{1,65},{33,97},{2,66},{34,98},{3,67},{35,99},{4,68}... | collective-permute-start | bytes 36872 | tf_op jit(solution)/shard_map/ppermute | solution.py:30
  210.4 2.4 collective-permute-start.28
  214.2 11.1 %shard_map.91 = f32[6,1024,128]{2,1,0:T(8,128)} custom-call(s32[6]{0:T(128)} %bitcast.112, s32[6]{0:T(128)} %get-tuple-element.43.b_ids.a_ids, bf16[32,1024,128]{2,1,0:T(8,128)(2,1)} %a_ref.7, bf16[3,1024,128]{2,1,0:T(8,128)(2,1)} %copy-done, f32[6,1,1024]{2,1,0:T(1,128)} %div.120.v_ref, f32[6,1024,1]{2,1,0:T(8,128)} %copy.11.w_ref), custom_call_target="tpu_custom_call" | custom-call | tf_op jit(solution)/shard_map/pallas_call | solution.py:112
  225.4 3.8 %select_reduce_fusion = f32[5,1024,128]{2,1,0:T(8,128)S(1)} fusion(f32[6,1024,128]{2,1,0:T(8,128)} %shard_map.91, pred[5,6]{1,0:T(8,128)(4,1)S(1)} %iota_compare_fusion.1), kind=kLoop, calls=%fused_computation.9 | loop fusion | flops 7208960 | bytes 5767198 | tf_op jit(solution)/shard_map/reduce_sum | solution.py:254
  230.5 3.8 %collective-permute-start.36 = (f32[1,1024,128]{2,1,0:T(8,128)}, f32[1,1024,128]{2,1,0:T(8,128)S(1)}, u32[]{:S(2)}, u32[]{:S(2)}) collective-permute-start(f32[1,1024,128]{2,1,0:T(8,128)} %get-tuple-element.11), channel_id=1, source_target_pairs={{1,0},{2,1},{3,2},{4,3},{5,4},{6,5},{7,6},{8,7},{9,8},{10,9},{11,1... | collective-permute-start | bytes 1572872 | tf_op jit(solution)/shard_map/ppermute | solution.py:30
  237.5 10.1 %collective-permute-start.39 = (f32[1,1024,128]{2,1,0:T(8,128)}, f32[1,1024,128]{2,1,0:T(8,128)}, u32[]{:S(2)}, u32[]{:S(2)}) collective-permute-start(f32[1,1024,128]{2,1,0:T(8,128)} %get-tuple-element.12), channel_id=1, source_target_pairs={{0,2},{1,3},{2,4},{3,5},{4,6},{5,7},{6,8},{7,9},{8,10},{9,11},{10,... | collective-permute-start | bytes 1572872 | tf_op jit(solution)/shard_map/ppermute | solution.py:30
  247.7 4.2 %collective-permute-start.29 = (f32[4,1024]{1,0:T(4,128)S(1)}, f32[4,1024]{1,0:T(4,128)S(1)}, u32[]{:S(2)}, u32[]{:S(2)}) collective-permute-start(f32[4,1024]{1,0:T(4,128)S(1)} %maximum_select_fusion.3), channel_id=1, source_target_pairs={{0,4},{1,5},{2,6},{3,7},{4,0},{5,1},{6,2},{7,3},{8,12},{9,13},{10,... | collective-permute-start | bytes 49160 | tf_op jit(solution)/shard_map/ppermute | solution.py:199
  251.9 10.9 %collective-permute-done.29 = f32[4,1024]{1,0:T(4,128)S(1)} collective-permute-done((f32[4,1024]{1,0:T(4,128)S(1)}, f32[4,1024]{1,0:T(4,128)S(1)}, u32[]{:S(2)}, u32[]{:S(2)}) %collective-permute-start.29) | collective-permute-done | bytes 16416 | tf_op jit(solution)/shard_map/ppermute | solution.py:199
  266.2 3.8 %collective-permute-start.31 = (f32[16,1024]{1,0:T(8,128)S(1)}, f32[16,1024]{1,0:T(8,128)S(1)}, u32[]{:S(2)}, u32[]{:S(2)}) collective-permute-start(f32[16,1024]{1,0:T(8,128)S(1)} %maximum_select_fusion.1), channel_id=1, source_target_pairs={{0,16},{1,17},{2,18},{3,19},{4,20},{5,21},{6,22},{7,23},{8,24},{9,... | collective-permute-start | bytes 196616 | tf_op jit(solution)/shard_map/ppermute | solution.py:199
  (205 shorter events, 62.1 us)
Async XLA Ops:
  0.6 13.3 %collective-permute-start = (bf16[1,1024,128]{2,1,0:T(8,128)(2,1)}, bf16[1,1024,128]{2,1,0:T(8,128)(2,1)S(1)}, u32[]{:S(2)}, u32[]{:S(2)}) collective-permute-start(bf16[1,1024,128]{2,1,0:T(8,128)(2,1)} %param.7), channel_id=1, source_target_pairs={{0,32},{32,64},{64,96},{1,33},{33,65},{65,97},{2,34},{34,66},{66,9... | collective-permute-start | bytes 786440 | tf_op jit(solution)/shard_map/ppermute | solution.py:19
  4.7 9.3 %collective-permute-start.1 = (bf16[1,1024,128]{2,1,0:T(8,128)(2,1)}, bf16[1,1024,128]{2,1,0:T(8,128)(2,1)S(1)}, u32[]{:S(2)}, u32[]{:S(2)}) collective-permute-start(bf16[1,1024,128]{2,1,0:T(8,128)(2,1)} %param.7), channel_id=1, source_target_pairs={{32,0},{64,32},{96,64},{33,1},{65,33},{97,65},{34,2},{66,34},{98,6... | collective-permute-start | bytes 786440 | tf_op jit(solution)/shard_map/ppermute | solution.py:22
  39.2 7.8 %collective-permute-start.7 = (f32[7,1024]{1,0:T(8,128)S(1)}, f32[7,1024]{1,0:T(8,128)S(1)}, u32[]{:S(2)}, u32[]{:S(2)}) collective-permute-start(f32[7,1024]{1,0:T(8,128)S(1)} %log_add_fusion.4), channel_id=1, source_target_pairs={{3,0},{4,1},{5,2},{6,3},{7,4},{8,5},{9,6},{10,7},{11,8},{12,9},{13... | collective-permute-start | bytes 86024 | tf_op jit(solution)/shard_map/ppermute | solution.py:30
  40.6 7.5 %collective-permute-start.8 = (f32[5,1024]{1,0:T(8,128)S(1)}, f32[5,1024]{1,0:T(8,128)S(1)}, u32[]{:S(2)}, u32[]{:S(2)}) collective-permute-start(f32[5,1024]{1,0:T(8,128)S(1)} %log_add_fusion.5), channel_id=1, source_target_pairs={{0,2},{31,29},{32,34},{63,61},{64,66},{95,93},{96,98},{127,125}} | collective-permute-start | bytes 61448 | tf_op jit(solution)/shard_map/ppermute | solution.py:170
  41.3 6.8 %collective-permute-start.6 = (f32[7,1024]{1,0:T(8,128)S(1)}, f32[7,1024]{1,0:T(8,128)S(1)}, u32[]{:S(2)}, u32[]{:S(2)}) collective-permute-start(f32[7,1024]{1,0:T(8,128)S(1)} %log_add_fusion.4), channel_id=1, source_target_pairs={{0,3},{1,4},{2,5},{3,6},{4,7},{5,8},{6,9},{7,10},{8,11},{9,12},{10... | collective-permute-start | bytes 86024 | tf_op jit(solution)/shard_map/ppermute | solution.py:30
  62.9 12.3 %collective-permute-start.9 = (f32[3,1024]{1,0:T(4,128)S(1)}, f32[3,1024]{1,0:T(4,128)S(1)}, u32[]{:S(2)}, u32[]{:S(2)}) collective-permute-start(f32[3,1024]{1,0:T(4,128)S(1)} %get-tuple-element.8), channel_id=1, source_target_pairs={{64,0},{96,32},{65,1},{97,33},{66,2},{98,34},{67,3},{99,35},{68,4}... | collective-permute-start | bytes 36872 | tf_op jit(solution)/shard_map/ppermute | solution.py:30
  64.2 18.1 %collective-permute-start.2 = (f32[1,1024]{1,0:T(1,128)S(1)}, f32[1,1024]{1,0:T(1,128)S(1)}, u32[]{:S(2)}, u32[]{:S(2)}) collective-permute-start(f32[1,1024]{1,0:T(1,128)S(1)} %copy-done.4), channel_id=1, source_target_pairs={{0,32},{32,64},{64,96},{1,33},{33,65},{65,97},{2,34},{34,66},{66,9... | collective-permute-start | bytes 12296 | tf_op jit(solution)/shard_map/ppermute | solution.py:19
  67.9 14.3 %collective-permute-start.3 = (f32[1,1024]{1,0:T(1,128)S(1)}, f32[1,1024]{1,0:T(1,128)S(1)}, u32[]{:S(2)}, u32[]{:S(2)}) collective-permute-start(f32[1,1024]{1,0:T(1,128)S(1)} %copy-done.4), channel_id=1, source_target_pairs={{32,0},{64,32},{96,64},{33,1},{65,33},{97,65},{34,2},{66,34},{98,6... | collective-permute-start | bytes 12296 | tf_op jit(solution)/shard_map/ppermute | solution.py:22
  69.2 12.1 %collective-permute-start.10 = (f32[3,1024]{1,0:T(4,128)S(1)}, f32[3,1024]{1,0:T(4,128)S(1)}, u32[]{:S(2)}, u32[]{:S(2)}) collective-permute-start(f32[3,1024]{1,0:T(4,128)S(1)} %get-tuple-element.8), channel_id=1, source_target_pairs={{32,0},{64,32},{96,64},{33,1},{65,33},{97,65},{34,2},{66,34},{98,6... | collective-permute-start | bytes 36872 | tf_op jit(solution)/shard_map/ppermute | solution.py:30
  70.5 10.8 %collective-permute-start.11 = (f32[3,1024]{1,0:T(4,128)S(1)}, f32[3,1024]{1,0:T(4,128)S(1)}, u32[]{:S(2)}, u32[]{:S(2)}) collective-permute-start(f32[3,1024]{1,0:T(4,128)S(1)} %get-tuple-element.8), channel_id=1, source_target_pairs={{0,32},{32,64},{64,96},{1,33},{33,65},{65,97},{2,34},{34,66},{66,9... | collective-permute-start | bytes 36872 | tf_op jit(solution)/shard_map/ppermute | solution.py:30
  75.2 7.0 %collective-permute-start.12 = (f32[3,1024]{1,0:T(4,128)S(1)}, f32[3,1024]{1,0:T(4,128)S(1)}, u32[]{:S(2)}, u32[]{:S(2)}) collective-permute-start(f32[3,1024]{1,0:T(4,128)S(1)} %get-tuple-element.8), channel_id=1, source_target_pairs={{0,64},{32,96},{1,65},{33,97},{2,66},{34,98},{3,67},{35,99},{4,68}... | collective-permute-start | bytes 36872 | tf_op jit(solution)/shard_map/ppermute | solution.py:30
  106.0 8.4 %collective-permute-start.16 = (f32[7,1024]{1,0:T(8,128)S(1)}, f32[7,1024]{1,0:T(8,128)S(1)}, u32[]{:S(2)}, u32[]{:S(2)}) collective-permute-start(f32[7,1024]{1,0:T(8,128)S(1)} %log_add_fusion.2), channel_id=1, source_target_pairs={{3,0},{4,1},{5,2},{6,3},{7,4},{8,5},{9,6},{10,7},{11,8},{12,9},{13... | collective-permute-start | bytes 86024 | tf_op jit(solution)/shard_map/ppermute | solution.py:30
  107.3 8.1 %collective-permute-start.17 = (f32[5,1024]{1,0:T(8,128)S(1)}, f32[5,1024]{1,0:T(8,128)S(1)}, u32[]{:S(2)}, u32[]{:S(2)}) collective-permute-start(f32[5,1024]{1,0:T(8,128)S(1)} %log_add_fusion.3), channel_id=1, source_target_pairs={{0,2},{31,29},{32,34},{63,61},{64,66},{95,93},{96,98},{127,125}} | collective-permute-start | bytes 61448 | tf_op jit(solution)/shard_map/ppermute | solution.py:170
  108.0 7.5 %collective-permute-start.15 = (f32[7,1024]{1,0:T(8,128)S(1)}, f32[7,1024]{1,0:T(8,128)S(1)}, u32[]{:S(2)}, u32[]{:S(2)}) collective-permute-start(f32[7,1024]{1,0:T(8,128)S(1)} %log_add_fusion.2), channel_id=1, source_target_pairs={{0,3},{1,4},{2,5},{3,6},{4,7},{5,8},{6,9},{7,10},{8,11},{9,12},{10... | collective-permute-start | bytes 86024 | tf_op jit(solution)/shard_map/ppermute | solution.py:30
  130.1 12.3 %collective-permute-start.18 = (f32[3,1024]{1,0:T(4,128)S(1)}, f32[3,1024]{1,0:T(4,128)S(1)}, u32[]{:S(2)}, u32[]{:S(2)}) collective-permute-start(f32[3,1024]{1,0:T(4,128)S(1)} %get-tuple-element.6), channel_id=1, source_target_pairs={{64,0},{96,32},{65,1},{97,33},{66,2},{98,34},{67,3},{99,35},{68,4}... | collective-permute-start | bytes 36872 | tf_op jit(solution)/shard_map/ppermute | solution.py:30
  131.4 11.0 %collective-permute-start.19 = (f32[3,1024]{1,0:T(4,128)S(1)}, f32[3,1024]{1,0:T(4,128)S(1)}, u32[]{:S(2)}, u32[]{:S(2)}) collective-permute-start(f32[3,1024]{1,0:T(4,128)S(1)} %get-tuple-element.6), channel_id=1, source_target_pairs={{32,0},{64,32},{96,64},{33,1},{65,33},{97,65},{34,2},{66,34},{98,6... | collective-permute-start | bytes 36872 | tf_op jit(solution)/shard_map/ppermute | solution.py:30
  132.7 9.8 %collective-permute-start.20 = (f32[3,1024]{1,0:T(4,128)S(1)}, f32[3,1024]{1,0:T(4,128)S(1)}, u32[]{:S(2)}, u32[]{:S(2)}) collective-permute-start(f32[3,1024]{1,0:T(4,128)S(1)} %get-tuple-element.6), channel_id=1, source_target_pairs={{0,32},{32,64},{64,96},{1,33},{33,65},{65,97},{2,34},{34,66},{66,9... | collective-permute-start | bytes 36872 | tf_op jit(solution)/shard_map/ppermute | solution.py:30
  157.7 8.0 %collective-permute-start.22 = (f32[5,1024]{1,0:T(8,128)S(1)}, f32[5,1024]{1,0:T(8,128)S(1)}, u32[]{:S(2)}, u32[]{:S(2)}) collective-permute-start(f32[5,1024]{1,0:T(8,128)S(1)} %log_add_fusion.1), channel_id=1, source_target_pairs={{0,1},{1,2},{2,3},{3,4},{4,5},{5,6},{6,7},{7,8},{8,9},{9,10},{10,1... | collective-permute-start | bytes 61448 | tf_op jit(solution)/shard_map/ppermute | solution.py:30
  169.1 10.6 %collective-permute-start.25 = (f32[7,1024]{1,0:T(8,128)S(1)}, f32[7,1024]{1,0:T(8,128)S(1)}, u32[]{:S(2)}, u32[]{:S(2)}) collective-permute-start(f32[7,1024]{1,0:T(8,128)S(1)} %log_add_fusion), channel_id=1, source_target_pairs={{3,0},{4,1},{5,2},{6,3},{7,4},{8,5},{9,6},{10,7},{11,8},{12,9},{13... | collective-permute-start | bytes 86024 | tf_op jit(solution)/shard_map/ppermute | solution.py:30
  170.4 10.2 %collective-permute-start.26 = (f32[5,1024]{1,0:T(8,128)S(1)}, f32[5,1024]{1,0:T(8,128)S(1)}, u32[]{:S(2)}, u32[]{:S(2)}) collective-permute-start(f32[5,1024]{1,0:T(8,128)S(1)} %log_add_fusion.1), channel_id=1, source_target_pairs={{0,2},{31,29},{32,34},{63,61},{64,66},{95,93},{96,98},{127,125}} | collective-permute-start | bytes 61448 | tf_op jit(solution)/shard_map/ppermute | solution.py:170
  171.1 9.6 %collective-permute-start.24 = (f32[7,1024]{1,0:T(8,128)S(1)}, f32[7,1024]{1,0:T(8,128)S(1)}, u32[]{:S(2)}, u32[]{:S(2)}) collective-permute-start(f32[7,1024]{1,0:T(8,128)S(1)} %log_add_fusion), channel_id=1, source_target_pairs={{0,3},{1,4},{2,5},{3,6},{4,7},{5,8},{6,9},{7,10},{8,11},{9,12},{10... | collective-permute-start | bytes 86024 | tf_op jit(solution)/shard_map/ppermute | solution.py:30
  195.3 15.0 %collective-permute-start.27 = (f32[1,1024]{1,0:T(1,128)S(1)}, f32[1,1024]{1,0:T(1,128)S(1)}, u32[]{:S(2)}, u32[]{:S(2)}) collective-permute-start(f32[1,1024]{1,0:T(1,128)S(1)} %slice.201), channel_id=1, source_target_pairs={{0,1},{1,0},{2,3},{3,2},{4,5},{5,4},{6,7},{7,6},{8,9},{9,8},{10,11... | collective-permute-start | bytes 12296 | tf_op jit(solution)/shard_map/ppermute | solution.py:199
  196.0 16.7 %collective-permute-start.32 = (f32[3,1024]{1,0:T(4,128)S(1)}, f32[3,1024]{1,0:T(4,128)S(1)}, u32[]{:S(2)}, u32[]{:S(2)}) collective-permute-start(f32[3,1024]{1,0:T(4,128)S(1)} %get-tuple-element.4), channel_id=1, source_target_pairs={{64,0},{96,32},{65,1},{97,33},{66,2},{98,34},{67,3},{99,35},{68,4}... | collective-permute-start | bytes 36872 | tf_op jit(solution)/shard_map/ppermute | solution.py:30
  197.3 15.4 %collective-permute-start.33 = (f32[3,1024]{1,0:T(4,128)S(1)}, f32[3,1024]{1,0:T(4,128)S(1)}, u32[]{:S(2)}, u32[]{:S(2)}) collective-permute-start(f32[3,1024]{1,0:T(4,128)S(1)} %get-tuple-element.4), channel_id=1, source_target_pairs={{32,0},{64,32},{96,64},{33,1},{65,33},{97,65},{34,2},{66,34},{98,6... | collective-permute-start | bytes 36872 | tf_op jit(solution)/shard_map/ppermute | solution.py:30
  198.6 14.2 %collective-permute-start.34 = (f32[3,1024]{1,0:T(4,128)S(1)}, f32[3,1024]{1,0:T(4,128)S(1)}, u32[]{:S(2)}, u32[]{:S(2)}) collective-permute-start(f32[3,1024]{1,0:T(4,128)S(1)} %get-tuple-element.4), channel_id=1, source_target_pairs={{0,32},{32,64},{64,96},{1,33},{33,65},{65,97},{2,34},{34,66},{66,9... | collective-permute-start | bytes 36872 | tf_op jit(solution)/shard_map/ppermute | solution.py:30
  202.6 10.2 %collective-permute-start.35 = (f32[3,1024]{1,0:T(4,128)S(1)}, f32[3,1024]{1,0:T(4,128)S(1)}, u32[]{:S(2)}, u32[]{:S(2)}) collective-permute-start(f32[3,1024]{1,0:T(4,128)S(1)} %get-tuple-element.4), channel_id=1, source_target_pairs={{0,64},{32,96},{1,65},{33,97},{2,66},{34,98},{3,67},{35,99},{4,68}... | collective-permute-start | bytes 36872 | tf_op jit(solution)/shard_map/ppermute | solution.py:30
  210.4 37.3 %collective-permute-start.28 = (f32[2,1024]{1,0:T(2,128)S(1)}, f32[2,1024]{1,0:T(2,128)S(1)}, u32[]{:S(2)}, u32[]{:S(2)}) collective-permute-start(f32[2,1024]{1,0:T(2,128)S(1)} %maximum_select_fusion.4), channel_id=1, source_target_pairs={{0,2},{1,3},{2,0},{3,1},{4,6},{5,7},{6,4},{7,5},{8,10},{9,11},{10,... | collective-permute-start | bytes 24584 | tf_op jit(solution)/shard_map/ppermute | solution.py:199
  230.5 41.9 %collective-permute-start.36 = (f32[1,1024,128]{2,1,0:T(8,128)}, f32[1,1024,128]{2,1,0:T(8,128)S(1)}, u32[]{:S(2)}, u32[]{:S(2)}) collective-permute-start(f32[1,1024,128]{2,1,0:T(8,128)} %get-tuple-element.11), channel_id=1, source_target_pairs={{1,0},{2,1},{3,2},{4,3},{5,4},{6,5},{7,6},{8,7},{9,8},{10,9},{11,1... | collective-permute-start | bytes 1572872 | tf_op jit(solution)/shard_map/ppermute | solution.py:30
  234.3 38.1 %collective-permute-start.37 = (f32[1,1024,128]{2,1,0:T(8,128)}, f32[1,1024,128]{2,1,0:T(8,128)}, u32[]{:S(2)}, u32[]{:S(2)}) collective-permute-start(f32[1,1024,128]{2,1,0:T(8,128)} %get-tuple-element.14), channel_id=1, source_target_pairs={{0,1},{1,2},{2,3},{3,4},{4,5},{5,6},{6,7},{7,8},{8,9},{9,10},{10,1... | collective-permute-start | bytes 1572872 | tf_op jit(solution)/shard_map/ppermute | solution.py:30
  236.2 36.2 %collective-permute-start.38 = (f32[1,1024,128]{2,1,0:T(8,128)}, f32[1,1024,128]{2,1,0:T(8,128)}, u32[]{:S(2)}, u32[]{:S(2)}) collective-permute-start(f32[1,1024,128]{2,1,0:T(8,128)} %get-tuple-element.13), channel_id=1, source_target_pairs={{2,0},{3,1},{4,2},{5,3},{6,4},{7,5},{8,6},{9,7},{10,8},{11,9},{12,... | collective-permute-start | bytes 1572872 | tf_op jit(solution)/shard_map/ppermute | solution.py:30
  237.5 34.9 %collective-permute-start.39 = (f32[1,1024,128]{2,1,0:T(8,128)}, f32[1,1024,128]{2,1,0:T(8,128)}, u32[]{:S(2)}, u32[]{:S(2)}) collective-permute-start(f32[1,1024,128]{2,1,0:T(8,128)} %get-tuple-element.12), channel_id=1, source_target_pairs={{0,2},{1,3},{2,4},{3,5},{4,6},{5,7},{6,8},{7,9},{8,10},{9,11},{10,... | collective-permute-start | bytes 1572872 | tf_op jit(solution)/shard_map/ppermute | solution.py:30
  247.7 15.1 %collective-permute-start.29 = (f32[4,1024]{1,0:T(4,128)S(1)}, f32[4,1024]{1,0:T(4,128)S(1)}, u32[]{:S(2)}, u32[]{:S(2)}) collective-permute-start(f32[4,1024]{1,0:T(4,128)S(1)} %maximum_select_fusion.3), channel_id=1, source_target_pairs={{0,4},{1,5},{2,6},{3,7},{4,0},{5,1},{6,2},{7,3},{8,12},{9,13},{10,... | collective-permute-start | bytes 49160 | tf_op jit(solution)/shard_map/ppermute | solution.py:199
  (14 other events, 137.2 us)

commit v6 on v5

--- a/solution.py
+++ b/solution.py
@@ -189,22 +189,6 @@
     )
 
 
-def gather_rows(row, axis):
-    index = lax.axis_index(axis)
-    count = lax.axis_size(axis)
-    block = row
-    step = 1
-    while step < count:
-        route = [(i, i ^ step) for i in range(count)]
-        other = lax.ppermute(block, axis, route)
-        upper = (index // step) % 2 == 1
-        block = jnp.where(
-            upper, jnp.concatenate([other, block], axis=0), jnp.concatenate([block, other], axis=0)
-        )
-        step *= 2
-    return block
-
-
 def body(src_points, tgt_points, src_log_mass, tgt_log_mass, near_pairs, target_slot):
     owned = tgt_points.shape[0]
     group_size = src_points.shape[0]
@@ -244,7 +228,11 @@
         part = part[:, 0] - 0.5 * pair_tgt_sq / EPSILON
         cols_total = spread(grouped_lse(window_mask, part), "gx", 2 * owned)
         g_window = EPSILON * window_mass - EPSILON * cols_total
-    f_pot = gather_rows(f_span[2 * owned : 3 * owned], "gy")
+    f_rows = jnp.zeros((group_size,) + f_span.shape[1:], f_span.dtype)
+    f_rows = lax.dynamic_update_slice_in_dim(
+        f_rows, f_span[2 * owned : 3 * owned], gy_index * owned, 0
+    )
+    f_pot = lax.psum(f_rows, "gy")
     g_local = g_window[owned : 2 * owned]
     v_row = (g_window[window_ids] - 0.5 * pair_tgt_sq) / EPSILON
     w_col = (f_span[span_ids] - 0.5 * pair_src_sq) / EPSILON

time: 277 us -> 368 us (1.33)
  waiting for transfers between devices: 27.4 us -> 119 us
  starting transfers between devices: 125 us -> 111 us
  between operations: 1.84 us -> 15.2 us
    psum x0 -> x1, waiting for transfers between devices: none -> 97 us  [body(): f_pot = lax.psum(f_rows, 'gy')]
    ppermute x5 -> x0, waiting for transfers between devices: 13.3 us -> none  [gather_rows(): other = lax.ppermute(block, axis, route)]
    ppermute x5 -> x0, starting transfers between devices: 13.2 us -> none  [gather_rows(): other = lax.ppermute(block, axis, route)]
    ppermute x28, waiting for transfers between devices: 14.1 us -> 21.5 us  [passed_along(): return lax.ppermute(block, axis, route)]
  transfers between devices with their start and end apart: 40 -> 36, of which waited for: 11 -> 11; matrix products, arithmetic and copies ran while one was open for 7% -> 4% of each run, Pallas kernels for 4% -> 0%
where the time goes in v6:
time: 368 us; the launch traced here: 367 us
  waiting for transfers between devices  119 us (32%)
  starting transfers between devices  111 us (30%)
  Pallas kernels  84.8 us (23%)
  local copies, waits for them, and re-layouts  20.4 us (6%)
  other arithmetic  16.8 us (5%)
  between operations  15.2 us (4%)
    ppermute x28, starting transfers between devices, passed_along(): return lax.ppermute(block, axis, route)  98.5 us
    psum x1, waiting for transfers between devices, body(): f_pot = lax.psum(f_rows, 'gy')  97 us
    pallas_call x6, Pallas kernels, pair_lse(): pl.pallas_call(_lse_kernel, grid_spec=spec, out_shape=jax.ShapeDtypeStruc...  73.7 us
    ppermute x28, waiting for transfers between devices, passed_along(): return lax.ppermute(block, axis, route)  21.5 us
    pallas_call x1, Pallas kernels, pair_grad(): pl.pallas_call(_grad_kernel, grid_spec=spec, out_shape=jax.ShapeDtypeStru...  11.1 us
    ppermute x2, starting transfers between devices, padded(): lax.ppermute(lax.slice_in_dim(block, block.shape[dim] - width, None, axis...  7.82 us
  transfers between devices with their start and end apart: 36, of which 11 were waited for; matrix products, arithmetic and copies ran while one was open for 4% of the time, Pallas kernels for 0%

profile of v6, /device:TPU:1, one launch (start us, length us, event | category | flops | bytes accessed | tf_op | source)
XLA Modules:
  0.0 366.6 jit_solution(7359850510235602099)
XLA Ops:
  7.2 4.1 %collective-permute-start = (bf16[1,1024,128]{2,1,0:T(8,128)(2,1)}, bf16[1,1024,128]{2,1,0:T(8,128)(2,1)S(1)}, u32[]{:S(2)}, u32[]{:S(2)}) collective-permute-start(bf16[1,1024,128]{2,1,0:T(8,128)(2,1)} %param.7), channel_id=1, source_target_pairs={{0,32},{32,64},{64,96},{1,33},{33,65},{65,97},{2,34},{34,66},{66,9... | collective-permute-start | bytes 786440 | tf_op jit(solution)/shard_map/ppermute | solution.py:19
  14.8 4.2 %gather_fusion.2 = bf16[6,1024,128]{2,1,0:T(8,128)(2,1)S(1)} fusion(bf16[32,1024,128]{2,1,0:T(8,128)(2,1)} %a_ref.7, s32[1024]{0:T(1024)S(1)} %get-tuple-element.46), kind=kCustom, calls=%fused_computation.2 | custom fusion | bytes 3145752 | tf_op jit(solution)/shard_map/gather | solution.py:208
  22.5 12.4 %shard_map.85 = f32[6,1,1024]{2,1,0:T(1,128)} custom-call(s32[6]{0:T(128)} %bitcast.106, s32[6]{0:T(128)} %get-tuple-element.43.b_ids.a_ids, bf16[32,1024,128]{2,1,0:T(8,128)(2,1)} %a_ref.7, bf16[3,1024,128]{2,1,0:T(8,128)(2,1)} %copy-done, f32[6,8,1024]{2,1,0:T(8,128)} %broadcast_in_dim.241.v_ref), custom_call_target="tpu_custom_call" | custom-call | tf_op jit(solution)/shard_map/pallas_call | solution.py:77
  35.9 4.6 %collective-permute-start.4 = (f32[5,1024]{1,0:T(8,128)S(1)}, f32[5,1024]{1,0:T(8,128)S(1)}, u32[]{:S(2)}, u32[]{:S(2)}) collective-permute-start(f32[5,1024]{1,0:T(8,128)S(1)} %log_add_fusion.5), channel_id=1, source_target_pairs={{0,1},{1,2},{2,3},{3,4},{4,5},{5,6},{6,7},{7,8},{8,9},{9,10},{10,1... | collective-permute-start | bytes 61448 | tf_op jit(solution)/shard_map/ppermute | solution.py:30
  42.4 3.3 collective-permute-done.5
  47.8 5.8 %collective-permute-start.6 = (f32[7,1024]{1,0:T(8,128)S(1)}, f32[7,1024]{1,0:T(8,128)S(1)}, u32[]{:S(2)}, u32[]{:S(2)}) collective-permute-start(f32[7,1024]{1,0:T(8,128)S(1)} %log_add_fusion.4), channel_id=1, source_target_pairs={{0,3},{1,4},{2,5},{3,6},{4,7},{5,8},{6,9},{7,10},{8,11},{9,12},{10... | collective-permute-start | bytes 86024 | tf_op jit(solution)/shard_map/ppermute | solution.py:30
  56.1 12.4 %shard_map.86 = f32[6,1,1024]{2,1,0:T(1,128)} custom-call(s32[6]{0:T(128)} %get-tuple-element.43.b_ids.a_ids, s32[6]{0:T(128)} %bitcast.107, bf16[3,1024,128]{2,1,0:T(8,128)(2,1)} %copy-done, bf16[32,1024,128]{2,1,0:T(8,128)(2,1)} %a_ref.7, f32[6,8,1024]{2,1,0:T(8,128)} %broadcast_in_dim.245.v_ref), custom_call_target="tpu_custom_call" | custom-call | tf_op jit(solution)/shard_map/pallas_call | solution.py:77
  70.8 3.7 %collective-permute-start.2 = (f32[1,1024]{1,0:T(1,128)S(1)}, f32[1,1024]{1,0:T(1,128)S(1)}, u32[]{:S(2)}, u32[]{:S(2)}) collective-permute-start(f32[1,1024]{1,0:T(1,128)S(1)} %copy-done.5), channel_id=1, source_target_pairs={{0,32},{32,64},{64,96},{1,33},{33,65},{65,97},{2,34},{34,66},{66,9... | collective-permute-start | bytes 12296 | tf_op jit(solution)/shard_map/ppermute | solution.py:19
  77.1 4.6 %collective-permute-start.11 = (f32[3,1024]{1,0:T(4,128)S(1)}, f32[3,1024]{1,0:T(4,128)S(1)}, u32[]{:S(2)}, u32[]{:S(2)}) collective-permute-start(f32[3,1024]{1,0:T(4,128)S(1)} %get-tuple-element.8), channel_id=1, source_target_pairs={{0,32},{32,64},{64,96},{1,33},{33,65},{65,97},{2,34},{34,66},{66,9... | collective-permute-start | bytes 36872 | tf_op jit(solution)/shard_map/ppermute | solution.py:30
  81.8 6.1 %collective-permute-start.12 = (f32[3,1024]{1,0:T(4,128)S(1)}, f32[3,1024]{1,0:T(4,128)S(1)}, u32[]{:S(2)}, u32[]{:S(2)}) collective-permute-start(f32[3,1024]{1,0:T(4,128)S(1)} %get-tuple-element.8), channel_id=1, source_target_pairs={{0,64},{32,96},{1,65},{33,97},{2,66},{34,98},{3,67},{35,99},{4,68}... | collective-permute-start | bytes 36872 | tf_op jit(solution)/shard_map/ppermute | solution.py:30
  90.1 12.2 %shard_map.87 = f32[6,1,1024]{2,1,0:T(1,128)} custom-call(s32[6]{0:T(128)} %bitcast.108, s32[6]{0:T(128)} %get-tuple-element.43.b_ids.a_ids, bf16[32,1024,128]{2,1,0:T(8,128)(2,1)} %a_ref.7, bf16[3,1024,128]{2,1,0:T(8,128)(2,1)} %copy-done, f32[6,8,1024]{2,1,0:T(8,128)} %broadcast_in_dim.249.v_ref), custom_call_target="tpu_custom_call" | custom-call | tf_op jit(solution)/shard_map/pallas_call | solution.py:77
  103.4 3.8 %collective-permute-start.13 = (f32[5,1024]{1,0:T(8,128)S(1)}, f32[5,1024]{1,0:T(8,128)S(1)}, u32[]{:S(2)}, u32[]{:S(2)}) collective-permute-start(f32[5,1024]{1,0:T(8,128)S(1)} %log_add_fusion.3), channel_id=1, source_target_pairs={{0,1},{1,2},{2,3},{3,4},{4,5},{5,6},{6,7},{7,8},{8,9},{9,10},{10,1... | collective-permute-start | bytes 61448 | tf_op jit(solution)/shard_map/ppermute | solution.py:30
  109.2 3.3 collective-permute-done.14
  114.5 6.4 %collective-permute-start.15 = (f32[7,1024]{1,0:T(8,128)S(1)}, f32[7,1024]{1,0:T(8,128)S(1)}, u32[]{:S(2)}, u32[]{:S(2)}) collective-permute-start(f32[7,1024]{1,0:T(8,128)S(1)} %log_add_fusion.2), channel_id=1, source_target_pairs={{0,3},{1,4},{2,5},{3,6},{4,7},{5,8},{6,9},{7,10},{8,11},{9,12},{10... | collective-permute-start | bytes 86024 | tf_op jit(solution)/shard_map/ppermute | solution.py:30
  123.4 12.2 %shard_map.88 = f32[6,1,1024]{2,1,0:T(1,128)} custom-call(s32[6]{0:T(128)} %get-tuple-element.43.b_ids.a_ids, s32[6]{0:T(128)} %bitcast.109, bf16[3,1024,128]{2,1,0:T(8,128)(2,1)} %copy-done, bf16[32,1024,128]{2,1,0:T(8,128)(2,1)} %a_ref.7, f32[6,8,1024]{2,1,0:T(8,128)} %broadcast_in_dim.251.v_ref), custom_call_target="tpu_custom_call" | custom-call | tf_op jit(solution)/shard_map/pallas_call | solution.py:77
  139.3 4.0 %collective-permute-start.20 = (f32[3,1024]{1,0:T(4,128)S(1)}, f32[3,1024]{1,0:T(4,128)S(1)}, u32[]{:S(2)}, u32[]{:S(2)}) collective-permute-start(f32[3,1024]{1,0:T(4,128)S(1)} %get-tuple-element.6), channel_id=1, source_target_pairs={{0,32},{32,64},{64,96},{1,33},{33,65},{65,97},{2,34},{34,66},{66,9... | collective-permute-start | bytes 36872 | tf_op jit(solution)/shard_map/ppermute | solution.py:30
  143.2 5.7 %collective-permute-start.21 = (f32[3,1024]{1,0:T(4,128)S(1)}, f32[3,1024]{1,0:T(4,128)S(1)}, u32[]{:S(2)}, u32[]{:S(2)}) collective-permute-start(f32[3,1024]{1,0:T(4,128)S(1)} %get-tuple-element.6), channel_id=1, source_target_pairs={{0,64},{32,96},{1,65},{33,97},{2,66},{34,98},{3,67},{35,99},{4,68}... | collective-permute-start | bytes 36872 | tf_op jit(solution)/shard_map/ppermute | solution.py:30
  151.0 12.2 %shard_map.89 = f32[6,1,1024]{2,1,0:T(1,128)} custom-call(s32[6]{0:T(128)} %bitcast.110, s32[6]{0:T(128)} %get-tuple-element.43.b_ids.a_ids, bf16[32,1024,128]{2,1,0:T(8,128)(2,1)} %a_ref.7, bf16[3,1024,128]{2,1,0:T(8,128)(2,1)} %copy-done, f32[6,8,1024]{2,1,0:T(8,128)} %broadcast_in_dim.253.v_ref), custom_call_target="tpu_custom_call" | custom-call | tf_op jit(solution)/shard_map/pallas_call | solution.py:77
  164.3 6.0 %collective-permute-start.22 = (f32[5,1024]{1,0:T(8,128)S(1)}, f32[5,1024]{1,0:T(8,128)S(1)}, u32[]{:S(2)}, u32[]{:S(2)}) collective-permute-start(f32[5,1024]{1,0:T(8,128)S(1)} %log_add_fusion.1), channel_id=1, source_target_pairs={{0,1},{1,2},{2,3},{3,4},{4,5},{5,6},{6,7},{7,8},{8,9},{9,10},{10,1... | collective-permute-start | bytes 61448 | tf_op jit(solution)/shard_map/ppermute | solution.py:30
  172.3 3.3 collective-permute-done.23
  177.6 8.6 %collective-permute-start.24 = (f32[7,1024]{1,0:T(8,128)S(1)}, f32[7,1024]{1,0:T(8,128)S(1)}, u32[]{:S(2)}, u32[]{:S(2)}) collective-permute-start(f32[7,1024]{1,0:T(8,128)S(1)} %log_add_fusion), channel_id=1, source_target_pairs={{0,3},{1,4},{2,5},{3,6},{4,7},{5,8},{6,9},{7,10},{8,11},{9,12},{10... | collective-permute-start | bytes 86024 | tf_op jit(solution)/shard_map/ppermute | solution.py:30
  188.6 12.2 %shard_map.90 = f32[6,1,1024]{2,1,0:T(1,128)} custom-call(s32[6]{0:T(128)} %get-tuple-element.43.b_ids.a_ids, s32[6]{0:T(128)} %bitcast.111, bf16[3,1024,128]{2,1,0:T(8,128)(2,1)} %copy-done, bf16[32,1024,128]{2,1,0:T(8,128)(2,1)} %a_ref.7, f32[6,8,1024]{2,1,0:T(8,128)} %broadcast_in_dim.255.v_ref), custom_call_target="tpu_custom_call" | custom-call | tf_op jit(solution)/shard_map/pallas_call | solution.py:77
  204.5 4.0 %collective-permute-start.29 = (f32[3,1024]{1,0:T(4,128)S(1)}, f32[3,1024]{1,0:T(4,128)S(1)}, u32[]{:S(2)}, u32[]{:S(2)}) collective-permute-start(f32[3,1024]{1,0:T(4,128)S(1)} %get-tuple-element.4), channel_id=1, source_target_pairs={{0,32},{32,64},{64,96},{1,33},{33,65},{65,97},{2,34},{34,66},{66,9... | collective-permute-start | bytes 36872 | tf_op jit(solution)/shard_map/ppermute | solution.py:30
  208.5 5.5 %collective-permute-start.30 = (f32[3,1024]{1,0:T(4,128)S(1)}, f32[3,1024]{1,0:T(4,128)S(1)}, u32[]{:S(2)}, u32[]{:S(2)}) collective-permute-start(f32[3,1024]{1,0:T(4,128)S(1)} %get-tuple-element.4), channel_id=1, source_target_pairs={{0,64},{32,96},{1,65},{33,97},{2,66},{34,98},{3,67},{35,99},{4,68}... | collective-permute-start | bytes 36872 | tf_op jit(solution)/shard_map/ppermute | solution.py:30
  217.7 11.1 %shard_map.91 = f32[6,1024,128]{2,1,0:T(8,128)} custom-call(s32[6]{0:T(128)} %bitcast.112, s32[6]{0:T(128)} %get-tuple-element.43.b_ids.a_ids, bf16[32,1024,128]{2,1,0:T(8,128)(2,1)} %a_ref.7, bf16[3,1024,128]{2,1,0:T(8,128)(2,1)} %copy-done, f32[6,1,1024]{2,1,0:T(1,128)} %div.78.v_ref, f32[6,1024,1]{2,1,0:T(8,128)} %copy.11.w_ref), custom_call_target="tpu_custom_call" | custom-call | tf_op jit(solution)/shard_map/pallas_call | solution.py:112
  228.8 3.8 %select_reduce_fusion = f32[5,1024,128]{2,1,0:T(8,128)S(1)} fusion(f32[6,1024,128]{2,1,0:T(8,128)} %shard_map.91, pred[5,6]{1,0:T(8,128)(4,1)S(1)} %iota_compare_fusion.1), kind=kLoop, calls=%fused_computation.9 | loop fusion | flops 7208960 | bytes 5767198 | tf_op jit(solution)/shard_map/reduce_sum | solution.py:242
  234.0 3.7 collective-permute-start.31
  237.6 2.3 collective-permute-start.32
  241.2 8.8 %collective-permute-start.34 = (f32[1,1024,128]{2,1,0:T(8,128)}, f32[1,1024,128]{2,1,0:T(8,128)}, u32[]{:S(2)}, u32[]{:S(2)}) collective-permute-start(f32[1,1024,128]{2,1,0:T(8,128)} %get-tuple-element.12), channel_id=1, source_target_pairs={{0,2},{1,3},{2,4},{3,5},{4,6},{5,7},{6,8},{7,9},{8,10},{9,11},{10,... | collective-permute-start | bytes 1572872 | tf_op jit(solution)/shard_map/ppermute | solution.py:30
  251.5 5.7 %collective-permute-done.33 = f32[1,1024,128]{2,1,0:T(8,128)} collective-permute-done((f32[1,1024,128]{2,1,0:T(8,128)}, f32[1,1024,128]{2,1,0:T(8,128)}, u32[]{:S(2)}, u32[]{:S(2)}) %collective-permute-start.33) | collective-permute-done | bytes 524320 | tf_op jit(solution)/shard_map/ppermute | solution.py:30
  258.9 2.3 fusion.2
  261.2 97.0 %all-reduce.32.cloned.1.call-done = f32[32,1024]{1,0:T(8,128)} async-done(((f32[32,1024]{1,0:T(8,128)}), f32[32,1024]{1,0:T(8,128)}) %all-reduce.32.cloned.1.call-update) | async-done | bytes 131088 | tf_op jit(solution)/shard_map/psum | solution.py:235
  (198 shorter events, 56.2 us)
Async XLA Ops:
  7.2 351.0 %all-reduce.32.cloned.1.call-start = ((), (), s32[]{:S(2)}) async-start(), calls=%async_computation | async-start | bytes 262144 | tf_op jit(solution)/shard_map/psum | solution.py:235
  7.2 13.3 %collective-permute-start = (bf16[1,1024,128]{2,1,0:T(8,128)(2,1)}, bf16[1,1024,128]{2,1,0:T(8,128)(2,1)S(1)}, u32[]{:S(2)}, u32[]{:S(2)}) collective-permute-start(bf16[1,1024,128]{2,1,0:T(8,128)(2,1)} %param.7), channel_id=1, source_target_pairs={{0,32},{32,64},{64,96},{1,33},{33,65},{65,97},{2,34},{34,66},{66,9... | collective-permute-start | bytes 786440 | tf_op jit(solution)/shard_map/ppermute | solution.py:19
  11.3 9.3 %collective-permute-start.1 = (bf16[1,1024,128]{2,1,0:T(8,128)(2,1)}, bf16[1,1024,128]{2,1,0:T(8,128)(2,1)S(1)}, u32[]{:S(2)}, u32[]{:S(2)}) collective-permute-start(bf16[1,1024,128]{2,1,0:T(8,128)(2,1)} %param.7), channel_id=1, source_target_pairs={{32,0},{64,32},{96,64},{33,1},{65,33},{97,65},{34,2},{66,34},{98,6... | collective-permute-start | bytes 786440 | tf_op jit(solution)/shard_map/ppermute | solution.py:22
  35.9 6.5 %collective-permute-start.4 = (f32[5,1024]{1,0:T(8,128)S(1)}, f32[5,1024]{1,0:T(8,128)S(1)}, u32[]{:S(2)}, u32[]{:S(2)}) collective-permute-start(f32[5,1024]{1,0:T(8,128)S(1)} %log_add_fusion.5), channel_id=1, source_target_pairs={{0,1},{1,2},{2,3},{3,4},{4,5},{5,6},{6,7},{7,8},{8,9},{9,10},{10,1... | collective-permute-start | bytes 61448 | tf_op jit(solution)/shard_map/ppermute | solution.py:30
  45.8 7.8 %collective-permute-start.7 = (f32[7,1024]{1,0:T(8,128)S(1)}, f32[7,1024]{1,0:T(8,128)S(1)}, u32[]{:S(2)}, u32[]{:S(2)}) collective-permute-start(f32[7,1024]{1,0:T(8,128)S(1)} %log_add_fusion.4), channel_id=1, source_target_pairs={{3,0},{4,1},{5,2},{6,3},{7,4},{8,5},{9,6},{10,7},{11,8},{12,9},{13... | collective-permute-start | bytes 86024 | tf_op jit(solution)/shard_map/ppermute | solution.py:30
  47.2 7.5 %collective-permute-start.8 = (f32[5,1024]{1,0:T(8,128)S(1)}, f32[5,1024]{1,0:T(8,128)S(1)}, u32[]{:S(2)}, u32[]{:S(2)}) collective-permute-start(f32[5,1024]{1,0:T(8,128)S(1)} %log_add_fusion.5), channel_id=1, source_target_pairs={{0,2},{31,29},{32,34},{63,61},{64,66},{95,93},{96,98},{127,125}} | collective-permute-start | bytes 61448 | tf_op jit(solution)/shard_map/ppermute | solution.py:170
  47.8 6.8 %collective-permute-start.6 = (f32[7,1024]{1,0:T(8,128)S(1)}, f32[7,1024]{1,0:T(8,128)S(1)}, u32[]{:S(2)}, u32[]{:S(2)}) collective-permute-start(f32[7,1024]{1,0:T(8,128)S(1)} %log_add_fusion.4), channel_id=1, source_target_pairs={{0,3},{1,4},{2,5},{3,6},{4,7},{5,8},{6,9},{7,10},{8,11},{9,12},{10... | collective-permute-start | bytes 86024 | tf_op jit(solution)/shard_map/ppermute | solution.py:30
  69.4 12.3 %collective-permute-start.9 = (f32[3,1024]{1,0:T(4,128)S(1)}, f32[3,1024]{1,0:T(4,128)S(1)}, u32[]{:S(2)}, u32[]{:S(2)}) collective-permute-start(f32[3,1024]{1,0:T(4,128)S(1)} %get-tuple-element.8), channel_id=1, source_target_pairs={{64,0},{96,32},{65,1},{97,33},{66,2},{98,34},{67,3},{99,35},{68,4}... | collective-permute-start | bytes 36872 | tf_op jit(solution)/shard_map/ppermute | solution.py:30
  70.8 18.1 %collective-permute-start.2 = (f32[1,1024]{1,0:T(1,128)S(1)}, f32[1,1024]{1,0:T(1,128)S(1)}, u32[]{:S(2)}, u32[]{:S(2)}) collective-permute-start(f32[1,1024]{1,0:T(1,128)S(1)} %copy-done.5), channel_id=1, source_target_pairs={{0,32},{32,64},{64,96},{1,33},{33,65},{65,97},{2,34},{34,66},{66,9... | collective-permute-start | bytes 12296 | tf_op jit(solution)/shard_map/ppermute | solution.py:19
  74.5 14.3 %collective-permute-start.3 = (f32[1,1024]{1,0:T(1,128)S(1)}, f32[1,1024]{1,0:T(1,128)S(1)}, u32[]{:S(2)}, u32[]{:S(2)}) collective-permute-start(f32[1,1024]{1,0:T(1,128)S(1)} %copy-done.5), channel_id=1, source_target_pairs={{32,0},{64,32},{96,64},{33,1},{65,33},{97,65},{34,2},{66,34},{98,6... | collective-permute-start | bytes 12296 | tf_op jit(solution)/shard_map/ppermute | solution.py:22
  75.8 12.1 %collective-permute-start.10 = (f32[3,1024]{1,0:T(4,128)S(1)}, f32[3,1024]{1,0:T(4,128)S(1)}, u32[]{:S(2)}, u32[]{:S(2)}) collective-permute-start(f32[3,1024]{1,0:T(4,128)S(1)} %get-tuple-element.8), channel_id=1, source_target_pairs={{32,0},{64,32},{96,64},{33,1},{65,33},{97,65},{34,2},{66,34},{98,6... | collective-permute-start | bytes 36872 | tf_op jit(solution)/shard_map/ppermute | solution.py:30
  77.1 10.8 %collective-permute-start.11 = (f32[3,1024]{1,0:T(4,128)S(1)}, f32[3,1024]{1,0:T(4,128)S(1)}, u32[]{:S(2)}, u32[]{:S(2)}) collective-permute-start(f32[3,1024]{1,0:T(4,128)S(1)} %get-tuple-element.8), channel_id=1, source_target_pairs={{0,32},{32,64},{64,96},{1,33},{33,65},{65,97},{2,34},{34,66},{66,9... | collective-permute-start | bytes 36872 | tf_op jit(solution)/shard_map/ppermute | solution.py:30
  81.8 7.0 %collective-permute-start.12 = (f32[3,1024]{1,0:T(4,128)S(1)}, f32[3,1024]{1,0:T(4,128)S(1)}, u32[]{:S(2)}, u32[]{:S(2)}) collective-permute-start(f32[3,1024]{1,0:T(4,128)S(1)} %get-tuple-element.8), channel_id=1, source_target_pairs={{0,64},{32,96},{1,65},{33,97},{2,66},{34,98},{3,67},{35,99},{4,68}... | collective-permute-start | bytes 36872 | tf_op jit(solution)/shard_map/ppermute | solution.py:30
  112.6 8.4 %collective-permute-start.16 = (f32[7,1024]{1,0:T(8,128)S(1)}, f32[7,1024]{1,0:T(8,128)S(1)}, u32[]{:S(2)}, u32[]{:S(2)}) collective-permute-start(f32[7,1024]{1,0:T(8,128)S(1)} %log_add_fusion.2), channel_id=1, source_target_pairs={{3,0},{4,1},{5,2},{6,3},{7,4},{8,5},{9,6},{10,7},{11,8},{12,9},{13... | collective-permute-start | bytes 86024 | tf_op jit(solution)/shard_map/ppermute | solution.py:30
  113.9 8.1 %collective-permute-start.17 = (f32[5,1024]{1,0:T(8,128)S(1)}, f32[5,1024]{1,0:T(8,128)S(1)}, u32[]{:S(2)}, u32[]{:S(2)}) collective-permute-start(f32[5,1024]{1,0:T(8,128)S(1)} %log_add_fusion.3), channel_id=1, source_target_pairs={{0,2},{31,29},{32,34},{63,61},{64,66},{95,93},{96,98},{127,125}} | collective-permute-start | bytes 61448 | tf_op jit(solution)/shard_map/ppermute | solution.py:170
  114.5 7.5 %collective-permute-start.15 = (f32[7,1024]{1,0:T(8,128)S(1)}, f32[7,1024]{1,0:T(8,128)S(1)}, u32[]{:S(2)}, u32[]{:S(2)}) collective-permute-start(f32[7,1024]{1,0:T(8,128)S(1)} %log_add_fusion.2), channel_id=1, source_target_pairs={{0,3},{1,4},{2,5},{3,6},{4,7},{5,8},{6,9},{7,10},{8,11},{9,12},{10... | collective-permute-start | bytes 86024 | tf_op jit(solution)/shard_map/ppermute | solution.py:30
  136.7 12.3 %collective-permute-start.18 = (f32[3,1024]{1,0:T(4,128)S(1)}, f32[3,1024]{1,0:T(4,128)S(1)}, u32[]{:S(2)}, u32[]{:S(2)}) collective-permute-start(f32[3,1024]{1,0:T(4,128)S(1)} %get-tuple-element.6), channel_id=1, source_target_pairs={{64,0},{96,32},{65,1},{97,33},{66,2},{98,34},{67,3},{99,35},{68,4}... | collective-permute-start | bytes 36872 | tf_op jit(solution)/shard_map/ppermute | solution.py:30
  138.0 11.0 %collective-permute-start.19 = (f32[3,1024]{1,0:T(4,128)S(1)}, f32[3,1024]{1,0:T(4,128)S(1)}, u32[]{:S(2)}, u32[]{:S(2)}) collective-permute-start(f32[3,1024]{1,0:T(4,128)S(1)} %get-tuple-element.6), channel_id=1, source_target_pairs={{32,0},{64,32},{96,64},{33,1},{65,33},{97,65},{34,2},{66,34},{98,6... | collective-permute-start | bytes 36872 | tf_op jit(solution)/shard_map/ppermute | solution.py:30
  139.3 9.8 %collective-permute-start.20 = (f32[3,1024]{1,0:T(4,128)S(1)}, f32[3,1024]{1,0:T(4,128)S(1)}, u32[]{:S(2)}, u32[]{:S(2)}) collective-permute-start(f32[3,1024]{1,0:T(4,128)S(1)} %get-tuple-element.6), channel_id=1, source_target_pairs={{0,32},{32,64},{64,96},{1,33},{33,65},{65,97},{2,34},{34,66},{66,9... | collective-permute-start | bytes 36872 | tf_op jit(solution)/shard_map/ppermute | solution.py:30
  143.2 6.3 %collective-permute-start.21 = (f32[3,1024]{1,0:T(4,128)S(1)}, f32[3,1024]{1,0:T(4,128)S(1)}, u32[]{:S(2)}, u32[]{:S(2)}) collective-permute-start(f32[3,1024]{1,0:T(4,128)S(1)} %get-tuple-element.6), channel_id=1, source_target_pairs={{0,64},{32,96},{1,65},{33,97},{2,66},{34,98},{3,67},{35,99},{4,68}... | collective-permute-start | bytes 36872 | tf_op jit(solution)/shard_map/ppermute | solution.py:30
  164.3 8.0 %collective-permute-start.22 = (f32[5,1024]{1,0:T(8,128)S(1)}, f32[5,1024]{1,0:T(8,128)S(1)}, u32[]{:S(2)}, u32[]{:S(2)}) collective-permute-start(f32[5,1024]{1,0:T(8,128)S(1)} %log_add_fusion.1), channel_id=1, source_target_pairs={{0,1},{1,2},{2,3},{3,4},{4,5},{5,6},{6,7},{7,8},{8,9},{9,10},{10,1... | collective-permute-start | bytes 61448 | tf_op jit(solution)/shard_map/ppermute | solution.py:30
  175.7 10.5 %collective-permute-start.25 = (f32[7,1024]{1,0:T(8,128)S(1)}, f32[7,1024]{1,0:T(8,128)S(1)}, u32[]{:S(2)}, u32[]{:S(2)}) collective-permute-start(f32[7,1024]{1,0:T(8,128)S(1)} %log_add_fusion), channel_id=1, source_target_pairs={{3,0},{4,1},{5,2},{6,3},{7,4},{8,5},{9,6},{10,7},{11,8},{12,9},{13... | collective-permute-start | bytes 86024 | tf_op jit(solution)/shard_map/ppermute | solution.py:30
  177.0 10.3 %collective-permute-start.26 = (f32[5,1024]{1,0:T(8,128)S(1)}, f32[5,1024]{1,0:T(8,128)S(1)}, u32[]{:S(2)}, u32[]{:S(2)}) collective-permute-start(f32[5,1024]{1,0:T(8,128)S(1)} %log_add_fusion.1), channel_id=1, source_target_pairs={{0,2},{31,29},{32,34},{63,61},{64,66},{95,93},{96,98},{127,125}} | collective-permute-start | bytes 61448 | tf_op jit(solution)/shard_map/ppermute | solution.py:170
  177.6 9.6 %collective-permute-start.24 = (f32[7,1024]{1,0:T(8,128)S(1)}, f32[7,1024]{1,0:T(8,128)S(1)}, u32[]{:S(2)}, u32[]{:S(2)}) collective-permute-start(f32[7,1024]{1,0:T(8,128)S(1)} %log_add_fusion), channel_id=1, source_target_pairs={{0,3},{1,4},{2,5},{3,6},{4,7},{5,8},{6,9},{7,10},{8,11},{9,12},{10... | collective-permute-start | bytes 86024 | tf_op jit(solution)/shard_map/ppermute | solution.py:30
  201.9 14.3 %collective-permute-start.27 = (f32[3,1024]{1,0:T(4,128)S(1)}, f32[3,1024]{1,0:T(4,128)S(1)}, u32[]{:S(2)}, u32[]{:S(2)}) collective-permute-start(f32[3,1024]{1,0:T(4,128)S(1)} %get-tuple-element.4), channel_id=1, source_target_pairs={{64,0},{96,32},{65,1},{97,33},{66,2},{98,34},{67,3},{99,35},{68,4}... | collective-permute-start | bytes 36872 | tf_op jit(solution)/shard_map/ppermute | solution.py:30
  203.2 13.0 %collective-permute-start.28 = (f32[3,1024]{1,0:T(4,128)S(1)}, f32[3,1024]{1,0:T(4,128)S(1)}, u32[]{:S(2)}, u32[]{:S(2)}) collective-permute-start(f32[3,1024]{1,0:T(4,128)S(1)} %get-tuple-element.4), channel_id=1, source_target_pairs={{32,0},{64,32},{96,64},{33,1},{65,33},{97,65},{34,2},{66,34},{98,6... | collective-permute-start | bytes 36872 | tf_op jit(solution)/shard_map/ppermute | solution.py:30
  204.5 11.8 %collective-permute-start.29 = (f32[3,1024]{1,0:T(4,128)S(1)}, f32[3,1024]{1,0:T(4,128)S(1)}, u32[]{:S(2)}, u32[]{:S(2)}) collective-permute-start(f32[3,1024]{1,0:T(4,128)S(1)} %get-tuple-element.4), channel_id=1, source_target_pairs={{0,32},{32,64},{64,96},{1,33},{33,65},{65,97},{2,34},{34,66},{66,9... | collective-permute-start | bytes 36872 | tf_op jit(solution)/shard_map/ppermute | solution.py:30
  208.5 7.8 %collective-permute-start.30 = (f32[3,1024]{1,0:T(4,128)S(1)}, f32[3,1024]{1,0:T(4,128)S(1)}, u32[]{:S(2)}, u32[]{:S(2)}) collective-permute-start(f32[3,1024]{1,0:T(4,128)S(1)} %get-tuple-element.4), channel_id=1, source_target_pairs={{0,64},{32,96},{1,65},{33,97},{2,66},{34,98},{3,67},{35,99},{4,68}... | collective-permute-start | bytes 36872 | tf_op jit(solution)/shard_map/ppermute | solution.py:30
  234.0 17.5 %collective-permute-start.31 = (f32[1,1024,128]{2,1,0:T(8,128)}, f32[1,1024,128]{2,1,0:T(8,128)S(1)}, u32[]{:S(2)}, u32[]{:S(2)}) collective-permute-start(f32[1,1024,128]{2,1,0:T(8,128)} %get-tuple-element.11), channel_id=1, source_target_pairs={{1,0},{2,1},{3,2},{4,3},{5,4},{6,5},{7,6},{8,7},{9,8},{10,9},{11,1... | collective-permute-start | bytes 1572872 | tf_op jit(solution)/shard_map/ppermute | solution.py:30
  237.6 13.9 %collective-permute-start.32 = (f32[1,1024,128]{2,1,0:T(8,128)}, f32[1,1024,128]{2,1,0:T(8,128)}, u32[]{:S(2)}, u32[]{:S(2)}) collective-permute-start(f32[1,1024,128]{2,1,0:T(8,128)} %get-tuple-element.14), channel_id=1, source_target_pairs={{0,1},{1,2},{2,3},{3,4},{4,5},{5,6},{6,7},{7,8},{8,9},{9,10},{10,1... | collective-permute-start | bytes 1572872 | tf_op jit(solution)/shard_map/ppermute | solution.py:30
  239.9 17.2 %collective-permute-start.33 = (f32[1,1024,128]{2,1,0:T(8,128)}, f32[1,1024,128]{2,1,0:T(8,128)}, u32[]{:S(2)}, u32[]{:S(2)}) collective-permute-start(f32[1,1024,128]{2,1,0:T(8,128)} %get-tuple-element.13), channel_id=1, source_target_pairs={{2,0},{3,1},{4,2},{5,3},{6,4},{7,5},{8,6},{9,7},{10,8},{11,9},{12,... | collective-permute-start | bytes 1572872 | tf_op jit(solution)/shard_map/ppermute | solution.py:30
  241.2 17.7 %collective-permute-start.34 = (f32[1,1024,128]{2,1,0:T(8,128)}, f32[1,1024,128]{2,1,0:T(8,128)}, u32[]{:S(2)}, u32[]{:S(2)}) collective-permute-start(f32[1,1024,128]{2,1,0:T(8,128)} %get-tuple-element.12), channel_id=1, source_target_pairs={{0,2},{1,3},{2,4},{3,5},{4,6},{5,7},{6,8},{7,9},{8,10},{9,11},{10,... | collective-permute-start | bytes 1572872 | tf_op jit(solution)/shard_map/ppermute | solution.py:30
  (11 other events, 116.2 us)
Sparse Core Ops, SparseCore 0:
  251.0 107.1 all-reduce.31

commit v7 on v5

--- a/solution.py
+++ b/solution.py
@@ -130,14 +130,21 @@
     count = lax.axis_size(axis)
     parts = [block]
     pad = jnp.full((reach,) + block.shape[1:], EMPTY_LOG, block.dtype)
+    far = [reach, -reach] if count == 2 * reach else []
     for distance in range(-reach, reach + 1):
-        if distance == 0:
+        if distance == 0 or distance in far:
             continue
         got = passed_along(block, axis, distance)
         valid = (index - distance >= 0) & (index - distance < count)
         got = jnp.where(valid, got, EMPTY_LOG)
         got = jnp.concatenate([pad, got, pad], axis=0)
         parts.append(lax.slice_in_dim(got, reach + distance, reach + distance + width, axis=0))
+    if far:
+        got = lax.ppermute(block, axis, [(i, (i + reach) % count) for i in range(count)])
+        got = jnp.concatenate([pad, got, pad], axis=0)
+        upper = lax.slice_in_dim(got, 2 * reach, 2 * reach + width, axis=0)
+        lower = lax.slice_in_dim(got, 0, width, axis=0)
+        parts.append(jnp.where(index >= reach, upper, lower))
     parts = jnp.stack(parts)
     peak_val = jnp.max(parts, axis=0)
     return peak_val + jnp.log(jnp.sum(jnp.exp(parts - peak_val[None]), axis=0))

time: 277 us -> 266 us (0.960)
  starting transfers between devices: 125 us -> 113 us
    ppermute x28 -> x22, starting transfers between devices: 99.5 us -> 75.2 us  [passed_along(): return lax.ppermute(block, axis, route)]
    ppermute x0 -> x3, starting transfers between devices: none -> 13.2 us  [spread(): lax.ppermute(block, axis, [(i, (i + reach) % count) for i in range(count)])]
    ppermute x28 -> x22, waiting for transfers between devices: 14.1 us -> 12.8 us  [passed_along(): return lax.ppermute(block, axis, route)]
  transfers between devices with their start and end apart: 40 -> 37, of which waited for: 11 -> 11; matrix products, arithmetic and copies ran while one was open for 7% -> 7% of each run, Pallas kernels for 4% -> 4%
where the time goes in v7:
time: 266 us; the launch traced here: 263 us
  starting transfers between devices  113 us (42%)
  Pallas kernels  84.8 us (32%)
  waiting for transfers between devices  28.4 us (11%)
  local copies, waits for them, and re-layouts  17.8 us (7%)
  other arithmetic  17.4 us (7%)
    ppermute x22, starting transfers between devices, passed_along(): return lax.ppermute(block, axis, route)  75.2 us
    pallas_call x6, Pallas kernels, pair_lse(): pl.pallas_call(_lse_kernel, grid_spec=spec, out_shape=jax.ShapeDtypeStruc...  73.7 us
    ppermute x5, waiting for transfers between devices, gather_rows(): other = lax.ppermute(block, axis, route)  13.3 us
    ppermute x3, starting transfers between devices, spread(): lax.ppermute(block, axis, [(i, (i + reach) % count) for i in range(count)])  13.2 us
    ppermute x5, starting transfers between devices, gather_rows(): other = lax.ppermute(block, axis, route)  13 us
    ppermute x22, waiting for transfers between devices, passed_along(): return lax.ppermute(block, axis, route)  12.8 us
    pallas_call x1, Pallas kernels, pair_grad(): pl.pallas_call(_grad_kernel, grid_spec=spec, out_shape=jax.ShapeDtypeStru...  11.1 us
    ppermute x2, starting transfers between devices, padded(): lax.ppermute(lax.slice_in_dim(block, block.shape[dim] - width, None, axis...  7.19 us
  transfers between devices with their start and end apart: 37, of which 11 were waited for; matrix products, arithmetic and copies ran while one was open for 7% of the time, Pallas kernels for 4%

profile of v7, /device:TPU:1, one launch (start us, length us, event | category | flops | bytes accessed | tf_op | source)
XLA Modules:
  0.0 263.2 jit_solution(748019133344414966)
XLA Ops:
  0.6 4.1 %collective-permute-start = (bf16[1,1024,128]{2,1,0:T(8,128)(2,1)}, bf16[1,1024,128]{2,1,0:T(8,128)(2,1)S(1)}, u32[]{:S(2)}, u32[]{:S(2)}) collective-permute-start(bf16[1,1024,128]{2,1,0:T(8,128)(2,1)} %param.7), channel_id=1, source_target_pairs={{0,32},{32,64},{64,96},{1,33},{33,65},{65,97},{2,34},{34,66},{66,9... | collective-permute-start | bytes 786440 | tf_op jit(solution)/shard_map/ppermute | solution.py:19
  8.2 4.2 %gather_fusion.2 = bf16[6,1024,128]{2,1,0:T(8,128)(2,1)S(1)} fusion(bf16[32,1024,128]{2,1,0:T(8,128)(2,1)} %a_ref.7, s32[1024]{0:T(1024)S(1)} %get-tuple-element.52), kind=kCustom, calls=%fused_computation.2 | custom fusion | bytes 3145752 | tf_op jit(solution)/shard_map/gather | solution.py:231
  15.9 12.4 %shard_map.85 = f32[6,1,1024]{2,1,0:T(1,128)} custom-call(s32[6]{0:T(128)} %bitcast.100, s32[6]{0:T(128)} %get-tuple-element.49.b_ids.a_ids, bf16[32,1024,128]{2,1,0:T(8,128)(2,1)} %a_ref.7, bf16[3,1024,128]{2,1,0:T(8,128)(2,1)} %copy-done, f32[6,8,1024]{2,1,0:T(8,128)} %broadcast_in_dim.231.v_ref), custom_call_target="tpu_custom_call" | custom-call | tf_op jit(solution)/shard_map/pallas_call | solution.py:77
  29.3 4.6 %collective-permute-start.4 = (f32[5,1024]{1,0:T(8,128)S(1)}, f32[5,1024]{1,0:T(8,128)S(1)}, u32[]{:S(2)}, u32[]{:S(2)}) collective-permute-start(f32[5,1024]{1,0:T(8,128)S(1)} %log_add_fusion.5), channel_id=1, source_target_pairs={{0,1},{1,2},{2,3},{3,4},{4,5},{5,6},{6,7},{7,8},{8,9},{9,10},{10,1... | collective-permute-start | bytes 61448 | tf_op jit(solution)/shard_map/ppermute | solution.py:30
  35.9 3.3 %collective-permute-done.5 = f32[5,1024]{1,0:T(8,128)S(1)} collective-permute-done((f32[5,1024]{1,0:T(8,128)S(1)}, f32[5,1024]{1,0:T(8,128)S(1)}, u32[]{:S(2)}, u32[]{:S(2)}) %collective-permute-start.5) | collective-permute-done | bytes 20512 | tf_op jit(solution)/shard_map/ppermute | solution.py:30
  41.3 5.8 %collective-permute-start.6 = (f32[7,1024]{1,0:T(8,128)S(1)}, f32[7,1024]{1,0:T(8,128)S(1)}, u32[]{:S(2)}, u32[]{:S(2)}) collective-permute-start(f32[7,1024]{1,0:T(8,128)S(1)} %log_add_fusion.4), channel_id=1, source_target_pairs={{0,3},{1,4},{2,5},{3,6},{4,7},{5,8},{6,9},{7,10},{8,11},{9,12},{10... | collective-permute-start | bytes 86024 | tf_op jit(solution)/shard_map/ppermute | solution.py:30
  49.5 12.4 %shard_map.86 = f32[6,1,1024]{2,1,0:T(1,128)} custom-call(s32[6]{0:T(128)} %get-tuple-element.49.b_ids.a_ids, s32[6]{0:T(128)} %bitcast.101, bf16[3,1024,128]{2,1,0:T(8,128)(2,1)} %copy-done, bf16[32,1024,128]{2,1,0:T(8,128)(2,1)} %a_ref.7, f32[6,8,1024]{2,1,0:T(8,128)} %broadcast_in_dim.235.v_ref), custom_call_target="tpu_custom_call" | custom-call | tf_op jit(solution)/shard_map/pallas_call | solution.py:77
  62.9 3.7 %collective-permute-start.10 = (f32[3,1024]{1,0:T(4,128)S(1)}, f32[3,1024]{1,0:T(4,128)S(1)}, u32[]{:S(2)}, u32[]{:S(2)}) collective-permute-start(f32[3,1024]{1,0:T(4,128)S(1)} %log_add_fusion.8), channel_id=1, source_target_pairs={{0,32},{32,64},{64,96},{1,33},{33,65},{65,97},{2,34},{34,66},{66,9... | collective-permute-start | bytes 36872 | tf_op jit(solution)/shard_map/ppermute | solution.py:30
  66.6 3.1 %collective-permute-start.2 = (f32[1,1024]{1,0:T(1,128)S(1)}, f32[1,1024]{1,0:T(1,128)S(1)}, u32[]{:S(2)}, u32[]{:S(2)}) collective-permute-start(f32[1,1024]{1,0:T(1,128)S(1)} %copy-done.4), channel_id=1, source_target_pairs={{0,32},{32,64},{64,96},{1,33},{33,65},{65,97},{2,34},{34,66},{66,9... | collective-permute-start | bytes 12296 | tf_op jit(solution)/shard_map/ppermute | solution.py:19
  72.4 4.6 %collective-permute-start.11 = (f32[3,1024]{1,0:T(4,128)S(1)}, f32[3,1024]{1,0:T(4,128)S(1)}, u32[]{:S(2)}, u32[]{:S(2)}) collective-permute-start(f32[3,1024]{1,0:T(4,128)S(1)} %log_add_fusion.8), channel_id=1, source_target_pairs={{0,64},{32,96},{64,0},{96,32},{1,65},{33,97},{65,1},{97,33},{2,66}... | collective-permute-start | bytes 36872 | tf_op jit(solution)/shard_map/ppermute | solution.py:143
  79.5 12.2 %shard_map.87 = f32[6,1,1024]{2,1,0:T(1,128)} custom-call(s32[6]{0:T(128)} %bitcast.102, s32[6]{0:T(128)} %get-tuple-element.49.b_ids.a_ids, bf16[32,1024,128]{2,1,0:T(8,128)(2,1)} %a_ref.7, bf16[3,1024,128]{2,1,0:T(8,128)(2,1)} %copy-done, f32[6,8,1024]{2,1,0:T(8,128)} %broadcast_in_dim.239.v_ref), custom_call_target="tpu_custom_call" | custom-call | tf_op jit(solution)/shard_map/pallas_call | solution.py:77
  92.7 3.9 %collective-permute-start.12 = (f32[5,1024]{1,0:T(8,128)S(1)}, f32[5,1024]{1,0:T(8,128)S(1)}, u32[]{:S(2)}, u32[]{:S(2)}) collective-permute-start(f32[5,1024]{1,0:T(8,128)S(1)} %log_add_fusion.3), channel_id=1, source_target_pairs={{0,1},{1,2},{2,3},{3,4},{4,5},{5,6},{6,7},{7,8},{8,9},{9,10},{10,1... | collective-permute-start | bytes 61448 | tf_op jit(solution)/shard_map/ppermute | solution.py:30
  98.6 3.3 %collective-permute-done.13 = f32[5,1024]{1,0:T(8,128)S(1)} collective-permute-done((f32[5,1024]{1,0:T(8,128)S(1)}, f32[5,1024]{1,0:T(8,128)S(1)}, u32[]{:S(2)}, u32[]{:S(2)}) %collective-permute-start.13) | collective-permute-done | bytes 20512 | tf_op jit(solution)/shard_map/ppermute | solution.py:30
  104.0 6.3 %collective-permute-start.14 = (f32[7,1024]{1,0:T(8,128)S(1)}, f32[7,1024]{1,0:T(8,128)S(1)}, u32[]{:S(2)}, u32[]{:S(2)}) collective-permute-start(f32[7,1024]{1,0:T(8,128)S(1)} %log_add_fusion.2), channel_id=1, source_target_pairs={{0,3},{1,4},{2,5},{3,6},{4,7},{5,8},{6,9},{7,10},{8,11},{9,12},{10... | collective-permute-start | bytes 86024 | tf_op jit(solution)/shard_map/ppermute | solution.py:30
  112.7 12.2 %shard_map.88 = f32[6,1,1024]{2,1,0:T(1,128)} custom-call(s32[6]{0:T(128)} %get-tuple-element.49.b_ids.a_ids, s32[6]{0:T(128)} %bitcast.103, bf16[3,1024,128]{2,1,0:T(8,128)(2,1)} %copy-done, bf16[32,1024,128]{2,1,0:T(8,128)(2,1)} %a_ref.7, f32[6,8,1024]{2,1,0:T(8,128)} %broadcast_in_dim.241.v_ref), custom_call_target="tpu_custom_call" | custom-call | tf_op jit(solution)/shard_map/pallas_call | solution.py:77
  126.0 3.1 %collective-permute-start.18 = (f32[3,1024]{1,0:T(4,128)S(1)}, f32[3,1024]{1,0:T(4,128)S(1)}, u32[]{:S(2)}, u32[]{:S(2)}) collective-permute-start(f32[3,1024]{1,0:T(4,128)S(1)} %log_add_fusion.7), channel_id=1, source_target_pairs={{0,32},{32,64},{64,96},{1,33},{33,65},{65,97},{2,34},{34,66},{66,9... | collective-permute-start | bytes 36872 | tf_op jit(solution)/shard_map/ppermute | solution.py:30
  130.4 4.4 %collective-permute-start.19 = (f32[3,1024]{1,0:T(4,128)S(1)}, f32[3,1024]{1,0:T(4,128)S(1)}, u32[]{:S(2)}, u32[]{:S(2)}) collective-permute-start(f32[3,1024]{1,0:T(4,128)S(1)} %log_add_fusion.7), channel_id=1, source_target_pairs={{0,64},{32,96},{64,0},{96,32},{1,65},{33,97},{65,1},{97,33},{2,66}... | collective-permute-start | bytes 36872 | tf_op jit(solution)/shard_map/ppermute | solution.py:143
  137.3 12.2 %shard_map.89 = f32[6,1,1024]{2,1,0:T(1,128)} custom-call(s32[6]{0:T(128)} %bitcast.104, s32[6]{0:T(128)} %get-tuple-element.49.b_ids.a_ids, bf16[32,1024,128]{2,1,0:T(8,128)(2,1)} %a_ref.7, bf16[3,1024,128]{2,1,0:T(8,128)(2,1)} %copy-done, f32[6,8,1024]{2,1,0:T(8,128)} %broadcast_in_dim.243.v_ref), custom_call_target="tpu_custom_call" | custom-call | tf_op jit(solution)/shard_map/pallas_call | solution.py:77
  150.6 5.8 %collective-permute-start.20 = (f32[5,1024]{1,0:T(8,128)S(1)}, f32[5,1024]{1,0:T(8,128)S(1)}, u32[]{:S(2)}, u32[]{:S(2)}) collective-permute-start(f32[5,1024]{1,0:T(8,128)S(1)} %log_add_fusion.1), channel_id=1, source_target_pairs={{0,1},{1,2},{2,3},{3,4},{4,5},{5,6},{6,7},{7,8},{8,9},{9,10},{10,1... | collective-permute-start | bytes 61448 | tf_op jit(solution)/shard_map/ppermute | solution.py:30
  158.3 3.3 %collective-permute-done.21 = f32[5,1024]{1,0:T(8,128)S(1)} collective-permute-done((f32[5,1024]{1,0:T(8,128)S(1)}, f32[5,1024]{1,0:T(8,128)S(1)}, u32[]{:S(2)}, u32[]{:S(2)}) %collective-permute-start.21) | collective-permute-done | bytes 20512 | tf_op jit(solution)/shard_map/ppermute | solution.py:30
  163.7 8.6 %collective-permute-start.22 = (f32[7,1024]{1,0:T(8,128)S(1)}, f32[7,1024]{1,0:T(8,128)S(1)}, u32[]{:S(2)}, u32[]{:S(2)}) collective-permute-start(f32[7,1024]{1,0:T(8,128)S(1)} %log_add_fusion), channel_id=1, source_target_pairs={{0,3},{1,4},{2,5},{3,6},{4,7},{5,8},{6,9},{7,10},{8,11},{9,12},{10... | collective-permute-start | bytes 86024 | tf_op jit(solution)/shard_map/ppermute | solution.py:30
  174.7 12.2 %shard_map.90 = f32[6,1,1024]{2,1,0:T(1,128)} custom-call(s32[6]{0:T(128)} %get-tuple-element.49.b_ids.a_ids, s32[6]{0:T(128)} %bitcast.105, bf16[3,1024,128]{2,1,0:T(8,128)(2,1)} %copy-done, bf16[32,1024,128]{2,1,0:T(8,128)(2,1)} %a_ref.7, f32[6,8,1024]{2,1,0:T(8,128)} %broadcast_in_dim.245.v_ref), custom_call_target="tpu_custom_call" | custom-call | tf_op jit(solution)/shard_map/pallas_call | solution.py:77
  188.7 3.1 %collective-permute-start.31 = (f32[3,1024]{1,0:T(4,128)S(1)}, f32[3,1024]{1,0:T(4,128)S(1)}, u32[]{:S(2)}, u32[]{:S(2)}) collective-permute-start(f32[3,1024]{1,0:T(4,128)S(1)} %log_add_fusion.6), channel_id=1, source_target_pairs={{0,32},{32,64},{64,96},{1,33},{33,65},{65,97},{2,34},{34,66},{66,9... | collective-permute-start | bytes 36872 | tf_op jit(solution)/shard_map/ppermute | solution.py:30
  193.1 4.2 %collective-permute-start.32 = (f32[3,1024]{1,0:T(4,128)S(1)}, f32[3,1024]{1,0:T(4,128)S(1)}, u32[]{:S(2)}, u32[]{:S(2)}) collective-permute-start(f32[3,1024]{1,0:T(4,128)S(1)} %log_add_fusion.6), channel_id=1, source_target_pairs={{0,64},{32,96},{64,0},{96,32},{1,65},{33,97},{65,1},{97,33},{2,66}... | collective-permute-start | bytes 36872 | tf_op jit(solution)/shard_map/ppermute | solution.py:143
  199.5 2.4 collective-permute-start.26
  203.2 11.1 %shard_map.91 = f32[6,1024,128]{2,1,0:T(8,128)} custom-call(s32[6]{0:T(128)} %bitcast.106, s32[6]{0:T(128)} %get-tuple-element.49.b_ids.a_ids, bf16[32,1024,128]{2,1,0:T(8,128)(2,1)} %a_ref.7, bf16[3,1024,128]{2,1,0:T(8,128)(2,1)} %copy-done, f32[6,1,1024]{2,1,0:T(1,128)} %div.120.v_ref, f32[6,1024,1]{2,1,0:T(8,128)} %copy.11.w_ref), custom_call_target="tpu_custom_call" | custom-call | tf_op jit(solution)/shard_map/pallas_call | solution.py:112
  214.4 3.8 %select_reduce_fusion = f32[5,1024,128]{2,1,0:T(8,128)S(1)} fusion(f32[6,1024,128]{2,1,0:T(8,128)} %shard_map.91, pred[5,6]{1,0:T(8,128)(4,1)S(1)} %iota_compare_fusion.1), kind=kLoop, calls=%fused_computation.9 | loop fusion | flops 7208960 | bytes 5767198 | tf_op jit(solution)/shard_map/reduce_sum | solution.py:261
  219.5 3.5 %collective-permute-start.33 = (f32[1,1024,128]{2,1,0:T(8,128)}, f32[1,1024,128]{2,1,0:T(8,128)S(1)}, u32[]{:S(2)}, u32[]{:S(2)}) collective-permute-start(f32[1,1024,128]{2,1,0:T(8,128)} %get-tuple-element.5), channel_id=1, source_target_pairs={{1,0},{2,1},{3,2},{4,3},{5,4},{6,5},{7,6},{8,7},{9,8},{10,9},{11,1... | collective-permute-start | bytes 1572872 | tf_op jit(solution)/shard_map/ppermute | solution.py:30
  226.4 10.0 %collective-permute-start.36 = (f32[1,1024,128]{2,1,0:T(8,128)}, f32[1,1024,128]{2,1,0:T(8,128)}, u32[]{:S(2)}, u32[]{:S(2)}) collective-permute-start(f32[1,1024,128]{2,1,0:T(8,128)} %get-tuple-element.6), channel_id=1, source_target_pairs={{0,2},{1,3},{2,4},{3,5},{4,6},{5,7},{6,8},{7,9},{8,10},{9,11},{10,... | collective-permute-start | bytes 1572872 | tf_op jit(solution)/shard_map/ppermute | solution.py:30
  236.4 4.2 %collective-permute-start.27 = (f32[4,1024]{1,0:T(4,128)S(1)}, f32[4,1024]{1,0:T(4,128)S(1)}, u32[]{:S(2)}, u32[]{:S(2)}) collective-permute-start(f32[4,1024]{1,0:T(4,128)S(1)} %maximum_select_fusion.3), channel_id=1, source_target_pairs={{0,4},{1,5},{2,6},{3,7},{4,0},{5,1},{6,2},{7,3},{8,12},{9,13},{10,... | collective-permute-start | bytes 49160 | tf_op jit(solution)/shard_map/ppermute | solution.py:206
  240.6 10.9 %collective-permute-done.27 = f32[4,1024]{1,0:T(4,128)S(1)} collective-permute-done((f32[4,1024]{1,0:T(4,128)S(1)}, f32[4,1024]{1,0:T(4,128)S(1)}, u32[]{:S(2)}, u32[]{:S(2)}) %collective-permute-start.27) | collective-permute-done | bytes 16416 | tf_op jit(solution)/shard_map/ppermute | solution.py:206
  255.0 3.6 %collective-permute-start.29 = (f32[16,1024]{1,0:T(8,128)S(1)}, f32[16,1024]{1,0:T(8,128)S(1)}, u32[]{:S(2)}, u32[]{:S(2)}) collective-permute-start(f32[16,1024]{1,0:T(8,128)S(1)} %maximum_select_fusion.1), channel_id=1, source_target_pairs={{0,16},{1,17},{2,18},{3,19},{4,20},{5,21},{6,22},{7,23},{8,24},{9,... | collective-permute-start | bytes 196616 | tf_op jit(solution)/shard_map/ppermute | solution.py:206
  (181 shorter events, 59.1 us)
Async XLA Ops:
  0.6 13.3 %collective-permute-start = (bf16[1,1024,128]{2,1,0:T(8,128)(2,1)}, bf16[1,1024,128]{2,1,0:T(8,128)(2,1)S(1)}, u32[]{:S(2)}, u32[]{:S(2)}) collective-permute-start(bf16[1,1024,128]{2,1,0:T(8,128)(2,1)} %param.7), channel_id=1, source_target_pairs={{0,32},{32,64},{64,96},{1,33},{33,65},{65,97},{2,34},{34,66},{66,9... | collective-permute-start | bytes 786440 | tf_op jit(solution)/shard_map/ppermute | solution.py:19
  4.7 9.3 %collective-permute-start.1 = (bf16[1,1024,128]{2,1,0:T(8,128)(2,1)}, bf16[1,1024,128]{2,1,0:T(8,128)(2,1)S(1)}, u32[]{:S(2)}, u32[]{:S(2)}) collective-permute-start(bf16[1,1024,128]{2,1,0:T(8,128)(2,1)} %param.7), channel_id=1, source_target_pairs={{32,0},{64,32},{96,64},{33,1},{65,33},{97,65},{34,2},{66,34},{98,6... | collective-permute-start | bytes 786440 | tf_op jit(solution)/shard_map/ppermute | solution.py:22
  29.3 6.5 %collective-permute-start.4 = (f32[5,1024]{1,0:T(8,128)S(1)}, f32[5,1024]{1,0:T(8,128)S(1)}, u32[]{:S(2)}, u32[]{:S(2)}) collective-permute-start(f32[5,1024]{1,0:T(8,128)S(1)} %log_add_fusion.5), channel_id=1, source_target_pairs={{0,1},{1,2},{2,3},{3,4},{4,5},{5,6},{6,7},{7,8},{8,9},{9,10},{10,1... | collective-permute-start | bytes 61448 | tf_op jit(solution)/shard_map/ppermute | solution.py:30
  39.2 7.8 %collective-permute-start.7 = (f32[7,1024]{1,0:T(8,128)S(1)}, f32[7,1024]{1,0:T(8,128)S(1)}, u32[]{:S(2)}, u32[]{:S(2)}) collective-permute-start(f32[7,1024]{1,0:T(8,128)S(1)} %log_add_fusion.4), channel_id=1, source_target_pairs={{3,0},{4,1},{5,2},{6,3},{7,4},{8,5},{9,6},{10,7},{11,8},{12,9},{13... | collective-permute-start | bytes 86024 | tf_op jit(solution)/shard_map/ppermute | solution.py:30
  40.6 7.5 %collective-permute-start.8 = (f32[5,1024]{1,0:T(8,128)S(1)}, f32[5,1024]{1,0:T(8,128)S(1)}, u32[]{:S(2)}, u32[]{:S(2)}) collective-permute-start(f32[5,1024]{1,0:T(8,128)S(1)} %log_add_fusion.5), channel_id=1, source_target_pairs={{0,2},{31,29},{32,34},{63,61},{64,66},{95,93},{96,98},{127,125}} | collective-permute-start | bytes 61448 | tf_op jit(solution)/shard_map/ppermute | solution.py:177
  41.3 6.8 %collective-permute-start.6 = (f32[7,1024]{1,0:T(8,128)S(1)}, f32[7,1024]{1,0:T(8,128)S(1)}, u32[]{:S(2)}, u32[]{:S(2)}) collective-permute-start(f32[7,1024]{1,0:T(8,128)S(1)} %log_add_fusion.4), channel_id=1, source_target_pairs={{0,3},{1,4},{2,5},{3,6},{4,7},{5,8},{6,9},{7,10},{8,11},{9,12},{10... | collective-permute-start | bytes 86024 | tf_op jit(solution)/shard_map/ppermute | solution.py:30
  62.9 14.1 %collective-permute-start.10 = (f32[3,1024]{1,0:T(4,128)S(1)}, f32[3,1024]{1,0:T(4,128)S(1)}, u32[]{:S(2)}, u32[]{:S(2)}) collective-permute-start(f32[3,1024]{1,0:T(4,128)S(1)} %log_add_fusion.8), channel_id=1, source_target_pairs={{0,32},{32,64},{64,96},{1,33},{33,65},{65,97},{2,34},{34,66},{66,9... | collective-permute-start | bytes 36872 | tf_op jit(solution)/shard_map/ppermute | solution.py:30
  66.6 11.5 %collective-permute-start.2 = (f32[1,1024]{1,0:T(1,128)S(1)}, f32[1,1024]{1,0:T(1,128)S(1)}, u32[]{:S(2)}, u32[]{:S(2)}) collective-permute-start(f32[1,1024]{1,0:T(1,128)S(1)} %copy-done.4), channel_id=1, source_target_pairs={{0,32},{32,64},{64,96},{1,33},{33,65},{65,97},{2,34},{34,66},{66,9... | collective-permute-start | bytes 12296 | tf_op jit(solution)/shard_map/ppermute | solution.py:19
  69.7 8.4 %collective-permute-start.3 = (f32[1,1024]{1,0:T(1,128)S(1)}, f32[1,1024]{1,0:T(1,128)S(1)}, u32[]{:S(2)}, u32[]{:S(2)}) collective-permute-start(f32[1,1024]{1,0:T(1,128)S(1)} %copy-done.4), channel_id=1, source_target_pairs={{32,0},{64,32},{96,64},{33,1},{65,33},{97,65},{34,2},{66,34},{98,6... | collective-permute-start | bytes 12296 | tf_op jit(solution)/shard_map/ppermute | solution.py:22
  71.1 5.9 %collective-permute-start.9 = (f32[3,1024]{1,0:T(4,128)S(1)}, f32[3,1024]{1,0:T(4,128)S(1)}, u32[]{:S(2)}, u32[]{:S(2)}) collective-permute-start(f32[3,1024]{1,0:T(4,128)S(1)} %log_add_fusion.8), channel_id=1, source_target_pairs={{32,0},{64,32},{96,64},{33,1},{65,33},{97,65},{34,2},{66,34},{98,6... | collective-permute-start | bytes 36872 | tf_op jit(solution)/shard_map/ppermute | solution.py:30
  72.4 5.7 %collective-permute-start.11 = (f32[3,1024]{1,0:T(4,128)S(1)}, f32[3,1024]{1,0:T(4,128)S(1)}, u32[]{:S(2)}, u32[]{:S(2)}) collective-permute-start(f32[3,1024]{1,0:T(4,128)S(1)} %log_add_fusion.8), channel_id=1, source_target_pairs={{0,64},{32,96},{64,0},{96,32},{1,65},{33,97},{65,1},{97,33},{2,66}... | collective-permute-start | bytes 36872 | tf_op jit(solution)/shard_map/ppermute | solution.py:143
  92.7 5.9 %collective-permute-start.12 = (f32[5,1024]{1,0:T(8,128)S(1)}, f32[5,1024]{1,0:T(8,128)S(1)}, u32[]{:S(2)}, u32[]{:S(2)}) collective-permute-start(f32[5,1024]{1,0:T(8,128)S(1)} %log_add_fusion.3), channel_id=1, source_target_pairs={{0,1},{1,2},{2,3},{3,4},{4,5},{5,6},{6,7},{7,8},{8,9},{9,10},{10,1... | collective-permute-start | bytes 61448 | tf_op jit(solution)/shard_map/ppermute | solution.py:30
  102.0 8.3 %collective-permute-start.15 = (f32[7,1024]{1,0:T(8,128)S(1)}, f32[7,1024]{1,0:T(8,128)S(1)}, u32[]{:S(2)}, u32[]{:S(2)}) collective-permute-start(f32[7,1024]{1,0:T(8,128)S(1)} %log_add_fusion.2), channel_id=1, source_target_pairs={{3,0},{4,1},{5,2},{6,3},{7,4},{8,5},{9,6},{10,7},{11,8},{12,9},{13... | collective-permute-start | bytes 86024 | tf_op jit(solution)/shard_map/ppermute | solution.py:30
  103.3 8.0 %collective-permute-start.16 = (f32[5,1024]{1,0:T(8,128)S(1)}, f32[5,1024]{1,0:T(8,128)S(1)}, u32[]{:S(2)}, u32[]{:S(2)}) collective-permute-start(f32[5,1024]{1,0:T(8,128)S(1)} %log_add_fusion.3), channel_id=1, source_target_pairs={{0,2},{31,29},{32,34},{63,61},{64,66},{95,93},{96,98},{127,125}} | collective-permute-start | bytes 61448 | tf_op jit(solution)/shard_map/ppermute | solution.py:177
  104.0 7.3 %collective-permute-start.14 = (f32[7,1024]{1,0:T(8,128)S(1)}, f32[7,1024]{1,0:T(8,128)S(1)}, u32[]{:S(2)}, u32[]{:S(2)}) collective-permute-start(f32[7,1024]{1,0:T(8,128)S(1)} %log_add_fusion.2), channel_id=1, source_target_pairs={{0,3},{1,4},{2,5},{3,6},{4,7},{5,8},{6,9},{7,10},{8,11},{9,12},{10... | collective-permute-start | bytes 86024 | tf_op jit(solution)/shard_map/ppermute | solution.py:30
  126.0 8.8 %collective-permute-start.18 = (f32[3,1024]{1,0:T(4,128)S(1)}, f32[3,1024]{1,0:T(4,128)S(1)}, u32[]{:S(2)}, u32[]{:S(2)}) collective-permute-start(f32[3,1024]{1,0:T(4,128)S(1)} %log_add_fusion.7), channel_id=1, source_target_pairs={{0,32},{32,64},{64,96},{1,33},{33,65},{65,97},{2,34},{34,66},{66,9... | collective-permute-start | bytes 36872 | tf_op jit(solution)/shard_map/ppermute | solution.py:30
  129.1 5.7 %collective-permute-start.17 = (f32[3,1024]{1,0:T(4,128)S(1)}, f32[3,1024]{1,0:T(4,128)S(1)}, u32[]{:S(2)}, u32[]{:S(2)}) collective-permute-start(f32[3,1024]{1,0:T(4,128)S(1)} %log_add_fusion.7), channel_id=1, source_target_pairs={{32,0},{64,32},{96,64},{33,1},{65,33},{97,65},{34,2},{66,34},{98,6... | collective-permute-start | bytes 36872 | tf_op jit(solution)/shard_map/ppermute | solution.py:30
  130.4 5.5 %collective-permute-start.19 = (f32[3,1024]{1,0:T(4,128)S(1)}, f32[3,1024]{1,0:T(4,128)S(1)}, u32[]{:S(2)}, u32[]{:S(2)}) collective-permute-start(f32[3,1024]{1,0:T(4,128)S(1)} %log_add_fusion.7), channel_id=1, source_target_pairs={{0,64},{32,96},{64,0},{96,32},{1,65},{33,97},{65,1},{97,33},{2,66}... | collective-permute-start | bytes 36872 | tf_op jit(solution)/shard_map/ppermute | solution.py:143
  150.6 7.7 %collective-permute-start.20 = (f32[5,1024]{1,0:T(8,128)S(1)}, f32[5,1024]{1,0:T(8,128)S(1)}, u32[]{:S(2)}, u32[]{:S(2)}) collective-permute-start(f32[5,1024]{1,0:T(8,128)S(1)} %log_add_fusion.1), channel_id=1, source_target_pairs={{0,1},{1,2},{2,3},{3,4},{4,5},{5,6},{6,7},{7,8},{8,9},{9,10},{10,1... | collective-permute-start | bytes 61448 | tf_op jit(solution)/shard_map/ppermute | solution.py:30
  161.7 10.6 %collective-permute-start.23 = (f32[7,1024]{1,0:T(8,128)S(1)}, f32[7,1024]{1,0:T(8,128)S(1)}, u32[]{:S(2)}, u32[]{:S(2)}) collective-permute-start(f32[7,1024]{1,0:T(8,128)S(1)} %log_add_fusion), channel_id=1, source_target_pairs={{3,0},{4,1},{5,2},{6,3},{7,4},{8,5},{9,6},{10,7},{11,8},{12,9},{13... | collective-permute-start | bytes 86024 | tf_op jit(solution)/shard_map/ppermute | solution.py:30
  163.0 10.3 %collective-permute-start.24 = (f32[5,1024]{1,0:T(8,128)S(1)}, f32[5,1024]{1,0:T(8,128)S(1)}, u32[]{:S(2)}, u32[]{:S(2)}) collective-permute-start(f32[5,1024]{1,0:T(8,128)S(1)} %log_add_fusion.1), channel_id=1, source_target_pairs={{0,2},{31,29},{32,34},{63,61},{64,66},{95,93},{96,98},{127,125}} | collective-permute-start | bytes 61448 | tf_op jit(solution)/shard_map/ppermute | solution.py:177
  163.7 9.6 %collective-permute-start.22 = (f32[7,1024]{1,0:T(8,128)S(1)}, f32[7,1024]{1,0:T(8,128)S(1)}, u32[]{:S(2)}, u32[]{:S(2)}) collective-permute-start(f32[7,1024]{1,0:T(8,128)S(1)} %log_add_fusion), channel_id=1, source_target_pairs={{0,3},{1,4},{2,5},{3,6},{4,7},{5,8},{6,9},{7,10},{8,11},{9,12},{10... | collective-permute-start | bytes 86024 | tf_op jit(solution)/shard_map/ppermute | solution.py:30
  187.9 11.6 %collective-permute-start.25 = (f32[1,1024]{1,0:T(1,128)S(1)}, f32[1,1024]{1,0:T(1,128)S(1)}, u32[]{:S(2)}, u32[]{:S(2)}) collective-permute-start(f32[1,1024]{1,0:T(1,128)S(1)} %slice.207), channel_id=1, source_target_pairs={{0,1},{1,0},{2,3},{3,2},{4,5},{5,4},{6,7},{7,6},{8,9},{9,8},{10,11... | collective-permute-start | bytes 12296 | tf_op jit(solution)/shard_map/ppermute | solution.py:206
  188.7 13.2 %collective-permute-start.31 = (f32[3,1024]{1,0:T(4,128)S(1)}, f32[3,1024]{1,0:T(4,128)S(1)}, u32[]{:S(2)}, u32[]{:S(2)}) collective-permute-start(f32[3,1024]{1,0:T(4,128)S(1)} %log_add_fusion.6), channel_id=1, source_target_pairs={{0,32},{32,64},{64,96},{1,33},{33,65},{65,97},{2,34},{34,66},{66,9... | collective-permute-start | bytes 36872 | tf_op jit(solution)/shard_map/ppermute | solution.py:30
  191.8 10.1 %collective-permute-start.30 = (f32[3,1024]{1,0:T(4,128)S(1)}, f32[3,1024]{1,0:T(4,128)S(1)}, u32[]{:S(2)}, u32[]{:S(2)}) collective-permute-start(f32[3,1024]{1,0:T(4,128)S(1)} %log_add_fusion.6), channel_id=1, source_target_pairs={{32,0},{64,32},{96,64},{33,1},{65,33},{97,65},{34,2},{66,34},{98,6... | collective-permute-start | bytes 36872 | tf_op jit(solution)/shard_map/ppermute | solution.py:30
  193.1 8.8 %collective-permute-start.32 = (f32[3,1024]{1,0:T(4,128)S(1)}, f32[3,1024]{1,0:T(4,128)S(1)}, u32[]{:S(2)}, u32[]{:S(2)}) collective-permute-start(f32[3,1024]{1,0:T(4,128)S(1)} %log_add_fusion.6), channel_id=1, source_target_pairs={{0,64},{32,96},{64,0},{96,32},{1,65},{33,97},{65,1},{97,33},{2,66}... | collective-permute-start | bytes 36872 | tf_op jit(solution)/shard_map/ppermute | solution.py:143
  199.5 36.9 %collective-permute-start.26 = (f32[2,1024]{1,0:T(2,128)S(1)}, f32[2,1024]{1,0:T(2,128)S(1)}, u32[]{:S(2)}, u32[]{:S(2)}) collective-permute-start(f32[2,1024]{1,0:T(2,128)S(1)} %maximum_select_fusion.4), channel_id=1, source_target_pairs={{0,2},{1,3},{2,0},{3,1},{4,6},{5,7},{6,4},{7,5},{8,10},{9,11},{10,... | collective-permute-start | bytes 24584 | tf_op jit(solution)/shard_map/ppermute | solution.py:206
  219.5 41.4 %collective-permute-start.33 = (f32[1,1024,128]{2,1,0:T(8,128)}, f32[1,1024,128]{2,1,0:T(8,128)S(1)}, u32[]{:S(2)}, u32[]{:S(2)}) collective-permute-start(f32[1,1024,128]{2,1,0:T(8,128)} %get-tuple-element.5), channel_id=1, source_target_pairs={{1,0},{2,1},{3,2},{4,3},{5,4},{6,5},{7,6},{8,7},{9,8},{10,9},{11,1... | collective-permute-start | bytes 1572872 | tf_op jit(solution)/shard_map/ppermute | solution.py:30
  223.0 37.9 %collective-permute-start.34 = (f32[1,1024,128]{2,1,0:T(8,128)}, f32[1,1024,128]{2,1,0:T(8,128)}, u32[]{:S(2)}, u32[]{:S(2)}) collective-permute-start(f32[1,1024,128]{2,1,0:T(8,128)} %get-tuple-element.8), channel_id=1, source_target_pairs={{0,1},{1,2},{2,3},{3,4},{4,5},{5,6},{6,7},{7,8},{8,9},{9,10},{10,1... | collective-permute-start | bytes 1572872 | tf_op jit(solution)/shard_map/ppermute | solution.py:30
  225.1 35.8 %collective-permute-start.35 = (f32[1,1024,128]{2,1,0:T(8,128)}, f32[1,1024,128]{2,1,0:T(8,128)}, u32[]{:S(2)}, u32[]{:S(2)}) collective-permute-start(f32[1,1024,128]{2,1,0:T(8,128)} %get-tuple-element.7), channel_id=1, source_target_pairs={{2,0},{3,1},{4,2},{5,3},{6,4},{7,5},{8,6},{9,7},{10,8},{11,9},{12,... | collective-permute-start | bytes 1572872 | tf_op jit(solution)/shard_map/ppermute | solution.py:30
  226.4 34.6 %collective-permute-start.36 = (f32[1,1024,128]{2,1,0:T(8,128)}, f32[1,1024,128]{2,1,0:T(8,128)}, u32[]{:S(2)}, u32[]{:S(2)}) collective-permute-start(f32[1,1024,128]{2,1,0:T(8,128)} %get-tuple-element.6), channel_id=1, source_target_pairs={{0,2},{1,3},{2,4},{3,5},{4,6},{5,7},{6,8},{7,9},{8,10},{9,11},{10,... | collective-permute-start | bytes 1572872 | tf_op jit(solution)/shard_map/ppermute | solution.py:30
  236.4 15.1 %collective-permute-start.27 = (f32[4,1024]{1,0:T(4,128)S(1)}, f32[4,1024]{1,0:T(4,128)S(1)}, u32[]{:S(2)}, u32[]{:S(2)}) collective-permute-start(f32[4,1024]{1,0:T(4,128)S(1)} %maximum_select_fusion.3), channel_id=1, source_target_pairs={{0,4},{1,5},{2,6},{3,7},{4,0},{5,1},{6,2},{7,3},{8,12},{9,13},{10,... | collective-permute-start | bytes 49160 | tf_op jit(solution)/shard_map/ppermute | solution.py:206
  (11 other events, 120.9 us)

commit v8 on v7

--- a/solution.py
+++ b/solution.py
@@ -30,6 +30,10 @@
     return lax.ppermute(block, axis, route)
 
 
+def pick(table, position):
+    return lax.dynamic_index_in_dim(table, position, 0, keepdims=False)
+
+
 def squares(points):
     return jnp.sum(jnp.square(points.astype(jnp.float32)), axis=-1)
 
@@ -37,10 +41,6 @@
 def fetch_points(tgt_points):
     window_pts = padded(tgt_points, (("gx", 0),), tgt_points.shape[0])
     return (window_pts, squares(window_pts))
-
-
-def fetch_potential(g_local):
-    return padded(g_local, (("gx", 0),), g_local.shape[0])
 
 
 EPSILON = 0.03
@@ -124,19 +124,23 @@
     return peak_val + jnp.log(jnp.sum(jnp.exp(masked - peak_val[:, None]), axis=1))
 
 
-def spread(block, axis, reach):
+def spread(block, axis, reach, extra):
     width = block.shape[0]
-    index = lax.axis_index(axis)
-    count = lax.axis_size(axis)
+    owned = extra.shape[0]
+    index = lax.axis_index(axis)
+    count = lax.axis_size(axis)
+    sent = jnp.concatenate([block, extra], axis=0)
     parts = [block]
     pad = jnp.full((reach,) + block.shape[1:], EMPTY_LOG, block.dtype)
     far = [reach, -reach] if count == 2 * reach else []
+    extras = {}
     for distance in range(-reach, reach + 1):
         if distance == 0 or distance in far:
             continue
-        got = passed_along(block, axis, distance)
+        got_all = passed_along(sent, axis, distance)
         valid = (index - distance >= 0) & (index - distance < count)
-        got = jnp.where(valid, got, EMPTY_LOG)
+        got = jnp.where(valid, got_all[:width], EMPTY_LOG)
+        extras[distance] = jnp.where(valid, got_all[width:], 0.0)
         got = jnp.concatenate([pad, got, pad], axis=0)
         parts.append(lax.slice_in_dim(got, reach + distance, reach + distance + width, axis=0))
     if far:
@@ -147,7 +151,8 @@
         parts.append(jnp.where(index >= reach, upper, lower))
     parts = jnp.stack(parts)
     peak_val = jnp.max(parts, axis=0)
-    return peak_val + jnp.log(jnp.sum(jnp.exp(parts - peak_val[None]), axis=0))
+    total = peak_val + jnp.log(jnp.sum(jnp.exp(parts - peak_val[None]), axis=0))
+    return total, jnp.concatenate([extras[owned], extra, extras[-owned]], axis=0)
 
 
 def shifted(block, shift, width):
@@ -228,10 +233,9 @@
     span_ids = jnp.clip(source_local - (gy_index - 2) * owned, 0, 5 * owned - 1)
     span_mask = span_ids[None, :] == jnp.arange(5 * owned, dtype=jnp.int32)[:, None]
     window_mask = window_ids[None, :] == jnp.arange(3 * owned, dtype=jnp.int32)[:, None]
-    pair_src_sq = squares(src_points[source_local])
+    pair_src_sq = jnp.stack([squares(pick(src_points, source_local[p])) for p in range(source_local.shape[0])])
     window_pts, window_sq = fetch_points(tgt_points)
     pair_tgt_sq = window_sq[window_ids]
-    window_mass = fetch_potential(tgt_log_mass)
     mass_pad = jnp.zeros((2 * owned,) + src_log_mass.shape[1:], src_log_mass.dtype)
     span_mass = lax.dynamic_slice_in_dim(
         jnp.concatenate([mass_pad, src_log_mass, mass_pad], axis=0), gy_index * owned, 5 * owned, 0
@@ -249,7 +253,9 @@
             jnp.broadcast_to(v_col[:, None, :], (v_col.shape[0], 8, v_col.shape[1])),
         )
         part = part[:, 0] - 0.5 * pair_tgt_sq / EPSILON
-        cols_total = spread(grouped_lse(window_mask, part), "gx", 2 * owned)
+        cols_total, window_mass = spread(
+            grouped_lse(window_mask, part), "gx", 2 * owned, tgt_log_mass
+        )
         g_window = EPSILON * window_mass - EPSILON * cols_total
     f_pot = gather_rows(f_span[2 * owned : 3 * owned], "gy")
     g_local = g_window[owned : 2 * owned]

time: 266 us -> 271 us (1.019)
  between operations: 1.65 us -> 13.1 us
  starting transfers between devices: 113 us -> 108 us
  local copies, waits for them, and re-layouts: 17.8 us -> 14.1 us
  other arithmetic: 17.4 us -> 20.9 us
    gather x1 -> x0, local copies, waits for them, and re-layouts: 4.23 us -> none  [body(): pair_src_sq = squares(src_points[source_local])]
    ppermute x2 -> x1, starting transfers between devices: 7.19 us -> 3.95 us  [padded(): lax.ppermute(lax.slice_in_dim(block, block.shape[dim] - width, None, axis...]
  transfers between devices with their start and end apart: 37 -> 35, of which waited for: 11 -> 11; matrix products, arithmetic and copies ran while one was open for 7% -> 7% of each run, Pallas kernels for 4% -> 4%
where the time goes in v8:
time: 271 us; the launch traced here: 269 us
  starting transfers between devices  108 us (40%)
  Pallas kernels  84.8 us (31%)
  waiting for transfers between devices  27.5 us (10%)
  other arithmetic  20.9 us (8%)
  local copies, waits for them, and re-layouts  14.1 us (5%)
  between operations  13.1 us (5%)
    ppermute x22, starting transfers between devices, passed_along(): return lax.ppermute(block, axis, route)  74.8 us
    pallas_call x6, Pallas kernels, pair_lse(): pl.pallas_call(_lse_kernel, grid_spec=spec, out_shape=jax.ShapeDtypeStruc...  73.7 us
    ppermute x5, starting transfers between devices, gather_rows(): other = lax.ppermute(block, axis, route)  15 us
    ppermute x22, waiting for transfers between devices, passed_along(): return lax.ppermute(block, axis, route)  12.8 us
    ppermute x5, waiting for transfers between devices, gather_rows(): other = lax.ppermute(block, axis, route)  12.5 us
    ppermute x3, starting transfers between devices, spread(): lax.ppermute(block, axis, [(i, (i + reach) % count) for i in range(count)])  11.3 us
    pallas_call x1, Pallas kernels, pair_grad(): pl.pallas_call(_grad_kernel, grid_spec=spec, out_shape=jax.ShapeDtypeStru...  11.1 us
  transfers between devices with their start and end apart: 35, of which 11 were waited for; matrix products, arithmetic and copies ran while one was open for 7% of the time, Pallas kernels for 4%

profile of v8, /device:TPU:1, one launch (start us, length us, event | category | flops | bytes accessed | tf_op | source)
XLA Modules:
  0.0 268.8 jit_solution(14375927854836276120)
XLA Ops:
  0.6 4.0 %collective-permute-start = (bf16[1,1024,128]{2,1,0:T(8,128)(2,1)}, bf16[1,1024,128]{2,1,0:T(8,128)(2,1)S(1)}, u32[]{:S(2)}, u32[]{:S(2)}) collective-permute-start(bf16[1,1024,128]{2,1,0:T(8,128)(2,1)} %param.7), channel_id=1, source_target_pairs={{0,32},{32,64},{64,96},{1,33},{33,65},{65,97},{2,34},{34,66},{66,9... | collective-permute-start | bytes 786440 | tf_op jit(solution)/shard_map/ppermute | solution.py:19
  26.0 12.4 %shard_map.85 = f32[6,1,1024]{2,1,0:T(1,128)} custom-call(s32[6]{0:T(128)} %bitcast.116, s32[6]{0:T(128)} %get-tuple-element.61.b_ids.a_ids, bf16[32,1024,128]{2,1,0:T(8,128)(2,1)} %a_ref.7, bf16[3,1024,128]{2,1,0:T(8,128)(2,1)} %copy-done, f32[6,8,1024]{2,1,0:T(8,128)} %broadcast_in_dim.239.v_ref), custom_call_target="tpu_custom_call" | custom-call | tf_op jit(solution)/shard_map/pallas_call | solution.py:77
  39.4 4.1 %collective-permute-start.2 = (f32[5,1024]{1,0:T(8,128)S(1)}, f32[5,1024]{1,0:T(8,128)S(1)}, u32[]{:S(2)}, u32[]{:S(2)}) collective-permute-start(f32[5,1024]{1,0:T(8,128)S(1)} %log_add_fusion.5), channel_id=1, source_target_pairs={{0,1},{1,2},{2,3},{3,4},{4,5},{5,6},{6,7},{7,8},{8,9},{9,10},{10,1... | collective-permute-start | bytes 61448 | tf_op jit(solution)/shard_map/ppermute | solution.py:30
  45.5 3.3 %collective-permute-done.3 = f32[5,1024]{1,0:T(8,128)S(1)} collective-permute-done((f32[5,1024]{1,0:T(8,128)S(1)}, f32[5,1024]{1,0:T(8,128)S(1)}, u32[]{:S(2)}, u32[]{:S(2)}) %collective-permute-start.3) | collective-permute-done | bytes 20512 | tf_op jit(solution)/shard_map/ppermute | solution.py:30
  50.8 5.8 %collective-permute-start.4 = (f32[7,1024]{1,0:T(8,128)S(1)}, f32[7,1024]{1,0:T(8,128)S(1)}, u32[]{:S(2)}, u32[]{:S(2)}) collective-permute-start(f32[7,1024]{1,0:T(8,128)S(1)} %log_add_fusion.4), channel_id=1, source_target_pairs={{0,3},{1,4},{2,5},{3,6},{4,7},{5,8},{6,9},{7,10},{8,11},{9,12},{10... | collective-permute-start | bytes 86024 | tf_op jit(solution)/shard_map/ppermute | solution.py:30
  59.1 12.4 %shard_map.86 = f32[6,1,1024]{2,1,0:T(1,128)} custom-call(s32[6]{0:T(128)} %get-tuple-element.61.b_ids.a_ids, s32[6]{0:T(128)} %bitcast.117, bf16[3,1024,128]{2,1,0:T(8,128)(2,1)} %copy-done, bf16[32,1024,128]{2,1,0:T(8,128)(2,1)} %a_ref.7, f32[6,8,1024]{2,1,0:T(8,128)} %broadcast_in_dim.243.v_ref), custom_call_target="tpu_custom_call" | custom-call | tf_op jit(solution)/shard_map/pallas_call | solution.py:77
  72.5 4.2 %collective-permute-start.7 = (f32[4,1024]{1,0:T(4,128)S(1)}, f32[4,1024]{1,0:T(4,128)S(1)}, u32[]{:S(2)}, u32[]{:S(2)}) collective-permute-start(f32[4,1024]{1,0:T(4,128)S(1)} %pad_maximum_fusion.8), channel_id=1, source_target_pairs={{0,32},{32,64},{64,96},{1,33},{33,65},{65,97},{2,34},{34,66},{66,9... | collective-permute-start | bytes 49160 | tf_op jit(solution)/shard_map/ppermute | solution.py:30
  78.0 3.7 %collective-permute-start.9 = (f32[3,1024]{1,0:T(4,128)S(1)}, f32[3,1024]{1,0:T(4,128)S(1)}, u32[]{:S(2)}, u32[]{:S(2)}) collective-permute-start(f32[3,1024]{1,0:T(4,128)S(1)} %log_add_fusion.8), channel_id=1, source_target_pairs={{0,64},{32,96},{64,0},{96,32},{1,65},{33,97},{65,1},{97,33},{2,66}... | collective-permute-start | bytes 36872 | tf_op jit(solution)/shard_map/ppermute | solution.py:147
  84.3 12.2 %shard_map.87 = f32[6,1,1024]{2,1,0:T(1,128)} custom-call(s32[6]{0:T(128)} %bitcast.118, s32[6]{0:T(128)} %get-tuple-element.61.b_ids.a_ids, bf16[32,1024,128]{2,1,0:T(8,128)(2,1)} %a_ref.7, bf16[3,1024,128]{2,1,0:T(8,128)(2,1)} %copy-done, f32[6,8,1024]{2,1,0:T(8,128)} %broadcast_in_dim.248.v_ref), custom_call_target="tpu_custom_call" | custom-call | tf_op jit(solution)/shard_map/pallas_call | solution.py:77
  97.6 3.2 %collective-permute-start.10 = (f32[5,1024]{1,0:T(8,128)S(1)}, f32[5,1024]{1,0:T(8,128)S(1)}, u32[]{:S(2)}, u32[]{:S(2)}) collective-permute-start(f32[5,1024]{1,0:T(8,128)S(1)} %log_add_fusion.3), channel_id=1, source_target_pairs={{0,1},{1,2},{2,3},{3,4},{4,5},{5,6},{6,7},{7,8},{8,9},{9,10},{10,1... | collective-permute-start | bytes 61448 | tf_op jit(solution)/shard_map/ppermute | solution.py:30
  102.8 3.3 %collective-permute-done.11 = f32[5,1024]{1,0:T(8,128)S(1)} collective-permute-done((f32[5,1024]{1,0:T(8,128)S(1)}, f32[5,1024]{1,0:T(8,128)S(1)}, u32[]{:S(2)}, u32[]{:S(2)}) %collective-permute-start.11) | collective-permute-done | bytes 20512 | tf_op jit(solution)/shard_map/ppermute | solution.py:30
  108.2 6.4 %collective-permute-start.12 = (f32[7,1024]{1,0:T(8,128)S(1)}, f32[7,1024]{1,0:T(8,128)S(1)}, u32[]{:S(2)}, u32[]{:S(2)}) collective-permute-start(f32[7,1024]{1,0:T(8,128)S(1)} %log_add_fusion.2), channel_id=1, source_target_pairs={{0,3},{1,4},{2,5},{3,6},{4,7},{5,8},{6,9},{7,10},{8,11},{9,12},{10... | collective-permute-start | bytes 86024 | tf_op jit(solution)/shard_map/ppermute | solution.py:30
  117.0 12.2 %shard_map.88 = f32[6,1,1024]{2,1,0:T(1,128)} custom-call(s32[6]{0:T(128)} %get-tuple-element.61.b_ids.a_ids, s32[6]{0:T(128)} %bitcast.119, bf16[3,1024,128]{2,1,0:T(8,128)(2,1)} %copy-done, bf16[32,1024,128]{2,1,0:T(8,128)(2,1)} %a_ref.7, f32[6,8,1024]{2,1,0:T(8,128)} %broadcast_in_dim.250.v_ref), custom_call_target="tpu_custom_call" | custom-call | tf_op jit(solution)/shard_map/pallas_call | solution.py:77
  130.3 3.6 %collective-permute-start.15 = (f32[4,1024]{1,0:T(4,128)S(1)}, f32[4,1024]{1,0:T(4,128)S(1)}, u32[]{:S(2)}, u32[]{:S(2)}) collective-permute-start(f32[4,1024]{1,0:T(4,128)S(1)} %pad_maximum_fusion.7), channel_id=1, source_target_pairs={{0,32},{32,64},{64,96},{1,33},{33,65},{65,97},{2,34},{34,66},{66,9... | collective-permute-start | bytes 49160 | tf_op jit(solution)/shard_map/ppermute | solution.py:30
  135.2 3.9 %collective-permute-start.17 = (f32[3,1024]{1,0:T(4,128)S(1)}, f32[3,1024]{1,0:T(4,128)S(1)}, u32[]{:S(2)}, u32[]{:S(2)}) collective-permute-start(f32[3,1024]{1,0:T(4,128)S(1)} %log_add_fusion.7), channel_id=1, source_target_pairs={{0,64},{32,96},{64,0},{96,32},{1,65},{33,97},{65,1},{97,33},{2,66}... | collective-permute-start | bytes 36872 | tf_op jit(solution)/shard_map/ppermute | solution.py:147
  141.7 12.2 %shard_map.89 = f32[6,1,1024]{2,1,0:T(1,128)} custom-call(s32[6]{0:T(128)} %bitcast.120, s32[6]{0:T(128)} %get-tuple-element.61.b_ids.a_ids, bf16[32,1024,128]{2,1,0:T(8,128)(2,1)} %a_ref.7, bf16[3,1024,128]{2,1,0:T(8,128)(2,1)} %copy-done, f32[6,8,1024]{2,1,0:T(8,128)} %broadcast_in_dim.252.v_ref), custom_call_target="tpu_custom_call" | custom-call | tf_op jit(solution)/shard_map/pallas_call | solution.py:77
  154.9 5.9 %collective-permute-start.18 = (f32[5,1024]{1,0:T(8,128)S(1)}, f32[5,1024]{1,0:T(8,128)S(1)}, u32[]{:S(2)}, u32[]{:S(2)}) collective-permute-start(f32[5,1024]{1,0:T(8,128)S(1)} %log_add_fusion.1), channel_id=1, source_target_pairs={{0,1},{1,2},{2,3},{3,4},{4,5},{5,6},{6,7},{7,8},{8,9},{9,10},{10,1... | collective-permute-start | bytes 61448 | tf_op jit(solution)/shard_map/ppermute | solution.py:30
  162.8 3.3 %collective-permute-done.19 = f32[5,1024]{1,0:T(8,128)S(1)} collective-permute-done((f32[5,1024]{1,0:T(8,128)S(1)}, f32[5,1024]{1,0:T(8,128)S(1)}, u32[]{:S(2)}, u32[]{:S(2)}) %collective-permute-start.19) | collective-permute-done | bytes 20512 | tf_op jit(solution)/shard_map/ppermute | solution.py:30
  168.2 8.5 %collective-permute-start.20 = (f32[7,1024]{1,0:T(8,128)S(1)}, f32[7,1024]{1,0:T(8,128)S(1)}, u32[]{:S(2)}, u32[]{:S(2)}) collective-permute-start(f32[7,1024]{1,0:T(8,128)S(1)} %log_add_fusion), channel_id=1, source_target_pairs={{0,3},{1,4},{2,5},{3,6},{4,7},{5,8},{6,9},{7,10},{8,11},{9,12},{10... | collective-permute-start | bytes 86024 | tf_op jit(solution)/shard_map/ppermute | solution.py:30
  179.1 12.2 %shard_map.90 = f32[6,1,1024]{2,1,0:T(1,128)} custom-call(s32[6]{0:T(128)} %get-tuple-element.61.b_ids.a_ids, s32[6]{0:T(128)} %bitcast.121, bf16[3,1024,128]{2,1,0:T(8,128)(2,1)} %copy-done, bf16[32,1024,128]{2,1,0:T(8,128)(2,1)} %a_ref.7, f32[6,8,1024]{2,1,0:T(8,128)} %broadcast_in_dim.254.v_ref), custom_call_target="tpu_custom_call" | custom-call | tf_op jit(solution)/shard_map/pallas_call | solution.py:77
  192.3 3.6 %collective-permute-start.28 = (f32[4,1024]{1,0:T(4,128)S(1)}, f32[4,1024]{1,0:T(4,128)S(1)}, u32[]{:S(2)}, u32[]{:S(2)}) collective-permute-start(f32[4,1024]{1,0:T(4,128)S(1)} %pad_maximum_fusion.6), channel_id=1, source_target_pairs={{0,32},{32,64},{64,96},{1,33},{33,65},{65,97},{2,34},{34,66},{66,9... | collective-permute-start | bytes 49160 | tf_op jit(solution)/shard_map/ppermute | solution.py:30
  197.3 3.7 %collective-permute-start.30 = (f32[3,1024]{1,0:T(4,128)S(1)}, f32[3,1024]{1,0:T(4,128)S(1)}, u32[]{:S(2)}, u32[]{:S(2)}) collective-permute-start(f32[3,1024]{1,0:T(4,128)S(1)} %log_add_fusion.6), channel_id=1, source_target_pairs={{0,64},{32,96},{64,0},{96,32},{1,65},{33,97},{65,1},{97,33},{2,66}... | collective-permute-start | bytes 36872 | tf_op jit(solution)/shard_map/ppermute | solution.py:147
  208.5 11.1 %shard_map.91 = f32[6,1024,128]{2,1,0:T(8,128)} custom-call(s32[6]{0:T(128)} %bitcast.122, s32[6]{0:T(128)} %get-tuple-element.61.b_ids.a_ids, bf16[32,1024,128]{2,1,0:T(8,128)(2,1)} %a_ref.7, bf16[3,1024,128]{2,1,0:T(8,128)(2,1)} %copy-done, f32[6,1,1024]{2,1,0:T(1,128)} %div.120.v_ref, f32[6,1024,1]{2,1,0:T(8,128)} %broadcast_multiply_fusion.w_ref), custom_call_target="tpu_custom_call" | custom-call | tf_op jit(solution)/shard_map/pallas_call | solution.py:112
  219.7 3.8 %select_reduce_fusion = f32[5,1024,128]{2,1,0:T(8,128)S(1)} fusion(f32[6,1024,128]{2,1,0:T(8,128)} %shard_map.91, pred[5,6]{1,0:T(8,128)(4,1)S(1)} %iota_compare_fusion.1), kind=kLoop, calls=%fused_computation.8 | loop fusion | flops 7208960 | bytes 5767198 | tf_op jit(solution)/shard_map/reduce_sum | solution.py:267
  224.8 2.7 collective-permute-start.31
  227.5 2.9 %collective-permute-start.32 = (f32[1,1024,128]{2,1,0:T(8,128)}, f32[1,1024,128]{2,1,0:T(8,128)}, u32[]{:S(2)}, u32[]{:S(2)}) collective-permute-start(f32[1,1024,128]{2,1,0:T(8,128)} %get-tuple-element.14), channel_id=1, source_target_pairs={{0,1},{1,2},{2,3},{3,4},{4,5},{5,6},{6,7},{7,8},{8,9},{9,10},{10,1... | collective-permute-start | bytes 1572872 | tf_op jit(solution)/shard_map/ppermute | solution.py:30
  231.7 9.2 %collective-permute-start.34 = (f32[1,1024,128]{2,1,0:T(8,128)}, f32[1,1024,128]{2,1,0:T(8,128)}, u32[]{:S(2)}, u32[]{:S(2)}) collective-permute-start(f32[1,1024,128]{2,1,0:T(8,128)} %get-tuple-element.12), channel_id=1, source_target_pairs={{0,2},{1,3},{2,4},{3,5},{4,6},{5,7},{6,8},{7,9},{8,10},{9,11},{10,... | collective-permute-start | bytes 1572872 | tf_op jit(solution)/shard_map/ppermute | solution.py:30
  240.9 5.1 %collective-permute-start.25 = (f32[4,1024]{1,0:T(4,128)S(1)}, f32[4,1024]{1,0:T(4,128)S(1)}, u32[]{:S(2)}, u32[]{:S(2)}) collective-permute-start(f32[4,1024]{1,0:T(4,128)S(1)} %maximum_select_fusion.3), channel_id=1, source_target_pairs={{0,4},{1,5},{2,6},{3,7},{4,0},{5,1},{6,2},{7,3},{8,12},{9,13},{10,... | collective-permute-start | bytes 49160 | tf_op jit(solution)/shard_map/ppermute | solution.py:211
  245.9 10.1 %collective-permute-done.25 = f32[4,1024]{1,0:T(4,128)S(1)} collective-permute-done((f32[4,1024]{1,0:T(4,128)S(1)}, f32[4,1024]{1,0:T(4,128)S(1)}, u32[]{:S(2)}, u32[]{:S(2)}) %collective-permute-start.25) | collective-permute-done | bytes 16416 | tf_op jit(solution)/shard_map/ppermute | solution.py:211
  256.0 3.3 %collective-permute-start.26 = (f32[8,1024]{1,0:T(8,128)S(1)}, f32[8,1024]{1,0:T(8,128)S(1)}, u32[]{:S(2)}, u32[]{:S(2)}) collective-permute-start(f32[8,1024]{1,0:T(8,128)S(1)} %maximum_select_fusion.2), channel_id=1, source_target_pairs={{0,8},{1,9},{2,10},{3,11},{4,12},{5,13},{6,14},{7,15},{8,0},{9,1},... | collective-permute-start | bytes 98312 | tf_op jit(solution)/shard_map/ppermute | solution.py:211
  260.7 3.5 %collective-permute-start.27 = (f32[16,1024]{1,0:T(8,128)S(1)}, f32[16,1024]{1,0:T(8,128)S(1)}, u32[]{:S(2)}, u32[]{:S(2)}) collective-permute-start(f32[16,1024]{1,0:T(8,128)S(1)} %maximum_select_fusion.1), channel_id=1, source_target_pairs={{0,16},{1,17},{2,18},{3,19},{4,20},{5,21},{6,22},{7,23},{8,24},{9,... | collective-permute-start | bytes 196616 | tf_op jit(solution)/shard_map/ppermute | solution.py:211
  266.5 2.3 fusion.2
  (192 shorter events, 57.8 us)
Async XLA Ops:
  0.6 22.5 %collective-permute-start = (bf16[1,1024,128]{2,1,0:T(8,128)(2,1)}, bf16[1,1024,128]{2,1,0:T(8,128)(2,1)S(1)}, u32[]{:S(2)}, u32[]{:S(2)}) collective-permute-start(bf16[1,1024,128]{2,1,0:T(8,128)(2,1)} %param.7), channel_id=1, source_target_pairs={{0,32},{32,64},{64,96},{1,33},{33,65},{65,97},{2,34},{34,66},{66,9... | collective-permute-start | bytes 786440 | tf_op jit(solution)/shard_map/ppermute | solution.py:19
  4.6 19.5 %collective-permute-start.1 = (bf16[1,1024,128]{2,1,0:T(8,128)(2,1)}, bf16[1,1024,128]{2,1,0:T(8,128)(2,1)S(1)}, u32[]{:S(2)}, u32[]{:S(2)}) collective-permute-start(bf16[1,1024,128]{2,1,0:T(8,128)(2,1)} %param.7), channel_id=1, source_target_pairs={{32,0},{64,32},{96,64},{33,1},{65,33},{97,65},{34,2},{66,34},{98,6... | collective-permute-start | bytes 786440 | tf_op jit(solution)/shard_map/ppermute | solution.py:22
  39.4 6.0 %collective-permute-start.2 = (f32[5,1024]{1,0:T(8,128)S(1)}, f32[5,1024]{1,0:T(8,128)S(1)}, u32[]{:S(2)}, u32[]{:S(2)}) collective-permute-start(f32[5,1024]{1,0:T(8,128)S(1)} %log_add_fusion.5), channel_id=1, source_target_pairs={{0,1},{1,2},{2,3},{3,4},{4,5},{5,6},{6,7},{7,8},{8,9},{9,10},{10,1... | collective-permute-start | bytes 61448 | tf_op jit(solution)/shard_map/ppermute | solution.py:30
  43.5 5.2 %collective-permute-start.3 = (f32[5,1024]{1,0:T(8,128)S(1)}, f32[5,1024]{1,0:T(8,128)S(1)}, u32[]{:S(2)}, u32[]{:S(2)}) collective-permute-start(f32[5,1024]{1,0:T(8,128)S(1)} %log_add_fusion.5), channel_id=1, source_target_pairs={{1,0},{2,1},{3,2},{4,3},{5,4},{6,5},{7,6},{8,7},{9,8},{10,9},{11,1... | collective-permute-start | bytes 61448 | tf_op jit(solution)/shard_map/ppermute | solution.py:30
  48.8 7.8 %collective-permute-start.5 = (f32[7,1024]{1,0:T(8,128)S(1)}, f32[7,1024]{1,0:T(8,128)S(1)}, u32[]{:S(2)}, u32[]{:S(2)}) collective-permute-start(f32[7,1024]{1,0:T(8,128)S(1)} %log_add_fusion.4), channel_id=1, source_target_pairs={{3,0},{4,1},{5,2},{6,3},{7,4},{8,5},{9,6},{10,7},{11,8},{12,9},{13... | collective-permute-start | bytes 86024 | tf_op jit(solution)/shard_map/ppermute | solution.py:30
  50.2 7.5 %collective-permute-start.6 = (f32[5,1024]{1,0:T(8,128)S(1)}, f32[5,1024]{1,0:T(8,128)S(1)}, u32[]{:S(2)}, u32[]{:S(2)}) collective-permute-start(f32[5,1024]{1,0:T(8,128)S(1)} %log_add_fusion.5), channel_id=1, source_target_pairs={{0,2},{31,29},{32,34},{63,61},{64,66},{95,93},{96,98},{127,125}} | collective-permute-start | bytes 61448 | tf_op jit(solution)/shard_map/ppermute | solution.py:182
  50.8 6.8 %collective-permute-start.4 = (f32[7,1024]{1,0:T(8,128)S(1)}, f32[7,1024]{1,0:T(8,128)S(1)}, u32[]{:S(2)}, u32[]{:S(2)}) collective-permute-start(f32[7,1024]{1,0:T(8,128)S(1)} %log_add_fusion.4), channel_id=1, source_target_pairs={{0,3},{1,4},{2,5},{3,6},{4,7},{5,8},{6,9},{7,10},{8,11},{9,12},{10... | collective-permute-start | bytes 86024 | tf_op jit(solution)/shard_map/ppermute | solution.py:30
  72.5 9.3 %collective-permute-start.7 = (f32[4,1024]{1,0:T(4,128)S(1)}, f32[4,1024]{1,0:T(4,128)S(1)}, u32[]{:S(2)}, u32[]{:S(2)}) collective-permute-start(f32[4,1024]{1,0:T(4,128)S(1)} %pad_maximum_fusion.8), channel_id=1, source_target_pairs={{0,32},{32,64},{64,96},{1,33},{33,65},{65,97},{2,34},{34,66},{66,9... | collective-permute-start | bytes 49160 | tf_op jit(solution)/shard_map/ppermute | solution.py:30
  76.7 5.0 %collective-permute-start.8 = (f32[4,1024]{1,0:T(4,128)S(1)}, f32[4,1024]{1,0:T(4,128)S(1)}, u32[]{:S(2)}, u32[]{:S(2)}) collective-permute-start(f32[4,1024]{1,0:T(4,128)S(1)} %pad_maximum_fusion.8), channel_id=1, source_target_pairs={{32,0},{64,32},{96,64},{33,1},{65,33},{97,65},{34,2},{66,34},{98,6... | collective-permute-start | bytes 49160 | tf_op jit(solution)/shard_map/ppermute | solution.py:30
  97.6 5.1 %collective-permute-start.10 = (f32[5,1024]{1,0:T(8,128)S(1)}, f32[5,1024]{1,0:T(8,128)S(1)}, u32[]{:S(2)}, u32[]{:S(2)}) collective-permute-start(f32[5,1024]{1,0:T(8,128)S(1)} %log_add_fusion.3), channel_id=1, source_target_pairs={{0,1},{1,2},{2,3},{3,4},{4,5},{5,6},{6,7},{7,8},{8,9},{9,10},{10,1... | collective-permute-start | bytes 61448 | tf_op jit(solution)/shard_map/ppermute | solution.py:30
  100.8 5.2 %collective-permute-start.11 = (f32[5,1024]{1,0:T(8,128)S(1)}, f32[5,1024]{1,0:T(8,128)S(1)}, u32[]{:S(2)}, u32[]{:S(2)}) collective-permute-start(f32[5,1024]{1,0:T(8,128)S(1)} %log_add_fusion.3), channel_id=1, source_target_pairs={{1,0},{2,1},{3,2},{4,3},{5,4},{6,5},{7,6},{8,7},{9,8},{10,9},{11,1... | collective-permute-start | bytes 61448 | tf_op jit(solution)/shard_map/ppermute | solution.py:30
  106.2 8.4 %collective-permute-start.13 = (f32[7,1024]{1,0:T(8,128)S(1)}, f32[7,1024]{1,0:T(8,128)S(1)}, u32[]{:S(2)}, u32[]{:S(2)}) collective-permute-start(f32[7,1024]{1,0:T(8,128)S(1)} %log_add_fusion.2), channel_id=1, source_target_pairs={{3,0},{4,1},{5,2},{6,3},{7,4},{8,5},{9,6},{10,7},{11,8},{12,9},{13... | collective-permute-start | bytes 86024 | tf_op jit(solution)/shard_map/ppermute | solution.py:30
  107.5 8.1 %collective-permute-start.14 = (f32[5,1024]{1,0:T(8,128)S(1)}, f32[5,1024]{1,0:T(8,128)S(1)}, u32[]{:S(2)}, u32[]{:S(2)}) collective-permute-start(f32[5,1024]{1,0:T(8,128)S(1)} %log_add_fusion.3), channel_id=1, source_target_pairs={{0,2},{31,29},{32,34},{63,61},{64,66},{95,93},{96,98},{127,125}} | collective-permute-start | bytes 61448 | tf_op jit(solution)/shard_map/ppermute | solution.py:182
  108.2 7.5 %collective-permute-start.12 = (f32[7,1024]{1,0:T(8,128)S(1)}, f32[7,1024]{1,0:T(8,128)S(1)}, u32[]{:S(2)}, u32[]{:S(2)}) collective-permute-start(f32[7,1024]{1,0:T(8,128)S(1)} %log_add_fusion.2), channel_id=1, source_target_pairs={{0,3},{1,4},{2,5},{3,6},{4,7},{5,8},{6,9},{7,10},{8,11},{9,12},{10... | collective-permute-start | bytes 86024 | tf_op jit(solution)/shard_map/ppermute | solution.py:30
  130.3 8.8 %collective-permute-start.15 = (f32[4,1024]{1,0:T(4,128)S(1)}, f32[4,1024]{1,0:T(4,128)S(1)}, u32[]{:S(2)}, u32[]{:S(2)}) collective-permute-start(f32[4,1024]{1,0:T(4,128)S(1)} %pad_maximum_fusion.7), channel_id=1, source_target_pairs={{0,32},{32,64},{64,96},{1,33},{33,65},{65,97},{2,34},{34,66},{66,9... | collective-permute-start | bytes 49160 | tf_op jit(solution)/shard_map/ppermute | solution.py:30
  133.9 5.2 %collective-permute-start.16 = (f32[4,1024]{1,0:T(4,128)S(1)}, f32[4,1024]{1,0:T(4,128)S(1)}, u32[]{:S(2)}, u32[]{:S(2)}) collective-permute-start(f32[4,1024]{1,0:T(4,128)S(1)} %pad_maximum_fusion.7), channel_id=1, source_target_pairs={{32,0},{64,32},{96,64},{33,1},{65,33},{97,65},{34,2},{66,34},{98,6... | collective-permute-start | bytes 49160 | tf_op jit(solution)/shard_map/ppermute | solution.py:30
  135.2 5.0 %collective-permute-start.17 = (f32[3,1024]{1,0:T(4,128)S(1)}, f32[3,1024]{1,0:T(4,128)S(1)}, u32[]{:S(2)}, u32[]{:S(2)}) collective-permute-start(f32[3,1024]{1,0:T(4,128)S(1)} %log_add_fusion.7), channel_id=1, source_target_pairs={{0,64},{32,96},{64,0},{96,32},{1,65},{33,97},{65,1},{97,33},{2,66}... | collective-permute-start | bytes 36872 | tf_op jit(solution)/shard_map/ppermute | solution.py:147
  154.9 7.8 %collective-permute-start.18 = (f32[5,1024]{1,0:T(8,128)S(1)}, f32[5,1024]{1,0:T(8,128)S(1)}, u32[]{:S(2)}, u32[]{:S(2)}) collective-permute-start(f32[5,1024]{1,0:T(8,128)S(1)} %log_add_fusion.1), channel_id=1, source_target_pairs={{0,1},{1,2},{2,3},{3,4},{4,5},{5,6},{6,7},{7,8},{8,9},{9,10},{10,1... | collective-permute-start | bytes 61448 | tf_op jit(solution)/shard_map/ppermute | solution.py:30
  160.8 5.2 %collective-permute-start.19 = (f32[5,1024]{1,0:T(8,128)S(1)}, f32[5,1024]{1,0:T(8,128)S(1)}, u32[]{:S(2)}, u32[]{:S(2)}) collective-permute-start(f32[5,1024]{1,0:T(8,128)S(1)} %log_add_fusion.1), channel_id=1, source_target_pairs={{1,0},{2,1},{3,2},{4,3},{5,4},{6,5},{7,6},{8,7},{9,8},{10,9},{11,1... | collective-permute-start | bytes 61448 | tf_op jit(solution)/shard_map/ppermute | solution.py:30
  166.1 10.5 %collective-permute-start.21 = (f32[7,1024]{1,0:T(8,128)S(1)}, f32[7,1024]{1,0:T(8,128)S(1)}, u32[]{:S(2)}, u32[]{:S(2)}) collective-permute-start(f32[7,1024]{1,0:T(8,128)S(1)} %log_add_fusion), channel_id=1, source_target_pairs={{3,0},{4,1},{5,2},{6,3},{7,4},{8,5},{9,6},{10,7},{11,8},{12,9},{13... | collective-permute-start | bytes 86024 | tf_op jit(solution)/shard_map/ppermute | solution.py:30
  167.5 10.2 %collective-permute-start.22 = (f32[5,1024]{1,0:T(8,128)S(1)}, f32[5,1024]{1,0:T(8,128)S(1)}, u32[]{:S(2)}, u32[]{:S(2)}) collective-permute-start(f32[5,1024]{1,0:T(8,128)S(1)} %log_add_fusion.1), channel_id=1, source_target_pairs={{0,2},{31,29},{32,34},{63,61},{64,66},{95,93},{96,98},{127,125}} | collective-permute-start | bytes 61448 | tf_op jit(solution)/shard_map/ppermute | solution.py:182
  168.2 9.5 %collective-permute-start.20 = (f32[7,1024]{1,0:T(8,128)S(1)}, f32[7,1024]{1,0:T(8,128)S(1)}, u32[]{:S(2)}, u32[]{:S(2)}) collective-permute-start(f32[7,1024]{1,0:T(8,128)S(1)} %log_add_fusion), channel_id=1, source_target_pairs={{0,3},{1,4},{2,5},{3,6},{4,7},{5,8},{6,9},{7,10},{8,11},{9,12},{10... | collective-permute-start | bytes 86024 | tf_op jit(solution)/shard_map/ppermute | solution.py:30
  192.3 14.8 %collective-permute-start.28 = (f32[4,1024]{1,0:T(4,128)S(1)}, f32[4,1024]{1,0:T(4,128)S(1)}, u32[]{:S(2)}, u32[]{:S(2)}) collective-permute-start(f32[4,1024]{1,0:T(4,128)S(1)} %pad_maximum_fusion.6), channel_id=1, source_target_pairs={{0,32},{32,64},{64,96},{1,33},{33,65},{65,97},{2,34},{34,66},{66,9... | collective-permute-start | bytes 49160 | tf_op jit(solution)/shard_map/ppermute | solution.py:30
  196.0 11.2 %collective-permute-start.29 = (f32[4,1024]{1,0:T(4,128)S(1)}, f32[4,1024]{1,0:T(4,128)S(1)}, u32[]{:S(2)}, u32[]{:S(2)}) collective-permute-start(f32[4,1024]{1,0:T(4,128)S(1)} %pad_maximum_fusion.6), channel_id=1, source_target_pairs={{32,0},{64,32},{96,64},{33,1},{65,33},{97,65},{34,2},{66,34},{98,6... | collective-permute-start | bytes 49160 | tf_op jit(solution)/shard_map/ppermute | solution.py:30
  197.3 9.9 %collective-permute-start.30 = (f32[3,1024]{1,0:T(4,128)S(1)}, f32[3,1024]{1,0:T(4,128)S(1)}, u32[]{:S(2)}, u32[]{:S(2)}) collective-permute-start(f32[3,1024]{1,0:T(4,128)S(1)} %log_add_fusion.6), channel_id=1, source_target_pairs={{0,64},{32,96},{64,0},{96,32},{1,65},{33,97},{65,1},{97,33},{2,66}... | collective-permute-start | bytes 36872 | tf_op jit(solution)/shard_map/ppermute | solution.py:147
  205.6 35.2 %collective-permute-start.24 = (f32[2,1024]{1,0:T(2,128)S(1)}, f32[2,1024]{1,0:T(2,128)S(1)}, u32[]{:S(2)}, u32[]{:S(2)}) collective-permute-start(f32[2,1024]{1,0:T(2,128)S(1)} %maximum_select_fusion.4), channel_id=1, source_target_pairs={{0,2},{1,3},{2,0},{3,1},{4,6},{5,7},{6,4},{7,5},{8,10},{9,11},{10,... | collective-permute-start | bytes 24584 | tf_op jit(solution)/shard_map/ppermute | solution.py:211
  224.8 41.7 %collective-permute-start.31 = (f32[1,1024,128]{2,1,0:T(8,128)}, f32[1,1024,128]{2,1,0:T(8,128)S(1)}, u32[]{:S(2)}, u32[]{:S(2)}) collective-permute-start(f32[1,1024,128]{2,1,0:T(8,128)} %get-tuple-element.11), channel_id=1, source_target_pairs={{1,0},{2,1},{3,2},{4,3},{5,4},{6,5},{7,6},{8,7},{9,8},{10,9},{11,1... | collective-permute-start | bytes 1572872 | tf_op jit(solution)/shard_map/ppermute | solution.py:30
  227.5 39.0 %collective-permute-start.32 = (f32[1,1024,128]{2,1,0:T(8,128)}, f32[1,1024,128]{2,1,0:T(8,128)}, u32[]{:S(2)}, u32[]{:S(2)}) collective-permute-start(f32[1,1024,128]{2,1,0:T(8,128)} %get-tuple-element.14), channel_id=1, source_target_pairs={{0,1},{1,2},{2,3},{3,4},{4,5},{5,6},{6,7},{7,8},{8,9},{9,10},{10,1... | collective-permute-start | bytes 1572872 | tf_op jit(solution)/shard_map/ppermute | solution.py:30
  230.4 36.2 %collective-permute-start.33 = (f32[1,1024,128]{2,1,0:T(8,128)}, f32[1,1024,128]{2,1,0:T(8,128)}, u32[]{:S(2)}, u32[]{:S(2)}) collective-permute-start(f32[1,1024,128]{2,1,0:T(8,128)} %get-tuple-element.13), channel_id=1, source_target_pairs={{2,0},{3,1},{4,2},{5,3},{6,4},{7,5},{8,6},{9,7},{10,8},{11,9},{12,... | collective-permute-start | bytes 1572872 | tf_op jit(solution)/shard_map/ppermute | solution.py:30
  231.7 34.9 %collective-permute-start.34 = (f32[1,1024,128]{2,1,0:T(8,128)}, f32[1,1024,128]{2,1,0:T(8,128)}, u32[]{:S(2)}, u32[]{:S(2)}) collective-permute-start(f32[1,1024,128]{2,1,0:T(8,128)} %get-tuple-element.12), channel_id=1, source_target_pairs={{0,2},{1,3},{2,4},{3,5},{4,6},{5,7},{6,8},{7,9},{8,10},{9,11},{10,... | collective-permute-start | bytes 1572872 | tf_op jit(solution)/shard_map/ppermute | solution.py:30
  240.9 15.2 %collective-permute-start.25 = (f32[4,1024]{1,0:T(4,128)S(1)}, f32[4,1024]{1,0:T(4,128)S(1)}, u32[]{:S(2)}, u32[]{:S(2)}) collective-permute-start(f32[4,1024]{1,0:T(4,128)S(1)} %maximum_select_fusion.3), channel_id=1, source_target_pairs={{0,4},{1,5},{2,6},{3,7},{4,0},{5,1},{6,2},{7,3},{8,12},{9,13},{10,... | collective-permute-start | bytes 49160 | tf_op jit(solution)/shard_map/ppermute | solution.py:211
  260.7 5.2 %collective-permute-start.27 = (f32[16,1024]{1,0:T(8,128)S(1)}, f32[16,1024]{1,0:T(8,128)S(1)}, u32[]{:S(2)}, u32[]{:S(2)}) collective-permute-start(f32[16,1024]{1,0:T(8,128)S(1)} %maximum_select_fusion.1), channel_id=1, source_target_pairs={{0,16},{1,17},{2,18},{3,19},{4,20},{5,21},{6,22},{7,23},{8,24},{9,... | collective-permute-start | bytes 196616 | tf_op jit(solution)/shard_map/ppermute | solution.py:211
  (8 other events, 96.8 us)

commit v9 on v8

--- a/solution.py
+++ b/solution.py
@@ -28,10 +28,6 @@
     devices = range(lax.axis_size(axis))
     route = [(i - distance, i) for i in devices if i - distance in devices]
     return lax.ppermute(block, axis, route)
-
-
-def pick(table, position):
-    return lax.dynamic_index_in_dim(table, position, 0, keepdims=False)
 
 
 def squares(points):
@@ -205,16 +201,24 @@
     index = lax.axis_index(axis)
     count = lax.axis_size(axis)
     block = row
-    step = 1
-    while step < count:
+    order = [[i] for i in range(count)]
+    step = count // 2
+    while step >= 1:
         route = [(i, i ^ step) for i in range(count)]
         other = lax.ppermute(block, axis, route)
         upper = (index // step) % 2 == 1
         block = jnp.where(
             upper, jnp.concatenate([other, block], axis=0), jnp.concatenate([block, other], axis=0)
         )
-        step *= 2
-    return block
+        order = [
+            order[i ^ step] + order[i] if (i // step) % 2 == 1 else order[i] + order[i ^ step]
+            for i in range(count)
+        ]
+        step //= 2
+    rows = row.shape[0]
+    position = {device: place for place, device in enumerate(order[0])}
+    take = [position[device] * rows + r for device in range(count) for r in range(rows)]
+    return jnp.take(block, jnp.array(take, dtype=jnp.int32), axis=0)
 
 
 def body(src_points, tgt_points, src_log_mass, tgt_log_mass, near_pairs, target_slot):
@@ -233,7 +237,7 @@
     span_ids = jnp.clip(source_local - (gy_index - 2) * owned, 0, 5 * owned - 1)
     span_mask = span_ids[None, :] == jnp.arange(5 * owned, dtype=jnp.int32)[:, None]
     window_mask = window_ids[None, :] == jnp.arange(3 * owned, dtype=jnp.int32)[:, None]
-    pair_src_sq = jnp.stack([squares(pick(src_points, source_local[p])) for p in range(source_local.shape[0])])
+    pair_src_sq = squares(src_points[source_local])
     window_pts, window_sq = fetch_points(tgt_points)
     pair_tgt_sq = window_sq[window_ids]
     mass_pad = jnp.zeros((2 * owned,) + src_log_mass.shape[1:], src_log_mass.dtype)

time: 271 us -> 261 us (0.963)
  between operations: 13.1 us -> 1.76 us
  local copies, waits for them, and re-layouts: 14.1 us -> 19.1 us
  other arithmetic: 20.9 us -> 17.1 us
    gather x0 -> x2, local copies, waits for them, and re-layouts: none -> 5.49 us  [the longest x1 4.23 us: body(): pair_src_sq = squares(src_points[source_local])]
where the time goes in v9:
time: 261 us; the launch traced here: 259 us
  starting transfers between devices  106 us (41%)
  Pallas kernels  84.8 us (32%)
  waiting for transfers between devices  30.1 us (12%)
  local copies, waits for them, and re-layouts  19.1 us (7%)
  other arithmetic  17.1 us (7%)
    pallas_call x6, Pallas kernels, pair_lse(): pl.pallas_call(_lse_kernel, grid_spec=spec, out_shape=jax.ShapeDtypeStruc...  73.7 us
    ppermute x22, starting transfers between devices, passed_along(): return lax.ppermute(block, axis, route)  72.6 us
    ppermute x5, starting transfers between devices, gather_rows(): other = lax.ppermute(block, axis, route)  15.1 us
    ppermute x5, waiting for transfers between devices, gather_rows(): other = lax.ppermute(block, axis, route)  15 us
    ppermute x22, waiting for transfers between devices, passed_along(): return lax.ppermute(block, axis, route)  12.8 us
    ppermute x3, starting transfers between devices, spread(): lax.ppermute(block, axis, [(i, (i + reach) % count) for i in range(count)])  11.2 us
    pallas_call x1, Pallas kernels, pair_grad(): pl.pallas_call(_grad_kernel, grid_spec=spec, out_shape=jax.ShapeDtypeStru...  11.1 us
  transfers between devices with their start and end apart: 35, of which 11 were waited for; matrix products, arithmetic and copies ran while one was open for 7% of the time, Pallas kernels for 4%

profile of v9, /device:TPU:1, one launch (start us, length us, event | category | flops | bytes accessed | tf_op | source)
XLA Modules:
  0.0 259.0 jit_solution(10941815467485790964)
XLA Ops:
  0.6 4.1 %collective-permute-start = (bf16[1,1024,128]{2,1,0:T(8,128)(2,1)}, bf16[1,1024,128]{2,1,0:T(8,128)(2,1)S(1)}, u32[]{:S(2)}, u32[]{:S(2)}) collective-permute-start(bf16[1,1024,128]{2,1,0:T(8,128)(2,1)} %param.8), channel_id=1, source_target_pairs={{0,32},{32,64},{64,96},{1,33},{33,65},{65,97},{2,34},{34,66},{66,9... | collective-permute-start | bytes 786440 | tf_op jit(solution)/shard_map/ppermute | solution.py:19
  8.2 4.2 %gather_fusion.2 = bf16[6,1024,128]{2,1,0:T(8,128)(2,1)S(1)} fusion(bf16[32,1024,128]{2,1,0:T(8,128)(2,1)} %a_ref.7, s32[1024]{0:T(1024)S(1)} %get-tuple-element.52), kind=kCustom, calls=%fused_computation.2 | custom fusion | bytes 3145752 | tf_op jit(solution)/shard_map/gather | solution.py:240
  15.9 12.4 %shard_map.94 = f32[6,1,1024]{2,1,0:T(1,128)} custom-call(s32[6]{0:T(128)} %bitcast.100, s32[6]{0:T(128)} %get-tuple-element.49.b_ids.a_ids, bf16[32,1024,128]{2,1,0:T(8,128)(2,1)} %a_ref.7, bf16[3,1024,128]{2,1,0:T(8,128)(2,1)} %copy-done, f32[6,8,1024]{2,1,0:T(8,128)} %broadcast_in_dim.253.v_ref), custom_call_target="tpu_custom_call" | custom-call | tf_op jit(solution)/shard_map/pallas_call | solution.py:73
  29.3 4.6 %collective-permute-start.2 = (f32[5,1024]{1,0:T(8,128)S(1)}, f32[5,1024]{1,0:T(8,128)S(1)}, u32[]{:S(2)}, u32[]{:S(2)}) collective-permute-start(f32[5,1024]{1,0:T(8,128)S(1)} %log_add_fusion.5), channel_id=1, source_target_pairs={{0,1},{1,2},{2,3},{3,4},{4,5},{5,6},{6,7},{7,8},{8,9},{9,10},{10,1... | collective-permute-start | bytes 61448 | tf_op jit(solution)/shard_map/ppermute | solution.py:30
  35.9 3.3 %collective-permute-done.3 = f32[5,1024]{1,0:T(8,128)S(1)} collective-permute-done((f32[5,1024]{1,0:T(8,128)S(1)}, f32[5,1024]{1,0:T(8,128)S(1)}, u32[]{:S(2)}, u32[]{:S(2)}) %collective-permute-start.3) | collective-permute-done | bytes 20512 | tf_op jit(solution)/shard_map/ppermute | solution.py:30
  41.3 5.8 %collective-permute-start.4 = (f32[7,1024]{1,0:T(8,128)S(1)}, f32[7,1024]{1,0:T(8,128)S(1)}, u32[]{:S(2)}, u32[]{:S(2)}) collective-permute-start(f32[7,1024]{1,0:T(8,128)S(1)} %log_add_fusion.4), channel_id=1, source_target_pairs={{0,3},{1,4},{2,5},{3,6},{4,7},{5,8},{6,9},{7,10},{8,11},{9,12},{10... | collective-permute-start | bytes 86024 | tf_op jit(solution)/shard_map/ppermute | solution.py:30
  49.5 12.4 %shard_map.95 = f32[6,1,1024]{2,1,0:T(1,128)} custom-call(s32[6]{0:T(128)} %get-tuple-element.49.b_ids.a_ids, s32[6]{0:T(128)} %bitcast.101, bf16[3,1024,128]{2,1,0:T(8,128)(2,1)} %copy-done, bf16[32,1024,128]{2,1,0:T(8,128)(2,1)} %a_ref.7, f32[6,8,1024]{2,1,0:T(8,128)} %broadcast_in_dim.257.v_ref), custom_call_target="tpu_custom_call" | custom-call | tf_op jit(solution)/shard_map/pallas_call | solution.py:73
  62.9 3.7 %collective-permute-start.7 = (f32[4,1024]{1,0:T(4,128)S(1)}, f32[4,1024]{1,0:T(4,128)S(1)}, u32[]{:S(2)}, u32[]{:S(2)}) collective-permute-start(f32[4,1024]{1,0:T(4,128)S(1)} %pad_maximum_fusion.8), channel_id=1, source_target_pairs={{0,32},{32,64},{64,96},{1,33},{33,65},{65,97},{2,34},{34,66},{66,9... | collective-permute-start | bytes 49160 | tf_op jit(solution)/shard_map/ppermute | solution.py:30
  68.0 3.7 %collective-permute-start.9 = (f32[3,1024]{1,0:T(4,128)S(1)}, f32[3,1024]{1,0:T(4,128)S(1)}, u32[]{:S(2)}, u32[]{:S(2)}) collective-permute-start(f32[3,1024]{1,0:T(4,128)S(1)} %log_add_fusion.8), channel_id=1, source_target_pairs={{0,64},{32,96},{64,0},{96,32},{1,65},{33,97},{65,1},{97,33},{2,66}... | collective-permute-start | bytes 36872 | tf_op jit(solution)/shard_map/ppermute | solution.py:143
  74.3 12.2 %shard_map.96 = f32[6,1,1024]{2,1,0:T(1,128)} custom-call(s32[6]{0:T(128)} %bitcast.102, s32[6]{0:T(128)} %get-tuple-element.49.b_ids.a_ids, bf16[32,1024,128]{2,1,0:T(8,128)(2,1)} %a_ref.7, bf16[3,1024,128]{2,1,0:T(8,128)(2,1)} %copy-done, f32[6,8,1024]{2,1,0:T(8,128)} %broadcast_in_dim.262.v_ref), custom_call_target="tpu_custom_call" | custom-call | tf_op jit(solution)/shard_map/pallas_call | solution.py:73
  87.5 3.2 %collective-permute-start.10 = (f32[5,1024]{1,0:T(8,128)S(1)}, f32[5,1024]{1,0:T(8,128)S(1)}, u32[]{:S(2)}, u32[]{:S(2)}) collective-permute-start(f32[5,1024]{1,0:T(8,128)S(1)} %log_add_fusion.3), channel_id=1, source_target_pairs={{0,1},{1,2},{2,3},{3,4},{4,5},{5,6},{6,7},{7,8},{8,9},{9,10},{10,1... | collective-permute-start | bytes 61448 | tf_op jit(solution)/shard_map/ppermute | solution.py:30
  92.7 3.3 %collective-permute-done.11 = f32[5,1024]{1,0:T(8,128)S(1)} collective-permute-done((f32[5,1024]{1,0:T(8,128)S(1)}, f32[5,1024]{1,0:T(8,128)S(1)}, u32[]{:S(2)}, u32[]{:S(2)}) %collective-permute-start.11) | collective-permute-done | bytes 20512 | tf_op jit(solution)/shard_map/ppermute | solution.py:30
  98.0 6.4 %collective-permute-start.12 = (f32[7,1024]{1,0:T(8,128)S(1)}, f32[7,1024]{1,0:T(8,128)S(1)}, u32[]{:S(2)}, u32[]{:S(2)}) collective-permute-start(f32[7,1024]{1,0:T(8,128)S(1)} %log_add_fusion.2), channel_id=1, source_target_pairs={{0,3},{1,4},{2,5},{3,6},{4,7},{5,8},{6,9},{7,10},{8,11},{9,12},{10... | collective-permute-start | bytes 86024 | tf_op jit(solution)/shard_map/ppermute | solution.py:30
  106.9 12.2 %shard_map.97 = f32[6,1,1024]{2,1,0:T(1,128)} custom-call(s32[6]{0:T(128)} %get-tuple-element.49.b_ids.a_ids, s32[6]{0:T(128)} %bitcast.103, bf16[3,1024,128]{2,1,0:T(8,128)(2,1)} %copy-done, bf16[32,1024,128]{2,1,0:T(8,128)(2,1)} %a_ref.7, f32[6,8,1024]{2,1,0:T(8,128)} %broadcast_in_dim.264.v_ref), custom_call_target="tpu_custom_call" | custom-call | tf_op jit(solution)/shard_map/pallas_call | solution.py:73
  120.2 3.6 %collective-permute-start.15 = (f32[4,1024]{1,0:T(4,128)S(1)}, f32[4,1024]{1,0:T(4,128)S(1)}, u32[]{:S(2)}, u32[]{:S(2)}) collective-permute-start(f32[4,1024]{1,0:T(4,128)S(1)} %pad_maximum_fusion.7), channel_id=1, source_target_pairs={{0,32},{32,64},{64,96},{1,33},{33,65},{65,97},{2,34},{34,66},{66,9... | collective-permute-start | bytes 49160 | tf_op jit(solution)/shard_map/ppermute | solution.py:30
  125.1 3.9 %collective-permute-start.17 = (f32[3,1024]{1,0:T(4,128)S(1)}, f32[3,1024]{1,0:T(4,128)S(1)}, u32[]{:S(2)}, u32[]{:S(2)}) collective-permute-start(f32[3,1024]{1,0:T(4,128)S(1)} %log_add_fusion.7), channel_id=1, source_target_pairs={{0,64},{32,96},{64,0},{96,32},{1,65},{33,97},{65,1},{97,33},{2,66}... | collective-permute-start | bytes 36872 | tf_op jit(solution)/shard_map/ppermute | solution.py:143
  131.5 12.2 %shard_map.98 = f32[6,1,1024]{2,1,0:T(1,128)} custom-call(s32[6]{0:T(128)} %bitcast.104, s32[6]{0:T(128)} %get-tuple-element.49.b_ids.a_ids, bf16[32,1024,128]{2,1,0:T(8,128)(2,1)} %a_ref.7, bf16[3,1024,128]{2,1,0:T(8,128)(2,1)} %copy-done, f32[6,8,1024]{2,1,0:T(8,128)} %broadcast_in_dim.266.v_ref), custom_call_target="tpu_custom_call" | custom-call | tf_op jit(solution)/shard_map/pallas_call | solution.py:73
  144.8 5.9 %collective-permute-start.18 = (f32[5,1024]{1,0:T(8,128)S(1)}, f32[5,1024]{1,0:T(8,128)S(1)}, u32[]{:S(2)}, u32[]{:S(2)}) collective-permute-start(f32[5,1024]{1,0:T(8,128)S(1)} %log_add_fusion.1), channel_id=1, source_target_pairs={{0,1},{1,2},{2,3},{3,4},{4,5},{5,6},{6,7},{7,8},{8,9},{9,10},{10,1... | collective-permute-start | bytes 61448 | tf_op jit(solution)/shard_map/ppermute | solution.py:30
  152.6 3.3 %collective-permute-done.19 = f32[5,1024]{1,0:T(8,128)S(1)} collective-permute-done((f32[5,1024]{1,0:T(8,128)S(1)}, f32[5,1024]{1,0:T(8,128)S(1)}, u32[]{:S(2)}, u32[]{:S(2)}) %collective-permute-start.19) | collective-permute-done | bytes 20512 | tf_op jit(solution)/shard_map/ppermute | solution.py:30
  158.0 8.5 %collective-permute-start.20 = (f32[7,1024]{1,0:T(8,128)S(1)}, f32[7,1024]{1,0:T(8,128)S(1)}, u32[]{:S(2)}, u32[]{:S(2)}) collective-permute-start(f32[7,1024]{1,0:T(8,128)S(1)} %log_add_fusion), channel_id=1, source_target_pairs={{0,3},{1,4},{2,5},{3,6},{4,7},{5,8},{6,9},{7,10},{8,11},{9,12},{10... | collective-permute-start | bytes 86024 | tf_op jit(solution)/shard_map/ppermute | solution.py:30
  168.9 12.2 %shard_map.99 = f32[6,1,1024]{2,1,0:T(1,128)} custom-call(s32[6]{0:T(128)} %get-tuple-element.49.b_ids.a_ids, s32[6]{0:T(128)} %bitcast.105, bf16[3,1024,128]{2,1,0:T(8,128)(2,1)} %copy-done, bf16[32,1024,128]{2,1,0:T(8,128)(2,1)} %a_ref.7, f32[6,8,1024]{2,1,0:T(8,128)} %broadcast_in_dim.270.v_ref), custom_call_target="tpu_custom_call" | custom-call | tf_op jit(solution)/shard_map/pallas_call | solution.py:73
  182.2 11.2 %collective-permute-start.23 = (f32[1,1024]{1,0:T(1,128)S(1)}, f32[1,1024]{1,0:T(1,128)S(1)}, u32[]{:S(2)}, u32[]{:S(2)}) collective-permute-start(f32[1,1024]{1,0:T(1,128)S(1)} %slice.265), channel_id=1, source_target_pairs={{0,16},{1,17},{2,18},{3,19},{4,20},{5,21},{6,22},{7,23},{8,24},{9,... | collective-permute-start | bytes 12296 | tf_op jit(solution)/shard_map/ppermute | solution.py:208
  193.4 3.6 %collective-permute-start.28 = (f32[4,1024]{1,0:T(4,128)S(1)}, f32[4,1024]{1,0:T(4,128)S(1)}, u32[]{:S(2)}, u32[]{:S(2)}) collective-permute-start(f32[4,1024]{1,0:T(4,128)S(1)} %pad_maximum_fusion.6), channel_id=1, source_target_pairs={{0,32},{32,64},{64,96},{1,33},{33,65},{65,97},{2,34},{34,66},{66,9... | collective-permute-start | bytes 49160 | tf_op jit(solution)/shard_map/ppermute | solution.py:30
  198.3 3.7 %collective-permute-start.30 = (f32[3,1024]{1,0:T(4,128)S(1)}, f32[3,1024]{1,0:T(4,128)S(1)}, u32[]{:S(2)}, u32[]{:S(2)}) collective-permute-start(f32[3,1024]{1,0:T(4,128)S(1)} %log_add_fusion.6), channel_id=1, source_target_pairs={{0,64},{32,96},{64,0},{96,32},{1,65},{33,97},{65,1},{97,33},{2,66}... | collective-permute-start | bytes 36872 | tf_op jit(solution)/shard_map/ppermute | solution.py:143
  206.5 11.1 %shard_map.100 = f32[6,1024,128]{2,1,0:T(8,128)} custom-call(s32[6]{0:T(128)} %bitcast.106, s32[6]{0:T(128)} %get-tuple-element.49.b_ids.a_ids, bf16[32,1024,128]{2,1,0:T(8,128)(2,1)} %a_ref.7, bf16[3,1024,128]{2,1,0:T(8,128)(2,1)} %copy-done, f32[6,1,1024]{2,1,0:T(1,128)} %div.120.v_ref, f32[6,1024,1]{2,1,0:T(8,128)} %copy.12.w_ref), custom_call_target="tpu_custom_call" | custom-call | tf_op jit(solution)/shard_map/pallas_call | solution.py:108
  217.7 3.9 %select_reduce_fusion = f32[5,1024,128]{2,1,0:T(8,128)S(1)} fusion(f32[6,1024,128]{2,1,0:T(8,128)} %shard_map.100, pred[5,6]{1,0:T(8,128)(4,1)S(1)} %iota_compare_fusion.1), kind=kLoop, calls=%fused_computation.10 | loop fusion | flops 7208960 | bytes 5767198 | tf_op jit(solution)/shard_map/reduce_sum | solution.py:271
  224.8 5.7 %collective-permute-start.32 = (f32[1,1024,128]{2,1,0:T(8,128)}, f32[1,1024,128]{2,1,0:T(8,128)}, u32[]{:S(2)}, u32[]{:S(2)}) collective-permute-start(f32[1,1024,128]{2,1,0:T(8,128)} %get-tuple-element.8), channel_id=1, source_target_pairs={{0,1},{1,2},{2,3},{3,4},{4,5},{5,6},{6,7},{7,8},{8,9},{9,10},{10,1... | collective-permute-start | bytes 1572872 | tf_op jit(solution)/shard_map/ppermute | solution.py:30
  231.9 4.8 %collective-permute-start.34 = (f32[1,1024,128]{2,1,0:T(8,128)}, f32[1,1024,128]{2,1,0:T(8,128)}, u32[]{:S(2)}, u32[]{:S(2)}) collective-permute-start(f32[1,1024,128]{2,1,0:T(8,128)} %get-tuple-element.6), channel_id=1, source_target_pairs={{0,2},{1,3},{2,4},{3,5},{4,6},{5,7},{6,8},{7,9},{8,10},{9,11},{10,... | collective-permute-start | bytes 1572872 | tf_op jit(solution)/shard_map/ppermute | solution.py:30
  236.9 12.0 %collective-permute-done.25 = f32[4,1024]{1,0:T(4,128)S(1)} collective-permute-done((f32[4,1024]{1,0:T(4,128)S(1)}, f32[4,1024]{1,0:T(4,128)S(1)}, u32[]{:S(2)}, u32[]{:S(2)}) %collective-permute-start.25) | collective-permute-done | bytes 16416 | tf_op jit(solution)/shard_map/ppermute | solution.py:208
  249.1 2.7 %collective-permute-done.26 = f32[8,1024]{1,0:T(8,128)S(1)} collective-permute-done((f32[8,1024]{1,0:T(8,128)S(1)}, f32[8,1024]{1,0:T(8,128)S(1)}, u32[]{:S(2)}, u32[]{:S(2)}) %collective-permute-start.26) | collective-permute-done | bytes 32800 | tf_op jit(solution)/shard_map/ppermute | solution.py:208
  251.8 2.6 %collective-permute-start.27 = (f32[16,1024]{1,0:T(8,128)S(1)}, f32[16,1024]{1,0:T(8,128)S(1)}, u32[]{:S(2)}, u32[]{:S(2)}) collective-permute-start(f32[16,1024]{1,0:T(8,128)S(1)} %maximum_select_fusion.1), channel_id=1, source_target_pairs={{0,1},{1,0},{2,3},{3,2},{4,5},{5,4},{6,7},{7,6},{8,9},{9,8},{10,11... | collective-permute-start | bytes 196616 | tf_op jit(solution)/shard_map/ppermute | solution.py:208
  256.6 2.3 fusion.2
  (190 shorter events, 52.5 us)
Async XLA Ops:
  0.6 13.3 %collective-permute-start = (bf16[1,1024,128]{2,1,0:T(8,128)(2,1)}, bf16[1,1024,128]{2,1,0:T(8,128)(2,1)S(1)}, u32[]{:S(2)}, u32[]{:S(2)}) collective-permute-start(bf16[1,1024,128]{2,1,0:T(8,128)(2,1)} %param.8), channel_id=1, source_target_pairs={{0,32},{32,64},{64,96},{1,33},{33,65},{65,97},{2,34},{34,66},{66,9... | collective-permute-start | bytes 786440 | tf_op jit(solution)/shard_map/ppermute | solution.py:19
  4.7 9.3 %collective-permute-start.1 = (bf16[1,1024,128]{2,1,0:T(8,128)(2,1)}, bf16[1,1024,128]{2,1,0:T(8,128)(2,1)S(1)}, u32[]{:S(2)}, u32[]{:S(2)}) collective-permute-start(bf16[1,1024,128]{2,1,0:T(8,128)(2,1)} %param.8), channel_id=1, source_target_pairs={{32,0},{64,32},{96,64},{33,1},{65,33},{97,65},{34,2},{66,34},{98,6... | collective-permute-start | bytes 786440 | tf_op jit(solution)/shard_map/ppermute | solution.py:22
  29.3 6.5 %collective-permute-start.2 = (f32[5,1024]{1,0:T(8,128)S(1)}, f32[5,1024]{1,0:T(8,128)S(1)}, u32[]{:S(2)}, u32[]{:S(2)}) collective-permute-start(f32[5,1024]{1,0:T(8,128)S(1)} %log_add_fusion.5), channel_id=1, source_target_pairs={{0,1},{1,2},{2,3},{3,4},{4,5},{5,6},{6,7},{7,8},{8,9},{9,10},{10,1... | collective-permute-start | bytes 61448 | tf_op jit(solution)/shard_map/ppermute | solution.py:30
  33.9 5.2 %collective-permute-start.3 = (f32[5,1024]{1,0:T(8,128)S(1)}, f32[5,1024]{1,0:T(8,128)S(1)}, u32[]{:S(2)}, u32[]{:S(2)}) collective-permute-start(f32[5,1024]{1,0:T(8,128)S(1)} %log_add_fusion.5), channel_id=1, source_target_pairs={{1,0},{2,1},{3,2},{4,3},{5,4},{6,5},{7,6},{8,7},{9,8},{10,9},{11,1... | collective-permute-start | bytes 61448 | tf_op jit(solution)/shard_map/ppermute | solution.py:30
  39.2 7.8 %collective-permute-start.5 = (f32[7,1024]{1,0:T(8,128)S(1)}, f32[7,1024]{1,0:T(8,128)S(1)}, u32[]{:S(2)}, u32[]{:S(2)}) collective-permute-start(f32[7,1024]{1,0:T(8,128)S(1)} %log_add_fusion.4), channel_id=1, source_target_pairs={{3,0},{4,1},{5,2},{6,3},{7,4},{8,5},{9,6},{10,7},{11,8},{12,9},{13... | collective-permute-start | bytes 86024 | tf_op jit(solution)/shard_map/ppermute | solution.py:30
  40.6 7.5 %collective-permute-start.6 = (f32[5,1024]{1,0:T(8,128)S(1)}, f32[5,1024]{1,0:T(8,128)S(1)}, u32[]{:S(2)}, u32[]{:S(2)}) collective-permute-start(f32[5,1024]{1,0:T(8,128)S(1)} %log_add_fusion.5), channel_id=1, source_target_pairs={{0,2},{31,29},{32,34},{63,61},{64,66},{95,93},{96,98},{127,125}} | collective-permute-start | bytes 61448 | tf_op jit(solution)/shard_map/ppermute | solution.py:178
  41.3 6.8 %collective-permute-start.4 = (f32[7,1024]{1,0:T(8,128)S(1)}, f32[7,1024]{1,0:T(8,128)S(1)}, u32[]{:S(2)}, u32[]{:S(2)}) collective-permute-start(f32[7,1024]{1,0:T(8,128)S(1)} %log_add_fusion.4), channel_id=1, source_target_pairs={{0,3},{1,4},{2,5},{3,6},{4,7},{5,8},{6,9},{7,10},{8,11},{9,12},{10... | collective-permute-start | bytes 86024 | tf_op jit(solution)/shard_map/ppermute | solution.py:30
  62.9 8.8 %collective-permute-start.7 = (f32[4,1024]{1,0:T(4,128)S(1)}, f32[4,1024]{1,0:T(4,128)S(1)}, u32[]{:S(2)}, u32[]{:S(2)}) collective-permute-start(f32[4,1024]{1,0:T(4,128)S(1)} %pad_maximum_fusion.8), channel_id=1, source_target_pairs={{0,32},{32,64},{64,96},{1,33},{33,65},{65,97},{2,34},{34,66},{66,9... | collective-permute-start | bytes 49160 | tf_op jit(solution)/shard_map/ppermute | solution.py:30
  66.7 5.0 %collective-permute-start.8 = (f32[4,1024]{1,0:T(4,128)S(1)}, f32[4,1024]{1,0:T(4,128)S(1)}, u32[]{:S(2)}, u32[]{:S(2)}) collective-permute-start(f32[4,1024]{1,0:T(4,128)S(1)} %pad_maximum_fusion.8), channel_id=1, source_target_pairs={{32,0},{64,32},{96,64},{33,1},{65,33},{97,65},{34,2},{66,34},{98,6... | collective-permute-start | bytes 49160 | tf_op jit(solution)/shard_map/ppermute | solution.py:30
  87.5 5.1 %collective-permute-start.10 = (f32[5,1024]{1,0:T(8,128)S(1)}, f32[5,1024]{1,0:T(8,128)S(1)}, u32[]{:S(2)}, u32[]{:S(2)}) collective-permute-start(f32[5,1024]{1,0:T(8,128)S(1)} %log_add_fusion.3), channel_id=1, source_target_pairs={{0,1},{1,2},{2,3},{3,4},{4,5},{5,6},{6,7},{7,8},{8,9},{9,10},{10,1... | collective-permute-start | bytes 61448 | tf_op jit(solution)/shard_map/ppermute | solution.py:30
  90.7 5.2 %collective-permute-start.11 = (f32[5,1024]{1,0:T(8,128)S(1)}, f32[5,1024]{1,0:T(8,128)S(1)}, u32[]{:S(2)}, u32[]{:S(2)}) collective-permute-start(f32[5,1024]{1,0:T(8,128)S(1)} %log_add_fusion.3), channel_id=1, source_target_pairs={{1,0},{2,1},{3,2},{4,3},{5,4},{6,5},{7,6},{8,7},{9,8},{10,9},{11,1... | collective-permute-start | bytes 61448 | tf_op jit(solution)/shard_map/ppermute | solution.py:30
  96.1 8.4 %collective-permute-start.13 = (f32[7,1024]{1,0:T(8,128)S(1)}, f32[7,1024]{1,0:T(8,128)S(1)}, u32[]{:S(2)}, u32[]{:S(2)}) collective-permute-start(f32[7,1024]{1,0:T(8,128)S(1)} %log_add_fusion.2), channel_id=1, source_target_pairs={{3,0},{4,1},{5,2},{6,3},{7,4},{8,5},{9,6},{10,7},{11,8},{12,9},{13... | collective-permute-start | bytes 86024 | tf_op jit(solution)/shard_map/ppermute | solution.py:30
  97.4 8.1 %collective-permute-start.14 = (f32[5,1024]{1,0:T(8,128)S(1)}, f32[5,1024]{1,0:T(8,128)S(1)}, u32[]{:S(2)}, u32[]{:S(2)}) collective-permute-start(f32[5,1024]{1,0:T(8,128)S(1)} %log_add_fusion.3), channel_id=1, source_target_pairs={{0,2},{31,29},{32,34},{63,61},{64,66},{95,93},{96,98},{127,125}} | collective-permute-start | bytes 61448 | tf_op jit(solution)/shard_map/ppermute | solution.py:178
  98.0 7.5 %collective-permute-start.12 = (f32[7,1024]{1,0:T(8,128)S(1)}, f32[7,1024]{1,0:T(8,128)S(1)}, u32[]{:S(2)}, u32[]{:S(2)}) collective-permute-start(f32[7,1024]{1,0:T(8,128)S(1)} %log_add_fusion.2), channel_id=1, source_target_pairs={{0,3},{1,4},{2,5},{3,6},{4,7},{5,8},{6,9},{7,10},{8,11},{9,12},{10... | collective-permute-start | bytes 86024 | tf_op jit(solution)/shard_map/ppermute | solution.py:30
  120.2 8.8 %collective-permute-start.15 = (f32[4,1024]{1,0:T(4,128)S(1)}, f32[4,1024]{1,0:T(4,128)S(1)}, u32[]{:S(2)}, u32[]{:S(2)}) collective-permute-start(f32[4,1024]{1,0:T(4,128)S(1)} %pad_maximum_fusion.7), channel_id=1, source_target_pairs={{0,32},{32,64},{64,96},{1,33},{33,65},{65,97},{2,34},{34,66},{66,9... | collective-permute-start | bytes 49160 | tf_op jit(solution)/shard_map/ppermute | solution.py:30
  123.8 5.2 %collective-permute-start.16 = (f32[4,1024]{1,0:T(4,128)S(1)}, f32[4,1024]{1,0:T(4,128)S(1)}, u32[]{:S(2)}, u32[]{:S(2)}) collective-permute-start(f32[4,1024]{1,0:T(4,128)S(1)} %pad_maximum_fusion.7), channel_id=1, source_target_pairs={{32,0},{64,32},{96,64},{33,1},{65,33},{97,65},{34,2},{66,34},{98,6... | collective-permute-start | bytes 49160 | tf_op jit(solution)/shard_map/ppermute | solution.py:30
  125.1 5.0 %collective-permute-start.17 = (f32[3,1024]{1,0:T(4,128)S(1)}, f32[3,1024]{1,0:T(4,128)S(1)}, u32[]{:S(2)}, u32[]{:S(2)}) collective-permute-start(f32[3,1024]{1,0:T(4,128)S(1)} %log_add_fusion.7), channel_id=1, source_target_pairs={{0,64},{32,96},{64,0},{96,32},{1,65},{33,97},{65,1},{97,33},{2,66}... | collective-permute-start | bytes 36872 | tf_op jit(solution)/shard_map/ppermute | solution.py:143
  144.8 7.8 %collective-permute-start.18 = (f32[5,1024]{1,0:T(8,128)S(1)}, f32[5,1024]{1,0:T(8,128)S(1)}, u32[]{:S(2)}, u32[]{:S(2)}) collective-permute-start(f32[5,1024]{1,0:T(8,128)S(1)} %log_add_fusion.1), channel_id=1, source_target_pairs={{0,1},{1,2},{2,3},{3,4},{4,5},{5,6},{6,7},{7,8},{8,9},{9,10},{10,1... | collective-permute-start | bytes 61448 | tf_op jit(solution)/shard_map/ppermute | solution.py:30
  150.7 5.2 %collective-permute-start.19 = (f32[5,1024]{1,0:T(8,128)S(1)}, f32[5,1024]{1,0:T(8,128)S(1)}, u32[]{:S(2)}, u32[]{:S(2)}) collective-permute-start(f32[5,1024]{1,0:T(8,128)S(1)} %log_add_fusion.1), channel_id=1, source_target_pairs={{1,0},{2,1},{3,2},{4,3},{5,4},{6,5},{7,6},{8,7},{9,8},{10,9},{11,1... | collective-permute-start | bytes 61448 | tf_op jit(solution)/shard_map/ppermute | solution.py:30
  156.0 10.5 %collective-permute-start.21 = (f32[7,1024]{1,0:T(8,128)S(1)}, f32[7,1024]{1,0:T(8,128)S(1)}, u32[]{:S(2)}, u32[]{:S(2)}) collective-permute-start(f32[7,1024]{1,0:T(8,128)S(1)} %log_add_fusion), channel_id=1, source_target_pairs={{3,0},{4,1},{5,2},{6,3},{7,4},{8,5},{9,6},{10,7},{11,8},{12,9},{13... | collective-permute-start | bytes 86024 | tf_op jit(solution)/shard_map/ppermute | solution.py:30
  157.4 10.2 %collective-permute-start.22 = (f32[5,1024]{1,0:T(8,128)S(1)}, f32[5,1024]{1,0:T(8,128)S(1)}, u32[]{:S(2)}, u32[]{:S(2)}) collective-permute-start(f32[5,1024]{1,0:T(8,128)S(1)} %log_add_fusion.1), channel_id=1, source_target_pairs={{0,2},{31,29},{32,34},{63,61},{64,66},{95,93},{96,98},{127,125}} | collective-permute-start | bytes 61448 | tf_op jit(solution)/shard_map/ppermute | solution.py:178
  158.0 9.5 %collective-permute-start.20 = (f32[7,1024]{1,0:T(8,128)S(1)}, f32[7,1024]{1,0:T(8,128)S(1)}, u32[]{:S(2)}, u32[]{:S(2)}) collective-permute-start(f32[7,1024]{1,0:T(8,128)S(1)} %log_add_fusion), channel_id=1, source_target_pairs={{0,3},{1,4},{2,5},{3,6},{4,7},{5,8},{6,9},{7,10},{8,11},{9,12},{10... | collective-permute-start | bytes 86024 | tf_op jit(solution)/shard_map/ppermute | solution.py:30
  182.2 22.0 %collective-permute-start.23 = (f32[1,1024]{1,0:T(1,128)S(1)}, f32[1,1024]{1,0:T(1,128)S(1)}, u32[]{:S(2)}, u32[]{:S(2)}) collective-permute-start(f32[1,1024]{1,0:T(1,128)S(1)} %slice.265), channel_id=1, source_target_pairs={{0,16},{1,17},{2,18},{3,19},{4,20},{5,21},{6,22},{7,23},{8,24},{9,... | collective-permute-start | bytes 12296 | tf_op jit(solution)/shard_map/ppermute | solution.py:208
  193.4 11.8 %collective-permute-start.28 = (f32[4,1024]{1,0:T(4,128)S(1)}, f32[4,1024]{1,0:T(4,128)S(1)}, u32[]{:S(2)}, u32[]{:S(2)}) collective-permute-start(f32[4,1024]{1,0:T(4,128)S(1)} %pad_maximum_fusion.6), channel_id=1, source_target_pairs={{0,32},{32,64},{64,96},{1,33},{33,65},{65,97},{2,34},{34,66},{66,9... | collective-permute-start | bytes 49160 | tf_op jit(solution)/shard_map/ppermute | solution.py:30
  197.0 8.1 %collective-permute-start.29 = (f32[4,1024]{1,0:T(4,128)S(1)}, f32[4,1024]{1,0:T(4,128)S(1)}, u32[]{:S(2)}, u32[]{:S(2)}) collective-permute-start(f32[4,1024]{1,0:T(4,128)S(1)} %pad_maximum_fusion.6), channel_id=1, source_target_pairs={{32,0},{64,32},{96,64},{33,1},{65,33},{97,65},{34,2},{66,34},{98,6... | collective-permute-start | bytes 49160 | tf_op jit(solution)/shard_map/ppermute | solution.py:30
  198.3 6.9 %collective-permute-start.30 = (f32[3,1024]{1,0:T(4,128)S(1)}, f32[3,1024]{1,0:T(4,128)S(1)}, u32[]{:S(2)}, u32[]{:S(2)}) collective-permute-start(f32[3,1024]{1,0:T(4,128)S(1)} %log_add_fusion.6), channel_id=1, source_target_pairs={{0,64},{32,96},{64,0},{96,32},{1,65},{33,97},{65,1},{97,33},{2,66}... | collective-permute-start | bytes 36872 | tf_op jit(solution)/shard_map/ppermute | solution.py:143
  204.2 32.5 %collective-permute-start.24 = (f32[2,1024]{1,0:T(2,128)S(1)}, f32[2,1024]{1,0:T(2,128)S(1)}, u32[]{:S(2)}, u32[]{:S(2)}) collective-permute-start(f32[2,1024]{1,0:T(2,128)S(1)} %maximum_select_fusion.4), channel_id=1, source_target_pairs={{0,8},{1,9},{2,10},{3,11},{4,12},{5,13},{6,14},{7,15},{8,0},{9,1},... | collective-permute-start | bytes 24584 | tf_op jit(solution)/shard_map/ppermute | solution.py:208
  222.9 33.7 %collective-permute-start.31 = (f32[1,1024,128]{2,1,0:T(8,128)}, f32[1,1024,128]{2,1,0:T(8,128)S(1)}, u32[]{:S(2)}, u32[]{:S(2)}) collective-permute-start(f32[1,1024,128]{2,1,0:T(8,128)} %get-tuple-element.5), channel_id=1, source_target_pairs={{1,0},{2,1},{3,2},{4,3},{5,4},{6,5},{7,6},{8,7},{9,8},{10,9},{11,1... | collective-permute-start | bytes 1572872 | tf_op jit(solution)/shard_map/ppermute | solution.py:30
  224.8 31.8 %collective-permute-start.32 = (f32[1,1024,128]{2,1,0:T(8,128)}, f32[1,1024,128]{2,1,0:T(8,128)}, u32[]{:S(2)}, u32[]{:S(2)}) collective-permute-start(f32[1,1024,128]{2,1,0:T(8,128)} %get-tuple-element.8), channel_id=1, source_target_pairs={{0,1},{1,2},{2,3},{3,4},{4,5},{5,6},{6,7},{7,8},{8,9},{9,10},{10,1... | collective-permute-start | bytes 1572872 | tf_op jit(solution)/shard_map/ppermute | solution.py:30
  230.6 26.1 %collective-permute-start.33 = (f32[1,1024,128]{2,1,0:T(8,128)}, f32[1,1024,128]{2,1,0:T(8,128)}, u32[]{:S(2)}, u32[]{:S(2)}) collective-permute-start(f32[1,1024,128]{2,1,0:T(8,128)} %get-tuple-element.7), channel_id=1, source_target_pairs={{2,0},{3,1},{4,2},{5,3},{6,4},{7,5},{8,6},{9,7},{10,8},{11,9},{12,... | collective-permute-start | bytes 1572872 | tf_op jit(solution)/shard_map/ppermute | solution.py:30
  231.9 24.8 %collective-permute-start.34 = (f32[1,1024,128]{2,1,0:T(8,128)}, f32[1,1024,128]{2,1,0:T(8,128)}, u32[]{:S(2)}, u32[]{:S(2)}) collective-permute-start(f32[1,1024,128]{2,1,0:T(8,128)} %get-tuple-element.6), channel_id=1, source_target_pairs={{0,2},{1,3},{2,4},{3,5},{4,6},{5,7},{6,8},{7,9},{8,10},{9,11},{10,... | collective-permute-start | bytes 1572872 | tf_op jit(solution)/shard_map/ppermute | solution.py:30
  236.7 12.2 %collective-permute-start.25 = (f32[4,1024]{1,0:T(4,128)S(1)}, f32[4,1024]{1,0:T(4,128)S(1)}, u32[]{:S(2)}, u32[]{:S(2)}) collective-permute-start(f32[4,1024]{1,0:T(4,128)S(1)} %maximum_select_fusion.3), channel_id=1, source_target_pairs={{0,4},{1,5},{2,6},{3,7},{4,0},{5,1},{6,2},{7,3},{8,12},{9,13},{10,... | collective-permute-start | bytes 49160 | tf_op jit(solution)/shard_map/ppermute | solution.py:208
  (10 other events, 136.9 us)

commit v10 on v8

--- a/solution.py
+++ b/solution.py
@@ -30,10 +30,6 @@
     return lax.ppermute(block, axis, route)
 
 
-def pick(table, position):
-    return lax.dynamic_index_in_dim(table, position, 0, keepdims=False)
-
-
 def squares(points):
     return jnp.sum(jnp.square(points.astype(jnp.float32)), axis=-1)
 
@@ -46,6 +42,7 @@
 EPSILON = 0.03
 INV_EPS = 1.0 / EPSILON
 CHUNK = 1024
+GRAD_CHUNK = 512
 KERNEL_PARAMS = pltpu.CompilerParams()
 
 
@@ -100,14 +97,14 @@
     cols = b_pts.shape[1]
     spec = pltpu.PrefetchScalarGridSpec(
         num_scalar_prefetch=2,
-        grid=(pairs, rows // CHUNK),
+        grid=(pairs, rows // GRAD_CHUNK),
         in_specs=[
-            pl.BlockSpec((1, CHUNK, coords), lambda p, c, ai, bi: (ai[p], c, 0)),
+            pl.BlockSpec((1, GRAD_CHUNK, coords), lambda p, c, ai, bi: (ai[p], c, 0)),
             pl.BlockSpec((1, cols, coords), lambda p, c, ai, bi: (bi[p], 0, 0)),
             pl.BlockSpec((1, 1, cols), lambda p, c, ai, bi: (p, 0, 0)),
-            pl.BlockSpec((1, CHUNK, 1), lambda p, c, ai, bi: (p, c, 0)),
+            pl.BlockSpec((1, GRAD_CHUNK, 1), lambda p, c, ai, bi: (p, c, 0)),
         ],
-        out_specs=pl.BlockSpec((1, CHUNK, coords), lambda p, c, ai, bi: (p, c, 0)),
+        out_specs=pl.BlockSpec((1, GRAD_CHUNK, coords), lambda p, c, ai, bi: (p, c, 0)),
     )
     return pl.pallas_call(
         _grad_kernel,
@@ -233,7 +230,7 @@
     span_ids = jnp.clip(source_local - (gy_index - 2) * owned, 0, 5 * owned - 1)
     span_mask = span_ids[None, :] == jnp.arange(5 * owned, dtype=jnp.int32)[:, None]
     window_mask = window_ids[None, :] == jnp.arange(3 * owned, dtype=jnp.int32)[:, None]
-    pair_src_sq = jnp.stack([squares(pick(src_points, source_local[p])) for p in range(source_local.shape[0])])
+    pair_src_sq = squares(src_points[source_local])
     window_pts, window_sq = fetch_points(tgt_points)
     pair_tgt_sq = window_sq[window_ids]
     mass_pad = jnp.zeros((2 * owned,) + src_log_mass.shape[1:], src_log_mass.dtype)

time: 271 us -> 263 us (0.970)
  between operations: 13.1 us -> 1.69 us
  local copies, waits for them, and re-layouts: 14.1 us -> 17.8 us
  other arithmetic: 20.9 us -> 17.5 us
  Pallas kernels: 84.8 us -> 87.9 us
    gather x0 -> x1, local copies, waits for them, and re-layouts: none -> 4.23 us  [body(): pair_src_sq = squares(src_points[source_local])]
    pallas_call x1, Pallas kernels: 11.1 us -> 14.3 us  [pair_grad(): pl.pallas_call(_grad_kernel, grid_spec=spec, out_shape=jax.ShapeDtypeStru...]
  transfers between devices with their start and end apart: 35 -> 35, of which waited for: 11 -> 11; matrix products, arithmetic and copies ran while one was open for 7% -> 7% of each run, Pallas kernels for 4% -> 5%
where the time goes in v10:
time: 263 us; the launch traced here: 261 us
  starting transfers between devices  107 us (41%)
  Pallas kernels  87.9 us (33%)
  waiting for transfers between devices  28.5 us (11%)
  local copies, waits for them, and re-layouts  17.8 us (7%)
  other arithmetic  17.5 us (7%)
    ppermute x22, starting transfers between devices, passed_along(): return lax.ppermute(block, axis, route)  75.6 us
    pallas_call x6, Pallas kernels, pair_lse(): pl.pallas_call(_lse_kernel, grid_spec=spec, out_shape=jax.ShapeDtypeStruc...  73.7 us
    pallas_call x1, Pallas kernels, pair_grad(): pl.pallas_call(_grad_kernel, grid_spec=spec, out_shape=jax.ShapeDtypeStru...  14.3 us
    ppermute x5, waiting for transfers between devices, gather_rows(): other = lax.ppermute(block, axis, route)  13.4 us
    ppermute x22, waiting for transfers between devices, passed_along(): return lax.ppermute(block, axis, route)  12.8 us
    ppermute x5, starting transfers between devices, gather_rows(): other = lax.ppermute(block, axis, route)  12.8 us
    ppermute x3, starting transfers between devices, spread(): lax.ppermute(block, axis, [(i, (i + reach) % count) for i in range(count)])  11.3 us
  transfers between devices with their start and end apart: 35, of which 11 were waited for; matrix products, arithmetic and copies ran while one was open for 7% of the time, Pallas kernels for 5%

profile of v10, /device:TPU:1, one launch (start us, length us, event | category | flops | bytes accessed | tf_op | source)
XLA Modules:
  0.0 260.5 jit_solution(1492358458881588652)
XLA Ops:
  0.6 4.1 %collective-permute-start = (bf16[1,1024,128]{2,1,0:T(8,128)(2,1)}, bf16[1,1024,128]{2,1,0:T(8,128)(2,1)S(1)}, u32[]{:S(2)}, u32[]{:S(2)}) collective-permute-start(bf16[1,1024,128]{2,1,0:T(8,128)(2,1)} %param.7), channel_id=1, source_target_pairs={{0,32},{32,64},{64,96},{1,33},{33,65},{65,97},{2,34},{34,66},{66,9... | collective-permute-start | bytes 786440 | tf_op jit(solution)/shard_map/ppermute | solution.py:19
  8.2 4.2 %gather_fusion.2 = bf16[6,1024,128]{2,1,0:T(8,128)(2,1)S(1)} fusion(bf16[32,1024,128]{2,1,0:T(8,128)(2,1)} %a_ref.7, s32[1024]{0:T(1024)S(1)} %get-tuple-element.52), kind=kCustom, calls=%fused_computation.2 | custom fusion | bytes 3145752 | tf_op jit(solution)/shard_map/gather | solution.py:233
  15.9 12.4 %shard_map.85 = f32[6,1,1024]{2,1,0:T(1,128)} custom-call(s32[6]{0:T(128)} %bitcast.100, s32[6]{0:T(128)} %get-tuple-element.49.b_ids.a_ids, bf16[32,1024,128]{2,1,0:T(8,128)(2,1)} %a_ref.7, bf16[3,1024,128]{2,1,0:T(8,128)(2,1)} %copy-done, f32[6,8,1024]{2,1,0:T(8,128)} %broadcast_in_dim.240.v_ref), custom_call_target="tpu_custom_call" | custom-call | tf_op jit(solution)/shard_map/pallas_call | solution.py:74
  29.3 4.6 %collective-permute-start.2 = (f32[5,1024]{1,0:T(8,128)S(1)}, f32[5,1024]{1,0:T(8,128)S(1)}, u32[]{:S(2)}, u32[]{:S(2)}) collective-permute-start(f32[5,1024]{1,0:T(8,128)S(1)} %log_add_fusion.5), channel_id=1, source_target_pairs={{0,1},{1,2},{2,3},{3,4},{4,5},{5,6},{6,7},{7,8},{8,9},{9,10},{10,1... | collective-permute-start | bytes 61448 | tf_op jit(solution)/shard_map/ppermute | solution.py:30
  35.9 3.3 %collective-permute-done.3 = f32[5,1024]{1,0:T(8,128)S(1)} collective-permute-done((f32[5,1024]{1,0:T(8,128)S(1)}, f32[5,1024]{1,0:T(8,128)S(1)}, u32[]{:S(2)}, u32[]{:S(2)}) %collective-permute-start.3) | collective-permute-done | bytes 20512 | tf_op jit(solution)/shard_map/ppermute | solution.py:30
  41.3 5.8 %collective-permute-start.4 = (f32[7,1024]{1,0:T(8,128)S(1)}, f32[7,1024]{1,0:T(8,128)S(1)}, u32[]{:S(2)}, u32[]{:S(2)}) collective-permute-start(f32[7,1024]{1,0:T(8,128)S(1)} %log_add_fusion.4), channel_id=1, source_target_pairs={{0,3},{1,4},{2,5},{3,6},{4,7},{5,8},{6,9},{7,10},{8,11},{9,12},{10... | collective-permute-start | bytes 86024 | tf_op jit(solution)/shard_map/ppermute | solution.py:30
  49.5 12.4 %shard_map.86 = f32[6,1,1024]{2,1,0:T(1,128)} custom-call(s32[6]{0:T(128)} %get-tuple-element.49.b_ids.a_ids, s32[6]{0:T(128)} %bitcast.101, bf16[3,1024,128]{2,1,0:T(8,128)(2,1)} %copy-done, bf16[32,1024,128]{2,1,0:T(8,128)(2,1)} %a_ref.7, f32[6,8,1024]{2,1,0:T(8,128)} %broadcast_in_dim.244.v_ref), custom_call_target="tpu_custom_call" | custom-call | tf_op jit(solution)/shard_map/pallas_call | solution.py:74
  62.9 3.7 %collective-permute-start.7 = (f32[4,1024]{1,0:T(4,128)S(1)}, f32[4,1024]{1,0:T(4,128)S(1)}, u32[]{:S(2)}, u32[]{:S(2)}) collective-permute-start(f32[4,1024]{1,0:T(4,128)S(1)} %pad_maximum_fusion.8), channel_id=1, source_target_pairs={{0,32},{32,64},{64,96},{1,33},{33,65},{65,97},{2,34},{34,66},{66,9... | collective-permute-start | bytes 49160 | tf_op jit(solution)/shard_map/ppermute | solution.py:30
  68.0 3.7 %collective-permute-start.9 = (f32[3,1024]{1,0:T(4,128)S(1)}, f32[3,1024]{1,0:T(4,128)S(1)}, u32[]{:S(2)}, u32[]{:S(2)}) collective-permute-start(f32[3,1024]{1,0:T(4,128)S(1)} %log_add_fusion.8), channel_id=1, source_target_pairs={{0,64},{32,96},{64,0},{96,32},{1,65},{33,97},{65,1},{97,33},{2,66}... | collective-permute-start | bytes 36872 | tf_op jit(solution)/shard_map/ppermute | solution.py:144
  74.3 12.2 %shard_map.87 = f32[6,1,1024]{2,1,0:T(1,128)} custom-call(s32[6]{0:T(128)} %bitcast.102, s32[6]{0:T(128)} %get-tuple-element.49.b_ids.a_ids, bf16[32,1024,128]{2,1,0:T(8,128)(2,1)} %a_ref.7, bf16[3,1024,128]{2,1,0:T(8,128)(2,1)} %copy-done, f32[6,8,1024]{2,1,0:T(8,128)} %broadcast_in_dim.249.v_ref), custom_call_target="tpu_custom_call" | custom-call | tf_op jit(solution)/shard_map/pallas_call | solution.py:74
  87.5 3.2 %collective-permute-start.10 = (f32[5,1024]{1,0:T(8,128)S(1)}, f32[5,1024]{1,0:T(8,128)S(1)}, u32[]{:S(2)}, u32[]{:S(2)}) collective-permute-start(f32[5,1024]{1,0:T(8,128)S(1)} %log_add_fusion.3), channel_id=1, source_target_pairs={{0,1},{1,2},{2,3},{3,4},{4,5},{5,6},{6,7},{7,8},{8,9},{9,10},{10,1... | collective-permute-start | bytes 61448 | tf_op jit(solution)/shard_map/ppermute | solution.py:30
  92.7 3.3 %collective-permute-done.11 = f32[5,1024]{1,0:T(8,128)S(1)} collective-permute-done((f32[5,1024]{1,0:T(8,128)S(1)}, f32[5,1024]{1,0:T(8,128)S(1)}, u32[]{:S(2)}, u32[]{:S(2)}) %collective-permute-start.11) | collective-permute-done | bytes 20512 | tf_op jit(solution)/shard_map/ppermute | solution.py:30
  98.0 6.4 %collective-permute-start.12 = (f32[7,1024]{1,0:T(8,128)S(1)}, f32[7,1024]{1,0:T(8,128)S(1)}, u32[]{:S(2)}, u32[]{:S(2)}) collective-permute-start(f32[7,1024]{1,0:T(8,128)S(1)} %log_add_fusion.2), channel_id=1, source_target_pairs={{0,3},{1,4},{2,5},{3,6},{4,7},{5,8},{6,9},{7,10},{8,11},{9,12},{10... | collective-permute-start | bytes 86024 | tf_op jit(solution)/shard_map/ppermute | solution.py:30
  106.9 12.2 %shard_map.88 = f32[6,1,1024]{2,1,0:T(1,128)} custom-call(s32[6]{0:T(128)} %get-tuple-element.49.b_ids.a_ids, s32[6]{0:T(128)} %bitcast.103, bf16[3,1024,128]{2,1,0:T(8,128)(2,1)} %copy-done, bf16[32,1024,128]{2,1,0:T(8,128)(2,1)} %a_ref.7, f32[6,8,1024]{2,1,0:T(8,128)} %broadcast_in_dim.251.v_ref), custom_call_target="tpu_custom_call" | custom-call | tf_op jit(solution)/shard_map/pallas_call | solution.py:74
  120.2 3.6 %collective-permute-start.15 = (f32[4,1024]{1,0:T(4,128)S(1)}, f32[4,1024]{1,0:T(4,128)S(1)}, u32[]{:S(2)}, u32[]{:S(2)}) collective-permute-start(f32[4,1024]{1,0:T(4,128)S(1)} %pad_maximum_fusion.7), channel_id=1, source_target_pairs={{0,32},{32,64},{64,96},{1,33},{33,65},{65,97},{2,34},{34,66},{66,9... | collective-permute-start | bytes 49160 | tf_op jit(solution)/shard_map/ppermute | solution.py:30
  125.1 3.9 %collective-permute-start.17 = (f32[3,1024]{1,0:T(4,128)S(1)}, f32[3,1024]{1,0:T(4,128)S(1)}, u32[]{:S(2)}, u32[]{:S(2)}) collective-permute-start(f32[3,1024]{1,0:T(4,128)S(1)} %log_add_fusion.7), channel_id=1, source_target_pairs={{0,64},{32,96},{64,0},{96,32},{1,65},{33,97},{65,1},{97,33},{2,66}... | collective-permute-start | bytes 36872 | tf_op jit(solution)/shard_map/ppermute | solution.py:144
  131.5 12.2 %shard_map.89 = f32[6,1,1024]{2,1,0:T(1,128)} custom-call(s32[6]{0:T(128)} %bitcast.104, s32[6]{0:T(128)} %get-tuple-element.49.b_ids.a_ids, bf16[32,1024,128]{2,1,0:T(8,128)(2,1)} %a_ref.7, bf16[3,1024,128]{2,1,0:T(8,128)(2,1)} %copy-done, f32[6,8,1024]{2,1,0:T(8,128)} %broadcast_in_dim.253.v_ref), custom_call_target="tpu_custom_call" | custom-call | tf_op jit(solution)/shard_map/pallas_call | solution.py:74
  144.8 5.9 %collective-permute-start.18 = (f32[5,1024]{1,0:T(8,128)S(1)}, f32[5,1024]{1,0:T(8,128)S(1)}, u32[]{:S(2)}, u32[]{:S(2)}) collective-permute-start(f32[5,1024]{1,0:T(8,128)S(1)} %log_add_fusion.1), channel_id=1, source_target_pairs={{0,1},{1,2},{2,3},{3,4},{4,5},{5,6},{6,7},{7,8},{8,9},{9,10},{10,1... | collective-permute-start | bytes 61448 | tf_op jit(solution)/shard_map/ppermute | solution.py:30
  152.6 3.3 %collective-permute-done.19 = f32[5,1024]{1,0:T(8,128)S(1)} collective-permute-done((f32[5,1024]{1,0:T(8,128)S(1)}, f32[5,1024]{1,0:T(8,128)S(1)}, u32[]{:S(2)}, u32[]{:S(2)}) %collective-permute-start.19) | collective-permute-done | bytes 20512 | tf_op jit(solution)/shard_map/ppermute | solution.py:30
  158.0 8.5 %collective-permute-start.20 = (f32[7,1024]{1,0:T(8,128)S(1)}, f32[7,1024]{1,0:T(8,128)S(1)}, u32[]{:S(2)}, u32[]{:S(2)}) collective-permute-start(f32[7,1024]{1,0:T(8,128)S(1)} %log_add_fusion), channel_id=1, source_target_pairs={{0,3},{1,4},{2,5},{3,6},{4,7},{5,8},{6,9},{7,10},{8,11},{9,12},{10... | collective-permute-start | bytes 86024 | tf_op jit(solution)/shard_map/ppermute | solution.py:30
  168.9 12.2 %shard_map.90 = f32[6,1,1024]{2,1,0:T(1,128)} custom-call(s32[6]{0:T(128)} %get-tuple-element.49.b_ids.a_ids, s32[6]{0:T(128)} %bitcast.105, bf16[3,1024,128]{2,1,0:T(8,128)(2,1)} %copy-done, bf16[32,1024,128]{2,1,0:T(8,128)(2,1)} %a_ref.7, f32[6,8,1024]{2,1,0:T(8,128)} %broadcast_in_dim.255.v_ref), custom_call_target="tpu_custom_call" | custom-call | tf_op jit(solution)/shard_map/pallas_call | solution.py:74
  182.9 3.6 %collective-permute-start.28 = (f32[4,1024]{1,0:T(4,128)S(1)}, f32[4,1024]{1,0:T(4,128)S(1)}, u32[]{:S(2)}, u32[]{:S(2)}) collective-permute-start(f32[4,1024]{1,0:T(4,128)S(1)} %pad_maximum_fusion.6), channel_id=1, source_target_pairs={{0,32},{32,64},{64,96},{1,33},{33,65},{65,97},{2,34},{34,66},{66,9... | collective-permute-start | bytes 49160 | tf_op jit(solution)/shard_map/ppermute | solution.py:30
  187.8 3.7 %collective-permute-start.30 = (f32[3,1024]{1,0:T(4,128)S(1)}, f32[3,1024]{1,0:T(4,128)S(1)}, u32[]{:S(2)}, u32[]{:S(2)}) collective-permute-start(f32[3,1024]{1,0:T(4,128)S(1)} %log_add_fusion.6), channel_id=1, source_target_pairs={{0,64},{32,96},{64,0},{96,32},{1,65},{33,97},{65,1},{97,33},{2,66}... | collective-permute-start | bytes 36872 | tf_op jit(solution)/shard_map/ppermute | solution.py:144
  193.8 2.4 collective-permute-start.24
  197.5 14.3 %shard_map.91 = f32[6,1024,128]{2,1,0:T(8,128)} custom-call(s32[6]{0:T(128)} %bitcast.106, s32[6]{0:T(128)} %get-tuple-element.49.b_ids.a_ids, bf16[32,1024,128]{2,1,0:T(8,128)(2,1)} %a_ref.7, bf16[3,1024,128]{2,1,0:T(8,128)(2,1)} %copy-done, f32[6,1,1024]{2,1,0:T(1,128)} %div.120.v_ref, f32[6,1024,1]{2,1,0:T(8,128)} %copy.11.w_ref), custom_call_target="tpu_custom_call" | custom-call | tf_op jit(solution)/shard_map/pallas_call | solution.py:109
  211.8 3.8 %select_reduce_fusion = f32[5,1024,128]{2,1,0:T(8,128)S(1)} fusion(f32[6,1024,128]{2,1,0:T(8,128)} %shard_map.91, pred[5,6]{1,0:T(8,128)(4,1)S(1)} %iota_compare_fusion.1), kind=kLoop, calls=%fused_computation.9 | loop fusion | flops 7208960 | bytes 5767198 | tf_op jit(solution)/shard_map/reduce_sum | solution.py:264
  216.9 3.5 %collective-permute-start.31 = (f32[1,1024,128]{2,1,0:T(8,128)}, f32[1,1024,128]{2,1,0:T(8,128)S(1)}, u32[]{:S(2)}, u32[]{:S(2)}) collective-permute-start(f32[1,1024,128]{2,1,0:T(8,128)} %get-tuple-element.5), channel_id=1, source_target_pairs={{1,0},{2,1},{3,2},{4,3},{5,4},{6,5},{7,6},{8,7},{9,8},{10,9},{11,1... | collective-permute-start | bytes 1572872 | tf_op jit(solution)/shard_map/ppermute | solution.py:30
  223.8 10.0 %collective-permute-start.34 = (f32[1,1024,128]{2,1,0:T(8,128)}, f32[1,1024,128]{2,1,0:T(8,128)}, u32[]{:S(2)}, u32[]{:S(2)}) collective-permute-start(f32[1,1024,128]{2,1,0:T(8,128)} %get-tuple-element.6), channel_id=1, source_target_pairs={{0,2},{1,3},{2,4},{3,5},{4,6},{5,7},{6,8},{7,9},{8,10},{9,11},{10,... | collective-permute-start | bytes 1572872 | tf_op jit(solution)/shard_map/ppermute | solution.py:30
  233.8 4.2 %collective-permute-start.25 = (f32[4,1024]{1,0:T(4,128)S(1)}, f32[4,1024]{1,0:T(4,128)S(1)}, u32[]{:S(2)}, u32[]{:S(2)}) collective-permute-start(f32[4,1024]{1,0:T(4,128)S(1)} %maximum_select_fusion.3), channel_id=1, source_target_pairs={{0,4},{1,5},{2,6},{3,7},{4,0},{5,1},{6,2},{7,3},{8,12},{9,13},{10,... | collective-permute-start | bytes 49160 | tf_op jit(solution)/shard_map/ppermute | solution.py:208
  238.0 10.9 %collective-permute-done.25 = f32[4,1024]{1,0:T(4,128)S(1)} collective-permute-done((f32[4,1024]{1,0:T(4,128)S(1)}, f32[4,1024]{1,0:T(4,128)S(1)}, u32[]{:S(2)}, u32[]{:S(2)}) %collective-permute-start.25) | collective-permute-done | bytes 16416 | tf_op jit(solution)/shard_map/ppermute | solution.py:208
  252.3 3.5 %collective-permute-start.27 = (f32[16,1024]{1,0:T(8,128)S(1)}, f32[16,1024]{1,0:T(8,128)S(1)}, u32[]{:S(2)}, u32[]{:S(2)}) collective-permute-start(f32[16,1024]{1,0:T(8,128)S(1)} %maximum_select_fusion.1), channel_id=1, source_target_pairs={{0,16},{1,17},{2,18},{3,19},{4,20},{5,21},{6,22},{7,23},{8,24},{9,... | collective-permute-start | bytes 196616 | tf_op jit(solution)/shard_map/ppermute | solution.py:208
  258.3 2.3 fusion.2
  (186 shorter events, 55.7 us)
Async XLA Ops:
  0.6 13.3 %collective-permute-start = (bf16[1,1024,128]{2,1,0:T(8,128)(2,1)}, bf16[1,1024,128]{2,1,0:T(8,128)(2,1)S(1)}, u32[]{:S(2)}, u32[]{:S(2)}) collective-permute-start(bf16[1,1024,128]{2,1,0:T(8,128)(2,1)} %param.7), channel_id=1, source_target_pairs={{0,32},{32,64},{64,96},{1,33},{33,65},{65,97},{2,34},{34,66},{66,9... | collective-permute-start | bytes 786440 | tf_op jit(solution)/shard_map/ppermute | solution.py:19
  4.7 9.3 %collective-permute-start.1 = (bf16[1,1024,128]{2,1,0:T(8,128)(2,1)}, bf16[1,1024,128]{2,1,0:T(8,128)(2,1)S(1)}, u32[]{:S(2)}, u32[]{:S(2)}) collective-permute-start(bf16[1,1024,128]{2,1,0:T(8,128)(2,1)} %param.7), channel_id=1, source_target_pairs={{32,0},{64,32},{96,64},{33,1},{65,33},{97,65},{34,2},{66,34},{98,6... | collective-permute-start | bytes 786440 | tf_op jit(solution)/shard_map/ppermute | solution.py:22
  29.3 6.5 %collective-permute-start.2 = (f32[5,1024]{1,0:T(8,128)S(1)}, f32[5,1024]{1,0:T(8,128)S(1)}, u32[]{:S(2)}, u32[]{:S(2)}) collective-permute-start(f32[5,1024]{1,0:T(8,128)S(1)} %log_add_fusion.5), channel_id=1, source_target_pairs={{0,1},{1,2},{2,3},{3,4},{4,5},{5,6},{6,7},{7,8},{8,9},{9,10},{10,1... | collective-permute-start | bytes 61448 | tf_op jit(solution)/shard_map/ppermute | solution.py:30
  33.9 5.2 %collective-permute-start.3 = (f32[5,1024]{1,0:T(8,128)S(1)}, f32[5,1024]{1,0:T(8,128)S(1)}, u32[]{:S(2)}, u32[]{:S(2)}) collective-permute-start(f32[5,1024]{1,0:T(8,128)S(1)} %log_add_fusion.5), channel_id=1, source_target_pairs={{1,0},{2,1},{3,2},{4,3},{5,4},{6,5},{7,6},{8,7},{9,8},{10,9},{11,1... | collective-permute-start | bytes 61448 | tf_op jit(solution)/shard_map/ppermute | solution.py:30
  39.2 7.8 %collective-permute-start.5 = (f32[7,1024]{1,0:T(8,128)S(1)}, f32[7,1024]{1,0:T(8,128)S(1)}, u32[]{:S(2)}, u32[]{:S(2)}) collective-permute-start(f32[7,1024]{1,0:T(8,128)S(1)} %log_add_fusion.4), channel_id=1, source_target_pairs={{3,0},{4,1},{5,2},{6,3},{7,4},{8,5},{9,6},{10,7},{11,8},{12,9},{13... | collective-permute-start | bytes 86024 | tf_op jit(solution)/shard_map/ppermute | solution.py:30
  40.6 7.5 %collective-permute-start.6 = (f32[5,1024]{1,0:T(8,128)S(1)}, f32[5,1024]{1,0:T(8,128)S(1)}, u32[]{:S(2)}, u32[]{:S(2)}) collective-permute-start(f32[5,1024]{1,0:T(8,128)S(1)} %log_add_fusion.5), channel_id=1, source_target_pairs={{0,2},{31,29},{32,34},{63,61},{64,66},{95,93},{96,98},{127,125}} | collective-permute-start | bytes 61448 | tf_op jit(solution)/shard_map/ppermute | solution.py:179
  41.3 6.8 %collective-permute-start.4 = (f32[7,1024]{1,0:T(8,128)S(1)}, f32[7,1024]{1,0:T(8,128)S(1)}, u32[]{:S(2)}, u32[]{:S(2)}) collective-permute-start(f32[7,1024]{1,0:T(8,128)S(1)} %log_add_fusion.4), channel_id=1, source_target_pairs={{0,3},{1,4},{2,5},{3,6},{4,7},{5,8},{6,9},{7,10},{8,11},{9,12},{10... | collective-permute-start | bytes 86024 | tf_op jit(solution)/shard_map/ppermute | solution.py:30
  62.9 8.8 %collective-permute-start.7 = (f32[4,1024]{1,0:T(4,128)S(1)}, f32[4,1024]{1,0:T(4,128)S(1)}, u32[]{:S(2)}, u32[]{:S(2)}) collective-permute-start(f32[4,1024]{1,0:T(4,128)S(1)} %pad_maximum_fusion.8), channel_id=1, source_target_pairs={{0,32},{32,64},{64,96},{1,33},{33,65},{65,97},{2,34},{34,66},{66,9... | collective-permute-start | bytes 49160 | tf_op jit(solution)/shard_map/ppermute | solution.py:30
  87.5 5.1 %collective-permute-start.10 = (f32[5,1024]{1,0:T(8,128)S(1)}, f32[5,1024]{1,0:T(8,128)S(1)}, u32[]{:S(2)}, u32[]{:S(2)}) collective-permute-start(f32[5,1024]{1,0:T(8,128)S(1)} %log_add_fusion.3), channel_id=1, source_target_pairs={{0,1},{1,2},{2,3},{3,4},{4,5},{5,6},{6,7},{7,8},{8,9},{9,10},{10,1... | collective-permute-start | bytes 61448 | tf_op jit(solution)/shard_map/ppermute | solution.py:30
  90.7 5.2 %collective-permute-start.11 = (f32[5,1024]{1,0:T(8,128)S(1)}, f32[5,1024]{1,0:T(8,128)S(1)}, u32[]{:S(2)}, u32[]{:S(2)}) collective-permute-start(f32[5,1024]{1,0:T(8,128)S(1)} %log_add_fusion.3), channel_id=1, source_target_pairs={{1,0},{2,1},{3,2},{4,3},{5,4},{6,5},{7,6},{8,7},{9,8},{10,9},{11,1... | collective-permute-start | bytes 61448 | tf_op jit(solution)/shard_map/ppermute | solution.py:30
  96.1 8.4 %collective-permute-start.13 = (f32[7,1024]{1,0:T(8,128)S(1)}, f32[7,1024]{1,0:T(8,128)S(1)}, u32[]{:S(2)}, u32[]{:S(2)}) collective-permute-start(f32[7,1024]{1,0:T(8,128)S(1)} %log_add_fusion.2), channel_id=1, source_target_pairs={{3,0},{4,1},{5,2},{6,3},{7,4},{8,5},{9,6},{10,7},{11,8},{12,9},{13... | collective-permute-start | bytes 86024 | tf_op jit(solution)/shard_map/ppermute | solution.py:30
  97.4 8.1 %collective-permute-start.14 = (f32[5,1024]{1,0:T(8,128)S(1)}, f32[5,1024]{1,0:T(8,128)S(1)}, u32[]{:S(2)}, u32[]{:S(2)}) collective-permute-start(f32[5,1024]{1,0:T(8,128)S(1)} %log_add_fusion.3), channel_id=1, source_target_pairs={{0,2},{31,29},{32,34},{63,61},{64,66},{95,93},{96,98},{127,125}} | collective-permute-start | bytes 61448 | tf_op jit(solution)/shard_map/ppermute | solution.py:179
  98.0 7.5 %collective-permute-start.12 = (f32[7,1024]{1,0:T(8,128)S(1)}, f32[7,1024]{1,0:T(8,128)S(1)}, u32[]{:S(2)}, u32[]{:S(2)}) collective-permute-start(f32[7,1024]{1,0:T(8,128)S(1)} %log_add_fusion.2), channel_id=1, source_target_pairs={{0,3},{1,4},{2,5},{3,6},{4,7},{5,8},{6,9},{7,10},{8,11},{9,12},{10... | collective-permute-start | bytes 86024 | tf_op jit(solution)/shard_map/ppermute | solution.py:30
  120.2 8.8 %collective-permute-start.15 = (f32[4,1024]{1,0:T(4,128)S(1)}, f32[4,1024]{1,0:T(4,128)S(1)}, u32[]{:S(2)}, u32[]{:S(2)}) collective-permute-start(f32[4,1024]{1,0:T(4,128)S(1)} %pad_maximum_fusion.7), channel_id=1, source_target_pairs={{0,32},{32,64},{64,96},{1,33},{33,65},{65,97},{2,34},{34,66},{66,9... | collective-permute-start | bytes 49160 | tf_op jit(solution)/shard_map/ppermute | solution.py:30
  123.8 5.2 %collective-permute-start.16 = (f32[4,1024]{1,0:T(4,128)S(1)}, f32[4,1024]{1,0:T(4,128)S(1)}, u32[]{:S(2)}, u32[]{:S(2)}) collective-permute-start(f32[4,1024]{1,0:T(4,128)S(1)} %pad_maximum_fusion.7), channel_id=1, source_target_pairs={{32,0},{64,32},{96,64},{33,1},{65,33},{97,65},{34,2},{66,34},{98,6... | collective-permute-start | bytes 49160 | tf_op jit(solution)/shard_map/ppermute | solution.py:30
  125.1 5.0 %collective-permute-start.17 = (f32[3,1024]{1,0:T(4,128)S(1)}, f32[3,1024]{1,0:T(4,128)S(1)}, u32[]{:S(2)}, u32[]{:S(2)}) collective-permute-start(f32[3,1024]{1,0:T(4,128)S(1)} %log_add_fusion.7), channel_id=1, source_target_pairs={{0,64},{32,96},{64,0},{96,32},{1,65},{33,97},{65,1},{97,33},{2,66}... | collective-permute-start | bytes 36872 | tf_op jit(solution)/shard_map/ppermute | solution.py:144
  144.8 7.8 %collective-permute-start.18 = (f32[5,1024]{1,0:T(8,128)S(1)}, f32[5,1024]{1,0:T(8,128)S(1)}, u32[]{:S(2)}, u32[]{:S(2)}) collective-permute-start(f32[5,1024]{1,0:T(8,128)S(1)} %log_add_fusion.1), channel_id=1, source_target_pairs={{0,1},{1,2},{2,3},{3,4},{4,5},{5,6},{6,7},{7,8},{8,9},{9,10},{10,1... | collective-permute-start | bytes 61448 | tf_op jit(solution)/shard_map/ppermute | solution.py:30
  150.7 5.2 %collective-permute-start.19 = (f32[5,1024]{1,0:T(8,128)S(1)}, f32[5,1024]{1,0:T(8,128)S(1)}, u32[]{:S(2)}, u32[]{:S(2)}) collective-permute-start(f32[5,1024]{1,0:T(8,128)S(1)} %log_add_fusion.1), channel_id=1, source_target_pairs={{1,0},{2,1},{3,2},{4,3},{5,4},{6,5},{7,6},{8,7},{9,8},{10,9},{11,1... | collective-permute-start | bytes 61448 | tf_op jit(solution)/shard_map/ppermute | solution.py:30
  156.0 10.5 %collective-permute-start.21 = (f32[7,1024]{1,0:T(8,128)S(1)}, f32[7,1024]{1,0:T(8,128)S(1)}, u32[]{:S(2)}, u32[]{:S(2)}) collective-permute-start(f32[7,1024]{1,0:T(8,128)S(1)} %log_add_fusion), channel_id=1, source_target_pairs={{3,0},{4,1},{5,2},{6,3},{7,4},{8,5},{9,6},{10,7},{11,8},{12,9},{13... | collective-permute-start | bytes 86024 | tf_op jit(solution)/shard_map/ppermute | solution.py:30
  157.4 10.2 %collective-permute-start.22 = (f32[5,1024]{1,0:T(8,128)S(1)}, f32[5,1024]{1,0:T(8,128)S(1)}, u32[]{:S(2)}, u32[]{:S(2)}) collective-permute-start(f32[5,1024]{1,0:T(8,128)S(1)} %log_add_fusion.1), channel_id=1, source_target_pairs={{0,2},{31,29},{32,34},{63,61},{64,66},{95,93},{96,98},{127,125}} | collective-permute-start | bytes 61448 | tf_op jit(solution)/shard_map/ppermute | solution.py:179
  158.0 9.5 %collective-permute-start.20 = (f32[7,1024]{1,0:T(8,128)S(1)}, f32[7,1024]{1,0:T(8,128)S(1)}, u32[]{:S(2)}, u32[]{:S(2)}) collective-permute-start(f32[7,1024]{1,0:T(8,128)S(1)} %log_add_fusion), channel_id=1, source_target_pairs={{0,3},{1,4},{2,5},{3,6},{4,7},{5,8},{6,9},{7,10},{8,11},{9,12},{10... | collective-permute-start | bytes 86024 | tf_op jit(solution)/shard_map/ppermute | solution.py:30
  182.2 11.6 %collective-permute-start.23 = (f32[1,1024]{1,0:T(1,128)S(1)}, f32[1,1024]{1,0:T(1,128)S(1)}, u32[]{:S(2)}, u32[]{:S(2)}) collective-permute-start(f32[1,1024]{1,0:T(1,128)S(1)} %slice.263), channel_id=1, source_target_pairs={{0,1},{1,0},{2,3},{3,2},{4,5},{5,4},{6,7},{7,6},{8,9},{9,8},{10,11... | collective-permute-start | bytes 12296 | tf_op jit(solution)/shard_map/ppermute | solution.py:208
  182.9 13.2 %collective-permute-start.28 = (f32[4,1024]{1,0:T(4,128)S(1)}, f32[4,1024]{1,0:T(4,128)S(1)}, u32[]{:S(2)}, u32[]{:S(2)}) collective-permute-start(f32[4,1024]{1,0:T(4,128)S(1)} %pad_maximum_fusion.6), channel_id=1, source_target_pairs={{0,32},{32,64},{64,96},{1,33},{33,65},{65,97},{2,34},{34,66},{66,9... | collective-permute-start | bytes 49160 | tf_op jit(solution)/shard_map/ppermute | solution.py:30
  186.5 9.6 %collective-permute-start.29 = (f32[4,1024]{1,0:T(4,128)S(1)}, f32[4,1024]{1,0:T(4,128)S(1)}, u32[]{:S(2)}, u32[]{:S(2)}) collective-permute-start(f32[4,1024]{1,0:T(4,128)S(1)} %pad_maximum_fusion.6), channel_id=1, source_target_pairs={{32,0},{64,32},{96,64},{33,1},{65,33},{97,65},{34,2},{66,34},{98,6... | collective-permute-start | bytes 49160 | tf_op jit(solution)/shard_map/ppermute | solution.py:30
  187.8 8.3 %collective-permute-start.30 = (f32[3,1024]{1,0:T(4,128)S(1)}, f32[3,1024]{1,0:T(4,128)S(1)}, u32[]{:S(2)}, u32[]{:S(2)}) collective-permute-start(f32[3,1024]{1,0:T(4,128)S(1)} %log_add_fusion.6), channel_id=1, source_target_pairs={{0,64},{32,96},{64,0},{96,32},{1,65},{33,97},{65,1},{97,33},{2,66}... | collective-permute-start | bytes 36872 | tf_op jit(solution)/shard_map/ppermute | solution.py:144
  193.8 40.0 %collective-permute-start.24 = (f32[2,1024]{1,0:T(2,128)S(1)}, f32[2,1024]{1,0:T(2,128)S(1)}, u32[]{:S(2)}, u32[]{:S(2)}) collective-permute-start(f32[2,1024]{1,0:T(2,128)S(1)} %maximum_select_fusion.4), channel_id=1, source_target_pairs={{0,2},{1,3},{2,0},{3,1},{4,6},{5,7},{6,4},{7,5},{8,10},{9,11},{10,... | collective-permute-start | bytes 24584 | tf_op jit(solution)/shard_map/ppermute | solution.py:208
  216.9 41.3 %collective-permute-start.31 = (f32[1,1024,128]{2,1,0:T(8,128)}, f32[1,1024,128]{2,1,0:T(8,128)S(1)}, u32[]{:S(2)}, u32[]{:S(2)}) collective-permute-start(f32[1,1024,128]{2,1,0:T(8,128)} %get-tuple-element.5), channel_id=1, source_target_pairs={{1,0},{2,1},{3,2},{4,3},{5,4},{6,5},{7,6},{8,7},{9,8},{10,9},{11,1... | collective-permute-start | bytes 1572872 | tf_op jit(solution)/shard_map/ppermute | solution.py:30
  220.4 37.8 %collective-permute-start.32 = (f32[1,1024,128]{2,1,0:T(8,128)}, f32[1,1024,128]{2,1,0:T(8,128)}, u32[]{:S(2)}, u32[]{:S(2)}) collective-permute-start(f32[1,1024,128]{2,1,0:T(8,128)} %get-tuple-element.8), channel_id=1, source_target_pairs={{0,1},{1,2},{2,3},{3,4},{4,5},{5,6},{6,7},{7,8},{8,9},{9,10},{10,1... | collective-permute-start | bytes 1572872 | tf_op jit(solution)/shard_map/ppermute | solution.py:30
  222.5 35.8 %collective-permute-start.33 = (f32[1,1024,128]{2,1,0:T(8,128)}, f32[1,1024,128]{2,1,0:T(8,128)}, u32[]{:S(2)}, u32[]{:S(2)}) collective-permute-start(f32[1,1024,128]{2,1,0:T(8,128)} %get-tuple-element.7), channel_id=1, source_target_pairs={{2,0},{3,1},{4,2},{5,3},{6,4},{7,5},{8,6},{9,7},{10,8},{11,9},{12,... | collective-permute-start | bytes 1572872 | tf_op jit(solution)/shard_map/ppermute | solution.py:30
  223.8 34.5 %collective-permute-start.34 = (f32[1,1024,128]{2,1,0:T(8,128)}, f32[1,1024,128]{2,1,0:T(8,128)}, u32[]{:S(2)}, u32[]{:S(2)}) collective-permute-start(f32[1,1024,128]{2,1,0:T(8,128)} %get-tuple-element.6), channel_id=1, source_target_pairs={{0,2},{1,3},{2,4},{3,5},{4,6},{5,7},{6,8},{7,9},{8,10},{9,11},{10,... | collective-permute-start | bytes 1572872 | tf_op jit(solution)/shard_map/ppermute | solution.py:30
  233.8 15.1 %collective-permute-start.25 = (f32[4,1024]{1,0:T(4,128)S(1)}, f32[4,1024]{1,0:T(4,128)S(1)}, u32[]{:S(2)}, u32[]{:S(2)}) collective-permute-start(f32[4,1024]{1,0:T(4,128)S(1)} %maximum_select_fusion.3), channel_id=1, source_target_pairs={{0,4},{1,5},{2,6},{3,7},{4,0},{5,1},{6,2},{7,3},{8,12},{9,13},{10,... | collective-permute-start | bytes 49160 | tf_op jit(solution)/shard_map/ppermute | solution.py:208
  252.3 5.3 %collective-permute-start.27 = (f32[16,1024]{1,0:T(8,128)S(1)}, f32[16,1024]{1,0:T(8,128)S(1)}, u32[]{:S(2)}, u32[]{:S(2)}) collective-permute-start(f32[16,1024]{1,0:T(8,128)S(1)} %maximum_select_fusion.1), channel_id=1, source_target_pairs={{0,16},{1,17},{2,18},{3,19},{4,20},{5,21},{6,22},{7,23},{8,24},{9,... | collective-permute-start | bytes 196616 | tf_op jit(solution)/shard_map/ppermute | solution.py:208
  (9 other events, 106.0 us)

commit v11 on v8

--- a/solution.py
+++ b/solution.py
@@ -30,10 +30,6 @@
     return lax.ppermute(block, axis, route)
 
 
-def pick(table, position):
-    return lax.dynamic_index_in_dim(table, position, 0, keepdims=False)
-
-
 def squares(points):
     return jnp.sum(jnp.square(points.astype(jnp.float32)), axis=-1)
 
@@ -46,6 +42,7 @@
 EPSILON = 0.03
 INV_EPS = 1.0 / EPSILON
 CHUNK = 1024
+LSE_PARAMS = pltpu.CompilerParams(allow_input_fusion=[False, False, False, False, True])
 KERNEL_PARAMS = pltpu.CompilerParams()
 
 
@@ -79,7 +76,7 @@
         grid_spec=spec,
         out_shape=jax.ShapeDtypeStruct((pairs, 1, rows), jnp.float32),
         interpret=interpret,
-        compiler_params=KERNEL_PARAMS,
+        compiler_params=LSE_PARAMS,
     )(a_ids, b_ids, a_pts, b_pts, v_rows)
 
 
@@ -233,7 +230,7 @@
     span_ids = jnp.clip(source_local - (gy_index - 2) * owned, 0, 5 * owned - 1)
     span_mask = span_ids[None, :] == jnp.arange(5 * owned, dtype=jnp.int32)[:, None]
     window_mask = window_ids[None, :] == jnp.arange(3 * owned, dtype=jnp.int32)[:, None]
-    pair_src_sq = jnp.stack([squares(pick(src_points, source_local[p])) for p in range(source_local.shape[0])])
+    pair_src_sq = squares(src_points[source_local])
     window_pts, window_sq = fetch_points(tgt_points)
     pair_tgt_sq = window_sq[window_ids]
     mass_pad = jnp.zeros((2 * owned,) + src_log_mass.shape[1:], src_log_mass.dtype)

time: 271 us -> 260 us (0.959)
  between operations: 13.1 us -> 1.69 us
  local copies, waits for them, and re-layouts: 14.1 us -> 17.8 us
  other arithmetic: 20.9 us -> 17.5 us
    gather x0 -> x1, local copies, waits for them, and re-layouts: none -> 4.23 us  [body(): pair_src_sq = squares(src_points[source_local])]
where the time goes in v11:
time: 260 us; the launch traced here: 257 us
  starting transfers between devices  107 us (41%)
  Pallas kernels  84.8 us (33%)
  waiting for transfers between devices  28.4 us (11%)
  local copies, waits for them, and re-layouts  17.8 us (7%)
  other arithmetic  17.5 us (7%)
    ppermute x22, starting transfers between devices, passed_along(): return lax.ppermute(block, axis, route)  75.6 us
    pallas_call x6, Pallas kernels, pair_lse(): pl.pallas_call(_lse_kernel, grid_spec=spec, out_shape=jax.ShapeDtypeStruc...  73.7 us
    ppermute x5, waiting for transfers between devices, gather_rows(): other = lax.ppermute(block, axis, route)  13.3 us
    ppermute x5, starting transfers between devices, gather_rows(): other = lax.ppermute(block, axis, route)  13 us
    ppermute x22, waiting for transfers between devices, passed_along(): return lax.ppermute(block, axis, route)  12.8 us
    ppermute x3, starting transfers between devices, spread(): lax.ppermute(block, axis, [(i, (i + reach) % count) for i in range(count)])  11.3 us
    pallas_call x1, Pallas kernels, pair_grad(): pl.pallas_call(_grad_kernel, grid_spec=spec, out_shape=jax.ShapeDtypeStru...  11.1 us
  transfers between devices with their start and end apart: 35, of which 11 were waited for; matrix products, arithmetic and copies ran while one was open for 7% of the time, Pallas kernels for 4%

profile of v11, /device:TPU:1, one launch (start us, length us, event | category | flops | bytes accessed | tf_op | source)
XLA Modules:
  0.0 257.5 jit_solution(637737551492155700)
XLA Ops:
  0.6 4.1 %collective-permute-start = (bf16[1,1024,128]{2,1,0:T(8,128)(2,1)}, bf16[1,1024,128]{2,1,0:T(8,128)(2,1)S(1)}, u32[]{:S(2)}, u32[]{:S(2)}) collective-permute-start(bf16[1,1024,128]{2,1,0:T(8,128)(2,1)} %param.7), channel_id=1, source_target_pairs={{0,32},{32,64},{64,96},{1,33},{33,65},{65,97},{2,34},{34,66},{66,9... | collective-permute-start | bytes 786440 | tf_op jit(solution)/shard_map/ppermute | solution.py:19
  8.2 4.2 %gather_fusion.2 = bf16[6,1024,128]{2,1,0:T(8,128)(2,1)S(1)} fusion(bf16[32,1024,128]{2,1,0:T(8,128)(2,1)} %a_ref.7, s32[1024]{0:T(1024)S(1)} %get-tuple-element.52), kind=kCustom, calls=%fused_computation.2 | custom fusion | bytes 3145752 | tf_op jit(solution)/shard_map/gather | solution.py:233
  15.9 12.4 %shard_map.85 = f32[6,1,1024]{2,1,0:T(1,128)} custom-call(s32[6]{0:T(128)} %bitcast.100, s32[6]{0:T(128)} %get-tuple-element.49.b_ids.a_ids, bf16[32,1024,128]{2,1,0:T(8,128)(2,1)} %a_ref.7, bf16[3,1024,128]{2,1,0:T(8,128)(2,1)} %copy-done, f32[6,8,1024]{2,1,0:T(8,128)} %broadcast_in_dim.240.v_ref), custom_call_target="tpu_custom_call" | custom-call | tf_op jit(solution)/shard_map/pallas_call | solution.py:74
  29.3 4.6 %collective-permute-start.2 = (f32[5,1024]{1,0:T(8,128)S(1)}, f32[5,1024]{1,0:T(8,128)S(1)}, u32[]{:S(2)}, u32[]{:S(2)}) collective-permute-start(f32[5,1024]{1,0:T(8,128)S(1)} %log_add_fusion.5), channel_id=1, source_target_pairs={{0,1},{1,2},{2,3},{3,4},{4,5},{5,6},{6,7},{7,8},{8,9},{9,10},{10,1... | collective-permute-start | bytes 61448 | tf_op jit(solution)/shard_map/ppermute | solution.py:30
  35.9 3.3 %collective-permute-done.3 = f32[5,1024]{1,0:T(8,128)S(1)} collective-permute-done((f32[5,1024]{1,0:T(8,128)S(1)}, f32[5,1024]{1,0:T(8,128)S(1)}, u32[]{:S(2)}, u32[]{:S(2)}) %collective-permute-start.3) | collective-permute-done | bytes 20512 | tf_op jit(solution)/shard_map/ppermute | solution.py:30
  41.3 5.8 %collective-permute-start.4 = (f32[7,1024]{1,0:T(8,128)S(1)}, f32[7,1024]{1,0:T(8,128)S(1)}, u32[]{:S(2)}, u32[]{:S(2)}) collective-permute-start(f32[7,1024]{1,0:T(8,128)S(1)} %log_add_fusion.4), channel_id=1, source_target_pairs={{0,3},{1,4},{2,5},{3,6},{4,7},{5,8},{6,9},{7,10},{8,11},{9,12},{10... | collective-permute-start | bytes 86024 | tf_op jit(solution)/shard_map/ppermute | solution.py:30
  49.5 12.4 %shard_map.86 = f32[6,1,1024]{2,1,0:T(1,128)} custom-call(s32[6]{0:T(128)} %get-tuple-element.49.b_ids.a_ids, s32[6]{0:T(128)} %bitcast.101, bf16[3,1024,128]{2,1,0:T(8,128)(2,1)} %copy-done, bf16[32,1024,128]{2,1,0:T(8,128)(2,1)} %a_ref.7, f32[6,8,1024]{2,1,0:T(8,128)} %broadcast_in_dim.244.v_ref), custom_call_target="tpu_custom_call" | custom-call | tf_op jit(solution)/shard_map/pallas_call | solution.py:74
  62.9 3.7 %collective-permute-start.7 = (f32[4,1024]{1,0:T(4,128)S(1)}, f32[4,1024]{1,0:T(4,128)S(1)}, u32[]{:S(2)}, u32[]{:S(2)}) collective-permute-start(f32[4,1024]{1,0:T(4,128)S(1)} %pad_maximum_fusion.8), channel_id=1, source_target_pairs={{0,32},{32,64},{64,96},{1,33},{33,65},{65,97},{2,34},{34,66},{66,9... | collective-permute-start | bytes 49160 | tf_op jit(solution)/shard_map/ppermute | solution.py:30
  68.0 3.7 %collective-permute-start.9 = (f32[3,1024]{1,0:T(4,128)S(1)}, f32[3,1024]{1,0:T(4,128)S(1)}, u32[]{:S(2)}, u32[]{:S(2)}) collective-permute-start(f32[3,1024]{1,0:T(4,128)S(1)} %log_add_fusion.8), channel_id=1, source_target_pairs={{0,64},{32,96},{64,0},{96,32},{1,65},{33,97},{65,1},{97,33},{2,66}... | collective-permute-start | bytes 36872 | tf_op jit(solution)/shard_map/ppermute | solution.py:144
  74.3 12.2 %shard_map.87 = f32[6,1,1024]{2,1,0:T(1,128)} custom-call(s32[6]{0:T(128)} %bitcast.102, s32[6]{0:T(128)} %get-tuple-element.49.b_ids.a_ids, bf16[32,1024,128]{2,1,0:T(8,128)(2,1)} %a_ref.7, bf16[3,1024,128]{2,1,0:T(8,128)(2,1)} %copy-done, f32[6,8,1024]{2,1,0:T(8,128)} %broadcast_in_dim.249.v_ref), custom_call_target="tpu_custom_call" | custom-call | tf_op jit(solution)/shard_map/pallas_call | solution.py:74
  87.5 3.2 %collective-permute-start.10 = (f32[5,1024]{1,0:T(8,128)S(1)}, f32[5,1024]{1,0:T(8,128)S(1)}, u32[]{:S(2)}, u32[]{:S(2)}) collective-permute-start(f32[5,1024]{1,0:T(8,128)S(1)} %log_add_fusion.3), channel_id=1, source_target_pairs={{0,1},{1,2},{2,3},{3,4},{4,5},{5,6},{6,7},{7,8},{8,9},{9,10},{10,1... | collective-permute-start | bytes 61448 | tf_op jit(solution)/shard_map/ppermute | solution.py:30
  92.7 3.3 %collective-permute-done.11 = f32[5,1024]{1,0:T(8,128)S(1)} collective-permute-done((f32[5,1024]{1,0:T(8,128)S(1)}, f32[5,1024]{1,0:T(8,128)S(1)}, u32[]{:S(2)}, u32[]{:S(2)}) %collective-permute-start.11) | collective-permute-done | bytes 20512 | tf_op jit(solution)/shard_map/ppermute | solution.py:30
  98.0 6.4 %collective-permute-start.12 = (f32[7,1024]{1,0:T(8,128)S(1)}, f32[7,1024]{1,0:T(8,128)S(1)}, u32[]{:S(2)}, u32[]{:S(2)}) collective-permute-start(f32[7,1024]{1,0:T(8,128)S(1)} %log_add_fusion.2), channel_id=1, source_target_pairs={{0,3},{1,4},{2,5},{3,6},{4,7},{5,8},{6,9},{7,10},{8,11},{9,12},{10... | collective-permute-start | bytes 86024 | tf_op jit(solution)/shard_map/ppermute | solution.py:30
  106.9 12.2 %shard_map.88 = f32[6,1,1024]{2,1,0:T(1,128)} custom-call(s32[6]{0:T(128)} %get-tuple-element.49.b_ids.a_ids, s32[6]{0:T(128)} %bitcast.103, bf16[3,1024,128]{2,1,0:T(8,128)(2,1)} %copy-done, bf16[32,1024,128]{2,1,0:T(8,128)(2,1)} %a_ref.7, f32[6,8,1024]{2,1,0:T(8,128)} %broadcast_in_dim.251.v_ref), custom_call_target="tpu_custom_call" | custom-call | tf_op jit(solution)/shard_map/pallas_call | solution.py:74
  120.2 3.6 %collective-permute-start.15 = (f32[4,1024]{1,0:T(4,128)S(1)}, f32[4,1024]{1,0:T(4,128)S(1)}, u32[]{:S(2)}, u32[]{:S(2)}) collective-permute-start(f32[4,1024]{1,0:T(4,128)S(1)} %pad_maximum_fusion.7), channel_id=1, source_target_pairs={{0,32},{32,64},{64,96},{1,33},{33,65},{65,97},{2,34},{34,66},{66,9... | collective-permute-start | bytes 49160 | tf_op jit(solution)/shard_map/ppermute | solution.py:30
  125.1 3.9 %collective-permute-start.17 = (f32[3,1024]{1,0:T(4,128)S(1)}, f32[3,1024]{1,0:T(4,128)S(1)}, u32[]{:S(2)}, u32[]{:S(2)}) collective-permute-start(f32[3,1024]{1,0:T(4,128)S(1)} %log_add_fusion.7), channel_id=1, source_target_pairs={{0,64},{32,96},{64,0},{96,32},{1,65},{33,97},{65,1},{97,33},{2,66}... | collective-permute-start | bytes 36872 | tf_op jit(solution)/shard_map/ppermute | solution.py:144
  131.5 12.2 %shard_map.89 = f32[6,1,1024]{2,1,0:T(1,128)} custom-call(s32[6]{0:T(128)} %bitcast.104, s32[6]{0:T(128)} %get-tuple-element.49.b_ids.a_ids, bf16[32,1024,128]{2,1,0:T(8,128)(2,1)} %a_ref.7, bf16[3,1024,128]{2,1,0:T(8,128)(2,1)} %copy-done, f32[6,8,1024]{2,1,0:T(8,128)} %broadcast_in_dim.253.v_ref), custom_call_target="tpu_custom_call" | custom-call | tf_op jit(solution)/shard_map/pallas_call | solution.py:74
  144.8 5.9 %collective-permute-start.18 = (f32[5,1024]{1,0:T(8,128)S(1)}, f32[5,1024]{1,0:T(8,128)S(1)}, u32[]{:S(2)}, u32[]{:S(2)}) collective-permute-start(f32[5,1024]{1,0:T(8,128)S(1)} %log_add_fusion.1), channel_id=1, source_target_pairs={{0,1},{1,2},{2,3},{3,4},{4,5},{5,6},{6,7},{7,8},{8,9},{9,10},{10,1... | collective-permute-start | bytes 61448 | tf_op jit(solution)/shard_map/ppermute | solution.py:30
  152.6 3.3 %collective-permute-done.19 = f32[5,1024]{1,0:T(8,128)S(1)} collective-permute-done((f32[5,1024]{1,0:T(8,128)S(1)}, f32[5,1024]{1,0:T(8,128)S(1)}, u32[]{:S(2)}, u32[]{:S(2)}) %collective-permute-start.19) | collective-permute-done | bytes 20512 | tf_op jit(solution)/shard_map/ppermute | solution.py:30
  158.0 8.5 %collective-permute-start.20 = (f32[7,1024]{1,0:T(8,128)S(1)}, f32[7,1024]{1,0:T(8,128)S(1)}, u32[]{:S(2)}, u32[]{:S(2)}) collective-permute-start(f32[7,1024]{1,0:T(8,128)S(1)} %log_add_fusion), channel_id=1, source_target_pairs={{0,3},{1,4},{2,5},{3,6},{4,7},{5,8},{6,9},{7,10},{8,11},{9,12},{10... | collective-permute-start | bytes 86024 | tf_op jit(solution)/shard_map/ppermute | solution.py:30
  168.9 12.2 %shard_map.90 = f32[6,1,1024]{2,1,0:T(1,128)} custom-call(s32[6]{0:T(128)} %get-tuple-element.49.b_ids.a_ids, s32[6]{0:T(128)} %bitcast.105, bf16[3,1024,128]{2,1,0:T(8,128)(2,1)} %copy-done, bf16[32,1024,128]{2,1,0:T(8,128)(2,1)} %a_ref.7, f32[6,8,1024]{2,1,0:T(8,128)} %broadcast_in_dim.255.v_ref), custom_call_target="tpu_custom_call" | custom-call | tf_op jit(solution)/shard_map/pallas_call | solution.py:74
  182.9 3.6 %collective-permute-start.28 = (f32[4,1024]{1,0:T(4,128)S(1)}, f32[4,1024]{1,0:T(4,128)S(1)}, u32[]{:S(2)}, u32[]{:S(2)}) collective-permute-start(f32[4,1024]{1,0:T(4,128)S(1)} %pad_maximum_fusion.6), channel_id=1, source_target_pairs={{0,32},{32,64},{64,96},{1,33},{33,65},{65,97},{2,34},{34,66},{66,9... | collective-permute-start | bytes 49160 | tf_op jit(solution)/shard_map/ppermute | solution.py:30
  187.8 3.7 %collective-permute-start.30 = (f32[3,1024]{1,0:T(4,128)S(1)}, f32[3,1024]{1,0:T(4,128)S(1)}, u32[]{:S(2)}, u32[]{:S(2)}) collective-permute-start(f32[3,1024]{1,0:T(4,128)S(1)} %log_add_fusion.6), channel_id=1, source_target_pairs={{0,64},{32,96},{64,0},{96,32},{1,65},{33,97},{65,1},{97,33},{2,66}... | collective-permute-start | bytes 36872 | tf_op jit(solution)/shard_map/ppermute | solution.py:144
  193.8 2.4 collective-permute-start.24
  197.5 11.1 %shard_map.91 = f32[6,1024,128]{2,1,0:T(8,128)} custom-call(s32[6]{0:T(128)} %bitcast.106, s32[6]{0:T(128)} %get-tuple-element.49.b_ids.a_ids, bf16[32,1024,128]{2,1,0:T(8,128)(2,1)} %a_ref.7, bf16[3,1024,128]{2,1,0:T(8,128)(2,1)} %copy-done, f32[6,1,1024]{2,1,0:T(1,128)} %div.120.v_ref, f32[6,1024,1]{2,1,0:T(8,128)} %copy.11.w_ref), custom_call_target="tpu_custom_call" | custom-call | tf_op jit(solution)/shard_map/pallas_call | solution.py:109
  208.7 3.8 %select_reduce_fusion = f32[5,1024,128]{2,1,0:T(8,128)S(1)} fusion(f32[6,1024,128]{2,1,0:T(8,128)} %shard_map.91, pred[5,6]{1,0:T(8,128)(4,1)S(1)} %iota_compare_fusion.1), kind=kLoop, calls=%fused_computation.9 | loop fusion | flops 7208960 | bytes 5767198 | tf_op jit(solution)/shard_map/reduce_sum | solution.py:264
  213.8 3.5 %collective-permute-start.31 = (f32[1,1024,128]{2,1,0:T(8,128)}, f32[1,1024,128]{2,1,0:T(8,128)S(1)}, u32[]{:S(2)}, u32[]{:S(2)}) collective-permute-start(f32[1,1024,128]{2,1,0:T(8,128)} %get-tuple-element.5), channel_id=1, source_target_pairs={{1,0},{2,1},{3,2},{4,3},{5,4},{6,5},{7,6},{8,7},{9,8},{10,9},{11,1... | collective-permute-start | bytes 1572872 | tf_op jit(solution)/shard_map/ppermute | solution.py:30
  220.7 10.0 %collective-permute-start.34 = (f32[1,1024,128]{2,1,0:T(8,128)}, f32[1,1024,128]{2,1,0:T(8,128)}, u32[]{:S(2)}, u32[]{:S(2)}) collective-permute-start(f32[1,1024,128]{2,1,0:T(8,128)} %get-tuple-element.6), channel_id=1, source_target_pairs={{0,2},{1,3},{2,4},{3,5},{4,6},{5,7},{6,8},{7,9},{8,10},{9,11},{10,... | collective-permute-start | bytes 1572872 | tf_op jit(solution)/shard_map/ppermute | solution.py:30
  230.7 4.2 %collective-permute-start.25 = (f32[4,1024]{1,0:T(4,128)S(1)}, f32[4,1024]{1,0:T(4,128)S(1)}, u32[]{:S(2)}, u32[]{:S(2)}) collective-permute-start(f32[4,1024]{1,0:T(4,128)S(1)} %maximum_select_fusion.3), channel_id=1, source_target_pairs={{0,4},{1,5},{2,6},{3,7},{4,0},{5,1},{6,2},{7,3},{8,12},{9,13},{10,... | collective-permute-start | bytes 49160 | tf_op jit(solution)/shard_map/ppermute | solution.py:208
  234.9 10.9 %collective-permute-done.25 = f32[4,1024]{1,0:T(4,128)S(1)} collective-permute-done((f32[4,1024]{1,0:T(4,128)S(1)}, f32[4,1024]{1,0:T(4,128)S(1)}, u32[]{:S(2)}, u32[]{:S(2)}) %collective-permute-start.25) | collective-permute-done | bytes 16416 | tf_op jit(solution)/shard_map/ppermute | solution.py:208
  249.2 3.6 %collective-permute-start.27 = (f32[16,1024]{1,0:T(8,128)S(1)}, f32[16,1024]{1,0:T(8,128)S(1)}, u32[]{:S(2)}, u32[]{:S(2)}) collective-permute-start(f32[16,1024]{1,0:T(8,128)S(1)} %maximum_select_fusion.1), channel_id=1, source_target_pairs={{0,16},{1,17},{2,18},{3,19},{4,20},{5,21},{6,22},{7,23},{8,24},{9,... | collective-permute-start | bytes 196616 | tf_op jit(solution)/shard_map/ppermute | solution.py:208
  255.2 2.3 fusion.2
  (186 shorter events, 55.7 us)
Async XLA Ops:
  0.6 13.3 %collective-permute-start = (bf16[1,1024,128]{2,1,0:T(8,128)(2,1)}, bf16[1,1024,128]{2,1,0:T(8,128)(2,1)S(1)}, u32[]{:S(2)}, u32[]{:S(2)}) collective-permute-start(bf16[1,1024,128]{2,1,0:T(8,128)(2,1)} %param.7), channel_id=1, source_target_pairs={{0,32},{32,64},{64,96},{1,33},{33,65},{65,97},{2,34},{34,66},{66,9... | collective-permute-start | bytes 786440 | tf_op jit(solution)/shard_map/ppermute | solution.py:19
  4.7 9.3 %collective-permute-start.1 = (bf16[1,1024,128]{2,1,0:T(8,128)(2,1)}, bf16[1,1024,128]{2,1,0:T(8,128)(2,1)S(1)}, u32[]{:S(2)}, u32[]{:S(2)}) collective-permute-start(bf16[1,1024,128]{2,1,0:T(8,128)(2,1)} %param.7), channel_id=1, source_target_pairs={{32,0},{64,32},{96,64},{33,1},{65,33},{97,65},{34,2},{66,34},{98,6... | collective-permute-start | bytes 786440 | tf_op jit(solution)/shard_map/ppermute | solution.py:22
  29.3 6.5 %collective-permute-start.2 = (f32[5,1024]{1,0:T(8,128)S(1)}, f32[5,1024]{1,0:T(8,128)S(1)}, u32[]{:S(2)}, u32[]{:S(2)}) collective-permute-start(f32[5,1024]{1,0:T(8,128)S(1)} %log_add_fusion.5), channel_id=1, source_target_pairs={{0,1},{1,2},{2,3},{3,4},{4,5},{5,6},{6,7},{7,8},{8,9},{9,10},{10,1... | collective-permute-start | bytes 61448 | tf_op jit(solution)/shard_map/ppermute | solution.py:30
  33.9 5.2 %collective-permute-start.3 = (f32[5,1024]{1,0:T(8,128)S(1)}, f32[5,1024]{1,0:T(8,128)S(1)}, u32[]{:S(2)}, u32[]{:S(2)}) collective-permute-start(f32[5,1024]{1,0:T(8,128)S(1)} %log_add_fusion.5), channel_id=1, source_target_pairs={{1,0},{2,1},{3,2},{4,3},{5,4},{6,5},{7,6},{8,7},{9,8},{10,9},{11,1... | collective-permute-start | bytes 61448 | tf_op jit(solution)/shard_map/ppermute | solution.py:30
  39.2 7.8 %collective-permute-start.5 = (f32[7,1024]{1,0:T(8,128)S(1)}, f32[7,1024]{1,0:T(8,128)S(1)}, u32[]{:S(2)}, u32[]{:S(2)}) collective-permute-start(f32[7,1024]{1,0:T(8,128)S(1)} %log_add_fusion.4), channel_id=1, source_target_pairs={{3,0},{4,1},{5,2},{6,3},{7,4},{8,5},{9,6},{10,7},{11,8},{12,9},{13... | collective-permute-start | bytes 86024 | tf_op jit(solution)/shard_map/ppermute | solution.py:30
  40.6 7.5 %collective-permute-start.6 = (f32[5,1024]{1,0:T(8,128)S(1)}, f32[5,1024]{1,0:T(8,128)S(1)}, u32[]{:S(2)}, u32[]{:S(2)}) collective-permute-start(f32[5,1024]{1,0:T(8,128)S(1)} %log_add_fusion.5), channel_id=1, source_target_pairs={{0,2},{31,29},{32,34},{63,61},{64,66},{95,93},{96,98},{127,125}} | collective-permute-start | bytes 61448 | tf_op jit(solution)/shard_map/ppermute | solution.py:179
  41.3 6.8 %collective-permute-start.4 = (f32[7,1024]{1,0:T(8,128)S(1)}, f32[7,1024]{1,0:T(8,128)S(1)}, u32[]{:S(2)}, u32[]{:S(2)}) collective-permute-start(f32[7,1024]{1,0:T(8,128)S(1)} %log_add_fusion.4), channel_id=1, source_target_pairs={{0,3},{1,4},{2,5},{3,6},{4,7},{5,8},{6,9},{7,10},{8,11},{9,12},{10... | collective-permute-start | bytes 86024 | tf_op jit(solution)/shard_map/ppermute | solution.py:30
  62.9 8.8 %collective-permute-start.7 = (f32[4,1024]{1,0:T(4,128)S(1)}, f32[4,1024]{1,0:T(4,128)S(1)}, u32[]{:S(2)}, u32[]{:S(2)}) collective-permute-start(f32[4,1024]{1,0:T(4,128)S(1)} %pad_maximum_fusion.8), channel_id=1, source_target_pairs={{0,32},{32,64},{64,96},{1,33},{33,65},{65,97},{2,34},{34,66},{66,9... | collective-permute-start | bytes 49160 | tf_op jit(solution)/shard_map/ppermute | solution.py:30
  87.5 5.1 %collective-permute-start.10 = (f32[5,1024]{1,0:T(8,128)S(1)}, f32[5,1024]{1,0:T(8,128)S(1)}, u32[]{:S(2)}, u32[]{:S(2)}) collective-permute-start(f32[5,1024]{1,0:T(8,128)S(1)} %log_add_fusion.3), channel_id=1, source_target_pairs={{0,1},{1,2},{2,3},{3,4},{4,5},{5,6},{6,7},{7,8},{8,9},{9,10},{10,1... | collective-permute-start | bytes 61448 | tf_op jit(solution)/shard_map/ppermute | solution.py:30
  90.7 5.2 %collective-permute-start.11 = (f32[5,1024]{1,0:T(8,128)S(1)}, f32[5,1024]{1,0:T(8,128)S(1)}, u32[]{:S(2)}, u32[]{:S(2)}) collective-permute-start(f32[5,1024]{1,0:T(8,128)S(1)} %log_add_fusion.3), channel_id=1, source_target_pairs={{1,0},{2,1},{3,2},{4,3},{5,4},{6,5},{7,6},{8,7},{9,8},{10,9},{11,1... | collective-permute-start | bytes 61448 | tf_op jit(solution)/shard_map/ppermute | solution.py:30
  96.1 8.4 %collective-permute-start.13 = (f32[7,1024]{1,0:T(8,128)S(1)}, f32[7,1024]{1,0:T(8,128)S(1)}, u32[]{:S(2)}, u32[]{:S(2)}) collective-permute-start(f32[7,1024]{1,0:T(8,128)S(1)} %log_add_fusion.2), channel_id=1, source_target_pairs={{3,0},{4,1},{5,2},{6,3},{7,4},{8,5},{9,6},{10,7},{11,8},{12,9},{13... | collective-permute-start | bytes 86024 | tf_op jit(solution)/shard_map/ppermute | solution.py:30
  97.4 8.1 %collective-permute-start.14 = (f32[5,1024]{1,0:T(8,128)S(1)}, f32[5,1024]{1,0:T(8,128)S(1)}, u32[]{:S(2)}, u32[]{:S(2)}) collective-permute-start(f32[5,1024]{1,0:T(8,128)S(1)} %log_add_fusion.3), channel_id=1, source_target_pairs={{0,2},{31,29},{32,34},{63,61},{64,66},{95,93},{96,98},{127,125}} | collective-permute-start | bytes 61448 | tf_op jit(solution)/shard_map/ppermute | solution.py:179
  98.0 7.5 %collective-permute-start.12 = (f32[7,1024]{1,0:T(8,128)S(1)}, f32[7,1024]{1,0:T(8,128)S(1)}, u32[]{:S(2)}, u32[]{:S(2)}) collective-permute-start(f32[7,1024]{1,0:T(8,128)S(1)} %log_add_fusion.2), channel_id=1, source_target_pairs={{0,3},{1,4},{2,5},{3,6},{4,7},{5,8},{6,9},{7,10},{8,11},{9,12},{10... | collective-permute-start | bytes 86024 | tf_op jit(solution)/shard_map/ppermute | solution.py:30
  120.2 8.8 %collective-permute-start.15 = (f32[4,1024]{1,0:T(4,128)S(1)}, f32[4,1024]{1,0:T(4,128)S(1)}, u32[]{:S(2)}, u32[]{:S(2)}) collective-permute-start(f32[4,1024]{1,0:T(4,128)S(1)} %pad_maximum_fusion.7), channel_id=1, source_target_pairs={{0,32},{32,64},{64,96},{1,33},{33,65},{65,97},{2,34},{34,66},{66,9... | collective-permute-start | bytes 49160 | tf_op jit(solution)/shard_map/ppermute | solution.py:30
  123.8 5.2 %collective-permute-start.16 = (f32[4,1024]{1,0:T(4,128)S(1)}, f32[4,1024]{1,0:T(4,128)S(1)}, u32[]{:S(2)}, u32[]{:S(2)}) collective-permute-start(f32[4,1024]{1,0:T(4,128)S(1)} %pad_maximum_fusion.7), channel_id=1, source_target_pairs={{32,0},{64,32},{96,64},{33,1},{65,33},{97,65},{34,2},{66,34},{98,6... | collective-permute-start | bytes 49160 | tf_op jit(solution)/shard_map/ppermute | solution.py:30
  125.1 5.0 %collective-permute-start.17 = (f32[3,1024]{1,0:T(4,128)S(1)}, f32[3,1024]{1,0:T(4,128)S(1)}, u32[]{:S(2)}, u32[]{:S(2)}) collective-permute-start(f32[3,1024]{1,0:T(4,128)S(1)} %log_add_fusion.7), channel_id=1, source_target_pairs={{0,64},{32,96},{64,0},{96,32},{1,65},{33,97},{65,1},{97,33},{2,66}... | collective-permute-start | bytes 36872 | tf_op jit(solution)/shard_map/ppermute | solution.py:144
  144.8 7.8 %collective-permute-start.18 = (f32[5,1024]{1,0:T(8,128)S(1)}, f32[5,1024]{1,0:T(8,128)S(1)}, u32[]{:S(2)}, u32[]{:S(2)}) collective-permute-start(f32[5,1024]{1,0:T(8,128)S(1)} %log_add_fusion.1), channel_id=1, source_target_pairs={{0,1},{1,2},{2,3},{3,4},{4,5},{5,6},{6,7},{7,8},{8,9},{9,10},{10,1... | collective-permute-start | bytes 61448 | tf_op jit(solution)/shard_map/ppermute | solution.py:30
  150.7 5.2 %collective-permute-start.19 = (f32[5,1024]{1,0:T(8,128)S(1)}, f32[5,1024]{1,0:T(8,128)S(1)}, u32[]{:S(2)}, u32[]{:S(2)}) collective-permute-start(f32[5,1024]{1,0:T(8,128)S(1)} %log_add_fusion.1), channel_id=1, source_target_pairs={{1,0},{2,1},{3,2},{4,3},{5,4},{6,5},{7,6},{8,7},{9,8},{10,9},{11,1... | collective-permute-start | bytes 61448 | tf_op jit(solution)/shard_map/ppermute | solution.py:30
  156.0 10.5 %collective-permute-start.21 = (f32[7,1024]{1,0:T(8,128)S(1)}, f32[7,1024]{1,0:T(8,128)S(1)}, u32[]{:S(2)}, u32[]{:S(2)}) collective-permute-start(f32[7,1024]{1,0:T(8,128)S(1)} %log_add_fusion), channel_id=1, source_target_pairs={{3,0},{4,1},{5,2},{6,3},{7,4},{8,5},{9,6},{10,7},{11,8},{12,9},{13... | collective-permute-start | bytes 86024 | tf_op jit(solution)/shard_map/ppermute | solution.py:30
  157.4 10.2 %collective-permute-start.22 = (f32[5,1024]{1,0:T(8,128)S(1)}, f32[5,1024]{1,0:T(8,128)S(1)}, u32[]{:S(2)}, u32[]{:S(2)}) collective-permute-start(f32[5,1024]{1,0:T(8,128)S(1)} %log_add_fusion.1), channel_id=1, source_target_pairs={{0,2},{31,29},{32,34},{63,61},{64,66},{95,93},{96,98},{127,125}} | collective-permute-start | bytes 61448 | tf_op jit(solution)/shard_map/ppermute | solution.py:179
  158.0 9.5 %collective-permute-start.20 = (f32[7,1024]{1,0:T(8,128)S(1)}, f32[7,1024]{1,0:T(8,128)S(1)}, u32[]{:S(2)}, u32[]{:S(2)}) collective-permute-start(f32[7,1024]{1,0:T(8,128)S(1)} %log_add_fusion), channel_id=1, source_target_pairs={{0,3},{1,4},{2,5},{3,6},{4,7},{5,8},{6,9},{7,10},{8,11},{9,12},{10... | collective-permute-start | bytes 86024 | tf_op jit(solution)/shard_map/ppermute | solution.py:30
  182.2 11.6 %collective-permute-start.23 = (f32[1,1024]{1,0:T(1,128)S(1)}, f32[1,1024]{1,0:T(1,128)S(1)}, u32[]{:S(2)}, u32[]{:S(2)}) collective-permute-start(f32[1,1024]{1,0:T(1,128)S(1)} %slice.263), channel_id=1, source_target_pairs={{0,1},{1,0},{2,3},{3,2},{4,5},{5,4},{6,7},{7,6},{8,9},{9,8},{10,11... | collective-permute-start | bytes 12296 | tf_op jit(solution)/shard_map/ppermute | solution.py:208
  182.9 13.2 %collective-permute-start.28 = (f32[4,1024]{1,0:T(4,128)S(1)}, f32[4,1024]{1,0:T(4,128)S(1)}, u32[]{:S(2)}, u32[]{:S(2)}) collective-permute-start(f32[4,1024]{1,0:T(4,128)S(1)} %pad_maximum_fusion.6), channel_id=1, source_target_pairs={{0,32},{32,64},{64,96},{1,33},{33,65},{65,97},{2,34},{34,66},{66,9... | collective-permute-start | bytes 49160 | tf_op jit(solution)/shard_map/ppermute | solution.py:30
  186.5 9.6 %collective-permute-start.29 = (f32[4,1024]{1,0:T(4,128)S(1)}, f32[4,1024]{1,0:T(4,128)S(1)}, u32[]{:S(2)}, u32[]{:S(2)}) collective-permute-start(f32[4,1024]{1,0:T(4,128)S(1)} %pad_maximum_fusion.6), channel_id=1, source_target_pairs={{32,0},{64,32},{96,64},{33,1},{65,33},{97,65},{34,2},{66,34},{98,6... | collective-permute-start | bytes 49160 | tf_op jit(solution)/shard_map/ppermute | solution.py:30
  187.8 8.3 %collective-permute-start.30 = (f32[3,1024]{1,0:T(4,128)S(1)}, f32[3,1024]{1,0:T(4,128)S(1)}, u32[]{:S(2)}, u32[]{:S(2)}) collective-permute-start(f32[3,1024]{1,0:T(4,128)S(1)} %log_add_fusion.6), channel_id=1, source_target_pairs={{0,64},{32,96},{64,0},{96,32},{1,65},{33,97},{65,1},{97,33},{2,66}... | collective-permute-start | bytes 36872 | tf_op jit(solution)/shard_map/ppermute | solution.py:144
  193.8 36.9 %collective-permute-start.24 = (f32[2,1024]{1,0:T(2,128)S(1)}, f32[2,1024]{1,0:T(2,128)S(1)}, u32[]{:S(2)}, u32[]{:S(2)}) collective-permute-start(f32[2,1024]{1,0:T(2,128)S(1)} %maximum_select_fusion.4), channel_id=1, source_target_pairs={{0,2},{1,3},{2,0},{3,1},{4,6},{5,7},{6,4},{7,5},{8,10},{9,11},{10,... | collective-permute-start | bytes 24584 | tf_op jit(solution)/shard_map/ppermute | solution.py:208
  213.8 41.4 %collective-permute-start.31 = (f32[1,1024,128]{2,1,0:T(8,128)}, f32[1,1024,128]{2,1,0:T(8,128)S(1)}, u32[]{:S(2)}, u32[]{:S(2)}) collective-permute-start(f32[1,1024,128]{2,1,0:T(8,128)} %get-tuple-element.5), channel_id=1, source_target_pairs={{1,0},{2,1},{3,2},{4,3},{5,4},{6,5},{7,6},{8,7},{9,8},{10,9},{11,1... | collective-permute-start | bytes 1572872 | tf_op jit(solution)/shard_map/ppermute | solution.py:30
  217.3 37.9 %collective-permute-start.32 = (f32[1,1024,128]{2,1,0:T(8,128)}, f32[1,1024,128]{2,1,0:T(8,128)}, u32[]{:S(2)}, u32[]{:S(2)}) collective-permute-start(f32[1,1024,128]{2,1,0:T(8,128)} %get-tuple-element.8), channel_id=1, source_target_pairs={{0,1},{1,2},{2,3},{3,4},{4,5},{5,6},{6,7},{7,8},{8,9},{9,10},{10,1... | collective-permute-start | bytes 1572872 | tf_op jit(solution)/shard_map/ppermute | solution.py:30
  219.4 35.8 %collective-permute-start.33 = (f32[1,1024,128]{2,1,0:T(8,128)}, f32[1,1024,128]{2,1,0:T(8,128)}, u32[]{:S(2)}, u32[]{:S(2)}) collective-permute-start(f32[1,1024,128]{2,1,0:T(8,128)} %get-tuple-element.7), channel_id=1, source_target_pairs={{2,0},{3,1},{4,2},{5,3},{6,4},{7,5},{8,6},{9,7},{10,8},{11,9},{12,... | collective-permute-start | bytes 1572872 | tf_op jit(solution)/shard_map/ppermute | solution.py:30
  220.7 34.5 %collective-permute-start.34 = (f32[1,1024,128]{2,1,0:T(8,128)}, f32[1,1024,128]{2,1,0:T(8,128)}, u32[]{:S(2)}, u32[]{:S(2)}) collective-permute-start(f32[1,1024,128]{2,1,0:T(8,128)} %get-tuple-element.6), channel_id=1, source_target_pairs={{0,2},{1,3},{2,4},{3,5},{4,6},{5,7},{6,8},{7,9},{8,10},{9,11},{10,... | collective-permute-start | bytes 1572872 | tf_op jit(solution)/shard_map/ppermute | solution.py:30
  230.7 15.1 %collective-permute-start.25 = (f32[4,1024]{1,0:T(4,128)S(1)}, f32[4,1024]{1,0:T(4,128)S(1)}, u32[]{:S(2)}, u32[]{:S(2)}) collective-permute-start(f32[4,1024]{1,0:T(4,128)S(1)} %maximum_select_fusion.3), channel_id=1, source_target_pairs={{0,4},{1,5},{2,6},{3,7},{4,0},{5,1},{6,2},{7,3},{8,12},{9,13},{10,... | collective-permute-start | bytes 49160 | tf_op jit(solution)/shard_map/ppermute | solution.py:208
  249.2 5.3 %collective-permute-start.27 = (f32[16,1024]{1,0:T(8,128)S(1)}, f32[16,1024]{1,0:T(8,128)S(1)}, u32[]{:S(2)}, u32[]{:S(2)}) collective-permute-start(f32[16,1024]{1,0:T(8,128)S(1)} %maximum_select_fusion.1), channel_id=1, source_target_pairs={{0,16},{1,17},{2,18},{3,19},{4,20},{5,21},{6,22},{7,23},{8,24},{9,... | collective-permute-start | bytes 196616 | tf_op jit(solution)/shard_map/ppermute | solution.py:208
  (9 other events, 106.0 us)
